TPU v7x, 256 devices: a whole 4x4x8 slice. The times are simulated.
256 devices in a mesh: node: 8 (over z_lo, core), drow: 4 (over x), dcol: 8 (over z_hi, y).
Axes of the slice: x: 4, y: 4, z: 8 (z_hi: 2, z_lo: 4; z = z_hi * 4 + z_lo), core: 2. Of those that a mesh axis runs over, the one named last changes fastest.
Arguments:
- freq_resp: bfloat16 [2, 8, 4096, 8192], P(None, None, ('drow', 'dcol'), 'node'), may hold values from -0.0625 to 0.0625
- node_coords: int32 [2, 8192], P(None, 'node'), may hold values from 0 to 1023
- heading_steps: int32 [2, 512], replicated, may hold values from -8 to 8
- spectral_weights: int32 [8, 512], replicated, may hold values from 1 to 64
Outputs:
- cross_spectra: float32 [2, 8, 4, 1024, 4096], P(None, None, 'drow', 'node', 'dcol')
All inputs are finite; a program needn't handle non-finite values.
Results may differ from a plain program's by a relative error of at most 0.0038.
Values may be sent and summed in bfloat16 or wider, within the bound.
No kernel may reach another device: no remote copies, remote signals or barrier semaphores. Data moves between devices by JAX's collectives and lax.ppermute only.
A program may use at most 128 MiB of HBM per device.

v0:
```python
import math

import jax
import jax.numpy as jnp
from jax import lax
from jax.sharding import PartitionSpec as P

DIRS = 512
FREQS = 8
GRID = 1024


def excitation(coords, heading_steps, spectral_weights):
    freq_index = (jnp.arange(FREQS, dtype=jnp.int32) + 1)[:, None, None]
    project = (
        coords[0][:, None] * heading_steps[0][None, :]
        + coords[1][:, None] * heading_steps[1][None, :]
    )
    turn_count = jnp.mod(freq_index * project[None], GRID)
    phase_angle = turn_count.astype(jnp.float32) * (2.0 * math.pi / GRID)
    spread = jnp.sqrt(spectral_weights.astype(jnp.float32) / (64.0 * DIRS))[:, None, :]
    load_re = (spread * jnp.cos(phase_angle)).astype(jnp.bfloat16)
    load_im = (-spread * jnp.sin(phase_angle)).astype(jnp.bfloat16)
    return (load_re, load_im)


def local(freq_resp, node_coords, heading_steps, spectral_weights):
    load_re, load_im = excitation(node_coords, heading_steps, spectral_weights)
    right_re = jnp.concatenate([load_re, load_im], axis=1)
    right_im = jnp.concatenate([load_im, load_re], axis=1)
    left_re = jnp.concatenate([freq_resp[0], -freq_resp[1]], axis=2)
    left_im = jnp.concatenate([freq_resp[0], freq_resp[1]], axis=2)
    amp_re = jnp.einsum("fkn,fnd->kfd", left_re, right_re, preferred_element_type=jnp.float32)
    amp_im = jnp.einsum("fkn,fnd->kfd", left_im, right_im, preferred_element_type=jnp.float32)
    partial_amp = jnp.stack([amp_re, amp_im], axis=1)
    by_dirs = lax.psum_scatter(partial_amp, "node", scatter_dimension=3, tiled=True).astype(
        jnp.bfloat16
    )
    amplitudes = lax.all_to_all(by_dirs, "node", split_axis=0, concat_axis=3, tiled=True)
    colset = lax.all_gather(amplitudes[None], ("node", "drow"), axis=0, tiled=True)
    col_cat = jnp.concatenate([colset[:, :, 0], colset[:, :, 1]], axis=-1)
    row_piece = lax.all_gather(amplitudes, "dcol", axis=0, tiled=True)
    lead_re = jnp.concatenate([row_piece[:, 0], row_piece[:, 1]], axis=-1)
    lead_im = jnp.concatenate([row_piece[:, 1], -row_piece[:, 0]], axis=-1)
    spec_re = jnp.einsum("kfe,gsfe->fkgs", lead_re, col_cat, preferred_element_type=jnp.float32)
    spec_im = jnp.einsum("kfe,gsfe->fkgs", lead_im, col_cat, preferred_element_type=jnp.float32)
    col_width = spec_re.shape[2] * spec_re.shape[3]
    spec_re = spec_re.reshape(spec_re.shape[0], spec_re.shape[1], col_width)
    spec_im = spec_im.reshape(spec_im.shape[0], spec_im.shape[1], col_width)
    return jnp.stack([spec_re, spec_im], axis=0)[:, :, None]


def solution(mesh):
    placed = (P(None, None, ("drow", "dcol"), "node"), P(None, "node"), P(), P())
    return jax.shard_map(
        local,
        mesh=mesh,
        in_specs=placed,
        out_specs=P(None, None, "drow", "node", "dcol"),
        check_vma=False,
    )
```

profile of v0, /device:TPU:33, one launch (start us, length us, event | category | flops | bytes accessed | tf_op | source)
XLA Modules:
  0.0 400.1 jit_solution(3338056714122250045)
XLA Ops:
  6.5 2.8 slice_bitcast_fusion
  9.4 0.6 copy-done
  10.0 0.1 fusion.33
  10.2 0.5 copy-done.5
  10.7 0.4 multiply_add_fusion
  11.1 71.0 %multiply_convert_fusion = (bf16[8,1024,512]{1,2,0:T(8,128)(2,1)}, bf16[8,1024,512]{1,2,0:T(8,128)(2,1)}) fusion(f32[8,512]{1,0:T(8,128)S(1)} %get-tuple-element.13, s32[1024,512]{0,1:T(8,128)S(1)} %multiply_add_fusion, s32[8]{0:T(128)S(1)} %iota_add_fusion, f32[8,512]{1,0:T(8,128)S(1)} %get-tuple-element.14), kind=kLoop, calls=%fused_computation.16 | loop fusion | flops 75497472 | bytes 18907168 | tf_op jit(solution)/shard_map/convert_element_type | solution.py:23
  82.1 9.2 %fusion.21 = f32[128,1,8,512]{0,3,2,1:T(8,128)} fusion(bf16[8,128,1024]{2,1,0:T(8,128)(2,1)S(1)} %get-tuple-element.8, bf16[8,128,1024]{2,1,0:T(8,128)(2,1)S(1)} %get-tuple-element.7, bf16[8,1024,512]{1,2,0:T(8,128)(2,1)} %get-tuple-element.10, bf16[8,1024,512]{1,2,0:T(8,128)(2,1)} %get-tuple-element.9), kind=kOutput, calls=%fused_computation.40 | convolution fusion | flops 2189426688 | bytes 23068672 | tf_op jit(solution)/shard_map/fkn,fnd->kfd/dot_general | solution.py:34
  91.3 9.3 %fusion.24 = f32[128,1,8,512]{0,3,2,1:T(8,128)} fusion(bf16[8,128,1024]{2,1,0:T(8,128)(2,1)S(1)} %get-tuple-element.8, bf16[8,128,1024]{2,1,0:T(8,128)(2,1)S(1)} %fusion.33, bf16[8,1024,512]{1,2,0:T(8,128)(2,1)} %get-tuple-element.9, bf16[8,1024,512]{1,2,0:T(8,128)(2,1)} %get-tuple-element.10), kind=kOutput, calls=%fused_computation.41 | convolution fusion | flops 2189426688 | bytes 23068672 | tf_op jit(solution)/shard_map/fkn,fnd->kfd/dot_general | solution.py:33
  100.6 3.9 pad_maximum_fusion.5
  104.6 0.0 all-gather.3.cloned.1.call-start
  104.6 56.3 %reduce-scatter.2.cloned.1.call-done = f32[128,2,8,64]{0,3,2,1:T(8,128)} async-done(((f32[128,2,8,512]{0,3,2,1:T(8,128)}), f32[128,2,8,64]{0,3,2,1:T(8,128)}) %reduce-scatter.2.cloned.1.call-update) | async-done | bytes 524304 | tf_op jit(solution)/shard_map/reduce_scatter | solution.py:36
  160.9 1.1 convert_element_type.19
  162.0 0.4 copy.14
  162.4 0.4 reshape.71
  162.8 12.1 %all_to_all.18 = bf16[8,2,8192]{2,1,0:T(2,128)(2,1)S(1)} all-to-all(bf16[8,2,8192]{2,1,0:T(2,128)(2,1)S(1)} %reshape.71), channel_id=1, replica_groups=mesh['node'=8,'drow'=4,'dcol'=8] {'node'}, dimensions={0} | all-to-all | bytes 524288 | tf_op jit(solution)/shard_map/all_to_all | solution.py:39
  174.9 0.3 reshape.72
  175.3 0.3 copy.15
  175.6 1.0 all_to_all.16
  176.7 0.0 all-gather.5.cloned.1.call-start
  176.7 0.6 copy.16
  177.3 1.0 broadcast_in_dim.4
  178.4 74.2 %all-gather.3.cloned.1.call-done = bf16[128,2,8,512]{3,0,2,1:T(8,128)(2,1)} async-done(((bf16[16,2,8,512]{3,0,2,1:T(8,128)(2,1)}), bf16[128,2,8,512]{3,0,2,1:T(8,128)(2,1)}) %all-gather.3.cloned.1.call-update) | async-done | bytes 2097168 | tf_op jit(solution)/shard_map/all_gather | solution.py:42
  252.6 1.3 fusion.32
  253.9 1.7 slice_bitcast_fusion.3
  255.7 92.0 %all-gather.5.cloned.1.call-done = bf16[32,16,2,8,512]{4,3,2,1,0:T(8,128)(2,1)} async-done(((bf16[1,16,2,8,512]{4,3,2,1,0:T(8,128)(2,1)}), bf16[32,16,2,8,512]{4,3,2,1,0:T(8,128)(2,1)}) %all-gather.5.cloned.1.call-update) | async-done | bytes 8388624 | tf_op jit(solution)/shard_map/all_gather | solution.py:40
  347.7 3.8 fusion.34
  351.5 11.6 %copy_bitcast_fusion = (bf16[32,16,8,512]{3,0,1,2:T(8,128)(2,1)}, bf16[32,16,8,512]{3,0,1,2:T(8,128)(2,1)}) fusion(bf16[32,16,1,8,512]{4,3,2,1,0:T(8,128)(2,1)S(1)} %get-tuple-element.6, bf16[32,16,1,8,512]{4,3,2,1,0:T(8,128)(2,1)S(1)} %get-tuple-element.5), kind=kLoop, calls=%fused_computation.29 | loop fusion | bytes 16777216 | tf_op jit(solution)/shard_map/squeeze | solution.py:41
  363.1 8.2 %pad_maximum_fusion = bf16[32,16,8,1024]{3,0,1,2:T(8,128)(2,1)} fusion(bf16[32,16,8,512]{3,0,1,2:T(8,128)(2,1)} %get-tuple-element.19, bf16[32,16,8,512]{3,0,1,2:T(8,128)(2,1)} %get-tuple-element.20), kind=kLoop, calls=%fused_computation.18 | loop fusion | flops 16777216 | bytes 16777216 | tf_op jit(solution)/shard_map/concatenate | solution.py:41
  371.3 10.0 %fusion.13 = f32[8,128,32,16]{1,3,2,0:T(8,128)S(1)} fusion(bf16[32,16,8,1024]{3,0,1,2:T(8,128)(2,1)} %pad_maximum_fusion, bf16[128,8,512]{2,0,1:T(8,128)(2,1)S(1)} %get-tuple-element.12, bf16[128,8,512]{2,0,1:T(8,128)(2,1)S(1)} %get-tuple-element.11), kind=kOutput, calls=%fused_computation.21 | convolution fusion | flops 1077936128 | bytes 12582912 | tf_op jit(solution)/shard_map/kfe,gsfe->fkgs/dot_general | solution.py:45
  381.3 4.6 %fusion.11 = f32[8,128,32,16]{1,3,2,0:T(8,128)S(1)} fusion(bf16[32,16,8,1024]{3,0,1,2:T(8,128)(2,1)S(1)} %copy-done.1, bf16[128,8,512]{2,0,1:T(8,128)(2,1)S(1)} %fusion.32, bf16[128,8,512]{2,0,1:T(8,128)(2,1)S(1)} %get-tuple-element.12), kind=kOutput, calls=%fused_computation.19 | convolution fusion | flops 1077936128 | bytes 12582912 | tf_op jit(solution)/shard_map/kfe,gsfe->fkgs/dot_general | solution.py:46
  385.9 2.2 maximum_bitcast_fusion
  388.2 5.3 %copy.21 = f32[2,8,1,128,512]{4,3,2,1,0:T(8,128)} copy(f32[2,8,1,128,512]{3,4,1,0,2:T(8,128)} %maximum_bitcast_fusion) | data formatting | bytes 8388608 | tf_op jit(solution)/shard_map/broadcast_in_dim | solution.py:50
  (18 shorter events, 0.1 us)
Async XLA Ops:
  6.5 154.4 %reduce-scatter.2.cloned.1.call-start = ((), (), s32[]{:S(2)}) async-start(), calls=%async_computation.2 | async-start | bytes 4718592 | tf_op jit(solution)/shard_map/reduce_scatter | solution.py:36
  6.5 3.4 copy-start
  6.5 3.6 copy-start.4
  10.0 0.7 copy-start.5
  10.0 0.7 copy-start.3
  91.3 9.3 %copy-start.2 = (f32[128,1,8,512]{0,3,2,1:T(8,128)S(1)}, f32[128,1,8,512]{0,3,2,1:T(8,128)}, u32[]{:S(2)}) copy-start(f32[128,1,8,512]{0,3,2,1:T(8,128)} %fusion.21) | copy-start | bytes 6291460
  104.6 148.0 %all-gather.3.cloned.1.call-start = ((), (), s32[]{:S(2)}) async-start(), calls=%async_computation.3 | async-start | bytes 2359296 | tf_op jit(solution)/shard_map/all_gather | solution.py:42
  176.7 171.0 %all-gather.5.cloned.1.call-start = ((), (), s32[]{:S(2)}) async-start(), calls=%async_computation.4 | async-start | bytes 8650752 | tf_op jit(solution)/shard_map/all_gather | solution.py:40
  371.3 10.0 %copy-start.1 = (bf16[32,16,8,1024]{3,0,1,2:T(8,128)(2,1)S(1)}, bf16[32,16,8,1024]{3,0,1,2:T(8,128)(2,1)}, u32[]{:S(2)}) copy-start(bf16[32,16,8,1024]{3,0,1,2:T(8,128)(2,1)} %pad_maximum_fusion) | copy-start | bytes 25165828
Sparse Core Ops, SparseCore 0:
  104.7 56.1 reduce-scatter.1
  176.8 75.7 all-gather.2
  254.4 93.1 all-gather.4
where the time goes:
time: 402 us; the launch traced here: 400 us
  waiting for transfers between devices  223 us (55%)
  other arithmetic  88.3 us (22%)
  matrix products  33.2 us (8%)
  local copies, waits for them, and re-layouts  30.6 us (8%)
  between operations  13.2 us (3%)
  blocking collectives  12.1 us (3%)
    all_gather x1, waiting for transfers between devices, local(): lax.all_gather(amplitudes[None], ('node', 'drow'), axis=0, tiled=True)  92 us
    all_gather x1, waiting for transfers between devices, local(): row_piece = lax.all_gather(amplitudes, 'dcol', axis=0, tiled=True)  74.2 us
    convert_element_type x1, other arithmetic, excitation(): load_im = (-spread * jnp.sin(phase_angle)).astype(jnp.bfloat16)  71 us
    reduce_scatter x1, waiting for transfers between devices, local(): lax.psum_scatter(partial_amp, 'node', scatter_dimension=3, tiled=True)  56.3 us
    all_to_all x1, blocking collectives, local(): lax.all_to_all(by_dirs, 'node', split_axis=0, concat_axis=3, tiled=True)  12.1 us
    squeeze x1, local copies, waits for them, and re-layouts, local(): col_cat = jnp.concatenate([colset[:, :, 0], colset[:, :, 1]], axis=-1)  11.6 us
    dot_general x1, matrix products, local(): jnp.einsum('kfe,gsfe->fkgs', lead_re, col_cat, preferred_element_type=jnp...  10 us
    dot_general x1, matrix products, local(): jnp.einsum('fkn,fnd->kfd', left_re, right_re, preferred_element_type=jnp....  9.32 us
  transfers between devices with their start and end apart: 3, of which 3 were waited for; matrix products, arithmetic and copies ran while one was open for 1% of the time, Pallas kernels for 0%

commit v1 on v0

v1 whole, which is shorter than its diff:
```python
import math

import jax
import jax.numpy as jnp
from jax import lax
from jax.sharding import PartitionSpec as P

DIRS = 512
FREQS = 8
GRID = 1024


def unit_phasor(turn):
    quarter = GRID // 4
    shifted = (turn + quarter // 2) & (GRID - 1)
    quadrant = shifted >> 8
    offset = (shifted & (quarter - 1)) - quarter // 2
    x = offset.astype(jnp.float32) * (2.0 * math.pi / GRID)
    x2 = x * x
    s = x * (1.0 + x2 * (-1.0 / 6 + x2 * (1.0 / 120 + x2 * (-1.0 / 5040 + x2 * (1.0 / 362880)))))
    c = 1.0 + x2 * (-0.5 + x2 * (1.0 / 24 + x2 * (-1.0 / 720 + x2 * (1.0 / 40320))))
    odd = (quadrant & 1) == 1
    cos_mag = jnp.where(odd, s, c)
    sin_mag = jnp.where(odd, c, s)
    cos_neg = (quadrant == 1) | (quadrant == 2)
    sin_neg = quadrant >= 2
    return jnp.where(cos_neg, -cos_mag, cos_mag), jnp.where(sin_neg, -sin_mag, sin_mag)


def excitation(coords, heading_steps, spectral_weights):
    freq_index = (jnp.arange(FREQS, dtype=jnp.int32) + 1)[:, None, None]
    project = (
        coords[0][:, None] * heading_steps[0][None, :]
        + coords[1][:, None] * heading_steps[1][None, :]
    )
    turn_count = (freq_index * project[None]) & (GRID - 1)
    cos_t, sin_t = unit_phasor(turn_count)
    spread = jnp.sqrt(spectral_weights.astype(jnp.float32) / (64.0 * DIRS))[:, None, :]
    load_re = (spread * cos_t).astype(jnp.bfloat16)
    load_im = (-spread * sin_t).astype(jnp.bfloat16)
    return load_re, load_im


def local(freq_resp, node_coords, heading_steps, spectral_weights):
    load_re, load_im = excitation(node_coords, heading_steps, spectral_weights)
    right = jnp.stack(
        [
            jnp.concatenate([load_re, load_im], axis=-1),
            jnp.concatenate([-load_im, load_re], axis=-1),
        ],
        axis=0,
    )
    partial_amp = jnp.einsum(
        "pfkn,pfne->fke", freq_resp, right, preferred_element_type=jnp.float32
    )
    amplitudes = lax.psum_scatter(partial_amp, "node", scatter_dimension=1, tiled=True).astype(
        jnp.bfloat16
    )
    cols = lax.all_gather(amplitudes, ("node", "drow"), axis=1, tiled=True)
    rows = lax.all_gather(amplitudes, "dcol", axis=1, tiled=True)
    rows_im = jnp.concatenate([rows[..., DIRS:], -rows[..., :DIRS]], axis=-1)
    lead = jnp.stack([rows, rows_im], axis=0)
    spec = jnp.einsum("pfke,fje->pfkj", lead, cols, preferred_element_type=jnp.float32)
    return spec[:, :, None]


def solution(mesh):
    placed = (P(None, None, ("drow", "dcol"), "node"), P(None, "node"), P(), P())
    return jax.shard_map(
        local,
        mesh=mesh,
        in_specs=placed,
        out_specs=P(None, None, "drow", "node", "dcol"),
        check_vma=False,
    )
```

time: 402 us -> 359 us (0.89)
  local copies, waits for them, and re-layouts: 30.6 us -> 15.1 us
  blocking collectives: 12.1 us -> 0 us
  other arithmetic: 88.3 us -> 77.5 us
  matrix products: 33.2 us -> 28.9 us
    convert_element_type x2, other arithmetic: 72.1 us -> 27.8 us  [the longest x1 26 us: excitation(): load_im = (-spread * sin_t).astype(jnp.bfloat16)]
    another operation x1 -> x2, other arithmetic: 3.91 us -> 26.5 us  [the longest x1 24.9 us: local(): jnp.stack([jnp.concatenate([load_re, load_im], axis=-1), jnp.concatenate(...]
    neg x3 -> x2, other arithmetic: 1.44 us -> 22.8 us  [the longest x1 22 us: local(): -load_im]
    squeeze x3 -> x0, local copies, waits for them, and re-layouts: 16.1 us -> none  [the longest x1 11.6 us: local(): col_cat = jnp.concatenate([colset[:, :, 0], colset[:, :, 1]], axis=-1)]
    all_to_all x1 -> x0, blocking collectives: 12.1 us -> none  [local(): lax.all_to_all(by_dirs, 'node', split_axis=0, concat_axis=3, tiled=True)]
    concatenate x1 -> x0, other arithmetic: 8.21 us -> none  [local(): col_cat = jnp.concatenate([colset[:, :, 0], colset[:, :, 1]], axis=-1)]
    dot_general x0 -> x1, local copies, waits for them, and re-layouts: none -> 5.51 us  [local(): jnp.einsum('pfkn,pfne->fke', freq_resp, right, preferred_element_type=jnp...]
    dot_general x4 -> x2, matrix products: 33.2 us -> 28.9 us  [the longest x1 17.9 us: local(): jnp.einsum('pfkn,pfne->fke', freq_resp, right, preferred_element_type=jnp...]
where the time goes in v1:
time: 359 us; the launch traced here: 357 us
  waiting for transfers between devices  222 us (62%)
  other arithmetic  77.5 us (22%)
  matrix products  28.9 us (8%)
  local copies, waits for them, and re-layouts  15.1 us (4%)
  between operations  13.1 us (4%)
    all_gather x1, waiting for transfers between devices, local(): cols = lax.all_gather(amplitudes, ('node', 'drow'), axis=1, tiled=True)  90.6 us
    all_gather x1, waiting for transfers between devices, local(): rows = lax.all_gather(amplitudes, 'dcol', axis=1, tiled=True)  74.8 us
    reduce_scatter x1, waiting for transfers between devices, local(): lax.psum_scatter(partial_amp, 'node', scatter_dimension=1, tiled=True)  56.3 us
    convert_element_type x1, other arithmetic, excitation(): load_im = (-spread * sin_t).astype(jnp.bfloat16)  26 us
    another operation x1, other arithmetic, local(): jnp.stack([jnp.concatenate([load_re, load_im], axis=-1), jnp.concatenate(...  24.9 us
    neg x1, other arithmetic, local(): -load_im  22 us
    dot_general x1, matrix products, local(): jnp.einsum('pfkn,pfne->fke', freq_resp, right, preferred_element_type=jnp...  17.9 us
    dot_general x1, matrix products, local(): jnp.einsum('pfke,fje->pfkj', lead, cols, preferred_element_type=jnp.float32)  11 us
  transfers between devices with their start and end apart: 3, of which 3 were waited for; matrix products, arithmetic and copies ran while one was open for 1% of the time, Pallas kernels for 0%

profile of v1, /device:TPU:33, one launch (start us, length us, event | category | flops | bytes accessed | tf_op | source)
XLA Modules:
  0.0 357.2 jit_solution(1211883478855104320)
XLA Ops:
  6.5 0.0 reduce-scatter.2.cloned.1.call-start
  6.5 0.8 fusion.37
  7.3 0.8 fusion.36
  8.1 0.7 fusion.33
  8.8 0.4 multiply_add_fusion.1
  9.2 22.0 %fusion.34 = bf16[8,1024,512]{1,2,0:T(8,128)(2,1)} fusion(s32[1024,512]{0,1:T(8,128)S(1)} %multiply_add_fusion.1, s32[8]{0:T(128)S(1)} %iota_add_fusion, f32[8,512]{1,0:T(8,128)S(1)} %get-tuple-element.13), kind=kLoop, calls=%fused_computation.43 | loop fusion | flops 159383552 | bytes 10502176 | tf_op jit(solution)/shard_map/neg | solution.py:49
  31.2 26.0 %fusion.7 = (bf16[8,1024,512]{1,2,0:T(8,128)(2,1)}, bf16[8,1024,512]{1,2,0:T(8,128)(2,1)}) fusion(f32[8,512]{1,0:T(8,128)S(1)} %get-tuple-element.13, s32[1024,512]{0,1:T(8,128)S(1)} %multiply_add_fusion.1, s32[8]{0:T(128)S(1)} %iota_add_fusion, f32[8,512]{1,0:T(8,128)S(1)} %get-tuple-element.14), kind=kLoop, calls=%fused_computation.9 | loop fusion | flops 180355072 | bytes 18907168 | tf_op jit(solution)/shard_map/convert_element_type | solution.py:40
  57.2 24.9 %maximum_bitcast_fusion = (bf16[1,8,1024,1024]{2,3,0,1:T(8,128)(2,1)}, bf16[1,8,1024,1024]{2,3,0,1:T(8,128)(2,1)}) fusion(bf16[8,1024,512]{1,2,0:T(8,128)(2,1)} %get-tuple-element.7, bf16[8,1024,512]{1,2,0:T(8,128)(2,1)} %get-tuple-element.8, bf16[8,1024,512]{1,2,0:T(8,128)(2,1)} %fusion.34), kind=kLoop, calls=%fused_computation.10 | loop fusion | flops 67108864 | bytes 58720256 | tf_op jit(solution)/shard_map/stack | solution.py:46
  82.1 17.9 %fusion.26 = f32[8,128,1024]{1,2,0:T(8,128)} fusion(bf16[2,8,128,1024]{3,2,1,0:T(8,128)(2,1)} %param.4, bf16[1,8,1024,1024]{2,3,0,1:T(8,128)(2,1)} %get-tuple-element.6, bf16[1,8,1024,1024]{2,3,0,1:T(8,128)(2,1)} %get-tuple-element.5), kind=kOutput, calls=%fused_computation.33 | convolution fusion | flops 4311744512 | bytes 41943040 | tf_op jit(solution)/shard_map/pfkn,pfne->fke/dot_general | solution.py:53
  100.0 5.5 %copy.12 = f32[8,128,1024]{2,0,1:T(8,128)} copy(f32[8,128,1024]{1,2,0:T(8,128)} %fusion.26) | data formatting | bytes 8388608 | tf_op jit(solution)/shard_map/pfkn,pfne->fke/dot_general | solution.py:53
  105.5 0.0 reduce-scatter.2.cloned.1.call-update
  105.5 0.0 all-gather.5.cloned.1.call-start
  105.6 56.3 %reduce-scatter.2.cloned.1.call-done = f32[8,16,1024]{2,0,1:T(8,128)} async-done(((f32[8,128,1024]{2,0,1:T(8,128)}), f32[8,16,1024]{2,0,1:T(8,128)}) %reduce-scatter.2.cloned.1.call-update) | async-done | bytes 524304 | tf_op jit(solution)/shard_map/reduce_scatter | solution.py:56
  161.9 1.8 convert_element_type.19
  163.7 0.0 all-gather.5.cloned.1.call-update
  163.7 0.2 all-gather.3.cloned.1.call-start
  163.9 0.5 all-gather.3.cloned.1.call-update
  164.4 74.8 %all-gather.5.cloned.1.call-done = bf16[8,128,1024]{2,0,1:T(8,128)(2,1)} async-done(((bf16[8,16,1024]{2,0,1:T(8,128)(2,1)}), bf16[8,128,1024]{2,0,1:T(8,128)(2,1)}) %all-gather.5.cloned.1.call-update) | async-done | bytes 2097168 | tf_op jit(solution)/shard_map/all_gather | solution.py:60
  239.2 2.7 copy.32
  242.0 0.1 fusion.35
  242.1 1.6 maximum_bitcast_fusion.2
  243.7 90.6 %all-gather.3.cloned.1.call-done = bf16[8,512,1024]{2,0,1:T(8,128)(2,1)} async-done(((bf16[8,16,1024]{2,0,1:T(8,128)(2,1)}), bf16[8,512,1024]{2,0,1:T(8,128)(2,1)}) %all-gather.3.cloned.1.call-update) | async-done | bytes 8388624 | tf_op jit(solution)/shard_map/all_gather | solution.py:59
  334.3 11.0 %fusion.21 = f32[2,8,1,128,512]{3,4,0,1,2:T(8,128)} fusion(bf16[1,8,128,1024]{3,2,0,1:T(8,128)(2,1)} %maximum_bitcast_fusion.2, bf16[1,8,128,1024]{3,2,0,1:T(8,128)(2,1)S(1)} %bitcast.25, bf16[8,512,1024,1]{2,0,1,3:T(8,128)(2,1)} %bitcast.30), kind=kOutput, calls=%fused_computation.32 | convolution fusion | flops 2155872256 | bytes 16777216 | tf_op jit(solution)/shard_map/pfke,fje->pfkj/dot_general | solution.py:63
  345.3 5.3 %copy.17 = f32[2,8,1,128,512]{4,3,2,1,0:T(8,128)} copy(f32[2,8,1,128,512]{3,4,0,1,2:T(8,128)} %fusion.21) | data formatting | bytes 8388608 | tf_op jit(solution)/shard_map/broadcast_in_dim | solution.py:64
  (1 shorter events, 0.0 us)
Async XLA Ops:
  6.5 155.3 %reduce-scatter.2.cloned.1.call-start = ((), (), s32[]{:S(2)}) async-start(), calls=%async_computation.1 | async-start | bytes 4718592 | tf_op jit(solution)/shard_map/reduce_scatter | solution.py:56
  105.5 133.7 %all-gather.5.cloned.1.call-start = ((), (), s32[]{:S(2)}) async-start(), calls=%async_computation.3 | async-start | bytes 2359296 | tf_op jit(solution)/shard_map/all_gather | solution.py:60
  163.7 170.6 %all-gather.3.cloned.1.call-start = ((), (), s32[]{:S(2)}) async-start(), calls=%async_computation.2 | async-start | bytes 8650752 | tf_op jit(solution)/shard_map/all_gather | solution.py:59
Sparse Core Ops, SparseCore 0:
  105.7 56.1 reduce-scatter.1
  164.5 74.7 all-gather.4
  241.1 93.1 all-gather.2

commit v2 on v1

--- a/solution.py
+++ b/solution.py
@@ -3,11 +3,14 @@
 import jax
 import jax.numpy as jnp
 from jax import lax
+from jax.experimental import pallas as pl
+from jax.experimental.pallas import tpu as pltpu
 from jax.sharding import PartitionSpec as P
 
 DIRS = 512
 FREQS = 8
 GRID = 1024
+NODE_TILE = 256
 
 
 def unit_phasor(turn):
@@ -27,32 +30,55 @@
     return jnp.where(cos_neg, -cos_mag, cos_mag), jnp.where(sin_neg, -sin_mag, sin_mag)
 
 
-def excitation(coords, heading_steps, spectral_weights):
-    freq_index = (jnp.arange(FREQS, dtype=jnp.int32) + 1)[:, None, None]
-    project = (
-        coords[0][:, None] * heading_steps[0][None, :]
-        + coords[1][:, None] * heading_steps[1][None, :]
-    )
-    turn_count = (freq_index * project[None]) & (GRID - 1)
-    cos_t, sin_t = unit_phasor(turn_count)
-    spread = jnp.sqrt(spectral_weights.astype(jnp.float32) / (64.0 * DIRS))[:, None, :]
-    load_re = (spread * cos_t).astype(jnp.bfloat16)
-    load_im = (-spread * sin_t).astype(jnp.bfloat16)
-    return load_re, load_im
+def amp_kernel(proj_ref, spread_ref, resp_ref, out_ref):
+    @pl.when(pl.program_id(0) == 0)
+    def _():
+        out_ref[...] = jnp.zeros_like(out_ref)
+
+    proj = proj_ref[...]
+    base_c, base_s = unit_phasor(proj & (GRID - 1))
+    rows = resp_ref.shape[2]
+    cos_f, sin_f = base_c, base_s
+    for f in range(FREQS):
+        if f > 0:
+            cos_f, sin_f = (
+                cos_f * base_c - sin_f * base_s,
+                sin_f * base_c + cos_f * base_s,
+            )
+        spread = spread_ref[f : f + 1, :]
+        load_re = (spread * cos_f).astype(jnp.bfloat16)
+        load_im = (-spread * sin_f).astype(jnp.bfloat16)
+        resp = resp_ref[:, f].reshape(2 * rows, resp_ref.shape[3])
+        by_re = jnp.dot(resp, load_re, preferred_element_type=jnp.float32)
+        by_im = jnp.dot(resp, load_im, preferred_element_type=jnp.float32)
+        out_ref[f, :, :DIRS] += by_re[:rows] - by_im[rows:]
+        out_ref[f, :, DIRS:] += by_im[:rows] + by_re[rows:]
+
+
+def partial_amplitudes(freq_resp, project, spread):
+    nodes = project.shape[0]
+    rows = freq_resp.shape[2]
+    return pl.pallas_call(
+        amp_kernel,
+        out_shape=jax.ShapeDtypeStruct((FREQS, rows, 2 * DIRS), jnp.float32),
+        grid=(nodes // NODE_TILE,),
+        in_specs=[
+            pl.BlockSpec((NODE_TILE, DIRS), lambda j: (j, 0)),
+            pl.BlockSpec((FREQS, DIRS), lambda j: (0, 0)),
+            pl.BlockSpec((2, FREQS, rows, NODE_TILE), lambda j: (0, 0, 0, j)),
+        ],
+        out_specs=pl.BlockSpec((FREQS, rows, 2 * DIRS), lambda j: (0, 0, 0)),
+        compiler_params=pltpu.CompilerParams(dimension_semantics=("arbitrary",)),
+    )(project, spread, freq_resp)
 
 
 def local(freq_resp, node_coords, heading_steps, spectral_weights):
-    load_re, load_im = excitation(node_coords, heading_steps, spectral_weights)
-    right = jnp.stack(
-        [
-            jnp.concatenate([load_re, load_im], axis=-1),
-            jnp.concatenate([-load_im, load_re], axis=-1),
-        ],
-        axis=0,
+    project = (
+        node_coords[0][:, None] * heading_steps[0][None, :]
+        + node_coords[1][:, None] * heading_steps[1][None, :]
     )
-    partial_amp = jnp.einsum(
-        "pfkn,pfne->fke", freq_resp, right, preferred_element_type=jnp.float32
-    )
+    spread = jnp.sqrt(spectral_weights.astype(jnp.float32) / (64.0 * DIRS))
+    partial_amp = partial_amplitudes(freq_resp, project, spread)
     amplitudes = lax.psum_scatter(partial_amp, "node", scatter_dimension=1, tiled=True).astype(
         jnp.bfloat16
     )

time: 359 us -> 277 us (0.77)
  other arithmetic: 77.5 us -> 8.03 us
  matrix products: 28.9 us -> 8.32 us
  Pallas kernels: 0 us -> 15.5 us
  local copies, waits for them, and re-layouts: 15.1 us -> 6.89 us
    convert_element_type x1 -> x0, other arithmetic: 26 us -> none  [excitation(): load_im = (-spread * sin_t).astype(jnp.bfloat16)]
    another operation x1 -> x0, other arithmetic: 24.9 us -> none  [local(): jnp.stack([jnp.concatenate([load_re, load_im], axis=-1), jnp.concatenate(...]
    neg x2 -> x0, other arithmetic: 22.8 us -> none  [the longest x1 22 us: local(): -load_im]
    dot_general x1 -> x0, matrix products: 17.9 us -> none  [local(): jnp.einsum('pfkn,pfne->fke', freq_resp, right, preferred_element_type=jnp...]
    pallas_call x0 -> x1, Pallas kernels: none -> 15.5 us  [partial_amplitudes(): pl.pallas_call(amp_kernel, out_shape=jax.ShapeDtypeStruct((FREQS, rows, 2...]
    dot_general x1 -> x0, local copies, waits for them, and re-layouts: 5.51 us -> none  [local(): jnp.einsum('pfkn,pfne->fke', freq_resp, right, preferred_element_type=jnp...]
where the time goes in v2:
time: 277 us; the launch traced here: 276 us
  waiting for transfers between devices  224 us (81%)
  Pallas kernels  15.5 us (6%)
  between operations  13.1 us (5%)
  matrix products  8.32 us (3%)
  other arithmetic  8.03 us (3%)
  local copies, waits for them, and re-layouts  6.89 us (2%)
    all_gather x1, waiting for transfers between devices, local(): cols = lax.all_gather(amplitudes, ('node', 'drow'), axis=1, tiled=True)  91.8 us
    all_gather x1, waiting for transfers between devices, local(): rows = lax.all_gather(amplitudes, 'dcol', axis=1, tiled=True)  74.8 us
    reduce_scatter x1, waiting for transfers between devices, local(): lax.psum_scatter(partial_amp, 'node', scatter_dimension=1, tiled=True)  56.3 us
    pallas_call x1, Pallas kernels, partial_amplitudes(): pl.pallas_call(amp_kernel, out_shape=jax.ShapeDtypeStruct((FREQS, rows, 2...  15.5 us
    dot_general x1, matrix products, local(): jnp.einsum('pfke,fje->pfkj', lead, cols, preferred_element_type=jnp.float32)  8.32 us
  transfers between devices with their start and end apart: 3, of which 3 were waited for; matrix products, arithmetic and copies ran while one was open for 1% of the time, Pallas kernels for 0%

profile of v2, /device:TPU:33, one launch (start us, length us, event | category | flops | bytes accessed | tf_op | source)
XLA Modules:
  0.0 275.5 jit_solution(8609788265415456146)
XLA Ops:
  6.5 0.0 reduce-scatter.2.cloned.1.call-start
  6.5 0.8 fusion.10
  7.3 0.8 fusion.9
  8.1 1.3 multiply_sqrt_fusion.spread_ref
  9.4 1.6 multiply_add_fusion.proj_ref
  11.1 15.5 %shard_map.46 = f32[8,128,1024]{2,1,0:T(8,128)} custom-call(s32[1024,512]{1,0:T(8,128)} %multiply_add_fusion.proj_ref, f32[8,512]{1,0:T(8,128)} %multiply_sqrt_fusion.spread_ref, bf16[2,8,128,1024]{3,2,1,0:T(8,128)(2,1)} %resp_ref.1), custom_call_target="tpu_custom_call" | custom-call | tf_op jit(solution)/shard_map/pallas_call | solution.py:61
  26.5 0.0 reduce-scatter.2.cloned.1.call-update
  26.6 0.0 all-gather.5.cloned.1.call-start
  26.6 56.3 %reduce-scatter.2.cloned.1.call-done = f32[8,16,1024]{2,1,0:T(8,128)} async-done(((f32[8,128,1024]{2,1,0:T(8,128)}), f32[8,16,1024]{2,1,0:T(8,128)}) %reduce-scatter.2.cloned.1.call-update) | async-done | bytes 524304 | tf_op jit(solution)/shard_map/reduce_scatter | solution.py:82
  82.9 1.8 convert_element_type.7
  84.7 0.0 all-gather.5.cloned.1.call-update
  84.7 0.0 all-gather.3.cloned.1.call-start
  84.7 0.7 all-gather.3.cloned.1.call-update
  85.4 74.8 %all-gather.5.cloned.1.call-done = bf16[8,128,1024]{2,1,0:T(8,128)(2,1)} async-done(((bf16[8,16,1024]{2,1,0:T(8,128)(2,1)}), bf16[8,128,1024]{2,1,0:T(8,128)(2,1)}) %all-gather.5.cloned.1.call-update) | async-done | bytes 2097168 | tf_op jit(solution)/shard_map/all_gather | solution.py:86
  160.2 1.7 fusion.8
  161.9 0.0 copy-start
  161.9 1.6 maximum_bitcast_fusion
  163.5 91.8 %all-gather.3.cloned.1.call-done = bf16[8,512,1024]{2,1,0:T(8,128)(2,1)} async-done(((bf16[8,16,1024]{2,1,0:T(8,128)(2,1)}), bf16[8,512,1024]{2,1,0:T(8,128)(2,1)}) %all-gather.3.cloned.1.call-update) | async-done | bytes 8388624 | tf_op jit(solution)/shard_map/all_gather | solution.py:85
  255.3 0.0 copy-done
  255.3 8.3 %fusion.3 = f32[2,8,1,128,512]{3,4,0,1,2:T(8,128)} fusion(bf16[8,512,1024]{2,1,0:T(8,128)(2,1)} %all-gather.3.cloned.1.call-done, bf16[1,8,128,1024]{3,2,1,0:T(8,128)(2,1)} %maximum_bitcast_fusion, bf16[1,8,128,1024]{3,2,1,0:T(8,128)(2,1)S(1)} %bitcast.18), kind=kOutput, calls=%fused_computation.4 | convolution fusion | flops 2149580800 | bytes 16777216 | tf_op jit(solution)/shard_map/pfke,fje->pfkj/dot_general | solution.py:89
  263.6 5.3 %copy.6 = f32[2,8,1,128,512]{4,3,2,1,0:T(8,128)} copy(f32[2,8,1,128,512]{3,4,0,1,2:T(8,128)} %fusion.3) | data formatting | bytes 8388608 | tf_op jit(solution)/shard_map/broadcast_in_dim | solution.py:90
Async XLA Ops:
  6.5 76.3 %reduce-scatter.2.cloned.1.call-start = ((), (), s32[]{:S(2)}) async-start(), calls=%async_computation.1 | async-start | bytes 4718592 | tf_op jit(solution)/shard_map/reduce_scatter | solution.py:82
  26.6 133.7 %all-gather.5.cloned.1.call-start = ((), (), s32[]{:S(2)}) async-start(), calls=%async_computation.3 | async-start | bytes 2359296 | tf_op jit(solution)/shard_map/all_gather | solution.py:86
  84.7 170.6 %all-gather.3.cloned.1.call-start = ((), (), s32[]{:S(2)}) async-start(), calls=%async_computation.2 | async-start | bytes 8650752 | tf_op jit(solution)/shard_map/all_gather | solution.py:85
  161.9 93.4 %copy-start = (bf16[8,128,1024]{2,1,0:T(8,128)(2,1)S(1)}, bf16[8,128,1024]{2,1,0:T(8,128)(2,1)}, u32[]{:S(2)}) copy-start(bf16[8,128,1024]{2,1,0:T(8,128)(2,1)} %all-gather.5.cloned.1.call-done) | copy-start | bytes 6291460
Sparse Core Ops, SparseCore 0:
  26.7 56.1 reduce-scatter.1
  85.5 74.6 all-gather.4
  162.1 93.2 all-gather.2

commit v3 on v2

--- a/solution.py
+++ b/solution.py
@@ -72,6 +72,20 @@
     )(project, spread, freq_resp)
 
 
+def gather_rows(amplitudes):
+    count = lax.axis_size("dcol")
+    ahead = [amplitudes]
+    for shift in range(1, count):
+        ahead.append(
+            lax.ppermute(
+                amplitudes, "dcol", perm=[(i, (i - shift) % count) for i in range(count)]
+            )
+        )
+    stacked = jnp.stack(ahead, axis=1)
+    rolled = jnp.roll(stacked, lax.axis_index("dcol"), axis=1)
+    return rolled.reshape(stacked.shape[0], -1, stacked.shape[-1])
+
+
 def local(freq_resp, node_coords, heading_steps, spectral_weights):
     project = (
         node_coords[0][:, None] * heading_steps[0][None, :]
@@ -83,7 +97,7 @@
         jnp.bfloat16
     )
     cols = lax.all_gather(amplitudes, ("node", "drow"), axis=1, tiled=True)
-    rows = lax.all_gather(amplitudes, "dcol", axis=1, tiled=True)
+    rows = gather_rows(amplitudes)
     rows_im = jnp.concatenate([rows[..., DIRS:], -rows[..., :DIRS]], axis=-1)
     lead = jnp.stack([rows, rows_im], axis=0)
     spec = jnp.einsum("pfke,fje->pfkj", lead, cols, preferred_element_type=jnp.float32)

time: 277 us -> 244 us (0.88)
  the two profiles are of different devices: /device:TPU:33 before, /device:TPU:35 now
where the time goes in v3:
time: 244 us; the launch traced here: 243 us
  waiting for transfers between devices  165 us (68%)
  local copies, waits for them, and re-layouts  20.6 us (8%)
  Pallas kernels  15.5 us (6%)
  starting transfers between devices  14.1 us (6%)
  between operations  13.4 us (5%)
  matrix products  8.31 us (3%)
  other arithmetic  6.6 us (3%)
    all_gather x1, waiting for transfers between devices, local(): cols = lax.all_gather(amplitudes, ('node', 'drow'), axis=1, tiled=True)  66.9 us
    reduce_scatter x1, waiting for transfers between devices, local(): lax.psum_scatter(partial_amp, 'node', scatter_dimension=1, tiled=True)  56.2 us
    ppermute x7, waiting for transfers between devices, gather_rows(): lax.ppermute(amplitudes, 'dcol', perm=[(i, (i - shift) % count) for i in...  41.5 us
    pallas_call x1, Pallas kernels, partial_amplitudes(): pl.pallas_call(amp_kernel, out_shape=jax.ShapeDtypeStruct((FREQS, rows, 2...  15.5 us
    ppermute x7, starting transfers between devices, gather_rows(): lax.ppermute(amplitudes, 'dcol', perm=[(i, (i - shift) % count) for i in...  14.1 us
    unnamed x14, local copies, waits for them, and re-layouts  11.1 us
    dot_general x1, matrix products, local(): jnp.einsum('pfke,fje->pfkj', lead, cols, preferred_element_type=jnp.float32)  8.31 us
    broadcast_in_dim x1, local copies, waits for them, and re-layouts, local(): return spec[:, :, None]  5.34 us
  transfers between devices with their start and end apart: 9, of which 8 were waited for; matrix products, arithmetic and copies ran while one was open for 6% of the time, Pallas kernels for 0%

profile of v3, /device:TPU:35, one launch (start us, length us, event | category | flops | bytes accessed | tf_op | source)
XLA Modules:
  0.0 243.2 jit_solution(550812126781472024)
XLA Ops:
  6.5 0.8 fusion.12
  7.3 0.8 fusion.13
  8.1 1.3 multiply_sqrt_fusion.spread_ref
  9.4 1.6 multiply_add_fusion.proj_ref
  11.1 15.5 %shard_map.46 = f32[8,128,1024]{2,1,0:T(8,128)} custom-call(s32[1024,512]{1,0:T(8,128)} %multiply_add_fusion.proj_ref, f32[8,512]{1,0:T(8,128)} %multiply_sqrt_fusion.spread_ref, bf16[2,8,128,1024]{3,2,1,0:T(8,128)(2,1)} %resp_ref.1), custom_call_target="tpu_custom_call" | custom-call | tf_op jit(solution)/shard_map/pallas_call | solution.py:61
  26.6 56.2 %reduce-scatter.2.cloned.1.call-done = f32[8,16,1024]{2,1,0:T(8,128)} async-done(((f32[8,128,1024]{2,1,0:T(8,128)}), f32[8,16,1024]{2,1,0:T(8,128)}) %reduce-scatter.2.cloned.1.call-update) | async-done | bytes 524304 | tf_op jit(solution)/shard_map/reduce_scatter | solution.py:96
  82.8 1.9 bitcast_dynamic-update-slice_fusion.14
  84.8 6.2 %collective-permute-start = (bf16[8,16,1024]{2,1,0:T(8,128)(2,1)}, bf16[8,16,1024]{2,1,0:T(8,128)(2,1)S(1)}, u32[]{:S(2)}, u32[]{:S(2)}) collective-permute-start(bf16[8,16,1024]{2,1,0:T(8,128)(2,1)} %get-tuple-element.6), channel_id=1, source_target_pairs={{0,7},{1,0},{2,1},{3,2},{4,3},{5,4},{6,5},{7,6},{8,15},{9,8},{10,9... | collective-permute-start | bytes 786440 | tf_op jit(solution)/shard_map/ppermute | solution.py:80
  91.5 1.7 collective-permute-start.2
  93.3 3.9 %collective-permute-start.3 = (bf16[8,16,1024]{2,1,0:T(8,128)(2,1)}, bf16[8,16,1024]{2,1,0:T(8,128)(2,1)S(1)}, u32[]{:S(2)}, u32[]{:S(2)}) collective-permute-start(bf16[8,16,1024]{2,1,0:T(8,128)(2,1)} %get-tuple-element.6), channel_id=1, source_target_pairs={{0,4},{1,5},{2,6},{3,7},{4,0},{5,1},{6,2},{7,3},{8,12},{9,13},{10,... | collective-permute-start | bytes 786440 | tf_op jit(solution)/shard_map/ppermute | solution.py:80
  97.2 2.8 %collective-permute-done = bf16[8,16,1024]{2,1,0:T(8,128)(2,1)S(1)} collective-permute-done((bf16[8,16,1024]{2,1,0:T(8,128)(2,1)}, bf16[8,16,1024]{2,1,0:T(8,128)(2,1)S(1)}, u32[]{:S(2)}, u32[]{:S(2)}) %collective-permute-start) | collective-permute-done | bytes 262176 | tf_op jit(solution)/shard_map/ppermute | solution.py:80
  100.0 1.6 collective-permute-start.5
  101.6 0.7 bitcast_dynamic-update-slice_fusion.12
  102.4 22.8 %collective-permute-done.1 = bf16[8,16,1024]{2,1,0:T(8,128)(2,1)S(1)} collective-permute-done((bf16[8,16,1024]{2,1,0:T(8,128)(2,1)}, bf16[8,16,1024]{2,1,0:T(8,128)(2,1)S(1)}, u32[]{:S(2)}, u32[]{:S(2)}) %collective-permute-start.1) | collective-permute-done | bytes 262176 | tf_op jit(solution)/shard_map/ppermute | solution.py:80
  125.1 0.7 bitcast_dynamic-update-slice_fusion.10
  125.9 6.2 %collective-permute-done.2 = bf16[8,16,1024]{2,1,0:T(8,128)(2,1)S(1)} collective-permute-done((bf16[8,16,1024]{2,1,0:T(8,128)(2,1)}, bf16[8,16,1024]{2,1,0:T(8,128)(2,1)S(1)}, u32[]{:S(2)}, u32[]{:S(2)}) %collective-permute-start.2) | collective-permute-done | bytes 262176 | tf_op jit(solution)/shard_map/ppermute | solution.py:80
  132.8 6.3 %collective-permute-done.3 = bf16[8,16,1024]{2,1,0:T(8,128)(2,1)S(1)} collective-permute-done((bf16[8,16,1024]{2,1,0:T(8,128)(2,1)}, bf16[8,16,1024]{2,1,0:T(8,128)(2,1)S(1)}, u32[]{:S(2)}, u32[]{:S(2)}) %collective-permute-start.3) | collective-permute-done | bytes 262176 | tf_op jit(solution)/shard_map/ppermute | solution.py:80
  139.1 0.7 bitcast_dynamic-update-slice_fusion.6
  139.8 0.7 bitcast_dynamic-update-slice_fusion.4
  140.5 1.3 collective-permute-done.5
  141.8 0.7 bitcast_dynamic-update-slice_fusion.2
  142.6 2.1 collective-permute-done.6
  144.7 0.7 bitcast_dynamic-update-slice_fusion
  145.4 1.7 bitcast_dynamic-update-slice_fusion.15
  147.1 0.7 bitcast_dynamic-update-slice_fusion.13
  147.8 0.7 bitcast_dynamic-update-slice_fusion.11
  148.5 0.7 bitcast_dynamic-update-slice_fusion.9
  152.1 1.8 constant_dynamic-slice_fusion
  154.3 1.6 maximum_bitcast_fusion
  155.8 66.9 %all-gather.2.cloned.1.call-done = bf16[8,512,1024]{2,1,0:T(8,128)(2,1)} async-done(((bf16[8,16,1024]{2,1,0:T(8,128)(2,1)}), bf16[8,512,1024]{2,1,0:T(8,128)(2,1)}) %all-gather.2.cloned.1.call-update) | async-done | bytes 8388624 | tf_op jit(solution)/shard_map/all_gather | solution.py:99
  222.8 8.3 %fusion.5 = f32[2,8,1,128,512]{3,4,0,1,2:T(8,128)} fusion(bf16[1,8,128,1024]{3,2,0,1:T(8,128)(2,1)} %maximum_bitcast_fusion, bf16[1,8,128,1024]{3,2,0,1:T(8,128)(2,1)S(1)} %bitcast.46, bf16[8,512,1024]{2,1,0:T(8,128)(2,1)} %all-gather.2.cloned.1.call-done), kind=kOutput, calls=%fused_computation.5 | convolution fusion | flops 2155872256 | bytes 16777216 | tf_op jit(solution)/shard_map/pfke,fje->pfkj/dot_general | solution.py:103
  231.1 5.3 %copy.9 = f32[2,8,1,128,512]{4,3,2,1,0:T(8,128)} copy(f32[2,8,1,128,512]{3,4,0,1,2:T(8,128)} %fusion.5) | data formatting | bytes 8388608 | tf_op jit(solution)/shard_map/broadcast_in_dim | solution.py:104
  (15 shorter events, 4.5 us)
Async XLA Ops:
  6.5 76.3 %reduce-scatter.2.cloned.1.call-start = ((), (), s32[]{:S(2)}) async-start(), calls=%async_computation.1 | async-start | bytes 4718592 | tf_op jit(solution)/shard_map/reduce_scatter | solution.py:96
  26.6 196.2 %all-gather.2.cloned.1.call-start = ((), (), s32[]{:S(2)}) async-start(), calls=%async_computation.2 | async-start | bytes 8650752 | tf_op jit(solution)/shard_map/all_gather | solution.py:99
  84.8 15.3 %collective-permute-start = (bf16[8,16,1024]{2,1,0:T(8,128)(2,1)}, bf16[8,16,1024]{2,1,0:T(8,128)(2,1)S(1)}, u32[]{:S(2)}, u32[]{:S(2)}) collective-permute-start(bf16[8,16,1024]{2,1,0:T(8,128)(2,1)} %get-tuple-element.6), channel_id=1, source_target_pairs={{0,7},{1,0},{2,1},{3,2},{4,3},{5,4},{6,5},{7,6},{8,15},{9,8},{10,9... | collective-permute-start | bytes 786440 | tf_op jit(solution)/shard_map/ppermute | solution.py:80
  91.0 34.1 %collective-permute-start.1 = (bf16[8,16,1024]{2,1,0:T(8,128)(2,1)}, bf16[8,16,1024]{2,1,0:T(8,128)(2,1)S(1)}, u32[]{:S(2)}, u32[]{:S(2)}) collective-permute-start(bf16[8,16,1024]{2,1,0:T(8,128)(2,1)} %get-tuple-element.6), channel_id=1, source_target_pairs={{0,6},{1,7},{2,0},{3,1},{4,2},{5,3},{6,4},{7,5},{8,14},{9,15},{10,... | collective-permute-start | bytes 786440 | tf_op jit(solution)/shard_map/ppermute | solution.py:80
  91.5 40.5 %collective-permute-start.2 = (bf16[8,16,1024]{2,1,0:T(8,128)(2,1)}, bf16[8,16,1024]{2,1,0:T(8,128)(2,1)S(1)}, u32[]{:S(2)}, u32[]{:S(2)}) collective-permute-start(bf16[8,16,1024]{2,1,0:T(8,128)(2,1)} %get-tuple-element.6), channel_id=1, source_target_pairs={{0,5},{1,6},{2,7},{3,0},{4,1},{5,2},{6,3},{7,4},{8,13},{9,14},{10,... | collective-permute-start | bytes 786440 | tf_op jit(solution)/shard_map/ppermute | solution.py:80
  93.3 45.8 %collective-permute-start.3 = (bf16[8,16,1024]{2,1,0:T(8,128)(2,1)}, bf16[8,16,1024]{2,1,0:T(8,128)(2,1)S(1)}, u32[]{:S(2)}, u32[]{:S(2)}) collective-permute-start(bf16[8,16,1024]{2,1,0:T(8,128)(2,1)} %get-tuple-element.6), channel_id=1, source_target_pairs={{0,4},{1,5},{2,6},{3,7},{4,0},{5,1},{6,2},{7,3},{8,12},{9,13},{10,... | collective-permute-start | bytes 786440 | tf_op jit(solution)/shard_map/ppermute | solution.py:80
  97.2 42.6 %collective-permute-start.4 = (bf16[8,16,1024]{2,1,0:T(8,128)(2,1)}, bf16[8,16,1024]{2,1,0:T(8,128)(2,1)S(1)}, u32[]{:S(2)}, u32[]{:S(2)}) collective-permute-start(bf16[8,16,1024]{2,1,0:T(8,128)(2,1)} %get-tuple-element.6), channel_id=1, source_target_pairs={{0,3},{1,4},{2,5},{3,6},{4,7},{5,0},{6,1},{7,2},{8,11},{9,12},{10,... | collective-permute-start | bytes 786440 | tf_op jit(solution)/shard_map/ppermute | solution.py:80
  100.0 41.8 %collective-permute-start.5 = (bf16[8,16,1024]{2,1,0:T(8,128)(2,1)}, bf16[8,16,1024]{2,1,0:T(8,128)(2,1)S(1)}, u32[]{:S(2)}, u32[]{:S(2)}) collective-permute-start(bf16[8,16,1024]{2,1,0:T(8,128)(2,1)} %get-tuple-element.6), channel_id=1, source_target_pairs={{0,2},{1,3},{2,4},{3,5},{4,6},{5,7},{6,0},{7,1},{8,10},{9,11},{10,... | collective-permute-start | bytes 786440 | tf_op jit(solution)/shard_map/ppermute | solution.py:80
  125.1 19.5 %collective-permute-start.6 = (bf16[8,16,1024]{2,1,0:T(8,128)(2,1)}, bf16[8,16,1024]{2,1,0:T(8,128)(2,1)S(1)}, u32[]{:S(2)}, u32[]{:S(2)}) collective-permute-start(bf16[8,16,1024]{2,1,0:T(8,128)(2,1)} %get-tuple-element.6), channel_id=1, source_target_pairs={{0,1},{1,2},{2,3},{3,4},{4,5},{5,6},{6,7},{7,0},{8,9},{9,10},{10,1... | collective-permute-start | bytes 786440 | tf_op jit(solution)/shard_map/ppermute | solution.py:80
Sparse Core Ops, SparseCore 0:
  26.7 56.1 reduce-scatter.1
  84.9 137.8 all-gather.1

commit v4 on v3

--- a/solution.py
+++ b/solution.py
@@ -72,17 +72,28 @@
     )(project, spread, freq_resp)
 
 
+def gather_cols(amplitudes):
+    freqs, piece, width = amplitudes.shape
+    along_z = lax.all_gather(amplitudes, "zlo", axis=1, tiled=True)
+    along_z = along_z.reshape(freqs, -1, piece, width)
+    mine = lax.all_gather(along_z, "drow", axis=2)
+    theirs = lax.ppermute(mine, "core", perm=[(0, 1), (1, 0)])
+    first = lax.axis_index("core") == 0
+    pair = jnp.where(first, jnp.stack([mine, theirs], axis=2), jnp.stack([theirs, mine], axis=2))
+    return pair.reshape(freqs, -1, width)
+
+
 def gather_rows(amplitudes):
-    count = lax.axis_size("dcol")
+    count = lax.axis_size("zhi") * lax.axis_size("y")
     ahead = [amplitudes]
     for shift in range(1, count):
         ahead.append(
             lax.ppermute(
-                amplitudes, "dcol", perm=[(i, (i - shift) % count) for i in range(count)]
+                amplitudes, ("zhi", "y"), perm=[(i, (i - shift) % count) for i in range(count)]
             )
         )
     stacked = jnp.stack(ahead, axis=1)
-    rolled = jnp.roll(stacked, lax.axis_index("dcol"), axis=1)
+    rolled = jnp.roll(stacked, lax.axis_index(("zhi", "y")), axis=1)
     return rolled.reshape(stacked.shape[0], -1, stacked.shape[-1])
 
 
@@ -93,10 +104,10 @@
     )
     spread = jnp.sqrt(spectral_weights.astype(jnp.float32) / (64.0 * DIRS))
     partial_amp = partial_amplitudes(freq_resp, project, spread)
-    amplitudes = lax.psum_scatter(partial_amp, "node", scatter_dimension=1, tiled=True).astype(
+    amplitudes = lax.psum_scatter(partial_amp, ("zlo", "core"), scatter_dimension=1, tiled=True).astype(
         jnp.bfloat16
     )
-    cols = lax.all_gather(amplitudes, ("node", "drow"), axis=1, tiled=True)
+    cols = gather_cols(amplitudes)
     rows = gather_rows(amplitudes)
     rows_im = jnp.concatenate([rows[..., DIRS:], -rows[..., :DIRS]], axis=-1)
     lead = jnp.stack([rows, rows_im], axis=0)
@@ -105,11 +116,13 @@
 
 
 def solution(mesh):
-    placed = (P(None, None, ("drow", "dcol"), "node"), P(None, "node"), P(), P())
+    from jax.sharding import Mesh
+    fine = Mesh(mesh.devices.reshape(4, 2, 4, 2, 4), ("zlo", "core", "drow", "zhi", "y"))
+    placed = (P(None, None, ("drow", "zhi", "y"), ("zlo", "core")), P(None, ("zlo", "core")), P(), P())
     return jax.shard_map(
         local,
-        mesh=mesh,
+        mesh=fine,
         in_specs=placed,
-        out_specs=P(None, None, "drow", "node", "dcol"),
+        out_specs=P(None, None, "drow", ("zlo", "core"), ("zhi", "y")),
         check_vma=False,
     )

time: 244 us -> 223 us (0.914)
  the two profiles are of different devices: /device:TPU:35 before, /device:TPU:33 now
where the time goes in v4:
time: 223 us; the launch traced here: 221 us
  waiting for transfers between devices  148 us (66%)
  starting transfers between devices  23.6 us (11%)
  Pallas kernels  15.5 us (7%)
  between operations  13.3 us (6%)
  local copies, waits for them, and re-layouts  10.6 us (5%)
  other arithmetic  6.17 us (3%)
  matrix products  3.92 us (2%)
    reduce_scatter x1, waiting for transfers between devices, local(): lax.psum_scatter(partial_amp, ('zlo', 'core'), scatter_dimension=1, tiled...  56.3 us
    all_gather x1, waiting for transfers between devices, gather_cols(): mine = lax.all_gather(along_z, 'drow', axis=2)  38.3 us
    all_gather x1, waiting for transfers between devices, gather_cols(): along_z = lax.all_gather(amplitudes, 'zlo', axis=1, tiled=True)  32.1 us
    ppermute x7, starting transfers between devices, gather_rows(): lax.ppermute(amplitudes, ('zhi', 'y'), perm=[(i, (i - shift) % count) for...  22.7 us
    ppermute x7, waiting for transfers between devices, gather_rows(): lax.ppermute(amplitudes, ('zhi', 'y'), perm=[(i, (i - shift) % count) for...  21.1 us
    pallas_call x1, Pallas kernels, partial_amplitudes(): pl.pallas_call(amp_kernel, out_shape=jax.ShapeDtypeStruct((FREQS, rows, 2...  15.5 us
    broadcast_in_dim x1, local copies, waits for them, and re-layouts, local(): return spec[:, :, None]  5.34 us
  transfers between devices with their start and end apart: 11, of which 5 were waited for; matrix products, arithmetic and copies ran while one was open for 2% of the time, Pallas kernels for 0%

profile of v4, /device:TPU:33, one launch (start us, length us, event | category | flops | bytes accessed | tf_op | source)
XLA Modules:
  0.0 220.9 jit_solution(921204225883079893)
XLA Ops:
  6.5 0.8 fusion.10
  7.3 0.8 fusion.9
  8.1 1.3 multiply_sqrt_fusion.spread_ref
  9.4 1.6 multiply_add_fusion.proj_ref
  11.1 15.5 %shard_map.46 = f32[8,128,1024]{2,1,0:T(8,128)} custom-call(s32[1024,512]{1,0:T(8,128)} %multiply_add_fusion.proj_ref, f32[8,512]{1,0:T(8,128)} %multiply_sqrt_fusion.spread_ref, bf16[2,8,128,1024]{3,2,1,0:T(8,128)(2,1)} %resp_ref.1), custom_call_target="tpu_custom_call" | custom-call | tf_op jit(solution)/shard_map/pallas_call | solution.py:61
  26.5 0.0 reduce-scatter.2.cloned.1.call-update
  26.5 0.0 all-gather.3.cloned.1.call-start
  26.6 56.3 %reduce-scatter.2.cloned.1.call-done = f32[8,16,1024]{2,1,0:T(8,128)} async-done(((f32[8,128,1024]{2,1,0:T(8,128)}), f32[8,16,1024]{2,1,0:T(8,128)}) %reduce-scatter.2.cloned.1.call-update) | async-done | bytes 524304 | tf_op jit(solution)/shard_map/reduce_scatter | solution.py:107
  82.9 1.9 bitcast_dynamic-update-slice_fusion.14
  84.8 0.0 all-gather.3.cloned.1.call-update
  84.8 0.0 all-gather.5.cloned.1.call-start
  84.8 32.1 %all-gather.3.cloned.1.call-done = bf16[8,64,1024]{2,1,0:T(8,128)(2,1)} async-done(((bf16[8,16,1024]{2,1,0:T(8,128)(2,1)}), bf16[8,64,1024]{2,1,0:T(8,128)(2,1)}) %all-gather.3.cloned.1.call-update) | async-done | bytes 1048592 | tf_op jit(solution)/shard_map/all_gather | solution.py:77
  116.9 0.0 all-gather.5.cloned.1.call-update
  117.0 6.8 %collective-permute-start.1 = (bf16[8,16,1024]{2,1,0:T(8,128)(2,1)}, bf16[8,16,1024]{2,1,0:T(8,128)(2,1)S(1)}, u32[]{:S(2)}, u32[]{:S(2)}) collective-permute-start(bf16[8,16,1024]{2,1,0:T(8,128)(2,1)} %get-tuple-element.6), channel_id=1, source_target_pairs={{0,7},{1,0},{2,1},{3,2},{4,3},{5,4},{6,5},{7,6},{8,15},{9,8},{10,9... | collective-permute-start | bytes 786440 | tf_op jit(solution)/shard_map/ppermute | solution.py:91
  123.7 0.5 collective-permute-start.2
  124.3 0.6 collective-permute-start.7
  124.9 1.8 collective-permute-start.6
  126.7 5.6 %collective-permute-start.3 = (bf16[8,16,1024]{2,1,0:T(8,128)(2,1)}, bf16[8,16,1024]{2,1,0:T(8,128)(2,1)S(1)}, u32[]{:S(2)}, u32[]{:S(2)}) collective-permute-start(bf16[8,16,1024]{2,1,0:T(8,128)(2,1)} %get-tuple-element.6), channel_id=1, source_target_pairs={{0,5},{1,6},{2,7},{3,0},{4,1},{5,2},{6,3},{7,4},{8,13},{9,14},{10,... | collective-permute-start | bytes 786440 | tf_op jit(solution)/shard_map/ppermute | solution.py:91
  132.3 38.3 %all-gather.5.cloned.1.call-done = bf16[8,4,4,16,1024]{4,3,1,0,2:T(8,128)(2,1)} async-done(((bf16[8,4,1,16,1024]{4,3,1,0,2:T(8,128)(2,1)}), bf16[8,4,4,16,1024]{4,3,1,0,2:T(8,128)(2,1)}) %all-gather.5.cloned.1.call-update) | async-done | bytes 4194320 | tf_op jit(solution)/shard_map/all_gather | solution.py:79
  170.7 2.8 %copy.25 = bf16[8,4,4,16,1024]{4,3,2,1,0:T(8,128)(2,1)S(1)} copy(bf16[8,4,4,16,1024]{4,3,1,0,2:T(8,128)(2,1)} %all-gather.5.cloned.1.call-done) | data formatting | bytes 8388608 | tf_op jit(solution)/shard_map/all_gather | solution.py:79
  173.5 0.8 collective-permute-start
  174.3 4.6 %collective-permute-start.4 = (bf16[8,16,1024]{2,1,0:T(8,128)(2,1)S(1)}, bf16[8,16,1024]{2,1,0:T(8,128)(2,1)S(1)}, u32[]{:S(2)}, u32[]{:S(2)}) collective-permute-start(bf16[8,16,1024]{2,1,0:T(8,128)(2,1)S(1)} %copy-done), channel_id=1, source_target_pairs={{0,4},{1,5},{2,6},{3,7},{4,0},{5,1},{6,2},{7,3},{8,12},{9,13},{10,... | collective-permute-start | bytes 786440 | tf_op jit(solution)/shard_map/ppermute | solution.py:91
  179.0 2.7 %collective-permute-start.5 = (bf16[8,16,1024]{2,1,0:T(8,128)(2,1)S(1)}, bf16[8,16,1024]{2,1,0:T(8,128)(2,1)S(1)}, u32[]{:S(2)}, u32[]{:S(2)}) collective-permute-start(bf16[8,16,1024]{2,1,0:T(8,128)(2,1)S(1)} %copy-done), channel_id=1, source_target_pairs={{0,3},{1,4},{2,5},{3,6},{4,7},{5,0},{6,1},{7,2},{8,11},{9,12},{10,... | collective-permute-start | bytes 786440 | tf_op jit(solution)/shard_map/ppermute | solution.py:91
  181.7 9.3 %collective-permute-done.4 = bf16[8,16,1024]{2,1,0:T(8,128)(2,1)S(1)} collective-permute-done((bf16[8,16,1024]{2,1,0:T(8,128)(2,1)S(1)}, bf16[8,16,1024]{2,1,0:T(8,128)(2,1)S(1)}, u32[]{:S(2)}, u32[]{:S(2)}) %collective-permute-start.4) | collective-permute-done | bytes 262176 | tf_op jit(solution)/shard_map/ppermute | solution.py:91
  191.0 11.8 %collective-permute-done.5 = bf16[8,16,1024]{2,1,0:T(8,128)(2,1)S(1)} collective-permute-done((bf16[8,16,1024]{2,1,0:T(8,128)(2,1)S(1)}, bf16[8,16,1024]{2,1,0:T(8,128)(2,1)S(1)}, u32[]{:S(2)}, u32[]{:S(2)}) %collective-permute-start.5) | collective-permute-done | bytes 262176 | tf_op jit(solution)/shard_map/ppermute | solution.py:91
  203.2 0.3 constant_dynamic-slice_fusion
  203.5 0.3 copy.18
  203.8 0.1 fusion.8
  203.9 0.3 maximum_bitcast_fusion
  204.2 0.9 maximum_select_fusion
  205.1 3.9 %fusion.4 = f32[2,8,1,128,512]{3,4,0,1,2:T(8,128)} fusion(bf16[8,512,1024,1]{2,1,3,0:T(8,128)(2,1)S(1)} %bitcast.50, bf16[1,8,128,1024]{3,2,0,1:T(8,128)(2,1)S(1)} %maximum_bitcast_fusion, bf16[1,8,128,1024]{3,2,0,1:T(8,128)(2,1)S(1)} %bitcast.52), kind=kOutput, calls=%fused_computation.5 | convolution fusion | flops 2155872256 | bytes 16777216 | tf_op jit(solution)/shard_map/pfke,fje->pfkj/dot_general | solution.py:114
  209.0 5.3 %copy.21 = f32[2,8,1,128,512]{4,3,2,1,0:T(8,128)} copy(f32[2,8,1,128,512]{3,4,0,1,2:T(8,128)} %fusion.4) | data formatting | bytes 8388608 | tf_op jit(solution)/shard_map/broadcast_in_dim | solution.py:115
  (26 shorter events, 0.3 us)
Async XLA Ops:
  6.5 76.3 %reduce-scatter.2.cloned.1.call-start = ((), (), s32[]{:S(2)}) async-start(), calls=%async_computation.1 | async-start | bytes 4718592 | tf_op jit(solution)/shard_map/reduce_scatter | solution.py:107
  26.5 90.4 %all-gather.3.cloned.1.call-start = ((), (), s32[]{:S(2)}) async-start(), calls=%async_computation.2 | async-start | bytes 1310720 | tf_op jit(solution)/shard_map/all_gather | solution.py:77
  84.8 85.9 %all-gather.5.cloned.1.call-start = ((), (), s32[]{:S(2)}) async-start(), calls=%async_computation.3 | async-start | bytes 5242880 | tf_op jit(solution)/shard_map/all_gather | solution.py:79
  117.0 56.5 %collective-permute-start.1 = (bf16[8,16,1024]{2,1,0:T(8,128)(2,1)}, bf16[8,16,1024]{2,1,0:T(8,128)(2,1)S(1)}, u32[]{:S(2)}, u32[]{:S(2)}) collective-permute-start(bf16[8,16,1024]{2,1,0:T(8,128)(2,1)} %get-tuple-element.6), channel_id=1, source_target_pairs={{0,7},{1,0},{2,1},{3,2},{4,3},{5,4},{6,5},{7,6},{8,15},{9,8},{10,9... | collective-permute-start | bytes 786440 | tf_op jit(solution)/shard_map/ppermute | solution.py:91
  123.7 50.5 %collective-permute-start.2 = (bf16[8,16,1024]{2,1,0:T(8,128)(2,1)}, bf16[8,16,1024]{2,1,0:T(8,128)(2,1)S(1)}, u32[]{:S(2)}, u32[]{:S(2)}) collective-permute-start(bf16[8,16,1024]{2,1,0:T(8,128)(2,1)} %get-tuple-element.6), channel_id=1, source_target_pairs={{0,6},{1,7},{2,0},{3,1},{4,2},{5,3},{6,4},{7,5},{8,14},{9,15},{10,... | collective-permute-start | bytes 786440 | tf_op jit(solution)/shard_map/ppermute | solution.py:91
  124.3 50.0 %copy-start = (bf16[8,16,1024]{2,1,0:T(8,128)(2,1)S(1)}, bf16[8,16,1024]{2,1,0:T(8,128)(2,1)}, u32[]{:S(2)}) copy-start(bf16[8,16,1024]{2,1,0:T(8,128)(2,1)} %get-tuple-element.6) | copy-start | bytes 786436
  124.3 78.6 %collective-permute-start.7 = (bf16[8,16,1024]{2,1,0:T(8,128)(2,1)}, bf16[8,16,1024]{2,1,0:T(8,128)(2,1)S(1)}, u32[]{:S(2)}, u32[]{:S(2)}) collective-permute-start(bf16[8,16,1024]{2,1,0:T(8,128)(2,1)} %get-tuple-element.6), channel_id=1, source_target_pairs={{0,1},{1,2},{2,3},{3,4},{4,5},{5,6},{6,7},{7,0},{8,9},{9,10},{10,1... | collective-permute-start | bytes 786440 | tf_op jit(solution)/shard_map/ppermute | solution.py:91
  124.9 78.0 %collective-permute-start.6 = (bf16[8,16,1024]{2,1,0:T(8,128)(2,1)}, bf16[8,16,1024]{2,1,0:T(8,128)(2,1)S(1)}, u32[]{:S(2)}, u32[]{:S(2)}) collective-permute-start(bf16[8,16,1024]{2,1,0:T(8,128)(2,1)} %get-tuple-element.6), channel_id=1, source_target_pairs={{0,2},{1,3},{2,4},{3,5},{4,6},{5,7},{6,0},{7,1},{8,10},{9,11},{10,... | collective-permute-start | bytes 786440 | tf_op jit(solution)/shard_map/ppermute | solution.py:91
  126.7 52.2 %collective-permute-start.3 = (bf16[8,16,1024]{2,1,0:T(8,128)(2,1)}, bf16[8,16,1024]{2,1,0:T(8,128)(2,1)S(1)}, u32[]{:S(2)}, u32[]{:S(2)}) collective-permute-start(bf16[8,16,1024]{2,1,0:T(8,128)(2,1)} %get-tuple-element.6), channel_id=1, source_target_pairs={{0,5},{1,6},{2,7},{3,0},{4,1},{5,2},{6,3},{7,4},{8,13},{9,14},{10,... | collective-permute-start | bytes 786440 | tf_op jit(solution)/shard_map/ppermute | solution.py:91
  170.7 3.6 %copy-start.1 = (bf16[8,16,16,1024]{3,2,0,1:T(8,128)(2,1)S(1)}, bf16[8,16,16,1024]{3,2,0,1:T(8,128)(2,1)}, u32[]{:S(2)}) copy-start(bf16[8,16,16,1024]{3,2,0,1:T(8,128)(2,1)} %get-tuple-element.5) | copy-start | bytes 12582916
  173.5 30.7 %collective-permute-start = (bf16[8,4,4,16,1024]{4,3,2,1,0:T(8,128)(2,1)S(1)}, bf16[8,4,4,16,1024]{4,3,2,1,0:T(8,128)(2,1)S(1)}, u32[]{:S(2)}, u32[]{:S(2)}) collective-permute-start(bf16[8,4,4,16,1024]{4,3,2,1,0:T(8,128)(2,1)S(1)} %copy.25), channel_id=1, source_target_pairs={{0,32},{32,0},{1,33},{33,1},{2,34},{34,2},{3,35},{35,3},{4,36},{36... | collective-permute-start | bytes 12582920 | tf_op jit(solution)/shard_map/ppermute | solution.py:80
  174.3 16.7 %collective-permute-start.4 = (bf16[8,16,1024]{2,1,0:T(8,128)(2,1)S(1)}, bf16[8,16,1024]{2,1,0:T(8,128)(2,1)S(1)}, u32[]{:S(2)}, u32[]{:S(2)}) collective-permute-start(bf16[8,16,1024]{2,1,0:T(8,128)(2,1)S(1)} %copy-done), channel_id=1, source_target_pairs={{0,4},{1,5},{2,6},{3,7},{4,0},{5,1},{6,2},{7,3},{8,12},{9,13},{10,... | collective-permute-start | bytes 786440 | tf_op jit(solution)/shard_map/ppermute | solution.py:91
  179.0 23.9 %collective-permute-start.5 = (bf16[8,16,1024]{2,1,0:T(8,128)(2,1)S(1)}, bf16[8,16,1024]{2,1,0:T(8,128)(2,1)S(1)}, u32[]{:S(2)}, u32[]{:S(2)}) collective-permute-start(bf16[8,16,1024]{2,1,0:T(8,128)(2,1)S(1)} %copy-done), channel_id=1, source_target_pairs={{0,3},{1,4},{2,5},{3,6},{4,7},{5,0},{6,1},{7,2},{8,11},{9,12},{10,... | collective-permute-start | bytes 786440 | tf_op jit(solution)/shard_map/ppermute | solution.py:91
Sparse Core Ops, SparseCore 0:
  26.7 56.1 reduce-scatter.1
  84.9 31.9 all-gather.2
  118.7 51.8 all-gather.4

commit v5 on v4

--- a/solution.py
+++ b/solution.py
@@ -74,9 +74,8 @@
 
 def gather_cols(amplitudes):
     freqs, piece, width = amplitudes.shape
-    along_z = lax.all_gather(amplitudes, "zlo", axis=1, tiled=True)
-    along_z = along_z.reshape(freqs, -1, piece, width)
-    mine = lax.all_gather(along_z, "drow", axis=2)
+    mine = lax.all_gather(amplitudes, ("zlo", "drow"), axis=1)
+    mine = mine.reshape(freqs, lax.axis_size("zlo"), -1, piece, width)
     theirs = lax.ppermute(mine, "core", perm=[(0, 1), (1, 0)])
     first = lax.axis_index("core") == 0
     pair = jnp.where(first, jnp.stack([mine, theirs], axis=2), jnp.stack([theirs, mine], axis=2))

time: 223 us -> 265 us (1.19)
  local copies, waits for them, and re-layouts: 10.6 us -> 30.9 us
  waiting for transfers between devices: 148 us -> 163 us
  matrix products: 3.92 us -> 9.6 us
  other arithmetic: 6.17 us -> 9.22 us
    all_gather x2 -> x1, waiting for transfers between devices: 70.4 us -> 83.1 us  [gather_cols(): mine = lax.all_gather(amplitudes, ('zlo', 'drow'), axis=1)]
    unnamed x18 -> x16, local copies, waits for them, and re-layouts: 0.27 us -> 12.8 us
    select_n x0 -> x1, local copies, waits for them, and re-layouts: none -> 8.53 us  [gather_cols(): jnp.where(first, jnp.stack([mine, theirs], axis=2), jnp.stack([theirs, mi...]
    ppermute x7, starting transfers between devices: 22.7 us -> 15.3 us  [gather_rows(): lax.ppermute(amplitudes, ('zhi', 'y'), perm=[(i, (i - shift) % count) for...]
    ppermute x1, starting transfers between devices: 0.76 us -> 6.77 us  [gather_cols(): theirs = lax.ppermute(mine, 'core', perm=[(0, 1), (1, 0)])]
    dot_general x1, matrix products: 3.92 us -> 9.6 us  [local(): jnp.einsum('pfke,fje->pfkj', lead, cols, preferred_element_type=jnp.float32)]
    select_n x1, other arithmetic: 0.9 us -> 3.95 us  [gather_cols(): jnp.where(first, jnp.stack([mine, theirs], axis=2), jnp.stack([theirs, mi...]
    ppermute x7, waiting for transfers between devices: 21.1 us -> 24 us  [gather_rows(): lax.ppermute(amplitudes, ('zhi', 'y'), perm=[(i, (i - shift) % count) for...]
  transfers between devices with their start and end apart: 11 -> 10, of which waited for: 5 -> 5; matrix products, arithmetic and copies ran while one was open for 2% -> 5% of each run, Pallas kernels for 0% -> 0%
where the time goes in v5:
time: 265 us; the launch traced here: 264 us
  waiting for transfers between devices  163 us (62%)
  local copies, waits for them, and re-layouts  30.9 us (12%)
  starting transfers between devices  22.1 us (8%)
  Pallas kernels  15.5 us (6%)
  between operations  13.5 us (5%)
  matrix products  9.6 us (4%)
  other arithmetic  9.22 us (3%)
    all_gather x1, waiting for transfers between devices, gather_cols(): mine = lax.all_gather(amplitudes, ('zlo', 'drow'), axis=1)  83.1 us
    reduce_scatter x1, waiting for transfers between devices, local(): lax.psum_scatter(partial_amp, ('zlo', 'core'), scatter_dimension=1, tiled...  56.3 us
    ppermute x7, waiting for transfers between devices, gather_rows(): lax.ppermute(amplitudes, ('zhi', 'y'), perm=[(i, (i - shift) % count) for...  24 us
    pallas_call x1, Pallas kernels, partial_amplitudes(): pl.pallas_call(amp_kernel, out_shape=jax.ShapeDtypeStruct((FREQS, rows, 2...  15.5 us
    ppermute x7, starting transfers between devices, gather_rows(): lax.ppermute(amplitudes, ('zhi', 'y'), perm=[(i, (i - shift) % count) for...  15.3 us
    unnamed x16, local copies, waits for them, and re-layouts  12.8 us
    dot_general x1, matrix products, local(): jnp.einsum('pfke,fje->pfkj', lead, cols, preferred_element_type=jnp.float32)  9.6 us
    select_n x1, local copies, waits for them, and re-layouts, gather_cols(): jnp.where(first, jnp.stack([mine, theirs], axis=2), jnp.stack([theirs, mi...  8.53 us
  transfers between devices with their start and end apart: 10, of which 5 were waited for; matrix products, arithmetic and copies ran while one was open for 5% of the time, Pallas kernels for 0%

profile of v5, /device:TPU:33, one launch (start us, length us, event | category | flops | bytes accessed | tf_op | source)
XLA Modules:
  0.0 264.2 jit_solution(11484152035735671622)
XLA Ops:
  6.5 0.8 fusion.10
  7.3 0.8 fusion.9
  8.1 1.3 multiply_sqrt_fusion.spread_ref
  9.4 1.6 multiply_add_fusion.proj_ref
  11.1 15.5 %shard_map.46 = f32[8,128,1024]{2,1,0:T(8,128)} custom-call(s32[1024,512]{1,0:T(8,128)} %multiply_add_fusion.proj_ref, f32[8,512]{1,0:T(8,128)} %multiply_sqrt_fusion.spread_ref, bf16[2,8,128,1024]{3,2,1,0:T(8,128)(2,1)} %resp_ref.1), custom_call_target="tpu_custom_call" | custom-call | tf_op jit(solution)/shard_map/pallas_call | solution.py:61
  26.6 56.3 %reduce-scatter.2.cloned.1.call-done = f32[8,16,1024]{2,1,0:T(8,128)} async-done(((f32[8,128,1024]{2,1,0:T(8,128)}), f32[8,16,1024]{2,1,0:T(8,128)}) %reduce-scatter.2.cloned.1.call-update) | async-done | bytes 524304 | tf_op jit(solution)/shard_map/reduce_scatter | solution.py:106
  82.9 1.9 bitcast_dynamic-update-slice_fusion.14
  84.8 6.2 %collective-permute-start.1 = (bf16[8,16,1024]{2,1,0:T(8,128)(2,1)}, bf16[8,16,1024]{2,1,0:T(8,128)(2,1)S(1)}, u32[]{:S(2)}, u32[]{:S(2)}) collective-permute-start(bf16[8,16,1024]{2,1,0:T(8,128)(2,1)} %get-tuple-element.6), channel_id=1, source_target_pairs={{0,7},{1,0},{2,1},{3,2},{4,3},{5,4},{6,5},{7,6},{8,15},{9,8},{10,9... | collective-permute-start | bytes 786440 | tf_op jit(solution)/shard_map/ppermute | solution.py:90
  92.1 1.8 collective-permute-start.6
  94.0 5.6 %collective-permute-start.3 = (bf16[8,16,1024]{2,1,0:T(8,128)(2,1)}, bf16[8,16,1024]{2,1,0:T(8,128)(2,1)S(1)}, u32[]{:S(2)}, u32[]{:S(2)}) collective-permute-start(bf16[8,16,1024]{2,1,0:T(8,128)(2,1)} %get-tuple-element.6), channel_id=1, source_target_pairs={{0,5},{1,6},{2,7},{3,0},{4,1},{5,2},{6,3},{7,4},{8,13},{9,14},{10,... | collective-permute-start | bytes 786440 | tf_op jit(solution)/shard_map/ppermute | solution.py:90
  99.6 4.0 %collective-permute-done.1 = bf16[8,16,1024]{2,1,0:T(8,128)(2,1)S(1)} collective-permute-done((bf16[8,16,1024]{2,1,0:T(8,128)(2,1)}, bf16[8,16,1024]{2,1,0:T(8,128)(2,1)S(1)}, u32[]{:S(2)}, u32[]{:S(2)}) %collective-permute-start.1) | collective-permute-done | bytes 262176 | tf_op jit(solution)/shard_map/ppermute | solution.py:90
  103.5 83.1 %all-gather.3.cloned.1.call-done = bf16[8,256,1024]{2,1,0:T(8,128)(2,1)} async-done(((bf16[8,16,1024]{2,1,0:T(8,128)(2,1)}), bf16[8,256,1024]{2,1,0:T(8,128)(2,1)}) %all-gather.3.cloned.1.call-update) | async-done | bytes 4194320 | tf_op jit(solution)/shard_map/all_gather | solution.py:77
  186.7 6.8 %collective-permute-start = (bf16[8,4,4,16,1024]{4,3,2,1,0:T(8,128)(2,1)}, bf16[8,4,4,16,1024]{4,3,2,1,0:T(8,128)(2,1)S(1)}, u32[]{:S(2)}, u32[]{:S(2)}) collective-permute-start(bf16[8,4,4,16,1024]{4,3,2,1,0:T(8,128)(2,1)} %bitcast.50), channel_id=1, source_target_pairs={{0,32},{32,0},{1,33},{33,1},{2,34},{34,2},{3,35},{35,3},{4,36},{36... | collective-permute-start | bytes 12582920 | tf_op jit(solution)/shard_map/ppermute | solution.py:79
  193.4 0.7 bitcast_dynamic-update-slice_fusion.12
  194.7 0.7 bitcast_dynamic-update-slice_fusion.10
  195.4 0.7 bitcast_dynamic-update-slice_fusion.8
  196.1 15.7 %collective-permute-done.4 = bf16[8,16,1024]{2,1,0:T(8,128)(2,1)S(1)} collective-permute-done((bf16[8,16,1024]{2,1,0:T(8,128)(2,1)}, bf16[8,16,1024]{2,1,0:T(8,128)(2,1)S(1)}, u32[]{:S(2)}, u32[]{:S(2)}) %collective-permute-start.4) | collective-permute-done | bytes 262176 | tf_op jit(solution)/shard_map/ppermute | solution.py:90
  212.6 4.3 %collective-permute-done.5 = bf16[8,16,1024]{2,1,0:T(8,128)(2,1)S(1)} collective-permute-done((bf16[8,16,1024]{2,1,0:T(8,128)(2,1)}, bf16[8,16,1024]{2,1,0:T(8,128)(2,1)S(1)}, u32[]{:S(2)}, u32[]{:S(2)}) %collective-permute-start.5) | collective-permute-done | bytes 262176 | tf_op jit(solution)/shard_map/ppermute | solution.py:90
  217.6 0.7 bitcast_dynamic-update-slice_fusion.2
  218.4 0.7 bitcast_dynamic-update-slice_fusion
  219.1 1.7 bitcast_dynamic-update-slice_fusion.15
  220.8 0.7 bitcast_dynamic-update-slice_fusion.13
  221.5 0.7 bitcast_dynamic-update-slice_fusion.11
  222.2 0.7 bitcast_dynamic-update-slice_fusion.9
  224.4 0.7 bitcast_dynamic-update-slice_fusion.3
  225.1 0.7 bitcast_dynamic-update-slice_fusion.1
  225.8 1.8 constant_dynamic-slice_fusion
  228.2 1.8 copy-done
  230.0 3.9 %maximum_select_fusion = bf16[8,4,2,4,16,1024]{5,4,3,1,0,2:T(8,128)(2,1)} fusion(bf16[8,4,1,4,16,1024]{5,4,3,1,0,2:T(8,128)(2,1)S(1)} %bitcast.52, bf16[8,4,1,4,16,1024]{5,4,3,1,0,2:T(8,128)(2,1)S(1)} %bitcast.51, pred[]{:T(512)S(6)} %eq.6), kind=kLoop, calls=%fused_computation | loop fusion | flops 12582912 | bytes 16777216 | tf_op jit(solution)/shard_map/jit(_where)/select_n | solution.py:81
  233.9 8.5 %copy.7 = bf16[8,4,2,4,16,1024]{5,4,3,2,1,0:T(8,128)(2,1)} copy(bf16[8,4,2,4,16,1024]{5,4,3,1,0,2:T(8,128)(2,1)} %maximum_select_fusion) | data formatting | bytes 16777216 | tf_op jit(solution)/shard_map/jit(_where)/select_n | solution.py:81
  242.5 9.6 %fusion.4 = f32[2,8,1,128,512]{3,4,0,1,2:T(8,128)} fusion(bf16[8,512,1024,1]{2,1,3,0:T(8,128)(2,1)} %bitcast.47, bf16[1,8,128,1024]{3,2,0,1:T(8,128)(2,1)S(1)} %maximum_bitcast_fusion, bf16[1,8,128,1024]{3,2,0,1:T(8,128)(2,1)S(1)} %bitcast.49), kind=kOutput, calls=%fused_computation.5 | convolution fusion | flops 2155872256 | bytes 16777216 | tf_op jit(solution)/shard_map/pfke,fje->pfkj/dot_general | solution.py:113
  252.1 5.3 %copy.11 = f32[2,8,1,128,512]{4,3,2,1,0:T(8,128)} copy(f32[2,8,1,128,512]{3,4,0,1,2:T(8,128)} %fusion.4) | data formatting | bytes 8388608 | tf_op jit(solution)/shard_map/broadcast_in_dim | solution.py:114
  (21 shorter events, 5.2 us)
Async XLA Ops:
  6.5 76.3 %reduce-scatter.2.cloned.1.call-start = ((), (), s32[]{:S(2)}) async-start(), calls=%async_computation.1 | async-start | bytes 4718592 | tf_op jit(solution)/shard_map/reduce_scatter | solution.py:106
  26.5 160.1 %all-gather.3.cloned.1.call-start = ((), (), s32[]{:S(2)}) async-start(), calls=%async_computation.2 | async-start | bytes 4456448 | tf_op jit(solution)/shard_map/all_gather | solution.py:77
  84.8 18.8 %collective-permute-start.1 = (bf16[8,16,1024]{2,1,0:T(8,128)(2,1)}, bf16[8,16,1024]{2,1,0:T(8,128)(2,1)S(1)}, u32[]{:S(2)}, u32[]{:S(2)}) collective-permute-start(bf16[8,16,1024]{2,1,0:T(8,128)(2,1)} %get-tuple-element.6), channel_id=1, source_target_pairs={{0,7},{1,0},{2,1},{3,2},{4,3},{5,4},{6,5},{7,6},{8,15},{9,8},{10,9... | collective-permute-start | bytes 786440 | tf_op jit(solution)/shard_map/ppermute | solution.py:90
  91.0 103.2 %collective-permute-start.2 = (bf16[8,16,1024]{2,1,0:T(8,128)(2,1)}, bf16[8,16,1024]{2,1,0:T(8,128)(2,1)S(1)}, u32[]{:S(2)}, u32[]{:S(2)}) collective-permute-start(bf16[8,16,1024]{2,1,0:T(8,128)(2,1)} %get-tuple-element.6), channel_id=1, source_target_pairs={{0,6},{1,7},{2,0},{3,1},{4,2},{5,3},{6,4},{7,5},{8,14},{9,15},{10,... | collective-permute-start | bytes 786440 | tf_op jit(solution)/shard_map/ppermute | solution.py:90
  91.5 126.8 %collective-permute-start.7 = (bf16[8,16,1024]{2,1,0:T(8,128)(2,1)}, bf16[8,16,1024]{2,1,0:T(8,128)(2,1)S(1)}, u32[]{:S(2)}, u32[]{:S(2)}) collective-permute-start(bf16[8,16,1024]{2,1,0:T(8,128)(2,1)} %get-tuple-element.6), channel_id=1, source_target_pairs={{0,1},{1,2},{2,3},{3,4},{4,5},{5,6},{6,7},{7,0},{8,9},{9,10},{10,1... | collective-permute-start | bytes 786440 | tf_op jit(solution)/shard_map/ppermute | solution.py:90
  92.1 125.5 %collective-permute-start.6 = (bf16[8,16,1024]{2,1,0:T(8,128)(2,1)}, bf16[8,16,1024]{2,1,0:T(8,128)(2,1)S(1)}, u32[]{:S(2)}, u32[]{:S(2)}) collective-permute-start(bf16[8,16,1024]{2,1,0:T(8,128)(2,1)} %get-tuple-element.6), channel_id=1, source_target_pairs={{0,2},{1,3},{2,4},{3,5},{4,6},{5,7},{6,0},{7,1},{8,10},{9,11},{10,... | collective-permute-start | bytes 786440 | tf_op jit(solution)/shard_map/ppermute | solution.py:90
  94.0 101.5 %collective-permute-start.3 = (bf16[8,16,1024]{2,1,0:T(8,128)(2,1)}, bf16[8,16,1024]{2,1,0:T(8,128)(2,1)S(1)}, u32[]{:S(2)}, u32[]{:S(2)}) collective-permute-start(bf16[8,16,1024]{2,1,0:T(8,128)(2,1)} %get-tuple-element.6), channel_id=1, source_target_pairs={{0,5},{1,6},{2,7},{3,0},{4,1},{5,2},{6,3},{7,4},{8,13},{9,14},{10,... | collective-permute-start | bytes 786440 | tf_op jit(solution)/shard_map/ppermute | solution.py:90
  186.7 41.6 %collective-permute-start = (bf16[8,4,4,16,1024]{4,3,2,1,0:T(8,128)(2,1)}, bf16[8,4,4,16,1024]{4,3,2,1,0:T(8,128)(2,1)S(1)}, u32[]{:S(2)}, u32[]{:S(2)}) collective-permute-start(bf16[8,4,4,16,1024]{4,3,2,1,0:T(8,128)(2,1)} %bitcast.50), channel_id=1, source_target_pairs={{0,32},{32,0},{1,33},{33,1},{2,34},{34,2},{3,35},{35,3},{4,36},{36... | collective-permute-start | bytes 12582920 | tf_op jit(solution)/shard_map/ppermute | solution.py:79
  194.2 17.7 %collective-permute-start.4 = (bf16[8,16,1024]{2,1,0:T(8,128)(2,1)}, bf16[8,16,1024]{2,1,0:T(8,128)(2,1)S(1)}, u32[]{:S(2)}, u32[]{:S(2)}) collective-permute-start(bf16[8,16,1024]{2,1,0:T(8,128)(2,1)} %get-tuple-element.6), channel_id=1, source_target_pairs={{0,4},{1,5},{2,6},{3,7},{4,0},{5,1},{6,2},{7,3},{8,12},{9,13},{10,... | collective-permute-start | bytes 786440 | tf_op jit(solution)/shard_map/ppermute | solution.py:90
  195.4 21.5 %collective-permute-start.5 = (bf16[8,16,1024]{2,1,0:T(8,128)(2,1)}, bf16[8,16,1024]{2,1,0:T(8,128)(2,1)S(1)}, u32[]{:S(2)}, u32[]{:S(2)}) collective-permute-start(bf16[8,16,1024]{2,1,0:T(8,128)(2,1)} %get-tuple-element.6), channel_id=1, source_target_pairs={{0,3},{1,4},{2,5},{3,6},{4,7},{5,0},{6,1},{7,2},{8,11},{9,12},{10,... | collective-permute-start | bytes 786440 | tf_op jit(solution)/shard_map/ppermute | solution.py:90
  227.8 2.2 copy-start
Sparse Core Ops, SparseCore 0:
  26.7 56.1 reduce-scatter.1
  84.9 101.7 all-gather.2

commit v6 on v4

--- a/solution.py
+++ b/solution.py
@@ -72,10 +72,19 @@
     )(project, spread, freq_resp)
 
 
+def gather_by_permutes(piece, axis_name, count):
+    ahead = [piece]
+    for shift in range(1, count):
+        ahead.append(
+            lax.ppermute(piece, axis_name, perm=[(i, (i - shift) % count) for i in range(count)])
+        )
+    stacked = jnp.stack(ahead, axis=1)
+    return jnp.roll(stacked, lax.axis_index(axis_name), axis=1)
+
+
 def gather_cols(amplitudes):
     freqs, piece, width = amplitudes.shape
-    along_z = lax.all_gather(amplitudes, "zlo", axis=1, tiled=True)
-    along_z = along_z.reshape(freqs, -1, piece, width)
+    along_z = gather_by_permutes(amplitudes, "zlo", lax.axis_size("zlo"))
     mine = lax.all_gather(along_z, "drow", axis=2)
     theirs = lax.ppermute(mine, "core", perm=[(0, 1), (1, 0)])
     first = lax.axis_index("core") == 0
@@ -85,16 +94,8 @@
 
 def gather_rows(amplitudes):
     count = lax.axis_size("zhi") * lax.axis_size("y")
-    ahead = [amplitudes]
-    for shift in range(1, count):
-        ahead.append(
-            lax.ppermute(
-                amplitudes, ("zhi", "y"), perm=[(i, (i - shift) % count) for i in range(count)]
-            )
-        )
-    stacked = jnp.stack(ahead, axis=1)
-    rolled = jnp.roll(stacked, lax.axis_index(("zhi", "y")), axis=1)
-    return rolled.reshape(stacked.shape[0], -1, stacked.shape[-1])
+    rows = gather_by_permutes(amplitudes, ("zhi", "y"), count)
+    return rows.reshape(amplitudes.shape[0], -1, amplitudes.shape[-1])
 
 
 def local(freq_resp, node_coords, heading_steps, spectral_weights):

time: 223 us -> 267 us (1.20)
  local copies, waits for them, and re-layouts: 10.6 us -> 31.3 us
  other arithmetic: 6.17 us -> 13.3 us
  starting transfers between devices: 23.6 us -> 30.2 us
  matrix products: 3.92 us -> 9.59 us
  waiting for transfers between devices: 148 us -> 152 us
    all_gather x1 -> x0, waiting for transfers between devices: 32.1 us -> none  [gather_cols(): along_z = lax.all_gather(amplitudes, 'zlo', axis=1, tiled=True)]
    ppermute x7 -> x10, waiting for transfers between devices: 21.1 us -> 42.7 us  [gather_by_permutes(): lax.ppermute(piece, axis_name, perm=[(i, (i - shift) % count) for i in ra...]
    all_gather x1, waiting for transfers between devices: 38.3 us -> 52.9 us  [gather_cols(): mine = lax.all_gather(along_z, 'drow', axis=2)]
    unnamed x18 -> x22, local copies, waits for them, and re-layouts: 0.27 us -> 12.1 us
    select_n x0 -> x1, local copies, waits for them, and re-layouts: none -> 8.53 us  [gather_cols(): jnp.where(first, jnp.stack([mine, theirs], axis=2), jnp.stack([theirs, mi...]
    select_n x1, other arithmetic: 0.9 us -> 8.15 us  [gather_cols(): jnp.where(first, jnp.stack([mine, theirs], axis=2), jnp.stack([theirs, mi...]
    ppermute x7 -> x10, starting transfers between devices: 22.7 us -> 29.4 us  [gather_by_permutes(): lax.ppermute(piece, axis_name, perm=[(i, (i - shift) % count) for i in ra...]
    dot_general x1, matrix products: 3.92 us -> 9.59 us  [local(): jnp.einsum('pfke,fje->pfkj', lead, cols, preferred_element_type=jnp.float32)]
  transfers between devices with their start and end apart: 11 -> 13, of which waited for: 5 -> 8; matrix products, arithmetic and copies ran while one was open for 2% -> 5% of each run, Pallas kernels for 0% -> 0%
where the time goes in v6:
time: 267 us; the launch traced here: 265 us
  waiting for transfers between devices  152 us (57%)
  local copies, waits for them, and re-layouts  31.3 us (12%)
  starting transfers between devices  30.2 us (11%)
  Pallas kernels  15.5 us (6%)
  between operations  13.5 us (5%)
  other arithmetic  13.3 us (5%)
  matrix products  9.59 us (4%)
    reduce_scatter x1, waiting for transfers between devices, local(): lax.psum_scatter(partial_amp, ('zlo', 'core'), scatter_dimension=1, tiled...  56.3 us
    all_gather x1, waiting for transfers between devices, gather_cols(): mine = lax.all_gather(along_z, 'drow', axis=2)  52.9 us
    ppermute x10, waiting for transfers between devices, gather_by_permutes(): lax.ppermute(piece, axis_name, perm=[(i, (i - shift) % count) for i in ra...  42.7 us
    ppermute x10, starting transfers between devices, gather_by_permutes(): lax.ppermute(piece, axis_name, perm=[(i, (i - shift) % count) for i in ra...  29.4 us
    pallas_call x1, Pallas kernels, partial_amplitudes(): pl.pallas_call(amp_kernel, out_shape=jax.ShapeDtypeStruct((FREQS, rows, 2...  15.5 us
    unnamed x22, local copies, waits for them, and re-layouts  12.1 us
    dot_general x1, matrix products, local(): jnp.einsum('pfke,fje->pfkj', lead, cols, preferred_element_type=jnp.float32)  9.59 us
    select_n x1, local copies, waits for them, and re-layouts, gather_cols(): jnp.where(first, jnp.stack([mine, theirs], axis=2), jnp.stack([theirs, mi...  8.53 us
  transfers between devices with their start and end apart: 13, of which 8 were waited for; matrix products, arithmetic and copies ran while one was open for 5% of the time, Pallas kernels for 0%

profile of v6, /device:TPU:33, one launch (start us, length us, event | category | flops | bytes accessed | tf_op | source)
XLA Modules:
  0.0 265.2 jit_solution(13638095944377673446)
XLA Ops:
  6.5 0.8 fusion.10
  7.3 0.8 fusion.9
  8.1 1.3 multiply_sqrt_fusion.spread_ref
  9.4 1.6 multiply_add_fusion.proj_ref
  11.1 15.5 %shard_map.46 = f32[8,128,1024]{2,1,0:T(8,128)} custom-call(s32[1024,512]{1,0:T(8,128)} %multiply_add_fusion.proj_ref, f32[8,512]{1,0:T(8,128)} %multiply_sqrt_fusion.spread_ref, bf16[2,8,128,1024]{3,2,1,0:T(8,128)(2,1)} %resp_ref.1), custom_call_target="tpu_custom_call" | custom-call | tf_op jit(solution)/shard_map/pallas_call | solution.py:61
  26.6 56.3 %reduce-scatter.2.cloned.1.call-done = f32[8,16,1024]{2,1,0:T(8,128)} async-done(((f32[8,128,1024]{2,1,0:T(8,128)}), f32[8,16,1024]{2,1,0:T(8,128)}) %reduce-scatter.2.cloned.1.call-update) | async-done | bytes 524304 | tf_op jit(solution)/shard_map/reduce_scatter | solution.py:108
  82.9 1.8 bitcast_dynamic-update-slice_fusion.21
  84.7 6.1 %collective-permute-start.4 = (bf16[8,16,1024]{2,1,0:T(8,128)(2,1)S(1)}, bf16[8,16,1024]{2,1,0:T(8,128)(2,1)S(1)}, u32[]{:S(2)}, u32[]{:S(2)}) collective-permute-start(bf16[8,16,1024]{2,1,0:T(8,128)(2,1)S(1)} %get-tuple-element.6), channel_id=1, source_target_pairs={{0,7},{1,0},{2,1},{3,2},{4,3},{5,4},{6,5},{7,6},{8,15},{9,8},{10,9... | collective-permute-start | bytes 786440 | tf_op jit(solution)/shard_map/ppermute | solution.py:79
  91.9 1.8 collective-permute-start.9
  93.8 3.2 %collective-permute-start.8 = (bf16[8,16,1024]{2,1,0:T(8,128)(2,1)S(1)}, bf16[8,16,1024]{2,1,0:T(8,128)(2,1)S(1)}, u32[]{:S(2)}, u32[]{:S(2)}) collective-permute-start(bf16[8,16,1024]{2,1,0:T(8,128)(2,1)S(1)} %get-tuple-element.6), channel_id=1, source_target_pairs={{0,3},{1,4},{2,5},{3,6},{4,7},{5,0},{6,1},{7,2},{8,11},{9,12},{10,... | collective-permute-start | bytes 786440 | tf_op jit(solution)/shard_map/ppermute | solution.py:79
  97.0 2.9 %collective-permute-done.4 = bf16[8,16,1024]{2,1,0:T(8,128)(2,1)S(1)} collective-permute-done((bf16[8,16,1024]{2,1,0:T(8,128)(2,1)S(1)}, bf16[8,16,1024]{2,1,0:T(8,128)(2,1)S(1)}, u32[]{:S(2)}, u32[]{:S(2)}) %collective-permute-start.4) | collective-permute-done | bytes 262176 | tf_op jit(solution)/shard_map/ppermute | solution.py:79
  100.0 0.7 bitcast_dynamic-update-slice_fusion.12
  100.8 8.4 %collective-permute-done.5 = bf16[8,16,1024]{2,1,0:T(8,128)(2,1)S(1)} collective-permute-done((bf16[8,16,1024]{2,1,0:T(8,128)(2,1)S(1)}, bf16[8,16,1024]{2,1,0:T(8,128)(2,1)S(1)}, u32[]{:S(2)}, u32[]{:S(2)}) %collective-permute-start.5) | collective-permute-done | bytes 262176 | tf_op jit(solution)/shard_map/ppermute | solution.py:79
  109.2 2.5 collective-permute-start.7
  112.4 5.9 %collective-permute-done.6 = bf16[8,16,1024]{2,1,0:T(8,128)(2,1)S(1)} collective-permute-done((bf16[8,16,1024]{2,1,0:T(8,128)(2,1)S(1)}, bf16[8,16,1024]{2,1,0:T(8,128)(2,1)S(1)}, u32[]{:S(2)}, u32[]{:S(2)}) %collective-permute-start.6) | collective-permute-done | bytes 262176 | tf_op jit(solution)/shard_map/ppermute | solution.py:79
  118.3 0.7 bitcast_dynamic-update-slice_fusion.8
  119.1 7.6 %collective-permute-done.7 = bf16[8,16,1024]{2,1,0:T(8,128)(2,1)S(1)} collective-permute-done((bf16[8,16,1024]{2,1,0:T(8,128)(2,1)S(1)}, bf16[8,16,1024]{2,1,0:T(8,128)(2,1)S(1)}, u32[]{:S(2)}, u32[]{:S(2)}) %collective-permute-start.7) | collective-permute-done | bytes 262176 | tf_op jit(solution)/shard_map/ppermute | solution.py:79
  126.6 14.4 %collective-permute-start.1 = (bf16[8,16,1024]{2,1,0:T(8,128)(2,1)S(1)}, bf16[8,16,1024]{2,1,0:T(8,128)(2,1)S(1)}, u32[]{:S(2)}, u32[]{:S(2)}) collective-permute-start(bf16[8,16,1024]{2,1,0:T(8,128)(2,1)S(1)} %get-tuple-element.6), channel_id=1, source_target_pairs={{0,128},{64,192},{128,0},{192,64},{1,129},{65,193},{129,1},{193,65... | collective-permute-start | bytes 786440 | tf_op jit(solution)/shard_map/ppermute | solution.py:79
  141.8 0.7 bitcast_dynamic-update-slice_fusion.4
  142.5 0.7 bitcast_dynamic-update-slice_fusion.2
  143.2 0.7 bitcast_dynamic-update-slice_fusion
  144.0 0.8 bitcast_dynamic-update-slice_fusion.22
  144.7 15.5 %collective-permute-done = bf16[8,16,1024]{2,1,0:T(8,128)(2,1)S(1)} collective-permute-done((bf16[8,16,1024]{2,1,0:T(8,128)(2,1)S(1)}, bf16[8,16,1024]{2,1,0:T(8,128)(2,1)S(1)}, u32[]{:S(2)}, u32[]{:S(2)}) %collective-permute-start) | collective-permute-done | bytes 262176 | tf_op jit(solution)/shard_map/ppermute | solution.py:79
  160.2 2.4 collective-permute-done.1
  162.8 1.1 constant_dynamic-slice_fusion.1
  163.9 52.9 %all-gather.3.cloned.1.call-done = bf16[8,4,64,1024]{3,2,0,1:T(8,128)(2,1)} async-done(((bf16[8,4,16,1024]{3,2,0,1:T(8,128)(2,1)}), bf16[8,4,64,1024]{3,2,0,1:T(8,128)(2,1)}) %all-gather.3.cloned.1.call-update) | async-done | bytes 4194320 | tf_op jit(solution)/shard_map/all_gather | solution.py:88
  222.6 1.8 constant_dynamic-slice_fusion
  225.0 1.8 copy-done
  226.8 8.1 %maximum_select_fusion = bf16[8,4,2,4,16,1024]{5,4,3,0,1,2:T(8,128)(2,1)} fusion(bf16[8,4,1,4,16,1024]{5,4,3,0,1,2:T(8,128)(2,1)} %bitcast.10, bf16[8,4,1,4,16,1024]{5,4,3,0,1,2:T(8,128)(2,1)S(1)} %bitcast.62, pred[]{:T(512)S(6)} %eq.8), kind=kLoop, calls=%fused_computation | loop fusion | flops 12582912 | bytes 16777216 | tf_op jit(solution)/shard_map/jit(_where)/select_n | solution.py:91
  234.9 8.5 %copy.7 = bf16[8,4,2,4,16,1024]{5,4,3,2,1,0:T(8,128)(2,1)} copy(bf16[8,4,2,4,16,1024]{5,4,3,0,1,2:T(8,128)(2,1)} %maximum_select_fusion) | data formatting | bytes 16777216 | tf_op jit(solution)/shard_map/jit(_where)/select_n | solution.py:91
  243.4 9.6 %fusion.4 = f32[2,8,1,128,512]{3,4,0,1,2:T(8,128)} fusion(bf16[8,512,1024,1]{2,1,3,0:T(8,128)(2,1)} %bitcast.58, bf16[1,8,128,1024]{3,2,0,1:T(8,128)(2,1)S(1)} %maximum_bitcast_fusion, bf16[1,8,128,1024]{3,2,0,1:T(8,128)(2,1)S(1)} %bitcast.60), kind=kOutput, calls=%fused_computation.5 | convolution fusion | flops 2155872256 | bytes 16777216 | tf_op jit(solution)/shard_map/pfke,fje->pfkj/dot_general | solution.py:115
  253.0 5.3 %copy.11 = f32[2,8,1,128,512]{4,3,2,1,0:T(8,128)} copy(f32[2,8,1,128,512]{3,4,0,1,2:T(8,128)} %fusion.4) | data formatting | bytes 8388608 | tf_op jit(solution)/shard_map/broadcast_in_dim | solution.py:116
  (35 shorter events, 9.4 us)
Async XLA Ops:
  6.5 76.3 %reduce-scatter.2.cloned.1.call-start = ((), (), s32[]{:S(2)}) async-start(), calls=%async_computation.1 | async-start | bytes 4718592 | tf_op jit(solution)/shard_map/reduce_scatter | solution.py:108
  26.5 190.3 %all-gather.3.cloned.1.call-start = ((), (), s32[]{:S(2)}) async-start(), calls=%async_computation.2 | async-start | bytes 5242880 | tf_op jit(solution)/shard_map/all_gather | solution.py:88
  84.7 15.2 %collective-permute-start.4 = (bf16[8,16,1024]{2,1,0:T(8,128)(2,1)S(1)}, bf16[8,16,1024]{2,1,0:T(8,128)(2,1)S(1)}, u32[]{:S(2)}, u32[]{:S(2)}) collective-permute-start(bf16[8,16,1024]{2,1,0:T(8,128)(2,1)S(1)} %get-tuple-element.6), channel_id=1, source_target_pairs={{0,7},{1,0},{2,1},{3,2},{4,3},{5,4},{6,5},{7,6},{8,15},{9,8},{10,9... | collective-permute-start | bytes 786440 | tf_op jit(solution)/shard_map/ppermute | solution.py:79
  90.8 18.4 %collective-permute-start.5 = (bf16[8,16,1024]{2,1,0:T(8,128)(2,1)S(1)}, bf16[8,16,1024]{2,1,0:T(8,128)(2,1)S(1)}, u32[]{:S(2)}, u32[]{:S(2)}) collective-permute-start(bf16[8,16,1024]{2,1,0:T(8,128)(2,1)S(1)} %get-tuple-element.6), channel_id=1, source_target_pairs={{0,6},{1,7},{2,0},{3,1},{4,2},{5,3},{6,4},{7,5},{8,14},{9,15},{10,... | collective-permute-start | bytes 786440 | tf_op jit(solution)/shard_map/ppermute | solution.py:79
  91.3 51.9 %collective-permute-start.10 = (bf16[8,16,1024]{2,1,0:T(8,128)(2,1)S(1)}, bf16[8,16,1024]{2,1,0:T(8,128)(2,1)S(1)}, u32[]{:S(2)}, u32[]{:S(2)}) collective-permute-start(bf16[8,16,1024]{2,1,0:T(8,128)(2,1)S(1)} %get-tuple-element.6), channel_id=1, source_target_pairs={{0,1},{1,2},{2,3},{3,4},{4,5},{5,6},{6,7},{7,0},{8,9},{9,10},{10,1... | collective-permute-start | bytes 786440 | tf_op jit(solution)/shard_map/ppermute | solution.py:79
  91.9 50.6 %collective-permute-start.9 = (bf16[8,16,1024]{2,1,0:T(8,128)(2,1)S(1)}, bf16[8,16,1024]{2,1,0:T(8,128)(2,1)S(1)}, u32[]{:S(2)}, u32[]{:S(2)}) collective-permute-start(bf16[8,16,1024]{2,1,0:T(8,128)(2,1)S(1)} %get-tuple-element.6), channel_id=1, source_target_pairs={{0,2},{1,3},{2,4},{3,5},{4,6},{5,7},{6,0},{7,1},{8,10},{9,11},{10,... | collective-permute-start | bytes 786440 | tf_op jit(solution)/shard_map/ppermute | solution.py:79
  93.8 48.0 %collective-permute-start.8 = (bf16[8,16,1024]{2,1,0:T(8,128)(2,1)S(1)}, bf16[8,16,1024]{2,1,0:T(8,128)(2,1)S(1)}, u32[]{:S(2)}, u32[]{:S(2)}) collective-permute-start(bf16[8,16,1024]{2,1,0:T(8,128)(2,1)S(1)} %get-tuple-element.6), channel_id=1, source_target_pairs={{0,3},{1,4},{2,5},{3,6},{4,7},{5,0},{6,1},{7,2},{8,11},{9,12},{10,... | collective-permute-start | bytes 786440 | tf_op jit(solution)/shard_map/ppermute | solution.py:79
  99.9 18.4 %collective-permute-start.6 = (bf16[8,16,1024]{2,1,0:T(8,128)(2,1)S(1)}, bf16[8,16,1024]{2,1,0:T(8,128)(2,1)S(1)}, u32[]{:S(2)}, u32[]{:S(2)}) collective-permute-start(bf16[8,16,1024]{2,1,0:T(8,128)(2,1)S(1)} %get-tuple-element.6), channel_id=1, source_target_pairs={{0,5},{1,6},{2,7},{3,0},{4,1},{5,2},{6,3},{7,4},{8,13},{9,14},{10,... | collective-permute-start | bytes 786440 | tf_op jit(solution)/shard_map/ppermute | solution.py:79
  109.2 17.4 %collective-permute-start.7 = (bf16[8,16,1024]{2,1,0:T(8,128)(2,1)S(1)}, bf16[8,16,1024]{2,1,0:T(8,128)(2,1)S(1)}, u32[]{:S(2)}, u32[]{:S(2)}) collective-permute-start(bf16[8,16,1024]{2,1,0:T(8,128)(2,1)S(1)} %get-tuple-element.6), channel_id=1, source_target_pairs={{0,4},{1,5},{2,6},{3,7},{4,0},{5,1},{6,2},{7,3},{8,12},{9,13},{10,... | collective-permute-start | bytes 786440 | tf_op jit(solution)/shard_map/ppermute | solution.py:79
  118.3 44.4 %collective-permute-start.2 = (bf16[8,16,1024]{2,1,0:T(8,128)(2,1)S(1)}, bf16[8,16,1024]{2,1,0:T(8,128)(2,1)S(1)}, u32[]{:S(2)}, u32[]{:S(2)}) collective-permute-start(bf16[8,16,1024]{2,1,0:T(8,128)(2,1)S(1)} %get-tuple-element.6), channel_id=1, source_target_pairs={{0,64},{64,128},{128,192},{192,0},{1,65},{65,129},{129,193},{193,1... | collective-permute-start | bytes 786440 | tf_op jit(solution)/shard_map/ppermute | solution.py:79
  126.6 36.1 %collective-permute-start.1 = (bf16[8,16,1024]{2,1,0:T(8,128)(2,1)S(1)}, bf16[8,16,1024]{2,1,0:T(8,128)(2,1)S(1)}, u32[]{:S(2)}, u32[]{:S(2)}) collective-permute-start(bf16[8,16,1024]{2,1,0:T(8,128)(2,1)S(1)} %get-tuple-element.6), channel_id=1, source_target_pairs={{0,128},{64,192},{128,0},{192,64},{1,129},{65,193},{129,1},{193,65... | collective-permute-start | bytes 786440 | tf_op jit(solution)/shard_map/ppermute | solution.py:79
  141.8 18.4 %collective-permute-start = (bf16[8,16,1024]{2,1,0:T(8,128)(2,1)S(1)}, bf16[8,16,1024]{2,1,0:T(8,128)(2,1)S(1)}, u32[]{:S(2)}, u32[]{:S(2)}) collective-permute-start(bf16[8,16,1024]{2,1,0:T(8,128)(2,1)S(1)} %get-tuple-element.6), channel_id=1, source_target_pairs={{0,192},{64,0},{128,64},{192,128},{1,193},{65,1},{129,65},{193,129... | collective-permute-start | bytes 786440 | tf_op jit(solution)/shard_map/ppermute | solution.py:79
  216.8 8.2 %collective-permute-start.3 = (bf16[8,4,4,16,1024]{4,3,2,0,1:T(8,128)(2,1)}, bf16[8,4,4,16,1024]{4,3,2,0,1:T(8,128)(2,1)}, u32[]{:S(2)}, u32[]{:S(2)}) collective-permute-start(bf16[8,4,4,16,1024]{4,3,2,0,1:T(8,128)(2,1)} %bitcast.61), channel_id=1, source_target_pairs={{0,32},{32,0},{1,33},{33,1},{2,34},{34,2},{3,35},{35,3},{4,36},{36... | collective-permute-start | bytes 12582920 | tf_op jit(solution)/shard_map/ppermute | solution.py:89
  224.6 2.2 copy-start
Sparse Core Ops, SparseCore 0:
  26.7 56.1 reduce-scatter.1
  164.1 52.6 all-gather.2

commit v7 on v4

--- a/solution.py
+++ b/solution.py
@@ -83,18 +83,23 @@
     return pair.reshape(freqs, -1, width)
 
 
-def gather_rows(amplitudes):
-    count = lax.axis_size("zhi") * lax.axis_size("y")
-    ahead = [amplitudes]
+def gather_by_permutes(piece, axis_name, count):
+    ahead = [piece]
     for shift in range(1, count):
         ahead.append(
-            lax.ppermute(
-                amplitudes, ("zhi", "y"), perm=[(i, (i - shift) % count) for i in range(count)]
-            )
+            lax.ppermute(piece, axis_name, perm=[(i, (i - shift) % count) for i in range(count)])
         )
     stacked = jnp.stack(ahead, axis=1)
-    rolled = jnp.roll(stacked, lax.axis_index(("zhi", "y")), axis=1)
-    return rolled.reshape(stacked.shape[0], -1, stacked.shape[-1])
+    return jnp.roll(stacked, lax.axis_index(axis_name), axis=1)
+
+
+def gather_rows(amplitudes):
+    freqs, piece, width = amplitudes.shape
+    other = lax.ppermute(amplitudes, "zhi", perm=[(0, 1), (1, 0)])
+    first = lax.axis_index("zhi") == 0
+    pair = jnp.where(first, jnp.stack([amplitudes, other], 1), jnp.stack([other, amplitudes], 1))
+    rows = gather_by_permutes(pair, "y", lax.axis_size("y"))
+    return rows.transpose(0, 2, 1, 3, 4).reshape(freqs, -1, width)
 
 
 def local(freq_resp, node_coords, heading_steps, spectral_weights):

time: 223 us -> 248 us (1.11)
  waiting for transfers between devices: 148 us -> 180 us
  starting transfers between devices: 23.6 us -> 9.06 us
  other arithmetic: 6.17 us -> 13.7 us
    ppermute x7 -> x4, waiting for transfers between devices: 21.1 us -> 37.8 us  [the longest x3 25.1 us: gather_by_permutes(): lax.ppermute(piece, axis_name, perm=[(i, (i - shift) % count) for i in ra...]
    all_gather x1, waiting for transfers between devices: 38.3 us -> 53.7 us  [gather_cols(): mine = lax.all_gather(along_z, 'drow', axis=2)]
    ppermute x7 -> x4, starting transfers between devices: 22.7 us -> 8.3 us  [the longest x1 4.56 us: gather_rows(): other = lax.ppermute(amplitudes, 'zhi', perm=[(0, 1), (1, 0)])]
    select_n x1, other arithmetic: 0.9 us -> 8.22 us  [gather_cols(): jnp.where(first, jnp.stack([mine, theirs], axis=2), jnp.stack([theirs, mi...]
  transfers between devices with their start and end apart: 11 -> 8, of which waited for: 5 -> 7; matrix products, arithmetic and copies ran while one was open for 2% -> 1% of each run, Pallas kernels for 0% -> 0%
where the time goes in v7:
time: 248 us
  waiting for transfers between devices  180 us (73%)
  Pallas kernels  15.5 us (6%)
  other arithmetic  13.7 us (6%)
  between operations  13.3 us (5%)
  local copies, waits for them, and re-layouts  12.6 us (5%)
  starting transfers between devices  9.06 us (4%)
  matrix products  3.94 us (2%)
    reduce_scatter x1, waiting for transfers between devices, local(): lax.psum_scatter(partial_amp, ('zlo', 'core'), scatter_dimension=1, tiled...  56.3 us
    all_gather x1, waiting for transfers between devices, gather_cols(): mine = lax.all_gather(along_z, 'drow', axis=2)  53.7 us
    all_gather x1, waiting for transfers between devices, gather_cols(): along_z = lax.all_gather(amplitudes, 'zlo', axis=1, tiled=True)  32.1 us
    ppermute x3, waiting for transfers between devices, gather_by_permutes(): lax.ppermute(piece, axis_name, perm=[(i, (i - shift) % count) for i in ra...  25.1 us
    pallas_call x1, Pallas kernels, partial_amplitudes(): pl.pallas_call(amp_kernel, out_shape=jax.ShapeDtypeStruct((FREQS, rows, 2...  15.5 us
    ppermute x1, waiting for transfers between devices, gather_rows(): other = lax.ppermute(amplitudes, 'zhi', perm=[(0, 1), (1, 0)])  12.6 us
    select_n x1, other arithmetic, gather_cols(): jnp.where(first, jnp.stack([mine, theirs], axis=2), jnp.stack([theirs, mi...  8.22 us
    broadcast_in_dim x1, local copies, waits for them, and re-layouts, local(): return spec[:, :, None]  5.34 us
  transfers between devices with their start and end apart: 8, of which 7 were waited for; matrix products, arithmetic and copies ran while one was open for 1% of the time, Pallas kernels for 0%

profile of v7, /device:TPU:33, one launch (start us, length us, event | category | flops | bytes accessed | tf_op | source)
XLA Modules:
  0.0 247.9 jit_solution(270162846120679909)
XLA Ops:
  6.5 0.8 fusion.12
  7.3 0.8 fusion.11
  8.1 1.3 multiply_sqrt_fusion.spread_ref
  9.4 1.6 multiply_add_fusion.proj_ref
  11.1 15.5 %shard_map.46 = f32[8,128,1024]{2,1,0:T(8,128)} custom-call(s32[1024,512]{1,0:T(8,128)} %multiply_add_fusion.proj_ref, f32[8,512]{1,0:T(8,128)} %multiply_sqrt_fusion.spread_ref, bf16[2,8,128,1024]{3,2,1,0:T(8,128)(2,1)} %resp_ref.1), custom_call_target="tpu_custom_call" | custom-call | tf_op jit(solution)/shard_map/pallas_call | solution.py:61
  26.5 0.0 all-gather.3.cloned.1.call-start
  26.6 56.3 %reduce-scatter.2.cloned.1.call-done = f32[8,16,1024]{2,1,0:T(8,128)} async-done(((f32[8,128,1024]{2,1,0:T(8,128)}), f32[8,16,1024]{2,1,0:T(8,128)}) %reduce-scatter.2.cloned.1.call-update) | async-done | bytes 524304 | tf_op jit(solution)/shard_map/reduce_scatter | solution.py:112
  82.9 1.8 convert_element_type.7
  84.7 0.0 all-gather.5.cloned.1.call-start
  84.7 32.1 %all-gather.3.cloned.1.call-done = bf16[8,64,1024]{2,1,0:T(8,128)(2,1)} async-done(((bf16[8,16,1024]{2,1,0:T(8,128)(2,1)}), bf16[8,64,1024]{2,1,0:T(8,128)(2,1)}) %all-gather.3.cloned.1.call-update) | async-done | bytes 1048592 | tf_op jit(solution)/shard_map/all_gather | solution.py:77
  116.8 0.0 all-gather.5.cloned.1.call-update
  116.8 53.7 %all-gather.5.cloned.1.call-done = bf16[8,4,4,16,1024]{4,3,1,0,2:T(8,128)(2,1)} async-done(((bf16[8,4,1,16,1024]{4,3,1,0,2:T(8,128)(2,1)}), bf16[8,4,4,16,1024]{4,3,1,0,2:T(8,128)(2,1)}) %all-gather.5.cloned.1.call-update) | async-done | bytes 4194320 | tf_op jit(solution)/shard_map/all_gather | solution.py:79
  170.5 5.0 %copy.25 = bf16[8,4,4,16,1024]{4,3,2,1,0:T(8,128)(2,1)} copy(bf16[8,4,4,16,1024]{4,3,1,0,2:T(8,128)(2,1)} %all-gather.5.cloned.1.call-done) | data formatting | bytes 8388608 | tf_op jit(solution)/shard_map/all_gather | solution.py:79
  175.6 0.7 collective-permute-start
  176.3 4.6 %collective-permute-start.1 = (bf16[8,16,1024]{2,1,0:T(8,128)(2,1)S(1)}, bf16[8,16,1024]{2,1,0:T(8,128)(2,1)S(1)}, u32[]{:S(2)}, u32[]{:S(2)}) collective-permute-start(bf16[8,16,1024]{2,1,0:T(8,128)(2,1)S(1)} %copy-done.1), channel_id=1, source_target_pairs={{0,4},{4,0},{1,5},{5,1},{2,6},{6,2},{3,7},{7,3},{8,12},{12,8},{9,1... | collective-permute-start | bytes 786440 | tf_op jit(solution)/shard_map/ppermute | solution.py:98
  180.9 12.6 %collective-permute-done.1 = bf16[8,16,1024]{2,1,0:T(8,128)(2,1)S(1)} collective-permute-done((bf16[8,16,1024]{2,1,0:T(8,128)(2,1)S(1)}, bf16[8,16,1024]{2,1,0:T(8,128)(2,1)S(1)}, u32[]{:S(2)}, u32[]{:S(2)}) %collective-permute-start.1) | collective-permute-done | bytes 262176 | tf_op jit(solution)/shard_map/ppermute | solution.py:98
  193.5 0.1 maximum_select_fusion.2
  193.6 2.5 %collective-permute-start.2 = (bf16[8,2,16,1024]{3,2,0,1:T(8,128)(2,1)S(1)}, bf16[8,2,16,1024]{3,2,0,1:T(8,128)(2,1)S(1)}, u32[]{:S(2)}, u32[]{:S(2)}) collective-permute-start(bf16[8,2,16,1024]{3,2,0,1:T(8,128)(2,1)S(1)} %maximum_select_fusion.2), channel_id=1, source_target_pairs={{0,3},{1,0},{2,1},{3,2},{4,7},{5,4},{6,5},{7,6},{8,11},{9,8},{10,9... | collective-permute-start | bytes 1572872 | tf_op jit(solution)/shard_map/ppermute | solution.py:90
  196.1 0.5 collective-permute-start.3
  196.7 0.7 collective-permute-start.4
  197.4 0.1 fusion.7
  197.5 9.9 %collective-permute-done.2 = bf16[8,2,16,1024]{3,2,0,1:T(8,128)(2,1)S(1)} collective-permute-done((bf16[8,2,16,1024]{3,2,0,1:T(8,128)(2,1)S(1)}, bf16[8,2,16,1024]{3,2,0,1:T(8,128)(2,1)S(1)}, u32[]{:S(2)}, u32[]{:S(2)}) %collective-permute-start.2) | collective-permute-done | bytes 524320 | tf_op jit(solution)/shard_map/ppermute | solution.py:90
  207.4 2.6 %collective-permute-done.3 = bf16[8,2,16,1024]{3,2,0,1:T(8,128)(2,1)S(1)} collective-permute-done((bf16[8,2,16,1024]{3,2,0,1:T(8,128)(2,1)S(1)}, bf16[8,2,16,1024]{3,2,0,1:T(8,128)(2,1)S(1)}, u32[]{:S(2)}, u32[]{:S(2)}) %collective-permute-start.3) | collective-permute-done | bytes 524320 | tf_op jit(solution)/shard_map/ppermute | solution.py:90
  210.0 12.6 %collective-permute-done.4 = bf16[8,2,16,1024]{3,2,0,1:T(8,128)(2,1)S(1)} collective-permute-done((bf16[8,2,16,1024]{3,2,0,1:T(8,128)(2,1)S(1)}, bf16[8,2,16,1024]{3,2,0,1:T(8,128)(2,1)S(1)}, u32[]{:S(2)}, u32[]{:S(2)}) %collective-permute-start.4) | collective-permute-done | bytes 524320 | tf_op jit(solution)/shard_map/ppermute | solution.py:90
  222.7 0.1 fusion.8
  223.0 0.3 dynamic-slice_bitcast_fusion
  223.3 0.2 copy.18
  223.5 0.1 fusion.10
  223.6 0.3 maximum_bitcast_fusion
  223.9 8.2 %maximum_select_fusion = bf16[8,4,2,4,16,1024]{5,4,3,2,1,0:T(8,128)(2,1)S(1)} fusion(bf16[8,4,1,4,16,1024]{5,4,3,2,1,0:T(8,128)(2,1)} %bitcast.6, bf16[8,4,1,4,16,1024]{5,4,3,2,1,0:T(8,128)(2,1)} %bitcast.41, pred[]{:T(512)S(6)} %eq.9), kind=kLoop, calls=%fused_computation | loop fusion | flops 12582912 | bytes 16777216 | tf_op jit(solution)/shard_map/jit(_where)/select_n | solution.py:82
  232.1 3.9 %fusion.4 = f32[2,8,1,128,512]{3,4,0,1,2:T(8,128)} fusion(bf16[8,512,1024,1]{2,1,3,0:T(8,128)(2,1)S(1)} %bitcast.42, bf16[1,8,128,1024]{3,2,0,1:T(8,128)(2,1)S(1)} %maximum_bitcast_fusion, bf16[1,8,128,1024]{3,2,0,1:T(8,128)(2,1)S(1)} %bitcast.44), kind=kOutput, calls=%fused_computation.5 | convolution fusion | flops 2155872256 | bytes 16777216 | tf_op jit(solution)/shard_map/pfke,fje->pfkj/dot_general | solution.py:119
  236.1 5.3 %copy.21 = f32[2,8,1,128,512]{4,3,2,1,0:T(8,128)} copy(f32[2,8,1,128,512]{3,4,0,1,2:T(8,128)} %fusion.4) | data formatting | bytes 8388608 | tf_op jit(solution)/shard_map/broadcast_in_dim | solution.py:120
  (16 shorter events, 0.3 us)
Async XLA Ops:
  6.5 76.3 %reduce-scatter.2.cloned.1.call-start = ((), (), s32[]{:S(2)}) async-start(), calls=%async_computation.1 | async-start | bytes 4718592 | tf_op jit(solution)/shard_map/reduce_scatter | solution.py:112
  26.5 90.3 %all-gather.3.cloned.1.call-start = ((), (), s32[]{:S(2)}) async-start(), calls=%async_computation.2 | async-start | bytes 1310720 | tf_op jit(solution)/shard_map/all_gather | solution.py:77
  84.7 85.8 %all-gather.5.cloned.1.call-start = ((), (), s32[]{:S(2)}) async-start(), calls=%async_computation.3 | async-start | bytes 5242880 | tf_op jit(solution)/shard_map/all_gather | solution.py:79
  116.8 59.4 %copy-start.1 = (bf16[8,16,1024]{2,1,0:T(8,128)(2,1)S(1)}, bf16[8,16,1024]{2,1,0:T(8,128)(2,1)}, u32[]{:S(2)}) copy-start(bf16[8,16,1024]{2,1,0:T(8,128)(2,1)} %convert_element_type.7) | copy-start | bytes 786436
  116.8 64.0 %copy-start = (f32[8,16,1024]{2,1,0:T(8,128)S(1)}, f32[8,16,1024]{2,1,0:T(8,128)}, u32[]{:S(2)}) copy-start(f32[8,16,1024]{2,1,0:T(8,128)} %reduce-scatter.2.cloned.1.call-done) | copy-start | bytes 1572868
  175.6 48.3 %collective-permute-start = (bf16[8,4,4,16,1024]{4,3,2,1,0:T(8,128)(2,1)}, bf16[8,4,4,16,1024]{4,3,2,1,0:T(8,128)(2,1)}, u32[]{:S(2)}, u32[]{:S(2)}) collective-permute-start(bf16[8,4,4,16,1024]{4,3,2,1,0:T(8,128)(2,1)} %copy.25), channel_id=1, source_target_pairs={{0,32},{32,0},{1,33},{33,1},{2,34},{34,2},{3,35},{35,3},{4,36},{36... | collective-permute-start | bytes 12582920 | tf_op jit(solution)/shard_map/ppermute | solution.py:80
  176.3 17.2 %collective-permute-start.1 = (bf16[8,16,1024]{2,1,0:T(8,128)(2,1)S(1)}, bf16[8,16,1024]{2,1,0:T(8,128)(2,1)S(1)}, u32[]{:S(2)}, u32[]{:S(2)}) collective-permute-start(bf16[8,16,1024]{2,1,0:T(8,128)(2,1)S(1)} %copy-done.1), channel_id=1, source_target_pairs={{0,4},{4,0},{1,5},{5,1},{2,6},{6,2},{3,7},{7,3},{8,12},{12,8},{9,1... | collective-permute-start | bytes 786440 | tf_op jit(solution)/shard_map/ppermute | solution.py:98
  193.6 13.8 %collective-permute-start.2 = (bf16[8,2,16,1024]{3,2,0,1:T(8,128)(2,1)S(1)}, bf16[8,2,16,1024]{3,2,0,1:T(8,128)(2,1)S(1)}, u32[]{:S(2)}, u32[]{:S(2)}) collective-permute-start(bf16[8,2,16,1024]{3,2,0,1:T(8,128)(2,1)S(1)} %maximum_select_fusion.2), channel_id=1, source_target_pairs={{0,3},{1,0},{2,1},{3,2},{4,7},{5,4},{6,5},{7,6},{8,11},{9,8},{10,9... | collective-permute-start | bytes 1572872 | tf_op jit(solution)/shard_map/ppermute | solution.py:90
  196.1 13.9 %collective-permute-start.3 = (bf16[8,2,16,1024]{3,2,0,1:T(8,128)(2,1)S(1)}, bf16[8,2,16,1024]{3,2,0,1:T(8,128)(2,1)S(1)}, u32[]{:S(2)}, u32[]{:S(2)}) collective-permute-start(bf16[8,2,16,1024]{3,2,0,1:T(8,128)(2,1)S(1)} %maximum_select_fusion.2), channel_id=1, source_target_pairs={{0,2},{1,3},{2,0},{3,1},{4,6},{5,7},{6,4},{7,5},{8,10},{9,11},{10,... | collective-permute-start | bytes 1572872 | tf_op jit(solution)/shard_map/ppermute | solution.py:90
  196.7 26.0 %collective-permute-start.4 = (bf16[8,2,16,1024]{3,2,0,1:T(8,128)(2,1)S(1)}, bf16[8,2,16,1024]{3,2,0,1:T(8,128)(2,1)S(1)}, u32[]{:S(2)}, u32[]{:S(2)}) collective-permute-start(bf16[8,2,16,1024]{3,2,0,1:T(8,128)(2,1)S(1)} %maximum_select_fusion.2), channel_id=1, source_target_pairs={{0,1},{1,2},{2,3},{3,0},{4,5},{5,6},{6,7},{7,4},{8,9},{9,10},{10,1... | collective-permute-start | bytes 1572872 | tf_op jit(solution)/shard_map/ppermute | solution.py:90
Sparse Core Ops, SparseCore 0:
  26.7 56.1 reduce-scatter.1
  84.8 31.9 all-gather.2
  118.6 51.8 all-gather.4

commit v8 on v4

--- a/solution.py
+++ b/solution.py
@@ -72,10 +72,8 @@
     )(project, spread, freq_resp)
 
 
-def gather_cols(amplitudes):
-    freqs, piece, width = amplitudes.shape
-    along_z = lax.all_gather(amplitudes, "zlo", axis=1, tiled=True)
-    along_z = along_z.reshape(freqs, -1, piece, width)
+def gather_cols(along_z):
+    freqs, width = along_z.shape[0], along_z.shape[-1]
     mine = lax.all_gather(along_z, "drow", axis=2)
     theirs = lax.ppermute(mine, "core", perm=[(0, 1), (1, 0)])
     first = lax.axis_index("core") == 0
@@ -104,10 +102,13 @@
     )
     spread = jnp.sqrt(spectral_weights.astype(jnp.float32) / (64.0 * DIRS))
     partial_amp = partial_amplitudes(freq_resp, project, spread)
-    amplitudes = lax.psum_scatter(partial_amp, ("zlo", "core"), scatter_dimension=1, tiled=True).astype(
-        jnp.bfloat16
-    )
-    cols = gather_cols(amplitudes)
+    summed = lax.psum(partial_amp, ("zlo", "core")).astype(jnp.bfloat16)
+    freqs, dofs, width = summed.shape
+    zlo_count = lax.axis_size("zlo")
+    split = summed.reshape(freqs, zlo_count, 2, dofs // (2 * zlo_count), width)
+    along_z = lax.dynamic_index_in_dim(split, lax.axis_index("core"), axis=2, keepdims=False)
+    amplitudes = lax.dynamic_index_in_dim(along_z, lax.axis_index("zlo"), axis=1, keepdims=False)
+    cols = gather_cols(along_z)
     rows = gather_rows(amplitudes)
     rows_im = jnp.concatenate([rows[..., DIRS:], -rows[..., :DIRS]], axis=-1)
     lead = jnp.stack([rows, rows_im], axis=0)

time: 223 us -> 263 us (1.18)
  blocking collectives: 0 us -> 89.1 us
  waiting for transfers between devices: 148 us -> 68.5 us
  local copies, waits for them, and re-layouts: 10.6 us -> 31.8 us
  matrix products: 3.92 us -> 9.6 us
  other arithmetic: 6.17 us -> 11.3 us
    psum x0 -> x1, blocking collectives: none -> 89.1 us  [local(): summed = lax.psum(partial_amp, ('zlo', 'core')).astype(jnp.bfloat16)]
    reduce_scatter x1 -> x0, waiting for transfers between devices: 56.3 us -> none  [local(): lax.psum_scatter(partial_amp, ('zlo', 'core'), scatter_dimension=1, tiled...]
    all_gather x1 -> x0, waiting for transfers between devices: 32.1 us -> none  [gather_cols(): along_z = lax.all_gather(amplitudes, 'zlo', axis=1, tiled=True)]
    unnamed x18 -> x17, local copies, waits for them, and re-layouts: 0.27 us -> 12.6 us
    select_n x0 -> x1, local copies, waits for them, and re-layouts: none -> 8.53 us  [gather_cols(): jnp.where(first, jnp.stack([mine, theirs], axis=2), jnp.stack([theirs, mi...]
    ppermute x7, waiting for transfers between devices: 21.1 us -> 28.9 us  [gather_rows(): lax.ppermute(amplitudes, ('zhi', 'y'), perm=[(i, (i - shift) % count) for...]
    select_n x1, other arithmetic: 0.9 us -> 7.97 us  [gather_cols(): jnp.where(first, jnp.stack([mine, theirs], axis=2), jnp.stack([theirs, mi...]
    dot_general x1, matrix products: 3.92 us -> 9.6 us  [local(): jnp.einsum('pfke,fje->pfkj', lead, cols, preferred_element_type=jnp.float32)]
  transfers between devices with their start and end apart: 11 -> 9, of which waited for: 5 -> 4; matrix products, arithmetic and copies ran while one was open for 2% -> 5% of each run, Pallas kernels for 0% -> 0%
where the time goes in v8:
time: 263 us; the launch traced here: 262 us
  blocking collectives  89.1 us (34%)
  waiting for transfers between devices  68.5 us (26%)
  local copies, waits for them, and re-layouts  31.8 us (12%)
  starting transfers between devices  22.9 us (9%)
  Pallas kernels  15.5 us (6%)
  between operations  13.5 us (5%)
  other arithmetic  11.3 us (4%)
  matrix products  9.6 us (4%)
    psum x1, blocking collectives, local(): summed = lax.psum(partial_amp, ('zlo', 'core')).astype(jnp.bfloat16)  89.1 us
    all_gather x1, waiting for transfers between devices, gather_cols(): mine = lax.all_gather(along_z, 'drow', axis=2)  39.5 us
    ppermute x7, waiting for transfers between devices, gather_rows(): lax.ppermute(amplitudes, ('zhi', 'y'), perm=[(i, (i - shift) % count) for...  28.9 us
    ppermute x7, starting transfers between devices, gather_rows(): lax.ppermute(amplitudes, ('zhi', 'y'), perm=[(i, (i - shift) % count) for...  22.1 us
    pallas_call x1, Pallas kernels, partial_amplitudes(): pl.pallas_call(amp_kernel, out_shape=jax.ShapeDtypeStruct((FREQS, rows, 2...  15.5 us
    unnamed x17, local copies, waits for them, and re-layouts  12.6 us
    dot_general x1, matrix products, local(): jnp.einsum('pfke,fje->pfkj', lead, cols, preferred_element_type=jnp.float32)  9.6 us
    select_n x1, local copies, waits for them, and re-layouts, gather_cols(): jnp.where(first, jnp.stack([mine, theirs], axis=2), jnp.stack([theirs, mi...  8.53 us
  transfers between devices with their start and end apart: 9, of which 4 were waited for; matrix products, arithmetic and copies ran while one was open for 5% of the time, Pallas kernels for 0%

profile of v8, /device:TPU:33, one launch (start us, length us, event | category | flops | bytes accessed | tf_op | source)
XLA Modules:
  0.0 262.1 jit_solution(12228929661686202264)
XLA Ops:
  6.5 0.8 fusion.10
  7.3 0.8 fusion.9
  8.1 1.3 multiply_sqrt_fusion.spread_ref
  9.4 1.6 multiply_add_fusion.proj_ref
  11.1 15.5 %shard_map.46 = f32[8,128,1024]{2,1,0:T(8,128)} custom-call(s32[1024,512]{1,0:T(8,128)} %multiply_add_fusion.proj_ref, f32[8,512]{1,0:T(8,128)} %multiply_sqrt_fusion.spread_ref, bf16[2,8,128,1024]{3,2,1,0:T(8,128)(2,1)} %resp_ref.1), custom_call_target="tpu_custom_call" | custom-call | tf_op jit(solution)/shard_map/pallas_call | solution.py:61
  26.5 89.1 %all-reduce.1 = bf16[8,128,1024]{2,1,0:T(8,128)(2,1)S(1)} all-reduce(f32[8,128,1024]{2,1,0:T(8,128)} %shard_map.46), channel_id=1, replica_groups=mesh['zlo'=4,'core'=2,'drow'=4,'zhi'=2,'y'=4] {'zlo','core'}, use_global_device_ids=true, to_apply=%region_0.0 | all-reduce | flops 1048576 | bytes 6291456 | tf_op jit(solution)/shard_map/psum | solution.py:105
  115.6 1.1 constant_dynamic-slice_fusion.1
  116.8 4.4 %collective-permute-start.1 = (bf16[8,16,1024]{2,1,0:T(8,128)(2,1)S(1)}, bf16[8,16,1024]{2,1,0:T(8,128)(2,1)S(1)}, u32[]{:S(2)}, u32[]{:S(2)}) collective-permute-start(bf16[8,16,1024]{2,1,0:T(8,128)(2,1)S(1)} %dynamic-slice_bitcast_fusion), channel_id=1, source_target_pairs={{0,7},{1,0},{2,1},{3,2},{4,3},{5,4},{6,5},{7,6},{8,15},{9,8},{10,9... | collective-permute-start | bytes 786440 | tf_op jit(solution)/shard_map/ppermute | solution.py:89
  121.2 7.8 %collective-permute-start.2 = (bf16[8,16,1024]{2,1,0:T(8,128)(2,1)S(1)}, bf16[8,16,1024]{2,1,0:T(8,128)(2,1)S(1)}, u32[]{:S(2)}, u32[]{:S(2)}) collective-permute-start(bf16[8,16,1024]{2,1,0:T(8,128)(2,1)S(1)} %dynamic-slice_bitcast_fusion), channel_id=1, source_target_pairs={{0,6},{1,7},{2,0},{3,1},{4,2},{5,3},{6,4},{7,5},{8,14},{9,15},{10,... | collective-permute-start | bytes 786440 | tf_op jit(solution)/shard_map/ppermute | solution.py:89
  129.0 39.5 %all-gather.2.cloned.1.call-done = bf16[8,4,4,16,1024]{4,3,2,1,0:T(8,128)(2,1)} async-done(((bf16[8,4,1,16,1024]{4,3,2,1,0:T(8,128)(2,1)}), bf16[8,4,4,16,1024]{4,3,2,1,0:T(8,128)(2,1)}) %all-gather.2.cloned.1.call-update) | async-done | bytes 4194320 | tf_op jit(solution)/shard_map/all_gather | solution.py:77
  169.9 5.5 %collective-permute-start.3 = (bf16[8,16,1024]{2,1,0:T(8,128)(2,1)S(1)}, bf16[8,16,1024]{2,1,0:T(8,128)(2,1)S(1)}, u32[]{:S(2)}, u32[]{:S(2)}) collective-permute-start(bf16[8,16,1024]{2,1,0:T(8,128)(2,1)S(1)} %dynamic-slice_bitcast_fusion), channel_id=1, source_target_pairs={{0,5},{1,6},{2,7},{3,0},{4,1},{5,2},{6,3},{7,4},{8,13},{9,14},{10,... | collective-permute-start | bytes 786440 | tf_op jit(solution)/shard_map/ppermute | solution.py:89
  175.4 0.7 bitcast_dynamic-update-slice_fusion.10
  176.1 0.8 collective-permute-start.4
  177.0 0.7 bitcast_dynamic-update-slice_fusion.8
  177.7 9.2 %collective-permute-done.3 = bf16[8,16,1024]{2,1,0:T(8,128)(2,1)S(1)} collective-permute-done((bf16[8,16,1024]{2,1,0:T(8,128)(2,1)S(1)}, bf16[8,16,1024]{2,1,0:T(8,128)(2,1)S(1)}, u32[]{:S(2)}, u32[]{:S(2)}) %collective-permute-start.3) | collective-permute-done | bytes 262176 | tf_op jit(solution)/shard_map/ppermute | solution.py:89
  186.8 3.7 %collective-permute-start.5 = (bf16[8,16,1024]{2,1,0:T(8,128)(2,1)S(1)}, bf16[8,16,1024]{2,1,0:T(8,128)(2,1)S(1)}, u32[]{:S(2)}, u32[]{:S(2)}) collective-permute-start(bf16[8,16,1024]{2,1,0:T(8,128)(2,1)S(1)} %dynamic-slice_bitcast_fusion), channel_id=1, source_target_pairs={{0,3},{1,4},{2,5},{3,6},{4,7},{5,0},{6,1},{7,2},{8,11},{9,12},{10,... | collective-permute-start | bytes 786440 | tf_op jit(solution)/shard_map/ppermute | solution.py:89
  191.2 7.7 %collective-permute-done.4 = bf16[8,16,1024]{2,1,0:T(8,128)(2,1)S(1)} collective-permute-done((bf16[8,16,1024]{2,1,0:T(8,128)(2,1)S(1)}, bf16[8,16,1024]{2,1,0:T(8,128)(2,1)S(1)}, u32[]{:S(2)}, u32[]{:S(2)}) %collective-permute-start.4) | collective-permute-done | bytes 262176 | tf_op jit(solution)/shard_map/ppermute | solution.py:89
  199.0 0.7 bitcast_dynamic-update-slice_fusion.4
  199.7 12.0 %collective-permute-done.5 = bf16[8,16,1024]{2,1,0:T(8,128)(2,1)S(1)} collective-permute-done((bf16[8,16,1024]{2,1,0:T(8,128)(2,1)S(1)}, bf16[8,16,1024]{2,1,0:T(8,128)(2,1)S(1)}, u32[]{:S(2)}, u32[]{:S(2)}) %collective-permute-start.5) | collective-permute-done | bytes 262176 | tf_op jit(solution)/shard_map/ppermute | solution.py:89
  211.7 0.7 bitcast_dynamic-update-slice_fusion.2
  212.4 0.7 bitcast_dynamic-update-slice_fusion
  213.2 0.7 bitcast_dynamic-update-slice_fusion.12
  214.6 0.7 bitcast_dynamic-update-slice_fusion.11
  215.3 0.7 bitcast_dynamic-update-slice_fusion.9
  218.2 0.7 bitcast_dynamic-update-slice_fusion.1
  219.0 0.7 bitcast_dynamic-update-slice_fusion.13
  219.7 1.9 constant_dynamic-slice_fusion
  222.0 1.8 copy-done
  223.8 8.0 %maximum_select_fusion = bf16[8,4,2,4,16,1024]{5,4,3,1,0,2:T(8,128)(2,1)} fusion(bf16[8,4,1,4,16,1024]{5,4,3,1,0,2:T(8,128)(2,1)} %bitcast.6, bf16[8,4,1,4,16,1024]{5,4,3,1,0,2:T(8,128)(2,1)S(1)} %bitcast.72, pred[]{:T(512)S(6)} %eq.6), kind=kLoop, calls=%fused_computation | loop fusion | flops 12582912 | bytes 16777216 | tf_op jit(solution)/shard_map/jit(_where)/select_n | solution.py:80
  231.7 8.5 %copy.5 = bf16[8,4,2,4,16,1024]{5,4,3,2,1,0:T(8,128)(2,1)} copy(bf16[8,4,2,4,16,1024]{5,4,3,1,0,2:T(8,128)(2,1)} %maximum_select_fusion) | data formatting | bytes 16777216 | tf_op jit(solution)/shard_map/jit(_where)/select_n | solution.py:80
  240.3 9.6 %fusion.4 = f32[2,8,1,128,512]{3,4,0,1,2:T(8,128)} fusion(bf16[8,512,1024,1]{2,1,3,0:T(8,128)(2,1)} %bitcast.65, bf16[1,8,128,1024]{3,2,0,1:T(8,128)(2,1)S(1)} %maximum_bitcast_fusion, bf16[1,8,128,1024]{3,2,0,1:T(8,128)(2,1)S(1)} %bitcast.67), kind=kOutput, calls=%fused_computation.5 | convolution fusion | flops 2155872256 | bytes 16777216 | tf_op jit(solution)/shard_map/pfke,fje->pfkj/dot_general | solution.py:115
  249.9 5.3 %copy.18 = f32[2,8,1,128,512]{4,3,2,1,0:T(8,128)} copy(f32[2,8,1,128,512]{3,4,0,1,2:T(8,128)} %fusion.4) | data formatting | bytes 8388608 | tf_op jit(solution)/shard_map/broadcast_in_dim | solution.py:116
  (20 shorter events, 5.5 us)
Async XLA Ops:
  6.5 162.0 %all-gather.2.cloned.1.call-start = ((), (), s32[]{:S(2)}) async-start(), calls=%async_computation | async-start | bytes 5242880 | tf_op jit(solution)/shard_map/all_gather | solution.py:77
  116.8 53.1 %collective-permute-start.1 = (bf16[8,16,1024]{2,1,0:T(8,128)(2,1)S(1)}, bf16[8,16,1024]{2,1,0:T(8,128)(2,1)S(1)}, u32[]{:S(2)}, u32[]{:S(2)}) collective-permute-start(bf16[8,16,1024]{2,1,0:T(8,128)(2,1)S(1)} %dynamic-slice_bitcast_fusion), channel_id=1, source_target_pairs={{0,7},{1,0},{2,1},{3,2},{4,3},{5,4},{6,5},{7,6},{8,15},{9,8},{10,9... | collective-permute-start | bytes 786440 | tf_op jit(solution)/shard_map/ppermute | solution.py:89
  121.2 92.0 %collective-permute-start.7 = (bf16[8,16,1024]{2,1,0:T(8,128)(2,1)S(1)}, bf16[8,16,1024]{2,1,0:T(8,128)(2,1)S(1)}, u32[]{:S(2)}, u32[]{:S(2)}) collective-permute-start(bf16[8,16,1024]{2,1,0:T(8,128)(2,1)S(1)} %dynamic-slice_bitcast_fusion), channel_id=1, source_target_pairs={{0,1},{1,2},{2,3},{3,4},{4,5},{5,6},{6,7},{7,0},{8,9},{9,10},{10,1... | collective-permute-start | bytes 786440 | tf_op jit(solution)/shard_map/ppermute | solution.py:89
  121.2 91.3 %collective-permute-start.6 = (bf16[8,16,1024]{2,1,0:T(8,128)(2,1)S(1)}, bf16[8,16,1024]{2,1,0:T(8,128)(2,1)S(1)}, u32[]{:S(2)}, u32[]{:S(2)}) collective-permute-start(bf16[8,16,1024]{2,1,0:T(8,128)(2,1)S(1)} %dynamic-slice_bitcast_fusion), channel_id=1, source_target_pairs={{0,2},{1,3},{2,4},{3,5},{4,6},{5,7},{6,0},{7,1},{8,10},{9,11},{10,... | collective-permute-start | bytes 786440 | tf_op jit(solution)/shard_map/ppermute | solution.py:89
  121.2 55.0 %collective-permute-start.2 = (bf16[8,16,1024]{2,1,0:T(8,128)(2,1)S(1)}, bf16[8,16,1024]{2,1,0:T(8,128)(2,1)S(1)}, u32[]{:S(2)}, u32[]{:S(2)}) collective-permute-start(bf16[8,16,1024]{2,1,0:T(8,128)(2,1)S(1)} %dynamic-slice_bitcast_fusion), channel_id=1, source_target_pairs={{0,6},{1,7},{2,0},{3,1},{4,2},{5,3},{6,4},{7,5},{8,14},{9,15},{10,... | collective-permute-start | bytes 786440 | tf_op jit(solution)/shard_map/ppermute | solution.py:89
  168.5 53.5 %collective-permute-start = (bf16[8,4,4,16,1024]{4,3,2,1,0:T(8,128)(2,1)}, bf16[8,4,4,16,1024]{4,3,2,1,0:T(8,128)(2,1)}, u32[]{:S(2)}, u32[]{:S(2)}) collective-permute-start(bf16[8,4,4,16,1024]{4,3,2,1,0:T(8,128)(2,1)} %all-gather.2.cloned.1.call-done), channel_id=1, source_target_pairs={{0,32},{32,0},{1,33},{33,1},{2,34},{34,2},{3,35},{35,3},{4,36},{36... | collective-permute-start | bytes 12582920 | tf_op jit(solution)/shard_map/ppermute | solution.py:78
  169.9 16.9 %collective-permute-start.3 = (bf16[8,16,1024]{2,1,0:T(8,128)(2,1)S(1)}, bf16[8,16,1024]{2,1,0:T(8,128)(2,1)S(1)}, u32[]{:S(2)}, u32[]{:S(2)}) collective-permute-start(bf16[8,16,1024]{2,1,0:T(8,128)(2,1)S(1)} %dynamic-slice_bitcast_fusion), channel_id=1, source_target_pairs={{0,5},{1,6},{2,7},{3,0},{4,1},{5,2},{6,3},{7,4},{8,13},{9,14},{10,... | collective-permute-start | bytes 786440 | tf_op jit(solution)/shard_map/ppermute | solution.py:89
  176.1 22.9 %collective-permute-start.4 = (bf16[8,16,1024]{2,1,0:T(8,128)(2,1)S(1)}, bf16[8,16,1024]{2,1,0:T(8,128)(2,1)S(1)}, u32[]{:S(2)}, u32[]{:S(2)}) collective-permute-start(bf16[8,16,1024]{2,1,0:T(8,128)(2,1)S(1)} %dynamic-slice_bitcast_fusion), channel_id=1, source_target_pairs={{0,4},{1,5},{2,6},{3,7},{4,0},{5,1},{6,2},{7,3},{8,12},{9,13},{10,... | collective-permute-start | bytes 786440 | tf_op jit(solution)/shard_map/ppermute | solution.py:89
  186.8 24.9 %collective-permute-start.5 = (bf16[8,16,1024]{2,1,0:T(8,128)(2,1)S(1)}, bf16[8,16,1024]{2,1,0:T(8,128)(2,1)S(1)}, u32[]{:S(2)}, u32[]{:S(2)}) collective-permute-start(bf16[8,16,1024]{2,1,0:T(8,128)(2,1)S(1)} %dynamic-slice_bitcast_fusion), channel_id=1, source_target_pairs={{0,3},{1,4},{2,5},{3,6},{4,7},{5,0},{6,1},{7,2},{8,11},{9,12},{10,... | collective-permute-start | bytes 786440 | tf_op jit(solution)/shard_map/ppermute | solution.py:89
  221.6 2.2 copy-start
Sparse Core Ops, SparseCore 0:
  116.9 51.5 all-gather.1

commit v9 on v4

--- a/solution.py
+++ b/solution.py
@@ -72,29 +72,24 @@
     )(project, spread, freq_resp)
 
 
-def gather_cols(amplitudes):
+def gather_cols(amplitudes, rows):
     freqs, piece, width = amplitudes.shape
     along_z = lax.all_gather(amplitudes, "zlo", axis=1, tiled=True)
+    along_z, rows = lax.optimization_barrier((along_z, rows))
     along_z = along_z.reshape(freqs, -1, piece, width)
     mine = lax.all_gather(along_z, "drow", axis=2)
     theirs = lax.ppermute(mine, "core", perm=[(0, 1), (1, 0)])
     first = lax.axis_index("core") == 0
     pair = jnp.where(first, jnp.stack([mine, theirs], axis=2), jnp.stack([theirs, mine], axis=2))
-    return pair.reshape(freqs, -1, width)
+    return pair.reshape(freqs, -1, width), rows
 
 
 def gather_rows(amplitudes):
     count = lax.axis_size("zhi") * lax.axis_size("y")
-    ahead = [amplitudes]
-    for shift in range(1, count):
-        ahead.append(
-            lax.ppermute(
-                amplitudes, ("zhi", "y"), perm=[(i, (i - shift) % count) for i in range(count)]
-            )
-        )
-    stacked = jnp.stack(ahead, axis=1)
-    rolled = jnp.roll(stacked, lax.axis_index(("zhi", "y")), axis=1)
-    return rolled.reshape(stacked.shape[0], -1, stacked.shape[-1])
+    freqs, piece, width = amplitudes.shape
+    copies = jnp.broadcast_to(amplitudes[None], (count, freqs, piece, width))
+    pieces = lax.all_to_all(copies, ("zhi", "y"), split_axis=0, concat_axis=0)
+    return pieces.transpose(1, 0, 2, 3).reshape(freqs, -1, width)
 
 
 def local(freq_resp, node_coords, heading_steps, spectral_weights):
@@ -107,8 +102,7 @@
     amplitudes = lax.psum_scatter(partial_amp, ("zlo", "core"), scatter_dimension=1, tiled=True).astype(
         jnp.bfloat16
     )
-    cols = gather_cols(amplitudes)
-    rows = gather_rows(amplitudes)
+    cols, rows = gather_cols(amplitudes, gather_rows(amplitudes))
     rows_im = jnp.concatenate([rows[..., DIRS:], -rows[..., :DIRS]], axis=-1)
     lead = jnp.stack([rows, rows_im], axis=0)
     spec = jnp.einsum("pfke,fje->pfkj", lead, cols, preferred_element_type=jnp.float32)

time: 223 us -> 251 us (1.13)
  waiting for transfers between devices: 148 us -> 179 us
  starting transfers between devices: 23.6 us -> 8.4 us
  other arithmetic: 6.17 us -> 12.7 us
  local copies, waits for them, and re-layouts: 10.6 us -> 16.6 us
    all_to_all x0 -> x1, waiting for transfers between devices: none -> 66.9 us  [gather_rows(): pieces = lax.all_to_all(copies, ('zhi', 'y'), split_axis=0, concat_axis=0)]
    all_gather x1, waiting for transfers between devices: 32.1 us -> 0.02 us  [gather_cols(): along_z = lax.all_gather(amplitudes, 'zlo', axis=1, tiled=True)]
    ppermute x7 -> x0, starting transfers between devices: 22.7 us -> none  [gather_rows(): lax.ppermute(amplitudes, ('zhi', 'y'), perm=[(i, (i - shift) % count) for...]
    ppermute x7 -> x0, waiting for transfers between devices: 21.1 us -> none  [gather_rows(): lax.ppermute(amplitudes, ('zhi', 'y'), perm=[(i, (i - shift) % count) for...]
    all_gather x1, waiting for transfers between devices: 38.3 us -> 48.7 us  [gather_cols(): mine = lax.all_gather(along_z, 'drow', axis=2)]
    all_to_all x0 -> x1, starting transfers between devices: none -> 7.65 us  [gather_rows(): pieces = lax.all_to_all(copies, ('zhi', 'y'), split_axis=0, concat_axis=0)]
    select_n x1, other arithmetic: 0.9 us -> 8.24 us  [gather_cols(): jnp.where(first, jnp.stack([mine, theirs], axis=2), jnp.stack([theirs, mi...]
    ppermute x1, waiting for transfers between devices: 0.01 us -> 6.73 us  [gather_cols(): theirs = lax.ppermute(mine, 'core', perm=[(0, 1), (1, 0)])]
  transfers between devices with their start and end apart: 11 -> 5, of which waited for: 5 -> 4; matrix products, arithmetic and copies ran while one was open for 2% -> 1% of each run, Pallas kernels for 0% -> 0%
where the time goes in v9:
time: 251 us; the launch traced here: 250 us
  waiting for transfers between devices  179 us (71%)
  local copies, waits for them, and re-layouts  16.6 us (7%)
  Pallas kernels  15.5 us (6%)
  between operations  13.2 us (5%)
  other arithmetic  12.7 us (5%)
  starting transfers between devices  8.4 us (3%)
  matrix products  3.95 us (2%)
    all_to_all x1, waiting for transfers between devices, gather_rows(): pieces = lax.all_to_all(copies, ('zhi', 'y'), split_axis=0, concat_axis=0)  66.9 us
    reduce_scatter x1, waiting for transfers between devices, local(): lax.psum_scatter(partial_amp, ('zlo', 'core'), scatter_dimension=1, tiled...  56.3 us
    all_gather x1, waiting for transfers between devices, gather_cols(): mine = lax.all_gather(along_z, 'drow', axis=2)  48.7 us
    pallas_call x1, Pallas kernels, partial_amplitudes(): pl.pallas_call(amp_kernel, out_shape=jax.ShapeDtypeStruct((FREQS, rows, 2...  15.5 us
    select_n x1, other arithmetic, gather_cols(): jnp.where(first, jnp.stack([mine, theirs], axis=2), jnp.stack([theirs, mi...  8.24 us
    all_to_all x1, starting transfers between devices, gather_rows(): pieces = lax.all_to_all(copies, ('zhi', 'y'), split_axis=0, concat_axis=0)  7.65 us
    ppermute x1, waiting for transfers between devices, gather_cols(): theirs = lax.ppermute(mine, 'core', perm=[(0, 1), (1, 0)])  6.73 us
    broadcast_in_dim x1, local copies, waits for them, and re-layouts, local(): return spec[:, :, None]  5.34 us
  transfers between devices with their start and end apart: 5, of which 4 were waited for; matrix products, arithmetic and copies ran while one was open for 1% of the time, Pallas kernels for 0%

profile of v9, /device:TPU:33, one launch (start us, length us, event | category | flops | bytes accessed | tf_op | source)
XLA Modules:
  0.0 249.6 jit_solution(2419908975828485142)
XLA Ops:
  6.5 0.0 reduce-scatter.2.cloned.1.call-start
  6.5 0.8 fusion.10
  7.3 0.8 fusion.9
  8.1 1.3 multiply_sqrt_fusion.spread_ref
  9.4 1.6 multiply_add_fusion.proj_ref
  11.1 15.5 %shard_map.46 = f32[8,128,1024]{2,1,0:T(8,128)} custom-call(s32[1024,512]{1,0:T(8,128)} %multiply_add_fusion.proj_ref, f32[8,512]{1,0:T(8,128)} %multiply_sqrt_fusion.spread_ref, bf16[2,8,128,1024]{3,2,1,0:T(8,128)(2,1)} %resp_ref.1), custom_call_target="tpu_custom_call" | custom-call | tf_op jit(solution)/shard_map/pallas_call | solution.py:61
  26.5 0.0 reduce-scatter.2.cloned.1.call-update
  26.6 56.3 %reduce-scatter.2.cloned.1.call-done = f32[8,16,1024]{2,1,0:T(8,128)} async-done(((f32[8,128,1024]{2,1,0:T(8,128)}), f32[8,16,1024]{2,1,0:T(8,128)}) %reduce-scatter.2.cloned.1.call-update) | async-done | bytes 524304 | tf_op jit(solution)/shard_map/reduce_scatter | solution.py:102
  82.9 1.1 convert_element_type.7
  84.0 0.0 copy-start.1
  84.0 1.6 broadcast_in_dim.4
  85.6 7.6 %all-to-all-start = ((bf16[8,8,16,1024]{3,2,1,0:T(8,128)(2,1)}), bf16[8,8,16,1024]{3,2,1,0:T(8,128)(2,1)S(1)}, u32[]{:S(2)}, u32[]{:S(2)}) async-start(bf16[8,8,16,1024]{3,2,1,0:T(8,128)(2,1)} %broadcast_in_dim.4), calls=%async_computation.1 | async-start | bytes 4194304 | tf_op jit(solution)/shard_map/all_to_all | solution.py:91
  93.2 0.0 all-gather.3.cloned.1.call-start
  93.2 0.0 copy-done.1
  93.3 0.7 all-gather.3.cloned.1.call-update
  94.0 0.0 all-gather.5.cloned.1.call-start
  94.0 66.9 %all-to-all-done = bf16[8,8,16,1024]{3,2,1,0:T(8,128)(2,1)S(1)} async-done(((bf16[8,8,16,1024]{3,2,1,0:T(8,128)(2,1)}), bf16[8,8,16,1024]{3,2,1,0:T(8,128)(2,1)S(1)}, u32[]{:S(2)}, u32[]{:S(2)}) %all-to-all-start) | async-done | bytes 2097184 | tf_op jit(solution)/shard_map/all_to_all | solution.py:91
  160.9 0.0 copy-start
  160.9 1.3 copy-done
  162.2 1.8 copy.11
  164.0 0.0 all-gather.3.cloned.1.call-done
  164.0 0.0 all-gather.5.cloned.1.call-update
  164.0 48.7 %all-gather.5.cloned.1.call-done = bf16[8,4,4,16,1024]{4,3,1,0,2:T(8,128)(2,1)} async-done(((bf16[8,4,1,16,1024]{4,3,1,0,2:T(8,128)(2,1)}), bf16[8,4,4,16,1024]{4,3,1,0,2:T(8,128)(2,1)}) %all-gather.5.cloned.1.call-update) | async-done | bytes 4194320 | tf_op jit(solution)/shard_map/all_gather | solution.py:80
  212.7 5.0 %copy.19 = bf16[8,4,4,16,1024]{4,3,2,1,0:T(8,128)(2,1)} copy(bf16[8,4,4,16,1024]{4,3,1,0,2:T(8,128)(2,1)} %all-gather.5.cloned.1.call-done) | data formatting | bytes 8388608 | tf_op jit(solution)/shard_map/all_gather | solution.py:80
  217.8 0.7 collective-permute-start
  218.4 0.1 fusion.8
  218.6 0.3 maximum_bitcast_fusion
  218.8 6.7 %collective-permute-done = bf16[8,4,4,16,1024]{4,3,2,1,0:T(8,128)(2,1)} collective-permute-done((bf16[8,4,4,16,1024]{4,3,2,1,0:T(8,128)(2,1)}, bf16[8,4,4,16,1024]{4,3,2,1,0:T(8,128)(2,1)}, u32[]{:S(2)}, u32[]{:S(2)}) %collective-permute-start) | collective-permute-done | bytes 4194336 | tf_op jit(solution)/shard_map/ppermute | solution.py:81
  225.6 8.2 %maximum_select_fusion = bf16[8,4,2,4,16,1024]{5,4,3,2,1,0:T(8,128)(2,1)S(1)} fusion(bf16[8,4,1,4,16,1024]{5,4,3,2,1,0:T(8,128)(2,1)} %bitcast.8, bf16[8,4,1,4,16,1024]{5,4,3,2,1,0:T(8,128)(2,1)} %bitcast.25, pred[]{:T(512)S(6)} %eq.3), kind=kLoop, calls=%fused_computation | loop fusion | flops 12582912 | bytes 16777216 | tf_op jit(solution)/shard_map/jit(_where)/select_n | solution.py:83
  233.8 3.9 %fusion.4 = f32[2,8,1,128,512]{3,4,0,1,2:T(8,128)} fusion(bf16[8,512,1024,1]{2,1,3,0:T(8,128)(2,1)S(1)} %bitcast.26, bf16[1,8,128,1024]{3,2,0,1:T(8,128)(2,1)S(1)} %maximum_bitcast_fusion, bf16[1,8,128,1024]{3,2,0,1:T(8,128)(2,1)S(1)} %bitcast.28), kind=kOutput, calls=%fused_computation.5 | convolution fusion | flops 2155872256 | bytes 16777216 | tf_op jit(solution)/shard_map/pfke,fje->pfkj/dot_general | solution.py:108
  237.8 5.3 %copy.15 = f32[2,8,1,128,512]{4,3,2,1,0:T(8,128)} copy(f32[2,8,1,128,512]{3,4,0,1,2:T(8,128)} %fusion.4) | data formatting | bytes 8388608 | tf_op jit(solution)/shard_map/broadcast_in_dim | solution.py:109
Async XLA Ops:
  6.5 76.3 %reduce-scatter.2.cloned.1.call-start = ((), (), s32[]{:S(2)}) async-start(), calls=%async_computation.2 | async-start | bytes 4718592 | tf_op jit(solution)/shard_map/reduce_scatter | solution.py:102
  84.0 9.3 %copy-start.1 = (bf16[8,16,1024]{2,1,0:T(8,128)(2,1)}, bf16[8,16,1024]{2,1,0:T(8,128)(2,1)S(1)}, u32[]{:S(2)}) copy-start(bf16[8,16,1024]{2,1,0:T(8,128)(2,1)S(1)} %convert_element_type.7) | copy-start | bytes 786436
  85.6 75.3 %all-to-all-start = ((bf16[8,8,16,1024]{3,2,1,0:T(8,128)(2,1)}), bf16[8,8,16,1024]{3,2,1,0:T(8,128)(2,1)S(1)}, u32[]{:S(2)}, u32[]{:S(2)}) async-start(bf16[8,8,16,1024]{3,2,1,0:T(8,128)(2,1)} %broadcast_in_dim.4), calls=%async_computation.1 | async-start | bytes 4194304 | tf_op jit(solution)/shard_map/all_to_all | solution.py:91
  93.2 70.8 %all-gather.3.cloned.1.call-start = ((), (), s32[]{:S(2)}) async-start(), calls=%async_computation.3 | async-start | bytes 1310720 | tf_op jit(solution)/shard_map/all_gather | solution.py:77
  94.0 118.8 %all-gather.5.cloned.1.call-start = ((), (), s32[]{:S(2)}) async-start(), calls=%async_computation.4 | async-start | bytes 5242880 | tf_op jit(solution)/shard_map/all_gather | solution.py:80
  160.9 1.3 copy-start
  217.8 7.8 %collective-permute-start = (bf16[8,4,4,16,1024]{4,3,2,1,0:T(8,128)(2,1)}, bf16[8,4,4,16,1024]{4,3,2,1,0:T(8,128)(2,1)}, u32[]{:S(2)}, u32[]{:S(2)}) collective-permute-start(bf16[8,4,4,16,1024]{4,3,2,1,0:T(8,128)(2,1)} %copy.19), channel_id=1, source_target_pairs={{0,32},{32,0},{1,33},{33,1},{2,34},{34,2},{3,35},{35,3},{4,36},{36... | collective-permute-start | bytes 12582920 | tf_op jit(solution)/shard_map/ppermute | solution.py:81
Sparse Core Ops, SparseCore 0:
  26.7 56.1 reduce-scatter.1
  95.9 56.2 all-gather.2
  164.2 48.5 all-gather.4

commit v10 on v9

--- a/solution.py
+++ b/solution.py
@@ -72,12 +72,14 @@
     )(project, spread, freq_resp)
 
 
-def gather_cols(amplitudes, rows):
+def gather_cols(amplitudes):
     freqs, piece, width = amplitudes.shape
     along_z = lax.all_gather(amplitudes, "zlo", axis=1, tiled=True)
-    along_z, rows = lax.optimization_barrier((along_z, rows))
+    along_z, amplitudes = lax.optimization_barrier((along_z, amplitudes))
+    rows = gather_rows(amplitudes)
     along_z = along_z.reshape(freqs, -1, piece, width)
     mine = lax.all_gather(along_z, "drow", axis=2)
+    mine, rows = lax.optimization_barrier((mine, rows))
     theirs = lax.ppermute(mine, "core", perm=[(0, 1), (1, 0)])
     first = lax.axis_index("core") == 0
     pair = jnp.where(first, jnp.stack([mine, theirs], axis=2), jnp.stack([theirs, mine], axis=2))
@@ -102,7 +104,7 @@
     amplitudes = lax.psum_scatter(partial_amp, ("zlo", "core"), scatter_dimension=1, tiled=True).astype(
         jnp.bfloat16
     )
-    cols, rows = gather_cols(amplitudes, gather_rows(amplitudes))
+    cols, rows = gather_cols(amplitudes)
     rows_im = jnp.concatenate([rows[..., DIRS:], -rows[..., :DIRS]], axis=-1)
     lead = jnp.stack([rows, rows_im], axis=0)
     spec = jnp.einsum("pfke,fje->pfkj", lead, cols, preferred_element_type=jnp.float32)

time: 251 us -> 218 us (0.87)
  waiting for transfers between devices: 179 us -> 95.1 us
  blocking collectives: 0 us -> 58.2 us
  starting transfers between devices: 8.4 us -> 3.23 us
  local copies, waits for them, and re-layouts: 16.6 us -> 13.3 us
    all_to_all x1 -> x0, waiting for transfers between devices: 66.9 us -> none  [gather_rows(): pieces = lax.all_to_all(copies, ('zhi', 'y'), split_axis=0, concat_axis=0)]
    all_to_all x0 -> x1, blocking collectives: none -> 58.2 us  [gather_rows(): pieces = lax.all_to_all(copies, ('zhi', 'y'), split_axis=0, concat_axis=0)]
    all_gather x1, waiting for transfers between devices: 48.7 us -> 0.02 us  [gather_cols(): mine = lax.all_gather(along_z, 'drow', axis=2)]
    all_gather x1, waiting for transfers between devices: 0.02 us -> 32.1 us  [gather_cols(): along_z = lax.all_gather(amplitudes, 'zlo', axis=1, tiled=True)]
    all_to_all x1 -> x0, starting transfers between devices: 7.65 us -> none  [gather_rows(): pieces = lax.all_to_all(copies, ('zhi', 'y'), split_axis=0, concat_axis=0)]
    optimization_barrier x0 -> x1, local copies, waits for them, and re-layouts: none -> 5.04 us  [gather_cols(): mine, rows = lax.optimization_barrier((mine, rows))]
    all_gather x1 -> x0, local copies, waits for them, and re-layouts: 5.04 us -> none  [gather_cols(): mine = lax.all_gather(along_z, 'drow', axis=2)]
  transfers between devices with their start and end apart: 5 -> 4, of which waited for: 4 -> 3; matrix products, arithmetic and copies ran while one was open for 1% -> 1% of each run, Pallas kernels for 0% -> 0%
where the time goes in v10:
time: 218 us; the launch traced here: 216 us
  waiting for transfers between devices  95.1 us (44%)
  blocking collectives  58.2 us (27%)
  Pallas kernels  15.5 us (7%)
  other arithmetic  13.4 us (6%)
  local copies, waits for them, and re-layouts  13.3 us (6%)
  between operations  13.2 us (6%)
  matrix products  3.95 us (2%)
  starting transfers between devices  3.23 us (1%)
    all_to_all x1, blocking collectives, gather_rows(): pieces = lax.all_to_all(copies, ('zhi', 'y'), split_axis=0, concat_axis=0)  58.2 us
    reduce_scatter x1, waiting for transfers between devices, local(): lax.psum_scatter(partial_amp, ('zlo', 'core'), scatter_dimension=1, tiled...  56.3 us
    all_gather x1, waiting for transfers between devices, gather_cols(): along_z = lax.all_gather(amplitudes, 'zlo', axis=1, tiled=True)  32.1 us
    pallas_call x1, Pallas kernels, partial_amplitudes(): pl.pallas_call(amp_kernel, out_shape=jax.ShapeDtypeStruct((FREQS, rows, 2...  15.5 us
    select_n x1, other arithmetic, gather_cols(): jnp.where(first, jnp.stack([mine, theirs], axis=2), jnp.stack([theirs, mi...  8.25 us
    ppermute x1, waiting for transfers between devices, gather_cols(): theirs = lax.ppermute(mine, 'core', perm=[(0, 1), (1, 0)])  6.71 us
    broadcast_in_dim x1, local copies, waits for them, and re-layouts, local(): return spec[:, :, None]  5.34 us
    optimization_barrier x1, local copies, waits for them, and re-layouts, gather_cols(): mine, rows = lax.optimization_barrier((mine, rows))  5.04 us
  transfers between devices with their start and end apart: 4, of which 3 were waited for; matrix products, arithmetic and copies ran while one was open for 1% of the time, Pallas kernels for 0%

profile of v10, /device:TPU:33, one launch (start us, length us, event | category | flops | bytes accessed | tf_op | source)
XLA Modules:
  0.0 215.9 jit_solution(9945567503799298478)
XLA Ops:
  6.5 0.0 reduce-scatter.2.cloned.1.call-start
  6.5 0.8 fusion.10
  7.3 0.8 fusion.9
  8.1 1.3 multiply_sqrt_fusion.spread_ref
  9.4 1.6 multiply_add_fusion.proj_ref
  11.1 15.5 %shard_map.46 = f32[8,128,1024]{2,1,0:T(8,128)} custom-call(s32[1024,512]{1,0:T(8,128)} %multiply_add_fusion.proj_ref, f32[8,512]{1,0:T(8,128)} %multiply_sqrt_fusion.spread_ref, bf16[2,8,128,1024]{3,2,1,0:T(8,128)(2,1)} %resp_ref.1), custom_call_target="tpu_custom_call" | custom-call | tf_op jit(solution)/shard_map/pallas_call | solution.py:61
  26.5 0.0 reduce-scatter.2.cloned.1.call-update
  26.6 0.0 all-gather.3.cloned.1.call-start
  26.6 56.3 %reduce-scatter.2.cloned.1.call-done = f32[8,16,1024]{2,1,0:T(8,128)} async-done(((f32[8,128,1024]{2,1,0:T(8,128)}), f32[8,16,1024]{2,1,0:T(8,128)}) %reduce-scatter.2.cloned.1.call-update) | async-done | bytes 524304 | tf_op jit(solution)/shard_map/reduce_scatter | solution.py:104
  82.9 1.8 convert_element_type.7
  84.7 0.0 all-gather.3.cloned.1.call-update
  84.7 0.0 all-gather.5.cloned.1.call-start
  84.7 32.1 %all-gather.3.cloned.1.call-done = bf16[8,64,1024]{2,1,0:T(8,128)(2,1)} async-done(((bf16[8,16,1024]{2,1,0:T(8,128)(2,1)}), bf16[8,64,1024]{2,1,0:T(8,128)(2,1)}) %all-gather.3.cloned.1.call-update) | async-done | bytes 1048592 | tf_op jit(solution)/shard_map/all_gather | solution.py:77
  116.8 0.0 all-gather.5.cloned.1.call-update
  116.8 1.2 broadcast_in_dim.4
  118.1 58.2 %all_to_all.5 = bf16[8,8,16,1024]{3,2,1,0:T(8,128)(2,1)S(1)} all-to-all(bf16[8,8,16,1024]{3,2,1,0:T(8,128)(2,1)S(1)} %broadcast_in_dim.4), channel_id=1, replica_groups=mesh['zlo'=4,'core'=2,'drow'=4,'zhi'=2,'y'=4] {'zhi','y'}, dimensions={0} | all-to-all | bytes 4194304 | tf_op jit(solution)/shard_map/all_to_all | solution.py:93
  176.3 0.2 copy.11
  176.5 0.0 all-gather.5.cloned.1.call-done
  176.5 5.0 %copy.19 = bf16[8,4,4,16,1024]{4,3,2,1,0:T(8,128)(2,1)} copy(bf16[8,4,4,16,1024]{4,3,1,0,2:T(8,128)(2,1)} %all-gather.5.cloned.1.call-done) | data formatting | bytes 8388608 | tf_op jit(solution)/shard_map/optimization_barrier | solution.py:82
  181.5 3.1 %collective-permute-start = (bf16[8,4,4,16,1024]{4,3,2,1,0:T(8,128)(2,1)}, bf16[8,4,4,16,1024]{4,3,2,1,0:T(8,128)(2,1)}, u32[]{:S(2)}, u32[]{:S(2)}) collective-permute-start(bf16[8,4,4,16,1024]{4,3,2,1,0:T(8,128)(2,1)} %copy.19), channel_id=1, source_target_pairs={{0,32},{32,0},{1,33},{33,1},{2,34},{34,2},{3,35},{35,3},{4,36},{36... | collective-permute-start | bytes 12582920 | tf_op jit(solution)/shard_map/ppermute | solution.py:83
  184.7 0.1 fusion.8
  184.8 0.3 maximum_bitcast_fusion
  185.1 6.7 %collective-permute-done = bf16[8,4,4,16,1024]{4,3,2,1,0:T(8,128)(2,1)} collective-permute-done((bf16[8,4,4,16,1024]{4,3,2,1,0:T(8,128)(2,1)}, bf16[8,4,4,16,1024]{4,3,2,1,0:T(8,128)(2,1)}, u32[]{:S(2)}, u32[]{:S(2)}) %collective-permute-start) | collective-permute-done | bytes 4194336 | tf_op jit(solution)/shard_map/ppermute | solution.py:83
  191.8 8.2 %maximum_select_fusion = bf16[8,4,2,4,16,1024]{5,4,3,2,1,0:T(8,128)(2,1)S(1)} fusion(bf16[8,4,1,4,16,1024]{5,4,3,2,1,0:T(8,128)(2,1)} %bitcast.8, bf16[8,4,1,4,16,1024]{5,4,3,2,1,0:T(8,128)(2,1)} %bitcast.25, pred[]{:T(512)S(6)} %eq.3), kind=kLoop, calls=%fused_computation | loop fusion | flops 12582912 | bytes 16777216 | tf_op jit(solution)/shard_map/jit(_where)/select_n | solution.py:85
  200.1 3.9 %fusion.4 = f32[2,8,1,128,512]{3,4,0,1,2:T(8,128)} fusion(bf16[8,512,1024,1]{2,1,3,0:T(8,128)(2,1)S(1)} %bitcast.26, bf16[1,8,128,1024]{3,2,0,1:T(8,128)(2,1)S(1)} %maximum_bitcast_fusion, bf16[1,8,128,1024]{3,2,0,1:T(8,128)(2,1)S(1)} %bitcast.28), kind=kOutput, calls=%fused_computation.5 | convolution fusion | flops 2155872256 | bytes 16777216 | tf_op jit(solution)/shard_map/pfke,fje->pfkj/dot_general | solution.py:110
  204.0 5.3 %copy.15 = f32[2,8,1,128,512]{4,3,2,1,0:T(8,128)} copy(f32[2,8,1,128,512]{3,4,0,1,2:T(8,128)} %fusion.4) | data formatting | bytes 8388608 | tf_op jit(solution)/shard_map/broadcast_in_dim | solution.py:111
Async XLA Ops:
  6.5 76.3 %reduce-scatter.2.cloned.1.call-start = ((), (), s32[]{:S(2)}) async-start(), calls=%async_computation.2 | async-start | bytes 4718592 | tf_op jit(solution)/shard_map/reduce_scatter | solution.py:104
  26.6 90.3 %all-gather.3.cloned.1.call-start = ((), (), s32[]{:S(2)}) async-start(), calls=%async_computation.3 | async-start | bytes 1310720 | tf_op jit(solution)/shard_map/all_gather | solution.py:77
  84.7 91.8 %all-gather.5.cloned.1.call-start = ((), (), s32[]{:S(2)}) async-start(), calls=%async_computation.4 | async-start | bytes 5242880 | tf_op jit(solution)/shard_map/all_gather | solution.py:81
  181.5 10.3 %collective-permute-start = (bf16[8,4,4,16,1024]{4,3,2,1,0:T(8,128)(2,1)}, bf16[8,4,4,16,1024]{4,3,2,1,0:T(8,128)(2,1)}, u32[]{:S(2)}, u32[]{:S(2)}) collective-permute-start(bf16[8,4,4,16,1024]{4,3,2,1,0:T(8,128)(2,1)} %copy.19), channel_id=1, source_target_pairs={{0,32},{32,0},{1,33},{33,1},{2,34},{34,2},{3,35},{35,3},{4,36},{36... | collective-permute-start | bytes 12582920 | tf_op jit(solution)/shard_map/ppermute | solution.py:83
Sparse Core Ops, SparseCore 0:
  26.7 56.1 reduce-scatter.1
  84.8 31.9 all-gather.2
  118.6 51.8 all-gather.4

commit v11 on v10

--- a/solution.py
+++ b/solution.py
@@ -78,12 +78,52 @@
     along_z, amplitudes = lax.optimization_barrier((along_z, amplitudes))
     rows = gather_rows(amplitudes)
     along_z = along_z.reshape(freqs, -1, piece, width)
-    mine = lax.all_gather(along_z, "drow", axis=2)
+    mine = lax.all_gather(along_z, "drow", axis=0)
     mine, rows = lax.optimization_barrier((mine, rows))
     theirs = lax.ppermute(mine, "core", perm=[(0, 1), (1, 0)])
-    first = lax.axis_index("core") == 0
-    pair = jnp.where(first, jnp.stack([mine, theirs], axis=2), jnp.stack([theirs, mine], axis=2))
-    return pair.reshape(freqs, -1, width), rows
+    return mine, theirs, rows
+
+
+def spec_kernel(core_ref, rows_ref, mine_ref, theirs_ref, out_ref):
+    rows = rows_ref[0]
+    first = core_ref[0] == 0
+    contract = (((1,), (1,)), ((), ()))
+
+    def dot(a, b):
+        return lax.dot_general(a, b, contract, preferred_element_type=jnp.float32)
+
+    zlo_count = mine_ref.shape[2]
+    block = 2 * mine_ref.shape[0] * mine_ref.shape[3]
+    for z in range(zlo_count):
+        own = mine_ref[:, 0, z].reshape(-1, mine_ref.shape[-1])
+        other = theirs_ref[:, 0, z].reshape(-1, mine_ref.shape[-1])
+        cols = jnp.where(
+            first, jnp.concatenate([own, other], axis=0), jnp.concatenate([other, own], axis=0)
+        )
+        out_ref[0, 0, :, z * block : (z + 1) * block] = dot(rows, cols)
+        out_ref[1, 0, :, z * block : (z + 1) * block] = dot(rows[:, DIRS:], cols[:, :DIRS]) - dot(
+            rows[:, :DIRS], cols[:, DIRS:]
+        )
+
+
+def cross_spectra(rows, mine, theirs):
+    freqs, row_count, width = rows.shape
+    col_count = 2 * mine.shape[0] * mine.shape[2] * mine.shape[3]
+    core = lax.axis_index("core").astype(jnp.int32).reshape(1)
+    col_spec = pl.BlockSpec((mine.shape[0], 1) + mine.shape[2:], lambda f: (0, f, 0, 0, 0))
+    return pl.pallas_call(
+        spec_kernel,
+        out_shape=jax.ShapeDtypeStruct((2, freqs, row_count, col_count), jnp.float32),
+        grid=(freqs,),
+        in_specs=[
+            pl.BlockSpec(memory_space=pltpu.SMEM),
+            pl.BlockSpec((1, row_count, width), lambda f: (f, 0, 0)),
+            col_spec,
+            col_spec,
+        ],
+        out_specs=pl.BlockSpec((2, 1, row_count, col_count), lambda f: (0, f, 0, 0)),
+        compiler_params=pltpu.CompilerParams(dimension_semantics=("arbitrary",)),
+    )(core, rows, mine, theirs)
 
 
 def gather_rows(amplitudes):
@@ -104,11 +144,8 @@
     amplitudes = lax.psum_scatter(partial_amp, ("zlo", "core"), scatter_dimension=1, tiled=True).astype(
         jnp.bfloat16
     )
-    cols, rows = gather_cols(amplitudes)
-    rows_im = jnp.concatenate([rows[..., DIRS:], -rows[..., :DIRS]], axis=-1)
-    lead = jnp.stack([rows, rows_im], axis=0)
-    spec = jnp.einsum("pfke,fje->pfkj", lead, cols, preferred_element_type=jnp.float32)
-    return spec[:, :, None]
+    mine, theirs, rows = gather_cols(amplitudes)
+    return cross_spectra(rows, mine, theirs)[:, :, None]
 
 
 def solution(mesh):

time: 218 us -> 207 us (0.950)
  Pallas kernels: 15.5 us -> 25.9 us
  local copies, waits for them, and re-layouts: 13.3 us -> 4.28 us
  other arithmetic: 13.4 us -> 4.76 us
  matrix products: 3.95 us -> 0 us
    pallas_call x0 -> x1, Pallas kernels: none -> 10.4 us  [cross_spectra(): pl.pallas_call(spec_kernel, out_shape=jax.ShapeDtypeStruct((2, freqs, row...]
    select_n x1 -> x0, other arithmetic: 8.25 us -> none  [gather_cols(): jnp.where(first, jnp.stack([mine, theirs], axis=2), jnp.stack([theirs, mi...]
    broadcast_in_dim x1 -> x0, local copies, waits for them, and re-layouts: 5.34 us -> none  [local(): return spec[:, :, None]]
    optimization_barrier x1 -> x0, local copies, waits for them, and re-layouts: 5.04 us -> none  [gather_cols(): mine, rows = lax.optimization_barrier((mine, rows))]
    dot_general x1 -> x0, matrix products: 3.95 us -> none  [local(): jnp.einsum('pfke,fje->pfkj', lead, cols, preferred_element_type=jnp.float32)]
where the time goes in v11:
time: 207 us; the launch traced here: 205 us
  waiting for transfers between devices  95.5 us (46%)
  blocking collectives  58.2 us (28%)
  Pallas kernels  25.9 us (13%)
  between operations  13.1 us (6%)
  other arithmetic  4.76 us (2%)
  local copies, waits for them, and re-layouts  4.28 us (2%)
  starting transfers between devices  3.23 us (2%)
    all_to_all x1, blocking collectives, gather_rows(): pieces = lax.all_to_all(copies, ('zhi', 'y'), split_axis=0, concat_axis=0)  58.2 us
    reduce_scatter x1, waiting for transfers between devices, local(): lax.psum_scatter(partial_amp, ('zlo', 'core'), scatter_dimension=1, tiled...  56.3 us
    all_gather x1, waiting for transfers between devices, gather_cols(): along_z = lax.all_gather(amplitudes, 'zlo', axis=1, tiled=True)  32.1 us
    pallas_call x1, Pallas kernels, partial_amplitudes(): pl.pallas_call(amp_kernel, out_shape=jax.ShapeDtypeStruct((FREQS, rows, 2...  15.5 us
    pallas_call x1, Pallas kernels, cross_spectra(): pl.pallas_call(spec_kernel, out_shape=jax.ShapeDtypeStruct((2, freqs, row...  10.4 us
    ppermute x1, waiting for transfers between devices, gather_cols(): theirs = lax.ppermute(mine, 'core', perm=[(0, 1), (1, 0)])  7.13 us
  transfers between devices with their start and end apart: 4, of which 3 were waited for; matrix products, arithmetic and copies ran while one was open for 1% of the time, Pallas kernels for 0%

profile of v11, /device:TPU:33, one launch (start us, length us, event | category | flops | bytes accessed | tf_op | source)
XLA Modules:
  0.0 205.0 jit_solution(5918444240358542254)
XLA Ops:
  6.5 0.0 reduce-scatter.2.cloned.1.call-start
  6.5 0.8 fusion.1
  7.3 0.8 fusion
  8.1 1.3 multiply_sqrt_fusion.spread_ref
  9.4 1.7 multiply_add_fusion.proj_ref
  11.1 15.5 %shard_map.46 = f32[8,128,1024]{2,1,0:T(8,128)} custom-call(s32[1024,512]{1,0:T(8,128)} %multiply_add_fusion.proj_ref, f32[8,512]{1,0:T(8,128)} %multiply_sqrt_fusion.spread_ref, bf16[2,8,128,1024]{3,2,1,0:T(8,128)(2,1)} %resp_ref.1), custom_call_target="tpu_custom_call" | custom-call | tf_op jit(solution)/shard_map/pallas_call | solution.py:61
  26.5 0.0 reduce-scatter.2.cloned.1.call-update
  26.5 0.0 all-gather.3.cloned.1.call-start
  26.6 56.3 %reduce-scatter.2.cloned.1.call-done = f32[8,16,1024]{2,1,0:T(8,128)} async-done(((f32[8,128,1024]{2,1,0:T(8,128)}), f32[8,16,1024]{2,1,0:T(8,128)}) %reduce-scatter.2.cloned.1.call-update) | async-done | bytes 524304 | tf_op jit(solution)/shard_map/reduce_scatter | solution.py:144
  82.9 1.8 convert_element_type.7
  84.7 0.0 all-gather.3.cloned.1.call-update
  84.7 0.0 all-gather.5.cloned.1.call-start
  84.7 32.1 %all-gather.3.cloned.1.call-done = bf16[8,64,1024]{2,1,0:T(8,128)(2,1)} async-done(((bf16[8,16,1024]{2,1,0:T(8,128)(2,1)}), bf16[8,64,1024]{2,1,0:T(8,128)(2,1)}) %all-gather.3.cloned.1.call-update) | async-done | bytes 1048592 | tf_op jit(solution)/shard_map/all_gather | solution.py:77
  116.8 0.0 all-gather.5.cloned.1.call-update
  116.8 1.2 broadcast_in_dim.4
  118.0 58.2 %all_to_all.5 = bf16[8,8,16,1024]{3,2,1,0:T(8,128)(2,1)S(1)} all-to-all(bf16[8,8,16,1024]{3,2,1,0:T(8,128)(2,1)S(1)} %broadcast_in_dim.4), channel_id=1, replica_groups=mesh['zlo'=4,'core'=2,'drow'=4,'zhi'=2,'y'=4] {'zhi','y'}, dimensions={0} | all-to-all | bytes 4194304 | tf_op jit(solution)/shard_map/all_to_all | solution.py:133
  176.3 1.5 copy.6
  177.8 0.0 all-gather.5.cloned.1.call-done.mine_ref
  177.8 3.1 %collective-permute-start = (bf16[4,8,4,16,1024]{4,3,2,1,0:T(8,128)(2,1)}, bf16[4,8,4,16,1024]{4,3,2,1,0:T(8,128)(2,1)}, u32[]{:S(2)}, u32[]{:S(2)}) collective-permute-start(bf16[4,8,4,16,1024]{4,3,2,1,0:T(8,128)(2,1)} %all-gather.5.cloned.1.call-done.mine_ref), channel_id=1, source_target_pairs={{0,32},{32,0},{1,33},{33,1},{2,34},{34,2},{3,35},{35,3},{4,36},{36... | collective-permute-start | bytes 12582920 | tf_op jit(solution)/shard_map/ppermute | solution.py:83
  180.9 7.1 %collective-permute-done.theirs_ref = bf16[4,8,4,16,1024]{4,3,2,1,0:T(8,128)(2,1)} collective-permute-done((bf16[4,8,4,16,1024]{4,3,2,1,0:T(8,128)(2,1)}, bf16[4,8,4,16,1024]{4,3,2,1,0:T(8,128)(2,1)}, u32[]{:S(2)}, u32[]{:S(2)}) %collective-permute-start) | collective-permute-done | bytes 4194336 | tf_op jit(solution)/shard_map/ppermute | solution.py:83
  188.1 10.4 %shard_map.47 = f32[2,8,128,512]{3,2,1,0:T(8,128)} custom-call(s32[1]{0:T(128)} %bitcast.core_ref, bf16[8,128,1024]{2,1,0:T(8,128)(2,1)} %bitcast.12, bf16[4,8,4,16,1024]{4,3,2,1,0:T(8,128)(2,1)} %all-gather.5.cloned.1.call-done.mine_ref, bf16[4,8,4,16,1024]{4,3,2,1,0:T(8,128)(2,1)} %collective-permute-done.theirs_ref), custom_call_target="tpu_custom_call" | custom-call | tf_op jit(solution)/shard_map/pallas_call | solution.py:114
Async XLA Ops:
  6.5 76.3 %reduce-scatter.2.cloned.1.call-start = ((), (), s32[]{:S(2)}) async-start(), calls=%async_computation.2 | async-start | bytes 4718592 | tf_op jit(solution)/shard_map/reduce_scatter | solution.py:144
  26.5 90.2 %all-gather.3.cloned.1.call-start = ((), (), s32[]{:S(2)}) async-start(), calls=%async_computation.3 | async-start | bytes 1310720 | tf_op jit(solution)/shard_map/all_gather | solution.py:77
  84.7 93.1 %all-gather.5.cloned.1.call-start = ((), (), s32[]{:S(2)}) async-start(), calls=%async_computation.4 | async-start | bytes 5242880 | tf_op jit(solution)/shard_map/all_gather | solution.py:81
  177.8 10.3 %collective-permute-start = (bf16[4,8,4,16,1024]{4,3,2,1,0:T(8,128)(2,1)}, bf16[4,8,4,16,1024]{4,3,2,1,0:T(8,128)(2,1)}, u32[]{:S(2)}, u32[]{:S(2)}) collective-permute-start(bf16[4,8,4,16,1024]{4,3,2,1,0:T(8,128)(2,1)} %all-gather.5.cloned.1.call-done.mine_ref), channel_id=1, source_target_pairs={{0,32},{32,0},{1,33},{33,1},{2,34},{34,2},{3,35},{35,3},{4,36},{36... | collective-permute-start | bytes 12582920 | tf_op jit(solution)/shard_map/ppermute | solution.py:83
Sparse Core Ops, SparseCore 0:
  26.7 56.1 reduce-scatter.1
  84.8 31.9 all-gather.2
  118.6 51.8 all-gather.4

commit v12 on v11

--- a/solution.py
+++ b/solution.py
@@ -74,10 +74,9 @@
 
 def gather_cols(amplitudes):
     freqs, piece, width = amplitudes.shape
-    along_z = lax.all_gather(amplitudes, "zlo", axis=1, tiled=True)
+    along_z = gather_by_all_to_all(amplitudes, "zlo", lax.axis_size("zlo"))
     along_z, amplitudes = lax.optimization_barrier((along_z, amplitudes))
     rows = gather_rows(amplitudes)
-    along_z = along_z.reshape(freqs, -1, piece, width)
     mine = lax.all_gather(along_z, "drow", axis=0)
     mine, rows = lax.optimization_barrier((mine, rows))
     theirs = lax.ppermute(mine, "core", perm=[(0, 1), (1, 0)])
@@ -92,11 +91,11 @@
     def dot(a, b):
         return lax.dot_general(a, b, contract, preferred_element_type=jnp.float32)
 
-    zlo_count = mine_ref.shape[2]
+    zlo_count = mine_ref.shape[1]
     block = 2 * mine_ref.shape[0] * mine_ref.shape[3]
     for z in range(zlo_count):
-        own = mine_ref[:, 0, z].reshape(-1, mine_ref.shape[-1])
-        other = theirs_ref[:, 0, z].reshape(-1, mine_ref.shape[-1])
+        own = mine_ref[:, z, 0].reshape(-1, mine_ref.shape[-1])
+        other = theirs_ref[:, z, 0].reshape(-1, mine_ref.shape[-1])
         cols = jnp.where(
             first, jnp.concatenate([own, other], axis=0), jnp.concatenate([other, own], axis=0)
         )
@@ -108,9 +107,9 @@
 
 def cross_spectra(rows, mine, theirs):
     freqs, row_count, width = rows.shape
-    col_count = 2 * mine.shape[0] * mine.shape[2] * mine.shape[3]
+    col_count = 2 * mine.shape[0] * mine.shape[1] * mine.shape[3]
     core = lax.axis_index("core").astype(jnp.int32).reshape(1)
-    col_spec = pl.BlockSpec((mine.shape[0], 1) + mine.shape[2:], lambda f: (0, f, 0, 0, 0))
+    col_spec = pl.BlockSpec(mine.shape[:2] + (1,) + mine.shape[3:], lambda f: (0, 0, f, 0, 0))
     return pl.pallas_call(
         spec_kernel,
         out_shape=jax.ShapeDtypeStruct((2, freqs, row_count, col_count), jnp.float32),
@@ -126,11 +125,15 @@
     )(core, rows, mine, theirs)
 
 
+def gather_by_all_to_all(piece, axis_name, count):
+    copies = jnp.broadcast_to(piece[None], (count,) + piece.shape)
+    return lax.all_to_all(copies, axis_name, split_axis=0, concat_axis=0)
+
+
 def gather_rows(amplitudes):
     count = lax.axis_size("zhi") * lax.axis_size("y")
     freqs, piece, width = amplitudes.shape
-    copies = jnp.broadcast_to(amplitudes[None], (count, freqs, piece, width))
-    pieces = lax.all_to_all(copies, ("zhi", "y"), split_axis=0, concat_axis=0)
+    pieces = gather_by_all_to_all(amplitudes, ("zhi", "y"), count)
     return pieces.transpose(1, 0, 2, 3).reshape(freqs, -1, width)
 
 

time: 207 us -> 202 us (0.976)
  waiting for transfers between devices: 95.5 us -> 63.4 us
  blocking collectives: 58.2 us -> 87.7 us
    all_gather x1 -> x0, waiting for transfers between devices: 32.1 us -> none  [gather_cols(): along_z = lax.all_gather(amplitudes, 'zlo', axis=1, tiled=True)]
    all_to_all x1 -> x2, blocking collectives: 58.2 us -> 87.7 us  [gather_by_all_to_all(): return lax.all_to_all(copies, axis_name, split_axis=0, concat_axis=0)]
  transfers between devices with their start and end apart: 4 -> 3, of which waited for: 3 -> 2; matrix products, arithmetic and copies ran while one was open for 1% -> 1% of each run, Pallas kernels for 0% -> 0%
where the time goes in v12:
time: 202 us; the launch traced here: 201 us
  blocking collectives  87.7 us (43%)
  waiting for transfers between devices  63.4 us (31%)
  Pallas kernels  25.9 us (13%)
  between operations  13.4 us (7%)
  other arithmetic  4.06 us (2%)
  local copies, waits for them, and re-layouts  3.45 us (2%)
  starting transfers between devices  2.85 us (1%)
    all_to_all x2, blocking collectives, gather_by_all_to_all(): return lax.all_to_all(copies, axis_name, split_axis=0, concat_axis=0)  87.7 us
    reduce_scatter x1, waiting for transfers between devices, local(): lax.psum_scatter(partial_amp, ('zlo', 'core'), scatter_dimension=1, tiled...  56.3 us
    pallas_call x1, Pallas kernels, partial_amplitudes(): pl.pallas_call(amp_kernel, out_shape=jax.ShapeDtypeStruct((FREQS, rows, 2...  15.5 us
    pallas_call x1, Pallas kernels, cross_spectra(): pl.pallas_call(spec_kernel, out_shape=jax.ShapeDtypeStruct((2, freqs, row...  10.4 us
    ppermute x1, waiting for transfers between devices, gather_cols(): theirs = lax.ppermute(mine, 'core', perm=[(0, 1), (1, 0)])  7.13 us
  transfers between devices with their start and end apart: 3, of which 2 were waited for; matrix products, arithmetic and copies ran while one was open for 1% of the time, Pallas kernels for 0%

profile of v12, /device:TPU:33, one launch (start us, length us, event | category | flops | bytes accessed | tf_op | source)
XLA Modules:
  0.0 200.8 jit_solution(13880537641765712687)
XLA Ops:
  6.5 0.0 reduce-scatter.2.cloned.1.call-start
  6.5 0.8 fusion.1
  7.3 0.8 fusion
  8.1 1.3 multiply_sqrt_fusion.spread_ref
  9.4 1.7 multiply_add_fusion.proj_ref
  11.1 15.5 %shard_map.46 = f32[8,128,1024]{2,1,0:T(8,128)} custom-call(s32[1024,512]{1,0:T(8,128)} %multiply_add_fusion.proj_ref, f32[8,512]{1,0:T(8,128)} %multiply_sqrt_fusion.spread_ref, bf16[2,8,128,1024]{3,2,1,0:T(8,128)(2,1)} %resp_ref.1), custom_call_target="tpu_custom_call" | custom-call | tf_op jit(solution)/shard_map/pallas_call | solution.py:61
  26.5 0.0 reduce-scatter.2.cloned.1.call-update
  26.6 0.0 all-gather.3.cloned.1.call-start
  26.6 56.3 %reduce-scatter.2.cloned.1.call-done = f32[8,16,1024]{2,1,0:T(8,128)} async-done(((f32[8,128,1024]{2,1,0:T(8,128)}), f32[8,16,1024]{2,1,0:T(8,128)}) %reduce-scatter.2.cloned.1.call-update) | async-done | bytes 524304 | tf_op jit(solution)/shard_map/reduce_scatter | solution.py:147
  82.9 1.1 convert_element_type.7
  84.0 0.1 broadcast_in_dim.6
  84.1 26.4 %all_to_all.10 = bf16[4,8,16,1024]{3,2,1,0:T(8,128)(2,1)} all-to-all(bf16[4,8,16,1024]{3,2,1,0:T(8,128)(2,1)S(1)} %broadcast_in_dim.6), channel_id=1, replica_groups=mesh['zlo'=4,'core'=2,'drow'=4,'zhi'=2,'y'=4] {'zlo'}, dimensions={0} | all-to-all | bytes 2097152 | tf_op jit(solution)/shard_map/all_to_all | solution.py:130
  110.4 0.0 all-gather.3.cloned.1.call-update
  110.5 0.3 broadcast_in_dim.7
  110.7 61.4 %all_to_all.11 = bf16[8,8,16,1024]{3,2,1,0:T(8,128)(2,1)S(1)} all-to-all(bf16[8,8,16,1024]{3,2,1,0:T(8,128)(2,1)S(1)} %broadcast_in_dim.7), channel_id=1, replica_groups=mesh['zlo'=4,'core'=2,'drow'=4,'zhi'=2,'y'=4] {'zhi','y'}, dimensions={0} | all-to-all | bytes 4194304 | tf_op jit(solution)/shard_map/all_to_all | solution.py:130
  172.1 1.5 copy.6
  173.6 0.0 all-gather.3.cloned.1.call-done
  173.6 2.8 %collective-permute-start = (bf16[4,4,8,16,1024]{4,3,2,1,0:T(8,128)(2,1)}, bf16[4,4,8,16,1024]{4,3,2,1,0:T(8,128)(2,1)}, u32[]{:S(2)}, u32[]{:S(2)}) collective-permute-start(bf16[4,4,8,16,1024]{4,3,2,1,0:T(8,128)(2,1)} %bitcast.13), channel_id=1, source_target_pairs={{0,32},{32,0},{1,33},{33,1},{2,34},{34,2},{3,35},{35,3},{4,36},{36... | collective-permute-start | bytes 12582920 | tf_op jit(solution)/shard_map/ppermute | solution.py:82
  176.4 7.1 %collective-permute-done.theirs_ref = bf16[4,4,8,16,1024]{4,3,2,1,0:T(8,128)(2,1)} collective-permute-done((bf16[4,4,8,16,1024]{4,3,2,1,0:T(8,128)(2,1)}, bf16[4,4,8,16,1024]{4,3,2,1,0:T(8,128)(2,1)}, u32[]{:S(2)}, u32[]{:S(2)}) %collective-permute-start) | collective-permute-done | bytes 4194336 | tf_op jit(solution)/shard_map/ppermute | solution.py:82
  183.6 10.4 %shard_map.47 = f32[2,8,128,512]{3,2,1,0:T(8,128)} custom-call(s32[1]{0:T(128)} %bitcast.core_ref, bf16[8,128,1024]{2,1,0:T(8,128)(2,1)} %bitcast.12, bf16[4,4,8,16,1024]{4,3,2,1,0:T(8,128)(2,1)} %bitcast.14, bf16[4,4,8,16,1024]{4,3,2,1,0:T(8,128)(2,1)} %collective-permute-done.theirs_ref), custom_call_target="tpu_custom_call" | custom-call | tf_op jit(solution)/shard_map/pallas_call | solution.py:113
Async XLA Ops:
  6.5 76.4 %reduce-scatter.2.cloned.1.call-start = ((), (), s32[]{:S(2)}) async-start(), calls=%async_computation.3 | async-start | bytes 4718592 | tf_op jit(solution)/shard_map/reduce_scatter | solution.py:147
  26.6 147.1 %all-gather.3.cloned.1.call-start = ((), (), s32[]{:S(2)}) async-start(), calls=%async_computation.4 | async-start | bytes 5242880 | tf_op jit(solution)/shard_map/all_gather | solution.py:80
  173.6 9.9 %collective-permute-start = (bf16[4,4,8,16,1024]{4,3,2,1,0:T(8,128)(2,1)}, bf16[4,4,8,16,1024]{4,3,2,1,0:T(8,128)(2,1)}, u32[]{:S(2)}, u32[]{:S(2)}) collective-permute-start(bf16[4,4,8,16,1024]{4,3,2,1,0:T(8,128)(2,1)} %bitcast.13), channel_id=1, source_target_pairs={{0,32},{32,0},{1,33},{33,1},{2,34},{34,2},{3,35},{35,3},{4,36},{36... | collective-permute-start | bytes 12582920 | tf_op jit(solution)/shard_map/ppermute | solution.py:82
Sparse Core Ops, SparseCore 0:
  26.7 56.1 reduce-scatter.1
  110.6 54.8 all-gather.2

commit v13 on v12

--- a/solution.py
+++ b/solution.py
@@ -85,6 +85,7 @@
 
 def spec_kernel(core_ref, rows_ref, mine_ref, theirs_ref, out_ref):
     rows = rows_ref[0]
+    rows_im = jnp.concatenate([rows[:, DIRS:], -rows[:, :DIRS]], axis=1)
     first = core_ref[0] == 0
     contract = (((1,), (1,)), ((), ()))
 
@@ -100,9 +101,7 @@
             first, jnp.concatenate([own, other], axis=0), jnp.concatenate([other, own], axis=0)
         )
         out_ref[0, 0, :, z * block : (z + 1) * block] = dot(rows, cols)
-        out_ref[1, 0, :, z * block : (z + 1) * block] = dot(rows[:, DIRS:], cols[:, :DIRS]) - dot(
-            rows[:, :DIRS], cols[:, DIRS:]
-        )
+        out_ref[1, 0, :, z * block : (z + 1) * block] = dot(rows_im, cols)
 
 
 def cross_spectra(rows, mine, theirs):

time: 202 us -> 202 us (level)
  no operation moved by 1% of the time
where the time goes in v13:
time: 202 us; the launch traced here: 201 us
  blocking collectives  87.7 us (43%)
  waiting for transfers between devices  63.4 us (31%)
  Pallas kernels  25.9 us (13%)
  between operations  13.4 us (7%)
  other arithmetic  4.06 us (2%)
  local copies, waits for them, and re-layouts  3.45 us (2%)
  starting transfers between devices  2.85 us (1%)
    all_to_all x2, blocking collectives, gather_by_all_to_all(): return lax.all_to_all(copies, axis_name, split_axis=0, concat_axis=0)  87.7 us
    reduce_scatter x1, waiting for transfers between devices, local(): lax.psum_scatter(partial_amp, ('zlo', 'core'), scatter_dimension=1, tiled...  56.3 us
    pallas_call x1, Pallas kernels, partial_amplitudes(): pl.pallas_call(amp_kernel, out_shape=jax.ShapeDtypeStruct((FREQS, rows, 2...  15.5 us
    pallas_call x1, Pallas kernels, cross_spectra(): pl.pallas_call(spec_kernel, out_shape=jax.ShapeDtypeStruct((2, freqs, row...  10.4 us
    ppermute x1, waiting for transfers between devices, gather_cols(): theirs = lax.ppermute(mine, 'core', perm=[(0, 1), (1, 0)])  7.13 us
  transfers between devices with their start and end apart: 3, of which 2 were waited for; matrix products, arithmetic and copies ran while one was open for 1% of the time, Pallas kernels for 0%

profile of v13, /device:TPU:33, one launch (start us, length us, event | category | flops | bytes accessed | tf_op | source)
XLA Modules:
  0.0 200.8 jit_solution(7408424811780529515)
XLA Ops:
  6.5 0.0 reduce-scatter.2.cloned.1.call-start
  6.5 0.8 fusion.1
  7.3 0.8 fusion
  8.1 1.3 multiply_sqrt_fusion.spread_ref
  9.4 1.7 multiply_add_fusion.proj_ref
  11.1 15.5 %shard_map.46 = f32[8,128,1024]{2,1,0:T(8,128)} custom-call(s32[1024,512]{1,0:T(8,128)} %multiply_add_fusion.proj_ref, f32[8,512]{1,0:T(8,128)} %multiply_sqrt_fusion.spread_ref, bf16[2,8,128,1024]{3,2,1,0:T(8,128)(2,1)} %resp_ref.1), custom_call_target="tpu_custom_call" | custom-call | tf_op jit(solution)/shard_map/pallas_call | solution.py:61
  26.5 0.0 reduce-scatter.2.cloned.1.call-update
  26.6 0.0 all-gather.3.cloned.1.call-start
  26.6 56.3 %reduce-scatter.2.cloned.1.call-done = f32[8,16,1024]{2,1,0:T(8,128)} async-done(((f32[8,128,1024]{2,1,0:T(8,128)}), f32[8,16,1024]{2,1,0:T(8,128)}) %reduce-scatter.2.cloned.1.call-update) | async-done | bytes 524304 | tf_op jit(solution)/shard_map/reduce_scatter | solution.py:146
  82.9 1.1 convert_element_type.7
  84.0 0.1 broadcast_in_dim.6
  84.1 26.4 %all_to_all.10 = bf16[4,8,16,1024]{3,2,1,0:T(8,128)(2,1)} all-to-all(bf16[4,8,16,1024]{3,2,1,0:T(8,128)(2,1)S(1)} %broadcast_in_dim.6), channel_id=1, replica_groups=mesh['zlo'=4,'core'=2,'drow'=4,'zhi'=2,'y'=4] {'zlo'}, dimensions={0} | all-to-all | bytes 2097152 | tf_op jit(solution)/shard_map/all_to_all | solution.py:129
  110.4 0.0 all-gather.3.cloned.1.call-update
  110.5 0.3 broadcast_in_dim.7
  110.7 61.4 %all_to_all.11 = bf16[8,8,16,1024]{3,2,1,0:T(8,128)(2,1)S(1)} all-to-all(bf16[8,8,16,1024]{3,2,1,0:T(8,128)(2,1)S(1)} %broadcast_in_dim.7), channel_id=1, replica_groups=mesh['zlo'=4,'core'=2,'drow'=4,'zhi'=2,'y'=4] {'zhi','y'}, dimensions={0} | all-to-all | bytes 4194304 | tf_op jit(solution)/shard_map/all_to_all | solution.py:129
  172.1 1.5 copy.6
  173.6 0.0 all-gather.3.cloned.1.call-done
  173.6 2.8 %collective-permute-start = (bf16[4,4,8,16,1024]{4,3,2,1,0:T(8,128)(2,1)}, bf16[4,4,8,16,1024]{4,3,2,1,0:T(8,128)(2,1)}, u32[]{:S(2)}, u32[]{:S(2)}) collective-permute-start(bf16[4,4,8,16,1024]{4,3,2,1,0:T(8,128)(2,1)} %bitcast.13), channel_id=1, source_target_pairs={{0,32},{32,0},{1,33},{33,1},{2,34},{34,2},{3,35},{35,3},{4,36},{36... | collective-permute-start | bytes 12582920 | tf_op jit(solution)/shard_map/ppermute | solution.py:82
  176.4 7.1 %collective-permute-done.theirs_ref = bf16[4,4,8,16,1024]{4,3,2,1,0:T(8,128)(2,1)} collective-permute-done((bf16[4,4,8,16,1024]{4,3,2,1,0:T(8,128)(2,1)}, bf16[4,4,8,16,1024]{4,3,2,1,0:T(8,128)(2,1)}, u32[]{:S(2)}, u32[]{:S(2)}) %collective-permute-start) | collective-permute-done | bytes 4194336 | tf_op jit(solution)/shard_map/ppermute | solution.py:82
  183.6 10.4 %shard_map.47 = f32[2,8,128,512]{3,2,1,0:T(8,128)} custom-call(s32[1]{0:T(128)} %bitcast.core_ref, bf16[8,128,1024]{2,1,0:T(8,128)(2,1)} %bitcast.12, bf16[4,4,8,16,1024]{4,3,2,1,0:T(8,128)(2,1)} %bitcast.14, bf16[4,4,8,16,1024]{4,3,2,1,0:T(8,128)(2,1)} %collective-permute-done.theirs_ref), custom_call_target="tpu_custom_call" | custom-call | tf_op jit(solution)/shard_map/pallas_call | solution.py:112
Async XLA Ops:
  6.5 76.4 %reduce-scatter.2.cloned.1.call-start = ((), (), s32[]{:S(2)}) async-start(), calls=%async_computation.3 | async-start | bytes 4718592 | tf_op jit(solution)/shard_map/reduce_scatter | solution.py:146
  26.6 147.1 %all-gather.3.cloned.1.call-start = ((), (), s32[]{:S(2)}) async-start(), calls=%async_computation.4 | async-start | bytes 5242880 | tf_op jit(solution)/shard_map/all_gather | solution.py:80
  173.6 9.9 %collective-permute-start = (bf16[4,4,8,16,1024]{4,3,2,1,0:T(8,128)(2,1)}, bf16[4,4,8,16,1024]{4,3,2,1,0:T(8,128)(2,1)}, u32[]{:S(2)}, u32[]{:S(2)}) collective-permute-start(bf16[4,4,8,16,1024]{4,3,2,1,0:T(8,128)(2,1)} %bitcast.13), channel_id=1, source_target_pairs={{0,32},{32,0},{1,33},{33,1},{2,34},{34,2},{3,35},{35,3},{4,36},{36... | collective-permute-start | bytes 12582920 | tf_op jit(solution)/shard_map/ppermute | solution.py:82
Sparse Core Ops, SparseCore 0:
  26.7 56.1 reduce-scatter.1
  110.6 54.8 all-gather.2

commit v14 on v13

--- a/solution.py
+++ b/solution.py
@@ -74,7 +74,7 @@
 
 def gather_cols(amplitudes):
     freqs, piece, width = amplitudes.shape
-    along_z = gather_by_all_to_all(amplitudes, "zlo", lax.axis_size("zlo"))
+    along_z = gather_by_permutes(amplitudes, "zlo", lax.axis_size("zlo"))
     along_z, amplitudes = lax.optimization_barrier((along_z, amplitudes))
     rows = gather_rows(amplitudes)
     mine = lax.all_gather(along_z, "drow", axis=0)
@@ -124,6 +124,15 @@
     )(core, rows, mine, theirs)
 
 
+def gather_by_permutes(piece, axis_name, count):
+    ahead = [piece]
+    for shift in range(1, count):
+        ahead.append(
+            lax.ppermute(piece, axis_name, perm=[(i, (i - shift) % count) for i in range(count)])
+        )
+    return jnp.roll(jnp.stack(ahead), lax.axis_index(axis_name), axis=0)
+
+
 def gather_by_all_to_all(piece, axis_name, count):
     copies = jnp.broadcast_to(piece[None], (count,) + piece.shape)
     return lax.all_to_all(copies, axis_name, split_axis=0, concat_axis=0)

time: 202 us -> 198 us (0.980); the launches traced: 201 us -> 195 us
  blocking collectives: 87.7 us -> 57.3 us
  waiting for transfers between devices: 63.4 us -> 84.9 us
    all_to_all x2 -> x1, blocking collectives: 87.7 us -> 57.3 us  [gather_by_all_to_all(): return lax.all_to_all(copies, axis_name, split_axis=0, concat_axis=0)]
    ppermute x0 -> x3, waiting for transfers between devices: none -> 21.5 us  [gather_by_permutes(): lax.ppermute(piece, axis_name, perm=[(i, (i - shift) % count) for i in ra...]
    ppermute x0 -> x3, starting transfers between devices: none -> 3.59 us  [gather_by_permutes(): lax.ppermute(piece, axis_name, perm=[(i, (i - shift) % count) for i in ra...]
    ppermute x1, starting transfers between devices: 2.81 us -> 0.79 us  [gather_cols(): theirs = lax.ppermute(mine, 'core', perm=[(0, 1), (1, 0)])]
  transfers between devices with their start and end apart: 3 -> 6, of which waited for: 2 -> 5; matrix products, arithmetic and copies ran while one was open for 1% -> 1% of each run, Pallas kernels for 0% -> 0%
where the time goes in v14:
time: 198 us; the launch traced here: 195 us
  waiting for transfers between devices  84.9 us (43%)
  blocking collectives  57.3 us (29%)
  Pallas kernels  25.9 us (13%)
  between operations  13.5 us (7%)
  local copies, waits for them, and re-layouts  4.52 us (2%)
  starting transfers between devices  4.42 us (2%)
  other arithmetic  4.08 us (2%)
    all_to_all x1, blocking collectives, gather_by_all_to_all(): return lax.all_to_all(copies, axis_name, split_axis=0, concat_axis=0)  57.3 us
    reduce_scatter x1, waiting for transfers between devices, local(): lax.psum_scatter(partial_amp, ('zlo', 'core'), scatter_dimension=1, tiled...  56.3 us
    ppermute x3, waiting for transfers between devices, gather_by_permutes(): lax.ppermute(piece, axis_name, perm=[(i, (i - shift) % count) for i in ra...  21.5 us
    pallas_call x1, Pallas kernels, partial_amplitudes(): pl.pallas_call(amp_kernel, out_shape=jax.ShapeDtypeStruct((FREQS, rows, 2...  15.5 us
    pallas_call x1, Pallas kernels, cross_spectra(): pl.pallas_call(spec_kernel, out_shape=jax.ShapeDtypeStruct((2, freqs, row...  10.4 us
    ppermute x1, waiting for transfers between devices, gather_cols(): theirs = lax.ppermute(mine, 'core', perm=[(0, 1), (1, 0)])  7.13 us
  transfers between devices with their start and end apart: 6, of which 5 were waited for; matrix products, arithmetic and copies ran while one was open for 1% of the time, Pallas kernels for 0%

profile of v14, /device:TPU:33, one launch (start us, length us, event | category | flops | bytes accessed | tf_op | source)
XLA Modules:
  0.0 194.5 jit_solution(17225335100561342115)
XLA Ops:
  6.5 0.0 reduce-scatter.2.cloned.1.call-start
  6.5 0.8 fusion.1
  7.3 0.8 fusion
  8.1 1.3 multiply_sqrt_fusion.spread_ref
  9.4 1.6 multiply_add_fusion.proj_ref
  11.1 15.5 %shard_map.46 = f32[8,128,1024]{2,1,0:T(8,128)} custom-call(s32[1024,512]{1,0:T(8,128)} %multiply_add_fusion.proj_ref, f32[8,512]{1,0:T(8,128)} %multiply_sqrt_fusion.spread_ref, bf16[2,8,128,1024]{3,2,1,0:T(8,128)(2,1)} %resp_ref.1), custom_call_target="tpu_custom_call" | custom-call | tf_op jit(solution)/shard_map/pallas_call | solution.py:61
  26.5 0.0 reduce-scatter.2.cloned.1.call-update
  26.6 0.0 all-gather.3.cloned.1.call-start
  26.6 56.3 %reduce-scatter.2.cloned.1.call-done = f32[8,16,1024]{2,1,0:T(8,128)} async-done(((f32[8,128,1024]{2,1,0:T(8,128)}), f32[8,16,1024]{2,1,0:T(8,128)}) %reduce-scatter.2.cloned.1.call-update) | async-done | bytes 524304 | tf_op jit(solution)/shard_map/reduce_scatter | solution.py:155
  82.9 1.1 bitcast_dynamic-update-slice_fusion.6
  84.0 0.1 collective-permute-start
  84.1 2.4 %collective-permute-start.1 = (bf16[8,16,1024]{2,1,0:T(8,128)(2,1)S(1)}, bf16[8,16,1024]{2,1,0:T(8,128)(2,1)S(1)}, u32[]{:S(2)}, u32[]{:S(2)}) collective-permute-start(bf16[8,16,1024]{2,1,0:T(8,128)(2,1)S(1)} %get-tuple-element.10), channel_id=1, source_target_pairs={{0,128},{64,192},{128,0},{192,64},{1,129},{65,193},{129,1},{193,65... | collective-permute-start | bytes 786440 | tf_op jit(solution)/shard_map/ppermute | solution.py:131
  86.5 1.1 collective-permute-start.2
  87.6 5.1 %collective-permute-done = bf16[8,16,1024]{2,1,0:T(8,128)(2,1)S(1)} collective-permute-done((bf16[8,16,1024]{2,1,0:T(8,128)(2,1)S(1)}, bf16[8,16,1024]{2,1,0:T(8,128)(2,1)S(1)}, u32[]{:S(2)}, u32[]{:S(2)}) %collective-permute-start) | collective-permute-done | bytes 262176 | tf_op jit(solution)/shard_map/ppermute | solution.py:131
  92.7 10.8 %collective-permute-done.1 = bf16[8,16,1024]{2,1,0:T(8,128)(2,1)S(1)} collective-permute-done((bf16[8,16,1024]{2,1,0:T(8,128)(2,1)S(1)}, bf16[8,16,1024]{2,1,0:T(8,128)(2,1)S(1)}, u32[]{:S(2)}, u32[]{:S(2)}) %collective-permute-start.1) | collective-permute-done | bytes 262176 | tf_op jit(solution)/shard_map/ppermute | solution.py:131
  103.5 5.6 %collective-permute-done.2 = bf16[8,16,1024]{2,1,0:T(8,128)(2,1)S(1)} collective-permute-done((bf16[8,16,1024]{2,1,0:T(8,128)(2,1)S(1)}, bf16[8,16,1024]{2,1,0:T(8,128)(2,1)S(1)}, u32[]{:S(2)}, u32[]{:S(2)}) %collective-permute-start.2) | collective-permute-done | bytes 262176 | tf_op jit(solution)/shard_map/ppermute | solution.py:131
  109.2 1.1 constant_dynamic-slice_fusion
  110.3 0.0 all-gather.3.cloned.1.call-update
  110.3 0.3 broadcast_in_dim.4
  110.5 57.3 %all_to_all.5 = bf16[8,8,16,1024]{3,2,1,0:T(8,128)(2,1)S(1)} all-to-all(bf16[8,8,16,1024]{3,2,1,0:T(8,128)(2,1)S(1)} %broadcast_in_dim.4), channel_id=1, replica_groups=mesh['zlo'=4,'core'=2,'drow'=4,'zhi'=2,'y'=4] {'zhi','y'}, dimensions={0} | all-to-all | bytes 4194304 | tf_op jit(solution)/shard_map/all_to_all | solution.py:138
  167.8 1.5 copy.6
  169.3 0.0 all-gather.3.cloned.1.call-done
  169.3 0.8 collective-permute-start.3
  170.1 7.1 %collective-permute-done.3.theirs_ref = bf16[4,4,8,16,1024]{4,3,2,1,0:T(8,128)(2,1)} collective-permute-done((bf16[4,4,8,16,1024]{4,3,2,1,0:T(8,128)(2,1)}, bf16[4,4,8,16,1024]{4,3,2,1,0:T(8,128)(2,1)}, u32[]{:S(2)}, u32[]{:S(2)}) %collective-permute-start.3) | collective-permute-done | bytes 4194336 | tf_op jit(solution)/shard_map/ppermute | solution.py:82
  177.3 10.4 %shard_map.47 = f32[2,8,128,512]{3,2,1,0:T(8,128)} custom-call(s32[1]{0:T(128)} %bitcast.core_ref, bf16[8,128,1024]{2,1,0:T(8,128)(2,1)} %bitcast.24, bf16[4,4,8,16,1024]{4,3,2,1,0:T(8,128)(2,1)} %bitcast.26, bf16[4,4,8,16,1024]{4,3,2,1,0:T(8,128)(2,1)} %collective-permute-done.3.theirs_ref), custom_call_target="tpu_custom_call" | custom-call | tf_op jit(solution)/shard_map/pallas_call | solution.py:112
  (7 shorter events, 0.1 us)
Async XLA Ops:
  6.5 76.3 %reduce-scatter.2.cloned.1.call-start = ((), (), s32[]{:S(2)}) async-start(), calls=%async_computation.2 | async-start | bytes 4718592 | tf_op jit(solution)/shard_map/reduce_scatter | solution.py:155
  26.6 142.8 %all-gather.3.cloned.1.call-start = ((), (), s32[]{:S(2)}) async-start(), calls=%async_computation.3 | async-start | bytes 5242880 | tf_op jit(solution)/shard_map/all_gather | solution.py:80
  84.0 8.7 %collective-permute-start = (bf16[8,16,1024]{2,1,0:T(8,128)(2,1)S(1)}, bf16[8,16,1024]{2,1,0:T(8,128)(2,1)S(1)}, u32[]{:S(2)}, u32[]{:S(2)}) collective-permute-start(bf16[8,16,1024]{2,1,0:T(8,128)(2,1)S(1)} %get-tuple-element.10), channel_id=1, source_target_pairs={{0,192},{64,0},{128,64},{192,128},{1,193},{65,1},{129,65},{193,129... | collective-permute-start | bytes 786440 | tf_op jit(solution)/shard_map/ppermute | solution.py:131
  84.1 19.4 %collective-permute-start.1 = (bf16[8,16,1024]{2,1,0:T(8,128)(2,1)S(1)}, bf16[8,16,1024]{2,1,0:T(8,128)(2,1)S(1)}, u32[]{:S(2)}, u32[]{:S(2)}) collective-permute-start(bf16[8,16,1024]{2,1,0:T(8,128)(2,1)S(1)} %get-tuple-element.10), channel_id=1, source_target_pairs={{0,128},{64,192},{128,0},{192,64},{1,129},{65,193},{129,1},{193,65... | collective-permute-start | bytes 786440 | tf_op jit(solution)/shard_map/ppermute | solution.py:131
  86.5 22.6 %collective-permute-start.2 = (bf16[8,16,1024]{2,1,0:T(8,128)(2,1)S(1)}, bf16[8,16,1024]{2,1,0:T(8,128)(2,1)S(1)}, u32[]{:S(2)}, u32[]{:S(2)}) collective-permute-start(bf16[8,16,1024]{2,1,0:T(8,128)(2,1)S(1)} %get-tuple-element.10), channel_id=1, source_target_pairs={{0,64},{64,128},{128,192},{192,0},{1,65},{65,129},{129,193},{193,1... | collective-permute-start | bytes 786440 | tf_op jit(solution)/shard_map/ppermute | solution.py:131
  169.3 7.9 %collective-permute-start.3 = (bf16[4,4,8,16,1024]{4,3,2,1,0:T(8,128)(2,1)}, bf16[4,4,8,16,1024]{4,3,2,1,0:T(8,128)(2,1)}, u32[]{:S(2)}, u32[]{:S(2)}) collective-permute-start(bf16[4,4,8,16,1024]{4,3,2,1,0:T(8,128)(2,1)} %bitcast.25), channel_id=1, source_target_pairs={{0,32},{32,0},{1,33},{33,1},{2,34},{34,2},{3,35},{35,3},{4,36},{36... | collective-permute-start | bytes 12582920 | tf_op jit(solution)/shard_map/ppermute | solution.py:82
Sparse Core Ops, SparseCore 0:
  26.7 56.1 reduce-scatter.1
  110.4 51.4 all-gather.2

commit v15 on v14

--- a/solution.py
+++ b/solution.py
@@ -145,6 +145,24 @@
     return pieces.transpose(1, 0, 2, 3).reshape(freqs, -1, width)
 
 
+def reduce_over_nodes(partial_amp):
+    freqs, dofs, width = partial_amp.shape
+    zlo_count = lax.axis_size("zlo")
+    split = partial_amp.reshape(freqs, zlo_count, 2, dofs // (2 * zlo_count), width)
+    first = lax.axis_index("core") == 0
+    keep = jnp.where(first, split[:, :, 0], split[:, :, 1])
+    send = jnp.where(first, split[:, :, 1], split[:, :, 0])
+    pair = keep + lax.ppermute(send, "core", perm=[(0, 1), (1, 0)])
+    zlo = lax.axis_index("zlo")
+    total = lax.dynamic_index_in_dim(pair, zlo, axis=1, keepdims=False)
+    for shift in range(1, zlo_count):
+        piece = lax.dynamic_index_in_dim(pair, (zlo + shift) % zlo_count, axis=1, keepdims=False)
+        total = total + lax.ppermute(
+            piece, "zlo", perm=[(i, (i + shift) % zlo_count) for i in range(zlo_count)]
+        )
+    return total
+
+
 def local(freq_resp, node_coords, heading_steps, spectral_weights):
     project = (
         node_coords[0][:, None] * heading_steps[0][None, :]
@@ -152,9 +170,7 @@
     )
     spread = jnp.sqrt(spectral_weights.astype(jnp.float32) / (64.0 * DIRS))
     partial_amp = partial_amplitudes(freq_resp, project, spread)
-    amplitudes = lax.psum_scatter(partial_amp, ("zlo", "core"), scatter_dimension=1, tiled=True).astype(
-        jnp.bfloat16
-    )
+    amplitudes = reduce_over_nodes(partial_amp).astype(jnp.bfloat16)
     mine, theirs, rows = gather_cols(amplitudes)
     return cross_spectra(rows, mine, theirs)[:, :, None]
 

time: 198 us -> 207 us (1.045)
  waiting for transfers between devices: 84.9 us -> 72 us
  other arithmetic: 4.08 us -> 11.3 us
  local copies, waits for them, and re-layouts: 4.52 us -> 11.7 us
  starting transfers between devices: 4.42 us -> 11.6 us
    reduce_scatter x1 -> x0, waiting for transfers between devices: 56.3 us -> none  [local(): lax.psum_scatter(partial_amp, ('zlo', 'core'), scatter_dimension=1, tiled...]
    ppermute x0 -> x4, waiting for transfers between devices: none -> 45.9 us  [the longest x3 42 us: reduce_over_nodes(): lax.ppermute(piece, 'zlo', perm=[(i, (i + shift) % zlo_count) for i in ra...]
    ppermute x0 -> x4, starting transfers between devices: none -> 5.22 us  [the longest x3 4.46 us: reduce_over_nodes(): lax.ppermute(piece, 'zlo', perm=[(i, (i + shift) % zlo_count) for i in ra...]
    unnamed x6, local copies, waits for them, and re-layouts: 0.11 us -> 4.35 us
    add x0 -> x1, other arithmetic: none -> 3.54 us  [reduce_over_nodes(): pair = keep + lax.ppermute(send, 'core', perm=[(0, 1), (1, 0)])]
    select_n x0 -> x1, other arithmetic: none -> 2.62 us  [reduce_over_nodes(): send = jnp.where(first, split[:, :, 1], split[:, :, 0])]
    ppermute x3, waiting for transfers between devices: 21.5 us -> 18.9 us  [gather_by_permutes(): lax.ppermute(piece, axis_name, perm=[(i, (i - shift) % count) for i in ra...]
  transfers between devices with their start and end apart: 6 -> 9, of which waited for: 5 -> 8; matrix products, arithmetic and copies ran while one was open for 1% -> 2% of each run, Pallas kernels for 0% -> 0%
where the time goes in v15:
time: 207 us; the launch traced here: 205 us
  waiting for transfers between devices  72 us (35%)
  blocking collectives  59 us (29%)
  Pallas kernels  25.9 us (13%)
  between operations  13.4 us (6%)
  local copies, waits for them, and re-layouts  11.7 us (6%)
  starting transfers between devices  11.6 us (6%)
  other arithmetic  11.3 us (5%)
    all_to_all x1, blocking collectives, gather_by_all_to_all(): return lax.all_to_all(copies, axis_name, split_axis=0, concat_axis=0)  59 us
    ppermute x3, waiting for transfers between devices, reduce_over_nodes(): lax.ppermute(piece, 'zlo', perm=[(i, (i + shift) % zlo_count) for i in ra...  42 us
    ppermute x3, waiting for transfers between devices, gather_by_permutes(): lax.ppermute(piece, axis_name, perm=[(i, (i - shift) % count) for i in ra...  18.9 us
    pallas_call x1, Pallas kernels, partial_amplitudes(): pl.pallas_call(amp_kernel, out_shape=jax.ShapeDtypeStruct((FREQS, rows, 2...  15.5 us
    pallas_call x1, Pallas kernels, cross_spectra(): pl.pallas_call(spec_kernel, out_shape=jax.ShapeDtypeStruct((2, freqs, row...  10.4 us
    ppermute x1, waiting for transfers between devices, gather_cols(): theirs = lax.ppermute(mine, 'core', perm=[(0, 1), (1, 0)])  7.13 us
    ppermute x3, starting transfers between devices, gather_by_permutes(): lax.ppermute(piece, axis_name, perm=[(i, (i - shift) % count) for i in ra...  5.57 us
    ppermute x3, starting transfers between devices, reduce_over_nodes(): lax.ppermute(piece, 'zlo', perm=[(i, (i + shift) % zlo_count) for i in ra...  4.46 us
  transfers between devices with their start and end apart: 9, of which 8 were waited for; matrix products, arithmetic and copies ran while one was open for 2% of the time, Pallas kernels for 0%

profile of v15, /device:TPU:33, one launch (start us, length us, event | category | flops | bytes accessed | tf_op | source)
XLA Modules:
  0.0 205.0 jit_solution(18077690073864570736)
XLA Ops:
  6.5 0.8 fusion.7
  7.3 0.8 fusion.6
  8.1 1.3 multiply_sqrt_fusion.spread_ref
  9.4 1.6 multiply_add_fusion.proj_ref
  11.1 15.5 %shard_map.46 = f32[8,128,1024]{2,1,0:T(8,128)} custom-call(s32[1024,512]{1,0:T(8,128)} %multiply_add_fusion.proj_ref, f32[8,512]{1,0:T(8,128)} %multiply_sqrt_fusion.spread_ref, bf16[2,8,128,1024]{3,2,1,0:T(8,128)(2,1)} %resp_ref.1), custom_call_target="tpu_custom_call" | custom-call | tf_op jit(solution)/shard_map/pallas_call | solution.py:61
  26.5 2.6 %select_bitcast_fusion = f32[8,4,16,1024]{3,2,1,0:T(8,128)S(1)} fusion(f32[8,4,2,16,1024]{4,3,2,1,0:T(8,128)} %bitcast.57, pred[]{:T(512)S(6)} %eq.10), kind=kLoop, calls=%fused_computation.3 | loop fusion | flops 524288 | bytes 6291457 | tf_op jit(solution)/shard_map/jit(_where)/select_n | solution.py:154
  29.2 0.8 collective-permute-start
  29.9 3.9 %collective-permute-done = f32[8,4,16,1024]{3,2,1,0:T(8,128)} collective-permute-done((f32[8,4,16,1024]{3,2,1,0:T(8,128)S(1)}, f32[8,4,16,1024]{3,2,1,0:T(8,128)}, u32[]{:S(2)}, u32[]{:S(2)}) %collective-permute-start) | collective-permute-done | bytes 2097184 | tf_op jit(solution)/shard_map/ppermute | solution.py:155
  33.8 3.5 %fusion.1 = f32[8,4,16,1024]{3,2,1,0:T(8,128)S(1)} fusion(f32[8,4,16,1024]{3,2,1,0:T(8,128)} %collective-permute-done, f32[8,4,2,16,1024]{4,3,2,1,0:T(8,128)} %bitcast.58, pred[]{:T(512)S(6)} %eq.10), kind=kLoop, calls=%fused_computation.2 | loop fusion | flops 1048576 | bytes 8388609 | tf_op jit(solution)/shard_map/add | solution.py:155
  37.4 1.0 dynamic-slice_bitcast_fusion.2
  38.3 1.6 collective-permute-start.1
  40.0 2.8 %collective-permute-start.2 = (f32[8,16,1024]{2,1,0:T(8,128)S(1)}, f32[8,16,1024]{2,1,0:T(8,128)}, u32[]{:S(2)}, u32[]{:S(2)}) collective-permute-start(f32[8,16,1024]{2,1,0:T(8,128)S(1)} %get-tuple-element.17), channel_id=1, source_target_pairs={{0,128},{64,192},{128,0},{192,64},{1,129},{65,193},{129,1},{193,65... | collective-permute-start | bytes 1572872 | tf_op jit(solution)/shard_map/ppermute | solution.py:160
  42.8 9.2 %collective-permute-done.1 = f32[8,16,1024]{2,1,0:T(8,128)} collective-permute-done((f32[8,16,1024]{2,1,0:T(8,128)}, f32[8,16,1024]{2,1,0:T(8,128)}, u32[]{:S(2)}, u32[]{:S(2)}) %collective-permute-start.1) | collective-permute-done | bytes 524320 | tf_op jit(solution)/shard_map/ppermute | solution.py:160
  52.0 12.8 %collective-permute-done.3 = f32[8,16,1024]{2,1,0:T(8,128)} collective-permute-done((f32[8,16,1024]{2,1,0:T(8,128)S(1)}, f32[8,16,1024]{2,1,0:T(8,128)}, u32[]{:S(2)}, u32[]{:S(2)}) %collective-permute-start.3) | collective-permute-done | bytes 524320 | tf_op jit(solution)/shard_map/ppermute | solution.py:160
  64.8 20.1 %collective-permute-done.2 = f32[8,16,1024]{2,1,0:T(8,128)} collective-permute-done((f32[8,16,1024]{2,1,0:T(8,128)S(1)}, f32[8,16,1024]{2,1,0:T(8,128)}, u32[]{:S(2)}, u32[]{:S(2)}) %collective-permute-start.2) | collective-permute-done | bytes 524320 | tf_op jit(solution)/shard_map/ppermute | solution.py:160
  84.8 2.2 %bitcast_dynamic-update-slice_fusion.6 = (bf16[8,8,16,1024]{3,2,1,0:T(8,128)(2,1)}, bf16[8,16,1024]{2,1,0:T(8,128)(2,1)S(1)}) fusion(f32[8,16,1024]{2,1,0:T(8,128)} %collective-permute-done.3, f32[8,16,1024]{2,1,0:T(8,128)} %collective-permute-done.2, f32[8,16,1024]{2,1,0:T(8,128)} %collective-permute-done.1, f32[8,4,16,1024]{3,2,1,0:T(8,128)S(1)} %fusion.1, ...), kind=kLoop, calls=%fused_computation.18 | loop fusion | flops 524287 | bytes 2621444
  87.0 3.6 %collective-permute-start.4 = (bf16[8,16,1024]{2,1,0:T(8,128)(2,1)S(1)}, bf16[8,16,1024]{2,1,0:T(8,128)(2,1)S(1)}, u32[]{:S(2)}, u32[]{:S(2)}) collective-permute-start(bf16[8,16,1024]{2,1,0:T(8,128)(2,1)S(1)} %get-tuple-element.10), channel_id=1, source_target_pairs={{0,192},{64,0},{128,64},{192,128},{1,193},{65,1},{129,65},{193,129... | collective-permute-start | bytes 786440 | tf_op jit(solution)/shard_map/ppermute | solution.py:131
  90.6 2.0 collective-permute-start.6
  92.6 3.7 %collective-permute-done.4 = bf16[8,16,1024]{2,1,0:T(8,128)(2,1)S(1)} collective-permute-done((bf16[8,16,1024]{2,1,0:T(8,128)(2,1)S(1)}, bf16[8,16,1024]{2,1,0:T(8,128)(2,1)S(1)}, u32[]{:S(2)}, u32[]{:S(2)}) %collective-permute-start.4) | collective-permute-done | bytes 262176 | tf_op jit(solution)/shard_map/ppermute | solution.py:131
  96.3 0.7 bitcast_dynamic-update-slice_fusion.4
  97.0 10.4 %collective-permute-done.5 = bf16[8,16,1024]{2,1,0:T(8,128)(2,1)S(1)} collective-permute-done((bf16[8,16,1024]{2,1,0:T(8,128)(2,1)S(1)}, bf16[8,16,1024]{2,1,0:T(8,128)(2,1)S(1)}, u32[]{:S(2)}, u32[]{:S(2)}) %collective-permute-start.5) | collective-permute-done | bytes 262176 | tf_op jit(solution)/shard_map/ppermute | solution.py:131
  107.4 0.7 bitcast_dynamic-update-slice_fusion.2
  108.1 4.9 %collective-permute-done.6 = bf16[8,16,1024]{2,1,0:T(8,128)(2,1)S(1)} collective-permute-done((bf16[8,16,1024]{2,1,0:T(8,128)(2,1)S(1)}, bf16[8,16,1024]{2,1,0:T(8,128)(2,1)S(1)}, u32[]{:S(2)}, u32[]{:S(2)}) %collective-permute-start.6) | collective-permute-done | bytes 262176 | tf_op jit(solution)/shard_map/ppermute | solution.py:131
  113.7 0.7 bitcast_dynamic-update-slice_fusion.7
  114.4 0.7 bitcast_dynamic-update-slice_fusion.5
  115.1 0.7 bitcast_dynamic-update-slice_fusion.3
  116.6 2.3 %constant_dynamic-slice_fusion = bf16[4,8,16,1024]{3,2,1,0:T(8,128)(2,1)} fusion(bf16[8,8,16,1024]{3,2,1,0:T(8,128)(2,1)} %bitcast_dynamic-update-slice_fusion.1, s32[]{:T(128)S(6)} %select_n.71), kind=kLoop, calls=%fused_computation.21 | loop fusion | bytes 2097156 | tf_op jit(solution)/shard_map/jit(_roll_dynamic)/dynamic_slice | solution.py:133
  119.2 59.0 %all_to_all.5 = bf16[8,8,16,1024]{3,2,1,0:T(8,128)(2,1)S(1)} all-to-all(bf16[8,8,16,1024]{3,2,1,0:T(8,128)(2,1)S(1)} %broadcast_in_dim.4), channel_id=1, replica_groups=mesh['zlo'=4,'core'=2,'drow'=4,'zhi'=2,'y'=4] {'zhi','y'}, dimensions={0} | all-to-all | bytes 4194304 | tf_op jit(solution)/shard_map/all_to_all | solution.py:138
  178.2 1.5 copy.14
  179.8 0.8 collective-permute-start.7
  180.6 7.1 %collective-permute-done.7.theirs_ref = bf16[4,4,8,16,1024]{4,3,2,1,0:T(8,128)(2,1)} collective-permute-done((bf16[4,4,8,16,1024]{4,3,2,1,0:T(8,128)(2,1)}, bf16[4,4,8,16,1024]{4,3,2,1,0:T(8,128)(2,1)}, u32[]{:S(2)}, u32[]{:S(2)}) %collective-permute-start.7) | collective-permute-done | bytes 4194336 | tf_op jit(solution)/shard_map/ppermute | solution.py:82
  187.7 10.4 %shard_map.47 = f32[2,8,128,512]{3,2,1,0:T(8,128)} custom-call(s32[1]{0:T(128)} %bitcast.core_ref, bf16[8,128,1024]{2,1,0:T(8,128)(2,1)} %bitcast.60, bf16[4,4,8,16,1024]{4,3,2,1,0:T(8,128)(2,1)} %bitcast.62, bf16[4,4,8,16,1024]{4,3,2,1,0:T(8,128)(2,1)} %collective-permute-done.7.theirs_ref), custom_call_target="tpu_custom_call" | custom-call | tf_op jit(solution)/shard_map/pallas_call | solution.py:112
  (8 shorter events, 1.7 us)
Async XLA Ops:
  6.5 173.2 %all-gather.3.cloned.1.call-start = ((), (), s32[]{:S(2)}) async-start(), calls=%async_computation.1 | async-start | bytes 5242880 | tf_op jit(solution)/shard_map/all_gather | solution.py:80
  29.2 4.7 %collective-permute-start = (f32[8,4,16,1024]{3,2,1,0:T(8,128)S(1)}, f32[8,4,16,1024]{3,2,1,0:T(8,128)}, u32[]{:S(2)}, u32[]{:S(2)}) collective-permute-start(f32[8,4,16,1024]{3,2,1,0:T(8,128)S(1)} %select_bitcast_fusion), channel_id=1, source_target_pairs={{0,32},{32,0},{1,33},{33,1},{2,34},{34,2},{3,35},{35,3},{4,36},{36... | collective-permute-start | bytes 6291464 | tf_op jit(solution)/shard_map/ppermute | solution.py:155
  38.3 13.7 %collective-permute-start.1 = (f32[8,16,1024]{2,1,0:T(8,128)}, f32[8,16,1024]{2,1,0:T(8,128)}, u32[]{:S(2)}, u32[]{:S(2)}) collective-permute-start(f32[8,16,1024]{2,1,0:T(8,128)} %get-tuple-element.15), channel_id=1, source_target_pairs={{0,64},{64,128},{128,192},{192,0},{1,65},{65,129},{129,193},{193,1... | collective-permute-start | bytes 1572872 | tf_op jit(solution)/shard_map/ppermute | solution.py:160
  40.0 24.8 %collective-permute-start.3 = (f32[8,16,1024]{2,1,0:T(8,128)S(1)}, f32[8,16,1024]{2,1,0:T(8,128)}, u32[]{:S(2)}, u32[]{:S(2)}) collective-permute-start(f32[8,16,1024]{2,1,0:T(8,128)S(1)} %get-tuple-element.16), channel_id=1, source_target_pairs={{0,192},{64,0},{128,64},{192,128},{1,193},{65,1},{129,65},{193,129... | collective-permute-start | bytes 1572872 | tf_op jit(solution)/shard_map/ppermute | solution.py:160
  40.0 44.9 %collective-permute-start.2 = (f32[8,16,1024]{2,1,0:T(8,128)S(1)}, f32[8,16,1024]{2,1,0:T(8,128)}, u32[]{:S(2)}, u32[]{:S(2)}) collective-permute-start(f32[8,16,1024]{2,1,0:T(8,128)S(1)} %get-tuple-element.17), channel_id=1, source_target_pairs={{0,128},{64,192},{128,0},{192,64},{1,129},{65,193},{129,1},{193,65... | collective-permute-start | bytes 1572872 | tf_op jit(solution)/shard_map/ppermute | solution.py:160
  87.0 9.2 %collective-permute-start.4 = (bf16[8,16,1024]{2,1,0:T(8,128)(2,1)S(1)}, bf16[8,16,1024]{2,1,0:T(8,128)(2,1)S(1)}, u32[]{:S(2)}, u32[]{:S(2)}) collective-permute-start(bf16[8,16,1024]{2,1,0:T(8,128)(2,1)S(1)} %get-tuple-element.10), channel_id=1, source_target_pairs={{0,192},{64,0},{128,64},{192,128},{1,193},{65,1},{129,65},{193,129... | collective-permute-start | bytes 786440 | tf_op jit(solution)/shard_map/ppermute | solution.py:131
  90.6 16.7 %collective-permute-start.5 = (bf16[8,16,1024]{2,1,0:T(8,128)(2,1)S(1)}, bf16[8,16,1024]{2,1,0:T(8,128)(2,1)S(1)}, u32[]{:S(2)}, u32[]{:S(2)}) collective-permute-start(bf16[8,16,1024]{2,1,0:T(8,128)(2,1)S(1)} %get-tuple-element.10), channel_id=1, source_target_pairs={{0,128},{64,192},{128,0},{192,64},{1,129},{65,193},{129,1},{193,65... | collective-permute-start | bytes 786440 | tf_op jit(solution)/shard_map/ppermute | solution.py:131
  90.6 22.3 %collective-permute-start.6 = (bf16[8,16,1024]{2,1,0:T(8,128)(2,1)S(1)}, bf16[8,16,1024]{2,1,0:T(8,128)(2,1)S(1)}, u32[]{:S(2)}, u32[]{:S(2)}) collective-permute-start(bf16[8,16,1024]{2,1,0:T(8,128)(2,1)S(1)} %get-tuple-element.10), channel_id=1, source_target_pairs={{0,64},{64,128},{128,192},{192,0},{1,65},{65,129},{129,193},{193,1... | collective-permute-start | bytes 786440 | tf_op jit(solution)/shard_map/ppermute | solution.py:131
  179.8 7.9 %collective-permute-start.7 = (bf16[4,4,8,16,1024]{4,3,2,1,0:T(8,128)(2,1)}, bf16[4,4,8,16,1024]{4,3,2,1,0:T(8,128)(2,1)}, u32[]{:S(2)}, u32[]{:S(2)}) collective-permute-start(bf16[4,4,8,16,1024]{4,3,2,1,0:T(8,128)(2,1)} %bitcast.61), channel_id=1, source_target_pairs={{0,32},{32,0},{1,33},{33,1},{2,34},{34,2},{3,35},{35,3},{4,36},{36... | collective-permute-start | bytes 12582920 | tf_op jit(solution)/shard_map/ppermute | solution.py:82
Sparse Core Ops, SparseCore 0:
  119.0 53.0 all-gather.2

commit v16 on v14

--- a/solution.py
+++ b/solution.py
@@ -141,7 +141,7 @@
 def gather_rows(amplitudes):
     count = lax.axis_size("zhi") * lax.axis_size("y")
     freqs, piece, width = amplitudes.shape
-    pieces = gather_by_all_to_all(amplitudes, ("zhi", "y"), count)
+    pieces = gather_by_permutes(amplitudes, ("zhi", "y"), count)
     return pieces.transpose(1, 0, 2, 3).reshape(freqs, -1, width)
 
 

time: 198 us -> 204 us (1.030)
  the two profiles are of different devices: /device:TPU:33 before, /device:TPU:207 now
where the time goes in v16:
time: 204 us; the launch traced here: 203 us
  waiting for transfers between devices  96 us (47%)
  starting transfers between devices  58.9 us (29%)
  Pallas kernels  25.9 us (13%)
  between operations  13.6 us (7%)
  local copies, waits for them, and re-layouts  4.9 us (2%)
  other arithmetic  4.07 us (2%)
    ppermute x10, starting transfers between devices, gather_by_permutes(): lax.ppermute(piece, axis_name, perm=[(i, (i - shift) % count) for i in ra...  57.8 us
    reduce_scatter x1, waiting for transfers between devices, local(): lax.psum_scatter(partial_amp, ('zlo', 'core'), scatter_dimension=1, tiled...  53.3 us
    ppermute x10, waiting for transfers between devices, gather_by_permutes(): lax.ppermute(piece, axis_name, perm=[(i, (i - shift) % count) for i in ra...  35.5 us
    pallas_call x1, Pallas kernels, partial_amplitudes(): pl.pallas_call(amp_kernel, out_shape=jax.ShapeDtypeStruct((FREQS, rows, 2...  15.5 us
    pallas_call x1, Pallas kernels, cross_spectra(): pl.pallas_call(spec_kernel, out_shape=jax.ShapeDtypeStruct((2, freqs, row...  10.4 us
    ppermute x1, waiting for transfers between devices, gather_cols(): theirs = lax.ppermute(mine, 'core', perm=[(0, 1), (1, 0)])  7.13 us
  transfers between devices with their start and end apart: 13, of which 7 were waited for; matrix products, arithmetic and copies ran while one was open for 1% of the time, Pallas kernels for 0%

profile of v16, /device:TPU:207, one launch (start us, length us, event | category | flops | bytes accessed | tf_op | source)
XLA Modules:
  0.0 203.4 jit_solution(4885018738742251885)
XLA Ops:
  6.5 0.8 fusion
  7.3 0.8 fusion.1
  8.1 1.3 multiply_sqrt_fusion.spread_ref
  9.4 1.7 multiply_add_fusion.proj_ref
  11.1 15.5 %shard_map.46 = f32[8,128,1024]{2,1,0:T(8,128)} custom-call(s32[1024,512]{1,0:T(8,128)} %multiply_add_fusion.proj_ref, f32[8,512]{1,0:T(8,128)} %multiply_sqrt_fusion.spread_ref, bf16[2,8,128,1024]{3,2,1,0:T(8,128)(2,1)} %resp_ref.1), custom_call_target="tpu_custom_call" | custom-call | tf_op jit(solution)/shard_map/pallas_call | solution.py:61
  26.5 0.0 reduce-scatter.2.cloned.1.call-update
  26.5 0.0 all-gather.3.cloned.1.call-start
  26.6 53.3 %reduce-scatter.2.cloned.1.call-done = f32[8,16,1024]{2,1,0:T(8,128)} async-done(((f32[8,128,1024]{2,1,0:T(8,128)}), f32[8,16,1024]{2,1,0:T(8,128)}) %reduce-scatter.2.cloned.1.call-update) | async-done | bytes 524304 | tf_op jit(solution)/shard_map/reduce_scatter | solution.py:155
  79.9 1.1 bitcast_dynamic-update-slice_fusion.22
  81.0 1.5 collective-permute-start
  82.5 3.4 %collective-permute-start.1 = (bf16[8,16,1024]{2,1,0:T(8,128)(2,1)S(1)}, bf16[8,16,1024]{2,1,0:T(8,128)(2,1)S(1)}, u32[]{:S(2)}, u32[]{:S(2)}) collective-permute-start(bf16[8,16,1024]{2,1,0:T(8,128)(2,1)S(1)} %get-tuple-element.10), channel_id=1, source_target_pairs={{0,128},{64,192},{128,0},{192,64},{1,129},{65,193},{129,1},{193,65... | collective-permute-start | bytes 786440 | tf_op jit(solution)/shard_map/ppermute | solution.py:131
  85.9 0.0 collective-permute-start.2
  85.9 4.7 %collective-permute-done = bf16[8,16,1024]{2,1,0:T(8,128)(2,1)S(1)} collective-permute-done((bf16[8,16,1024]{2,1,0:T(8,128)(2,1)S(1)}, bf16[8,16,1024]{2,1,0:T(8,128)(2,1)S(1)}, u32[]{:S(2)}, u32[]{:S(2)}) %collective-permute-start) | collective-permute-done | bytes 262176 | tf_op jit(solution)/shard_map/ppermute | solution.py:131
  90.7 13.5 %collective-permute-done.1 = bf16[8,16,1024]{2,1,0:T(8,128)(2,1)S(1)} collective-permute-done((bf16[8,16,1024]{2,1,0:T(8,128)(2,1)S(1)}, bf16[8,16,1024]{2,1,0:T(8,128)(2,1)S(1)}, u32[]{:S(2)}, u32[]{:S(2)}) %collective-permute-start.1) | collective-permute-done | bytes 262176 | tf_op jit(solution)/shard_map/ppermute | solution.py:131
  104.2 3.6 %collective-permute-done.2 = bf16[8,16,1024]{2,1,0:T(8,128)(2,1)S(1)} collective-permute-done((bf16[8,16,1024]{2,1,0:T(8,128)(2,1)S(1)}, bf16[8,16,1024]{2,1,0:T(8,128)(2,1)S(1)}, u32[]{:S(2)}, u32[]{:S(2)}) %collective-permute-start.2) | collective-permute-done | bytes 262176 | tf_op jit(solution)/shard_map/ppermute | solution.py:131
  108.0 1.1 constant_dynamic-slice_fusion
  109.0 0.0 all-gather.3.cloned.1.call-update
  109.0 0.3 collective-permute-start.3
  109.4 3.7 %collective-permute-start.4 = (bf16[8,16,1024]{2,1,0:T(8,128)(2,1)S(1)}, bf16[8,16,1024]{2,1,0:T(8,128)(2,1)S(1)}, u32[]{:S(2)}, u32[]{:S(2)}) collective-permute-start(bf16[8,16,1024]{2,1,0:T(8,128)(2,1)S(1)} %get-tuple-element.10), channel_id=1, source_target_pairs={{0,6},{1,7},{2,0},{3,1},{4,2},{5,3},{6,4},{7,5},{8,14},{9,15},{10,... | collective-permute-start | bytes 786440 | tf_op jit(solution)/shard_map/ppermute | solution.py:131
  113.1 4.8 %collective-permute-start.5 = (bf16[8,16,1024]{2,1,0:T(8,128)(2,1)S(1)}, bf16[8,16,1024]{2,1,0:T(8,128)(2,1)S(1)}, u32[]{:S(2)}, u32[]{:S(2)}) collective-permute-start(bf16[8,16,1024]{2,1,0:T(8,128)(2,1)S(1)} %get-tuple-element.10), channel_id=1, source_target_pairs={{0,5},{1,6},{2,7},{3,0},{4,1},{5,2},{6,3},{7,4},{8,13},{9,14},{10,... | collective-permute-start | bytes 786440 | tf_op jit(solution)/shard_map/ppermute | solution.py:131
  117.9 1.9 collective-permute-start.6
  119.8 3.2 %collective-permute-start.7 = (bf16[8,16,1024]{2,1,0:T(8,128)(2,1)S(1)}, bf16[8,16,1024]{2,1,0:T(8,128)(2,1)S(1)}, u32[]{:S(2)}, u32[]{:S(2)}) collective-permute-start(bf16[8,16,1024]{2,1,0:T(8,128)(2,1)S(1)} %get-tuple-element.10), channel_id=1, source_target_pairs={{0,3},{1,4},{2,5},{3,6},{4,7},{5,0},{6,1},{7,2},{8,11},{9,12},{10,... | collective-permute-start | bytes 786440 | tf_op jit(solution)/shard_map/ppermute | solution.py:131
  123.0 0.0 collective-permute-done.3
  123.0 29.3 %collective-permute-start.8 = (bf16[8,16,1024]{2,1,0:T(8,128)(2,1)S(1)}, bf16[8,16,1024]{2,1,0:T(8,128)(2,1)S(1)}, u32[]{:S(2)}, u32[]{:S(2)}) collective-permute-start(bf16[8,16,1024]{2,1,0:T(8,128)(2,1)S(1)} %get-tuple-element.10), channel_id=1, source_target_pairs={{0,2},{1,3},{2,4},{3,5},{4,6},{5,7},{6,0},{7,1},{8,10},{9,11},{10,... | collective-permute-start | bytes 786440 | tf_op jit(solution)/shard_map/ppermute | solution.py:131
  152.3 9.6 %collective-permute-start.9 = (bf16[8,16,1024]{2,1,0:T(8,128)(2,1)S(1)}, bf16[8,16,1024]{2,1,0:T(8,128)(2,1)S(1)}, u32[]{:S(2)}, u32[]{:S(2)}) collective-permute-start(bf16[8,16,1024]{2,1,0:T(8,128)(2,1)S(1)} %get-tuple-element.10), channel_id=1, source_target_pairs={{0,1},{1,2},{2,3},{3,4},{4,5},{5,6},{6,7},{7,0},{8,9},{9,10},{10,1... | collective-permute-start | bytes 786440 | tf_op jit(solution)/shard_map/ppermute | solution.py:131
  162.0 4.4 %collective-permute-done.5 = bf16[8,16,1024]{2,1,0:T(8,128)(2,1)S(1)} collective-permute-done((bf16[8,16,1024]{2,1,0:T(8,128)(2,1)S(1)}, bf16[8,16,1024]{2,1,0:T(8,128)(2,1)S(1)}, u32[]{:S(2)}, u32[]{:S(2)}) %collective-permute-start.5) | collective-permute-done | bytes 262176 | tf_op jit(solution)/shard_map/ppermute | solution.py:131
  166.5 9.3 %collective-permute-done.9 = bf16[8,16,1024]{2,1,0:T(8,128)(2,1)S(1)} collective-permute-done((bf16[8,16,1024]{2,1,0:T(8,128)(2,1)S(1)}, bf16[8,16,1024]{2,1,0:T(8,128)(2,1)S(1)}, u32[]{:S(2)}, u32[]{:S(2)}) %collective-permute-start.9) | collective-permute-done | bytes 262176 | tf_op jit(solution)/shard_map/ppermute | solution.py:131
  176.0 0.3 dynamic-slice_bitcast_fusion
  176.4 1.6 copy.7
  177.9 1.1 collective-permute-start.10
  179.0 7.1 %collective-permute-done.10.theirs_ref = bf16[4,4,8,16,1024]{4,3,2,1,0:T(8,128)(2,1)} collective-permute-done((bf16[4,4,8,16,1024]{4,3,2,1,0:T(8,128)(2,1)}, bf16[4,4,8,16,1024]{4,3,2,1,0:T(8,128)(2,1)}, u32[]{:S(2)}, u32[]{:S(2)}) %collective-permute-start.10) | collective-permute-done | bytes 4194336 | tf_op jit(solution)/shard_map/ppermute | solution.py:82
  186.2 10.4 %shard_map.47 = f32[2,8,128,512]{3,2,1,0:T(8,128)} custom-call(s32[1]{0:T(128)} %bitcast.core_ref, bf16[8,128,1024]{2,1,0:T(8,128)(2,1)} %bitcast.48, bf16[4,4,8,16,1024]{4,3,2,1,0:T(8,128)(2,1)} %bitcast.50, bf16[4,4,8,16,1024]{4,3,2,1,0:T(8,128)(2,1)} %collective-permute-done.10.theirs_ref), custom_call_target="tpu_custom_call" | custom-call | tf_op jit(solution)/shard_map/pallas_call | solution.py:112
  (29 shorter events, 0.4 us)
Async XLA Ops:
  6.5 73.4 %reduce-scatter.2.cloned.1.call-start = ((), (), s32[]{:S(2)}) async-start(), calls=%async_computation.1 | async-start | bytes 4718592 | tf_op jit(solution)/shard_map/reduce_scatter | solution.py:155
  26.5 151.4 %all-gather.3.cloned.1.call-start = ((), (), s32[]{:S(2)}) async-start(), calls=%async_computation.2 | async-start | bytes 5242880 | tf_op jit(solution)/shard_map/all_gather | solution.py:80
  81.0 9.6 %collective-permute-start = (bf16[8,16,1024]{2,1,0:T(8,128)(2,1)S(1)}, bf16[8,16,1024]{2,1,0:T(8,128)(2,1)S(1)}, u32[]{:S(2)}, u32[]{:S(2)}) collective-permute-start(bf16[8,16,1024]{2,1,0:T(8,128)(2,1)S(1)} %get-tuple-element.10), channel_id=1, source_target_pairs={{0,192},{64,0},{128,64},{192,128},{1,193},{65,1},{129,65},{193,129... | collective-permute-start | bytes 786440 | tf_op jit(solution)/shard_map/ppermute | solution.py:131
  82.5 21.6 %collective-permute-start.1 = (bf16[8,16,1024]{2,1,0:T(8,128)(2,1)S(1)}, bf16[8,16,1024]{2,1,0:T(8,128)(2,1)S(1)}, u32[]{:S(2)}, u32[]{:S(2)}) collective-permute-start(bf16[8,16,1024]{2,1,0:T(8,128)(2,1)S(1)} %get-tuple-element.10), channel_id=1, source_target_pairs={{0,128},{64,192},{128,0},{192,64},{1,129},{65,193},{129,1},{193,65... | collective-permute-start | bytes 786440 | tf_op jit(solution)/shard_map/ppermute | solution.py:131
  85.9 21.9 %collective-permute-start.2 = (bf16[8,16,1024]{2,1,0:T(8,128)(2,1)S(1)}, bf16[8,16,1024]{2,1,0:T(8,128)(2,1)S(1)}, u32[]{:S(2)}, u32[]{:S(2)}) collective-permute-start(bf16[8,16,1024]{2,1,0:T(8,128)(2,1)S(1)} %get-tuple-element.10), channel_id=1, source_target_pairs={{0,64},{64,128},{128,192},{192,0},{1,65},{65,129},{129,193},{193,1... | collective-permute-start | bytes 786440 | tf_op jit(solution)/shard_map/ppermute | solution.py:131
  109.0 13.9 %collective-permute-start.3 = (bf16[8,16,1024]{2,1,0:T(8,128)(2,1)S(1)}, bf16[8,16,1024]{2,1,0:T(8,128)(2,1)S(1)}, u32[]{:S(2)}, u32[]{:S(2)}) collective-permute-start(bf16[8,16,1024]{2,1,0:T(8,128)(2,1)S(1)} %get-tuple-element.10), channel_id=1, source_target_pairs={{0,7},{1,0},{2,1},{3,2},{4,3},{5,4},{6,5},{7,6},{8,15},{9,8},{10,9... | collective-permute-start | bytes 786440 | tf_op jit(solution)/shard_map/ppermute | solution.py:131
  109.4 42.9 %collective-permute-start.4 = (bf16[8,16,1024]{2,1,0:T(8,128)(2,1)S(1)}, bf16[8,16,1024]{2,1,0:T(8,128)(2,1)S(1)}, u32[]{:S(2)}, u32[]{:S(2)}) collective-permute-start(bf16[8,16,1024]{2,1,0:T(8,128)(2,1)S(1)} %get-tuple-element.10), channel_id=1, source_target_pairs={{0,6},{1,7},{2,0},{3,1},{4,2},{5,3},{6,4},{7,5},{8,14},{9,15},{10,... | collective-permute-start | bytes 786440 | tf_op jit(solution)/shard_map/ppermute | solution.py:131
  113.1 53.2 %collective-permute-start.5 = (bf16[8,16,1024]{2,1,0:T(8,128)(2,1)S(1)}, bf16[8,16,1024]{2,1,0:T(8,128)(2,1)S(1)}, u32[]{:S(2)}, u32[]{:S(2)}) collective-permute-start(bf16[8,16,1024]{2,1,0:T(8,128)(2,1)S(1)} %get-tuple-element.10), channel_id=1, source_target_pairs={{0,5},{1,6},{2,7},{3,0},{4,1},{5,2},{6,3},{7,4},{8,13},{9,14},{10,... | collective-permute-start | bytes 786440 | tf_op jit(solution)/shard_map/ppermute | solution.py:131
  117.9 48.5 %collective-permute-start.6 = (bf16[8,16,1024]{2,1,0:T(8,128)(2,1)S(1)}, bf16[8,16,1024]{2,1,0:T(8,128)(2,1)S(1)}, u32[]{:S(2)}, u32[]{:S(2)}) collective-permute-start(bf16[8,16,1024]{2,1,0:T(8,128)(2,1)S(1)} %get-tuple-element.10), channel_id=1, source_target_pairs={{0,4},{1,5},{2,6},{3,7},{4,0},{5,1},{6,2},{7,3},{8,12},{9,13},{10,... | collective-permute-start | bytes 786440 | tf_op jit(solution)/shard_map/ppermute | solution.py:131
  119.8 46.6 %collective-permute-start.7 = (bf16[8,16,1024]{2,1,0:T(8,128)(2,1)S(1)}, bf16[8,16,1024]{2,1,0:T(8,128)(2,1)S(1)}, u32[]{:S(2)}, u32[]{:S(2)}) collective-permute-start(bf16[8,16,1024]{2,1,0:T(8,128)(2,1)S(1)} %get-tuple-element.10), channel_id=1, source_target_pairs={{0,3},{1,4},{2,5},{3,6},{4,7},{5,0},{6,1},{7,2},{8,11},{9,12},{10,... | collective-permute-start | bytes 786440 | tf_op jit(solution)/shard_map/ppermute | solution.py:131
  123.0 43.5 %collective-permute-start.8 = (bf16[8,16,1024]{2,1,0:T(8,128)(2,1)S(1)}, bf16[8,16,1024]{2,1,0:T(8,128)(2,1)S(1)}, u32[]{:S(2)}, u32[]{:S(2)}) collective-permute-start(bf16[8,16,1024]{2,1,0:T(8,128)(2,1)S(1)} %get-tuple-element.10), channel_id=1, source_target_pairs={{0,2},{1,3},{2,4},{3,5},{4,6},{5,7},{6,0},{7,1},{8,10},{9,11},{10,... | collective-permute-start | bytes 786440 | tf_op jit(solution)/shard_map/ppermute | solution.py:131
  152.3 23.5 %collective-permute-start.9 = (bf16[8,16,1024]{2,1,0:T(8,128)(2,1)S(1)}, bf16[8,16,1024]{2,1,0:T(8,128)(2,1)S(1)}, u32[]{:S(2)}, u32[]{:S(2)}) collective-permute-start(bf16[8,16,1024]{2,1,0:T(8,128)(2,1)S(1)} %get-tuple-element.10), channel_id=1, source_target_pairs={{0,1},{1,2},{2,3},{3,4},{4,5},{5,6},{6,7},{7,0},{8,9},{9,10},{10,1... | collective-permute-start | bytes 786440 | tf_op jit(solution)/shard_map/ppermute | solution.py:131
  177.9 8.2 %collective-permute-start.10 = (bf16[4,4,8,16,1024]{4,3,2,1,0:T(8,128)(2,1)}, bf16[4,4,8,16,1024]{4,3,2,1,0:T(8,128)(2,1)}, u32[]{:S(2)}, u32[]{:S(2)}) collective-permute-start(bf16[4,4,8,16,1024]{4,3,2,1,0:T(8,128)(2,1)} %bitcast.49), channel_id=1, source_target_pairs={{0,32},{32,0},{1,33},{33,1},{2,34},{34,2},{3,35},{35,3},{4,36},{36... | collective-permute-start | bytes 12582920 | tf_op jit(solution)/shard_map/ppermute | solution.py:82
Sparse Core Ops, SparseCore 0:
  26.7 53.1 reduce-scatter.1
  109.2 49.2 all-gather.2

commit v17 on v16

--- a/solution.py
+++ b/solution.py
@@ -75,10 +75,12 @@
 def gather_cols(amplitudes):
     freqs, piece, width = amplitudes.shape
     along_z = gather_by_permutes(amplitudes, "zlo", lax.axis_size("zlo"))
-    along_z, amplitudes = lax.optimization_barrier((along_z, amplitudes))
-    rows = gather_rows(amplitudes)
+    same_half = gather_by_permutes(amplitudes, "y", lax.axis_size("y"))
+    along_z, same_half, amplitudes = lax.optimization_barrier((along_z, same_half, amplitudes))
+    other_half = from_other_half(amplitudes)
     mine = lax.all_gather(along_z, "drow", axis=0)
-    mine, rows = lax.optimization_barrier((mine, rows))
+    mine, other_half = lax.optimization_barrier((mine, other_half))
+    rows = join_rows(same_half, other_half)
     theirs = lax.ppermute(mine, "core", perm=[(0, 1), (1, 0)])
     return mine, theirs, rows
 
@@ -138,11 +140,22 @@
     return lax.all_to_all(copies, axis_name, split_axis=0, concat_axis=0)
 
 
-def gather_rows(amplitudes):
-    count = lax.axis_size("zhi") * lax.axis_size("y")
-    freqs, piece, width = amplitudes.shape
-    pieces = gather_by_permutes(amplitudes, ("zhi", "y"), count)
-    return pieces.transpose(1, 0, 2, 3).reshape(freqs, -1, width)
+def from_other_half(piece):
+    ys = lax.axis_size("y")
+    flat = [(z, y) for z in range(lax.axis_size("zhi")) for y in range(ys)]
+    ahead = []
+    for shift in range(ys):
+        perm = [(z * ys + y, (1 - z) * ys + (y - shift) % ys) for z, y in flat]
+        ahead.append(lax.ppermute(piece, ("zhi", "y"), perm=perm))
+    return jnp.roll(jnp.stack(ahead), lax.axis_index("y"), axis=0)
+
+
+def join_rows(same_half, other_half):
+    first = lax.axis_index("zhi") == 0
+    halves = jnp.where(first, jnp.stack([same_half, other_half]), jnp.stack([other_half, same_half]))
+    freqs, piece, width = halves.shape[2:]
+    halves = halves.reshape(-1, freqs, piece, width)
+    return halves.transpose(1, 0, 2, 3).reshape(freqs, -1, width)
 
 
 def local(freq_resp, node_coords, heading_steps, spectral_weights):

time: 204 us -> 196 us (0.961)
  the two profiles are of different devices: /device:TPU:207 before, /device:TPU:33 now
where the time goes in v17:
time: 196 us; the launch traced here: 195 us
  waiting for transfers between devices  123 us (63%)
  Pallas kernels  25.9 us (13%)
  starting transfers between devices  20.3 us (10%)
  between operations  13.4 us (7%)
  other arithmetic  9.98 us (5%)
  local copies, waits for them, and re-layouts  3.11 us (2%)
    reduce_scatter x1, waiting for transfers between devices, local(): lax.psum_scatter(partial_amp, ('zlo', 'core'), scatter_dimension=1, tiled...  56.3 us
    ppermute x4, waiting for transfers between devices, from_other_half(): ahead.append(lax.ppermute(piece, ('zhi', 'y'), perm=perm))  38.4 us
    ppermute x6, waiting for transfers between devices, gather_by_permutes(): lax.ppermute(piece, axis_name, perm=[(i, (i - shift) % count) for i in ra...  22.6 us
    pallas_call x1, Pallas kernels, partial_amplitudes(): pl.pallas_call(amp_kernel, out_shape=jax.ShapeDtypeStruct((FREQS, rows, 2...  15.5 us
    ppermute x4, starting transfers between devices, from_other_half(): ahead.append(lax.ppermute(piece, ('zhi', 'y'), perm=perm))  12.3 us
    pallas_call x1, Pallas kernels, cross_spectra(): pl.pallas_call(spec_kernel, out_shape=jax.ShapeDtypeStruct((2, freqs, row...  10.4 us
    ppermute x6, starting transfers between devices, gather_by_permutes(): lax.ppermute(piece, axis_name, perm=[(i, (i - shift) % count) for i in ra...  6.45 us
    ppermute x1, waiting for transfers between devices, gather_cols(): theirs = lax.ppermute(mine, 'core', perm=[(0, 1), (1, 0)])  5.22 us
  transfers between devices with their start and end apart: 13, of which 10 were waited for; matrix products, arithmetic and copies ran while one was open for 2% of the time, Pallas kernels for 0%

profile of v17, /device:TPU:33, one launch (start us, length us, event | category | flops | bytes accessed | tf_op | source)
XLA Modules:
  0.0 195.2 jit_solution(18334023508417532754)
XLA Ops:
  6.5 0.8 fusion.22
  7.3 0.8 fusion.21
  8.1 1.3 multiply_sqrt_fusion.spread_ref
  9.4 1.7 multiply_add_fusion.proj_ref
  11.1 15.5 %shard_map.46 = f32[8,128,1024]{2,1,0:T(8,128)} custom-call(s32[1024,512]{1,0:T(8,128)} %multiply_add_fusion.proj_ref, f32[8,512]{1,0:T(8,128)} %multiply_sqrt_fusion.spread_ref, bf16[2,8,128,1024]{3,2,1,0:T(8,128)(2,1)} %resp_ref.1), custom_call_target="tpu_custom_call" | custom-call | tf_op jit(solution)/shard_map/pallas_call | solution.py:61
  26.6 56.3 %reduce-scatter.2.cloned.1.call-done = f32[8,16,1024]{2,1,0:T(8,128)} async-done(((f32[8,128,1024]{2,1,0:T(8,128)}), f32[8,16,1024]{2,1,0:T(8,128)}) %reduce-scatter.2.cloned.1.call-update) | async-done | bytes 524304 | tf_op jit(solution)/shard_map/reduce_scatter | solution.py:168
  82.9 1.1 convert_element_type.7
  84.0 1.3 collective-permute-start.5
  85.2 2.5 %collective-permute-start.4 = (bf16[8,16,1024]{2,1,0:T(8,128)(2,1)S(1)}, bf16[8,16,1024]{2,1,0:T(8,128)(2,1)S(1)}, u32[]{:S(2)}, u32[]{:S(2)}) collective-permute-start(bf16[8,16,1024]{2,1,0:T(8,128)(2,1)S(1)} %convert_element_type.7), channel_id=1, source_target_pairs={{0,2},{1,3},{2,0},{3,1},{4,6},{5,7},{6,4},{7,5},{8,10},{9,11},{10,... | collective-permute-start | bytes 786440 | tf_op jit(solution)/shard_map/ppermute | solution.py:133
  87.7 1.2 collective-permute-start.3
  88.9 1.2 collective-permute-start.2
  90.1 0.3 collective-permute-start.1
  90.4 1.5 collective-permute-done.5
  91.9 1.1 convert_bitcast_fusion
  92.9 6.0 %collective-permute-done.4 = bf16[8,16,1024]{2,1,0:T(8,128)(2,1)S(1)} collective-permute-done((bf16[8,16,1024]{2,1,0:T(8,128)(2,1)S(1)}, bf16[8,16,1024]{2,1,0:T(8,128)(2,1)S(1)}, u32[]{:S(2)}, u32[]{:S(2)}) %collective-permute-start.4) | collective-permute-done | bytes 262176 | tf_op jit(solution)/shard_map/ppermute | solution.py:133
  98.9 14.1 %collective-permute-done.1 = bf16[8,16,1024]{2,1,0:T(8,128)(2,1)S(1)} collective-permute-done((bf16[8,16,1024]{2,1,0:T(8,128)(2,1)S(1)}, bf16[8,16,1024]{2,1,0:T(8,128)(2,1)S(1)}, u32[]{:S(2)}, u32[]{:S(2)}) %collective-permute-start.1) | collective-permute-done | bytes 262176 | tf_op jit(solution)/shard_map/ppermute | solution.py:133
  113.0 1.0 collective-permute-done
  114.1 3.3 %fusion.10 = (bf16[4,8,16,1024]{3,2,1,0:T(8,128)(2,1)S(1)}, bf16[4,8,16,1024]{3,2,1,0:T(8,128)(2,1)}) fusion(s32[]{:T(128)S(6)} %select_n.32, bf16[1,8,16,1024]{3,2,1,0:T(8,128)(2,1)S(1)} %bitcast.35, bf16[1,8,16,1024]{3,2,1,0:T(8,128)(2,1)S(1)} %bitcast.34, bf16[1,8,16,1024]{3,2,1,0:T(8,128)(2,1)S(1)} %bitcast.33, ...), kind=kLoop, calls=%fused_computation.36 | loop fusion | flops 7340032 | bytes 3932168 | tf_op jit(solution)/shard_map/jit(_roll_dynamic)/concatenate | solution.py:135
  117.4 4.7 %collective-permute-start.9 = (bf16[8,16,1024]{2,1,0:T(8,128)(2,1)S(1)}, bf16[8,16,1024]{2,1,0:T(8,128)(2,1)S(1)}, u32[]{:S(2)}, u32[]{:S(2)}) collective-permute-start(bf16[8,16,1024]{2,1,0:T(8,128)(2,1)S(1)} %convert_element_type.7), channel_id=1, source_target_pairs={{0,5},{1,6},{2,7},{3,4},{4,1},{5,2},{6,3},{7,0},{8,13},{9,14},{10,... | collective-permute-start | bytes 786440 | tf_op jit(solution)/shard_map/ppermute | solution.py:149
  122.0 1.5 collective-permute-start.8
  123.5 5.3 %collective-permute-start.7 = (bf16[8,16,1024]{2,1,0:T(8,128)(2,1)S(1)}, bf16[8,16,1024]{2,1,0:T(8,128)(2,1)S(1)}, u32[]{:S(2)}, u32[]{:S(2)}) collective-permute-start(bf16[8,16,1024]{2,1,0:T(8,128)(2,1)S(1)} %convert_element_type.7), channel_id=1, source_target_pairs={{0,7},{1,4},{2,5},{3,6},{4,3},{5,0},{6,1},{7,2},{8,15},{9,12},{10,... | collective-permute-start | bytes 786440 | tf_op jit(solution)/shard_map/ppermute | solution.py:149
  128.8 0.9 collective-permute-start.6
  129.7 7.6 %collective-permute-done.9 = bf16[8,16,1024]{2,1,0:T(8,128)(2,1)S(1)} collective-permute-done((bf16[8,16,1024]{2,1,0:T(8,128)(2,1)S(1)}, bf16[8,16,1024]{2,1,0:T(8,128)(2,1)S(1)}, u32[]{:S(2)}, u32[]{:S(2)}) %collective-permute-start.9) | collective-permute-done | bytes 262176 | tf_op jit(solution)/shard_map/ppermute | solution.py:149
  137.3 20.7 %collective-permute-done.8 = bf16[8,16,1024]{2,1,0:T(8,128)(2,1)S(1)} collective-permute-done((bf16[8,16,1024]{2,1,0:T(8,128)(2,1)S(1)}, bf16[8,16,1024]{2,1,0:T(8,128)(2,1)S(1)}, u32[]{:S(2)}, u32[]{:S(2)}) %collective-permute-start.8) | collective-permute-done | bytes 262176 | tf_op jit(solution)/shard_map/ppermute | solution.py:149
  158.0 3.8 %collective-permute-done.7 = bf16[8,16,1024]{2,1,0:T(8,128)(2,1)S(1)} collective-permute-done((bf16[8,16,1024]{2,1,0:T(8,128)(2,1)S(1)}, bf16[8,16,1024]{2,1,0:T(8,128)(2,1)S(1)}, u32[]{:S(2)}, u32[]{:S(2)}) %collective-permute-start.7) | collective-permute-done | bytes 262176 | tf_op jit(solution)/shard_map/ppermute | solution.py:149
  161.7 6.4 %collective-permute-done.6 = bf16[8,16,1024]{2,1,0:T(8,128)(2,1)S(1)} collective-permute-done((bf16[8,16,1024]{2,1,0:T(8,128)(2,1)S(1)}, bf16[8,16,1024]{2,1,0:T(8,128)(2,1)S(1)}, u32[]{:S(2)}, u32[]{:S(2)}) %collective-permute-start.6) | collective-permute-done | bytes 262176 | tf_op jit(solution)/shard_map/ppermute | solution.py:149
  168.1 1.2 fusion.3
  169.4 1.4 collective-permute-start.10
  170.8 0.3 maximum_select_fusion
  171.2 1.6 copy.7
  172.7 5.2 %collective-permute-done.10.theirs_ref = bf16[4,4,8,16,1024]{4,3,2,1,0:T(8,128)(2,1)} collective-permute-done((bf16[4,4,8,16,1024]{4,3,2,1,0:T(8,128)(2,1)}, bf16[4,4,8,16,1024]{4,3,2,1,0:T(8,128)(2,1)}, u32[]{:S(2)}, u32[]{:S(2)}) %collective-permute-start.10) | collective-permute-done | bytes 4194336 | tf_op jit(solution)/shard_map/ppermute | solution.py:84
  178.0 10.4 %shard_map.47 = f32[2,8,128,512]{3,2,1,0:T(8,128)} custom-call(s32[1]{0:T(128)} %bitcast.core_ref, bf16[8,128,1024]{2,1,0:T(8,128)(2,1)} %bitcast.28, bf16[4,4,8,16,1024]{4,3,2,1,0:T(8,128)(2,1)} %bitcast.30, bf16[4,4,8,16,1024]{4,3,2,1,0:T(8,128)(2,1)} %collective-permute-done.10.theirs_ref), custom_call_target="tpu_custom_call" | custom-call | tf_op jit(solution)/shard_map/pallas_call | solution.py:114
  (8 shorter events, 0.1 us)
Async XLA Ops:
  6.5 76.3 %reduce-scatter.2.cloned.1.call-start = ((), (), s32[]{:S(2)}) async-start(), calls=%async_computation.1 | async-start | bytes 4718592 | tf_op jit(solution)/shard_map/reduce_scatter | solution.py:168
  26.6 142.8 %all-gather.3.cloned.1.call-start = ((), (), s32[]{:S(2)}) async-start(), calls=%async_computation.2 | async-start | bytes 5242880 | tf_op jit(solution)/shard_map/all_gather | solution.py:81
  84.0 7.9 %collective-permute-start.5 = (bf16[8,16,1024]{2,1,0:T(8,128)(2,1)S(1)}, bf16[8,16,1024]{2,1,0:T(8,128)(2,1)S(1)}, u32[]{:S(2)}, u32[]{:S(2)}) collective-permute-start(bf16[8,16,1024]{2,1,0:T(8,128)(2,1)S(1)} %convert_element_type.7), channel_id=1, source_target_pairs={{0,1},{1,2},{2,3},{3,0},{4,5},{5,6},{6,7},{7,4},{8,9},{9,10},{10,1... | collective-permute-start | bytes 786440 | tf_op jit(solution)/shard_map/ppermute | solution.py:133
  85.2 13.7 %collective-permute-start.4 = (bf16[8,16,1024]{2,1,0:T(8,128)(2,1)S(1)}, bf16[8,16,1024]{2,1,0:T(8,128)(2,1)S(1)}, u32[]{:S(2)}, u32[]{:S(2)}) collective-permute-start(bf16[8,16,1024]{2,1,0:T(8,128)(2,1)S(1)} %convert_element_type.7), channel_id=1, source_target_pairs={{0,2},{1,3},{2,0},{3,1},{4,6},{5,7},{6,4},{7,5},{8,10},{9,11},{10,... | collective-permute-start | bytes 786440 | tf_op jit(solution)/shard_map/ppermute | solution.py:133
  87.7 11.2 %collective-permute-start.3 = (bf16[8,16,1024]{2,1,0:T(8,128)(2,1)S(1)}, bf16[8,16,1024]{2,1,0:T(8,128)(2,1)S(1)}, u32[]{:S(2)}, u32[]{:S(2)}) collective-permute-start(bf16[8,16,1024]{2,1,0:T(8,128)(2,1)S(1)} %convert_element_type.7), channel_id=1, source_target_pairs={{0,3},{1,0},{2,1},{3,2},{4,7},{5,4},{6,5},{7,6},{8,11},{9,8},{10,9... | collective-permute-start | bytes 786440 | tf_op jit(solution)/shard_map/ppermute | solution.py:133
  88.9 10.1 %collective-permute-start.2 = (bf16[8,16,1024]{2,1,0:T(8,128)(2,1)S(1)}, bf16[8,16,1024]{2,1,0:T(8,128)(2,1)S(1)}, u32[]{:S(2)}, u32[]{:S(2)}) collective-permute-start(bf16[8,16,1024]{2,1,0:T(8,128)(2,1)S(1)} %convert_element_type.7), channel_id=1, source_target_pairs={{0,64},{64,128},{128,192},{192,0},{1,65},{65,129},{129,193},{193,1... | collective-permute-start | bytes 786440 | tf_op jit(solution)/shard_map/ppermute | solution.py:133
  90.1 23.0 %collective-permute-start.1 = (bf16[8,16,1024]{2,1,0:T(8,128)(2,1)S(1)}, bf16[8,16,1024]{2,1,0:T(8,128)(2,1)S(1)}, u32[]{:S(2)}, u32[]{:S(2)}) collective-permute-start(bf16[8,16,1024]{2,1,0:T(8,128)(2,1)S(1)} %convert_element_type.7), channel_id=1, source_target_pairs={{0,128},{64,192},{128,0},{192,64},{1,129},{65,193},{129,1},{193,65... | collective-permute-start | bytes 786440 | tf_op jit(solution)/shard_map/ppermute | solution.py:133
  91.9 22.2 %collective-permute-start = (bf16[8,16,1024]{2,1,0:T(8,128)(2,1)S(1)}, bf16[8,16,1024]{2,1,0:T(8,128)(2,1)S(1)}, u32[]{:S(2)}, u32[]{:S(2)}) collective-permute-start(bf16[8,16,1024]{2,1,0:T(8,128)(2,1)S(1)} %convert_element_type.7), channel_id=1, source_target_pairs={{0,192},{64,0},{128,64},{192,128},{1,193},{65,1},{129,65},{193,129... | collective-permute-start | bytes 786440 | tf_op jit(solution)/shard_map/ppermute | solution.py:133
  117.4 19.9 %collective-permute-start.9 = (bf16[8,16,1024]{2,1,0:T(8,128)(2,1)S(1)}, bf16[8,16,1024]{2,1,0:T(8,128)(2,1)S(1)}, u32[]{:S(2)}, u32[]{:S(2)}) collective-permute-start(bf16[8,16,1024]{2,1,0:T(8,128)(2,1)S(1)} %convert_element_type.7), channel_id=1, source_target_pairs={{0,5},{1,6},{2,7},{3,4},{4,1},{5,2},{6,3},{7,0},{8,13},{9,14},{10,... | collective-permute-start | bytes 786440 | tf_op jit(solution)/shard_map/ppermute | solution.py:149
  122.0 35.9 %collective-permute-start.8 = (bf16[8,16,1024]{2,1,0:T(8,128)(2,1)S(1)}, bf16[8,16,1024]{2,1,0:T(8,128)(2,1)S(1)}, u32[]{:S(2)}, u32[]{:S(2)}) collective-permute-start(bf16[8,16,1024]{2,1,0:T(8,128)(2,1)S(1)} %convert_element_type.7), channel_id=1, source_target_pairs={{0,6},{1,7},{2,4},{3,5},{4,2},{5,3},{6,0},{7,1},{8,14},{9,15},{10,... | collective-permute-start | bytes 786440 | tf_op jit(solution)/shard_map/ppermute | solution.py:149
  123.5 38.3 %collective-permute-start.7 = (bf16[8,16,1024]{2,1,0:T(8,128)(2,1)S(1)}, bf16[8,16,1024]{2,1,0:T(8,128)(2,1)S(1)}, u32[]{:S(2)}, u32[]{:S(2)}) collective-permute-start(bf16[8,16,1024]{2,1,0:T(8,128)(2,1)S(1)} %convert_element_type.7), channel_id=1, source_target_pairs={{0,7},{1,4},{2,5},{3,6},{4,3},{5,0},{6,1},{7,2},{8,15},{9,12},{10,... | collective-permute-start | bytes 786440 | tf_op jit(solution)/shard_map/ppermute | solution.py:149
  128.8 39.4 %collective-permute-start.6 = (bf16[8,16,1024]{2,1,0:T(8,128)(2,1)S(1)}, bf16[8,16,1024]{2,1,0:T(8,128)(2,1)S(1)}, u32[]{:S(2)}, u32[]{:S(2)}) collective-permute-start(bf16[8,16,1024]{2,1,0:T(8,128)(2,1)S(1)} %convert_element_type.7), channel_id=1, source_target_pairs={{0,4},{1,5},{2,6},{3,7},{4,0},{5,1},{6,2},{7,3},{8,12},{9,13},{10,... | collective-permute-start | bytes 786440 | tf_op jit(solution)/shard_map/ppermute | solution.py:149
  169.4 8.6 %collective-permute-start.10 = (bf16[4,4,8,16,1024]{4,3,2,1,0:T(8,128)(2,1)}, bf16[4,4,8,16,1024]{4,3,2,1,0:T(8,128)(2,1)}, u32[]{:S(2)}, u32[]{:S(2)}) collective-permute-start(bf16[4,4,8,16,1024]{4,3,2,1,0:T(8,128)(2,1)} %bitcast.29), channel_id=1, source_target_pairs={{0,32},{32,0},{1,33},{33,1},{2,34},{34,2},{3,35},{35,3},{4,36},{36... | collective-permute-start | bytes 12582920 | tf_op jit(solution)/shard_map/ppermute | solution.py:84
Sparse Core Ops, SparseCore 0:
  26.7 56.1 reduce-scatter.1
  117.5 49.2 all-gather.2

commit v18 on v17

--- a/solution.py
+++ b/solution.py
@@ -78,7 +78,14 @@
     same_half = gather_by_permutes(amplitudes, "y", lax.axis_size("y"))
     along_z, same_half, amplitudes = lax.optimization_barrier((along_z, same_half, amplitudes))
     other_half = from_other_half(amplitudes)
-    mine = lax.all_gather(along_z, "drow", axis=0)
+    half = along_z.shape[1] // 2
+    mine = jnp.concatenate(
+        [
+            lax.all_gather(along_z[:, :half], "drow", axis=0),
+            gather_by_permutes(along_z[:, half:], "drow", lax.axis_size("drow")),
+        ],
+        axis=2,
+    )
     mine, other_half = lax.optimization_barrier((mine, other_half))
     rows = join_rows(same_half, other_half)
     theirs = lax.ppermute(mine, "core", perm=[(0, 1), (1, 0)])

time: 196 us -> 209 us (1.066)
  other arithmetic: 9.98 us -> 17.7 us
  starting transfers between devices: 20.3 us -> 27.7 us
  waiting for transfers between devices: 123 us -> 117 us
  local copies, waits for them, and re-layouts: 3.11 us -> 5.31 us
    ppermute x6 -> x9, starting transfers between devices: 6.45 us -> 14.4 us  [gather_by_permutes(): lax.ppermute(piece, axis_name, perm=[(i, (i - shift) % count) for i in ra...]
    ppermute x4, waiting for transfers between devices: 38.4 us -> 32 us  [from_other_half(): ahead.append(lax.ppermute(piece, ('zhi', 'y'), perm=perm))]
    concatenate x0 -> x1, other arithmetic: none -> 3.89 us  [gather_cols(): jnp.concatenate([lax.all_gather(along_z[:, :half], 'drow', axis=0), gathe...]
    ppermute x6 -> x9, waiting for transfers between devices: 22.6 us -> 25.4 us  [gather_by_permutes(): lax.ppermute(piece, axis_name, perm=[(i, (i - shift) % count) for i in ra...]
  transfers between devices with their start and end apart: 13 -> 16, of which waited for: 10 -> 11; matrix products, arithmetic and copies ran while one was open for 2% -> 4% of each run, Pallas kernels for 0% -> 0%
where the time goes in v18:
time: 209 us; the launch traced here: 208 us
  waiting for transfers between devices  117 us (56%)
  starting transfers between devices  27.7 us (13%)
  Pallas kernels  25.9 us (12%)
  other arithmetic  17.7 us (8%)
  between operations  13.5 us (6%)
  local copies, waits for them, and re-layouts  5.31 us (3%)
    reduce_scatter x1, waiting for transfers between devices, local(): lax.psum_scatter(partial_amp, ('zlo', 'core'), scatter_dimension=1, tiled...  56.3 us
    ppermute x4, waiting for transfers between devices, from_other_half(): ahead.append(lax.ppermute(piece, ('zhi', 'y'), perm=perm))  32 us
    ppermute x9, waiting for transfers between devices, gather_by_permutes(): lax.ppermute(piece, axis_name, perm=[(i, (i - shift) % count) for i in ra...  25.4 us
    pallas_call x1, Pallas kernels, partial_amplitudes(): pl.pallas_call(amp_kernel, out_shape=jax.ShapeDtypeStruct((FREQS, rows, 2...  15.5 us
    ppermute x9, starting transfers between devices, gather_by_permutes(): lax.ppermute(piece, axis_name, perm=[(i, (i - shift) % count) for i in ra...  14.4 us
    ppermute x4, starting transfers between devices, from_other_half(): ahead.append(lax.ppermute(piece, ('zhi', 'y'), perm=perm))  12.6 us
    pallas_call x1, Pallas kernels, cross_spectra(): pl.pallas_call(spec_kernel, out_shape=jax.ShapeDtypeStruct((2, freqs, row...  10.4 us
  transfers between devices with their start and end apart: 16, of which 11 were waited for; matrix products, arithmetic and copies ran while one was open for 4% of the time, Pallas kernels for 0%

profile of v18, /device:TPU:33, one launch (start us, length us, event | category | flops | bytes accessed | tf_op | source)
XLA Modules:
  0.0 207.6 jit_solution(6703359487460409099)
XLA Ops:
  8.1 1.3 multiply_sqrt_fusion.spread_ref
  9.4 1.6 multiply_add_fusion.proj_ref
  11.1 15.5 %shard_map.46 = f32[8,128,1024]{2,1,0:T(8,128)} custom-call(s32[1024,512]{1,0:T(8,128)} %multiply_add_fusion.proj_ref, f32[8,512]{1,0:T(8,128)} %multiply_sqrt_fusion.spread_ref, bf16[2,8,128,1024]{3,2,1,0:T(8,128)(2,1)} %resp_ref.1), custom_call_target="tpu_custom_call" | custom-call | tf_op jit(solution)/shard_map/pallas_call | solution.py:61
  26.6 56.3 %reduce-scatter.2.cloned.1.call-done = f32[8,16,1024]{2,1,0:T(8,128)} async-done(((f32[8,128,1024]{2,1,0:T(8,128)}), f32[8,16,1024]{2,1,0:T(8,128)}) %reduce-scatter.2.cloned.1.call-update) | async-done | bytes 524304 | tf_op jit(solution)/shard_map/reduce_scatter | solution.py:175
  82.9 1.1 convert_element_type.7
  83.9 2.8 %collective-permute-start.4 = (bf16[8,16,1024]{2,1,0:T(8,128)(2,1)S(1)}, bf16[8,16,1024]{2,1,0:T(8,128)(2,1)S(1)}, u32[]{:S(2)}, u32[]{:S(2)}) collective-permute-start(bf16[8,16,1024]{2,1,0:T(8,128)(2,1)S(1)} %convert_element_type.7), channel_id=1, source_target_pairs={{0,2},{1,3},{2,0},{3,1},{4,6},{5,7},{6,4},{7,5},{8,10},{9,11},{10,... | collective-permute-start | bytes 786440 | tf_op jit(solution)/shard_map/ppermute | solution.py:140
  87.1 2.4 %collective-permute-start.1 = (bf16[8,16,1024]{2,1,0:T(8,128)(2,1)S(1)}, bf16[8,16,1024]{2,1,0:T(8,128)(2,1)S(1)}, u32[]{:S(2)}, u32[]{:S(2)}) collective-permute-start(bf16[8,16,1024]{2,1,0:T(8,128)(2,1)S(1)} %convert_element_type.7), channel_id=1, source_target_pairs={{0,128},{64,192},{128,0},{192,64},{1,129},{65,193},{129,1},{193,65... | collective-permute-start | bytes 786440 | tf_op jit(solution)/shard_map/ppermute | solution.py:140
  89.5 1.1 collective-permute-start.2
  90.6 3.0 %collective-permute-done.4 = bf16[8,16,1024]{2,1,0:T(8,128)(2,1)S(1)} collective-permute-done((bf16[8,16,1024]{2,1,0:T(8,128)(2,1)S(1)}, bf16[8,16,1024]{2,1,0:T(8,128)(2,1)S(1)}, u32[]{:S(2)}, u32[]{:S(2)}) %collective-permute-start.4) | collective-permute-done | bytes 262176 | tf_op jit(solution)/shard_map/ppermute | solution.py:140
  93.6 1.5 collective-permute-start.3
  96.2 1.8 collective-permute-done.5
  98.0 8.4 %collective-permute-done.1 = bf16[8,16,1024]{2,1,0:T(8,128)(2,1)S(1)} collective-permute-done((bf16[8,16,1024]{2,1,0:T(8,128)(2,1)S(1)}, bf16[8,16,1024]{2,1,0:T(8,128)(2,1)S(1)}, u32[]{:S(2)}, u32[]{:S(2)}) %collective-permute-start.1) | collective-permute-done | bytes 262176 | tf_op jit(solution)/shard_map/ppermute | solution.py:140
  106.4 5.6 %collective-permute-done.2 = bf16[8,16,1024]{2,1,0:T(8,128)(2,1)S(1)} collective-permute-done((bf16[8,16,1024]{2,1,0:T(8,128)(2,1)S(1)}, bf16[8,16,1024]{2,1,0:T(8,128)(2,1)S(1)}, u32[]{:S(2)}, u32[]{:S(2)}) %collective-permute-start.2) | collective-permute-done | bytes 262176 | tf_op jit(solution)/shard_map/ppermute | solution.py:140
  112.8 3.6 %fusion.10 = (bf16[4,8,16,1024]{3,2,1,0:T(8,128)(2,1)S(1)}, bf16[4,8,16,1024]{3,2,1,0:T(8,128)(2,1)S(1)}) fusion(s32[]{:T(128)S(6)} %select_n.44, bf16[1,8,16,1024]{3,2,1,0:T(8,128)(2,1)} %bitcast.49, bf16[1,8,16,1024]{3,2,1,0:T(8,128)(2,1)S(1)} %bitcast.44, bf16[1,8,16,1024]{3,2,1,0:T(8,128)(2,1)S(1)} %bitcast.45, ...), kind=kLoop, calls=%fused_computation.37 | loop fusion | flops 7340032 | bytes 3932168 | tf_op jit(solution)/shard_map/jit(_roll_dynamic)/concatenate | solution.py:142
  117.3 4.1 %collective-permute-start.9 = (bf16[8,16,1024]{2,1,0:T(8,128)(2,1)S(1)}, bf16[8,16,1024]{2,1,0:T(8,128)(2,1)S(1)}, u32[]{:S(2)}, u32[]{:S(2)}) collective-permute-start(bf16[8,16,1024]{2,1,0:T(8,128)(2,1)S(1)} %convert_element_type.7), channel_id=1, source_target_pairs={{0,4},{1,5},{2,6},{3,7},{4,0},{5,1},{6,2},{7,3},{8,12},{9,13},{10,... | collective-permute-start | bytes 786440 | tf_op jit(solution)/shard_map/ppermute | solution.py:156
  121.5 3.4 %collective-permute-start.10 = (bf16[8,16,1024]{2,1,0:T(8,128)(2,1)S(1)}, bf16[8,16,1024]{2,1,0:T(8,128)(2,1)S(1)}, u32[]{:S(2)}, u32[]{:S(2)}) collective-permute-start(bf16[8,16,1024]{2,1,0:T(8,128)(2,1)S(1)} %convert_element_type.7), channel_id=1, source_target_pairs={{0,7},{1,4},{2,5},{3,6},{4,3},{5,0},{6,1},{7,2},{8,15},{9,12},{10,... | collective-permute-start | bytes 786440 | tf_op jit(solution)/shard_map/ppermute | solution.py:156
  124.9 3.0 %collective-permute-start.11 = (bf16[8,16,1024]{2,1,0:T(8,128)(2,1)S(1)}, bf16[8,16,1024]{2,1,0:T(8,128)(2,1)}, u32[]{:S(2)}, u32[]{:S(2)}) collective-permute-start(bf16[8,16,1024]{2,1,0:T(8,128)(2,1)S(1)} %convert_element_type.7), channel_id=1, source_target_pairs={{0,6},{1,7},{2,4},{3,5},{4,2},{5,3},{6,0},{7,1},{8,14},{9,15},{10,... | collective-permute-start | bytes 786440 | tf_op jit(solution)/shard_map/ppermute | solution.py:156
  127.8 2.1 %collective-permute-start.12 = (bf16[8,16,1024]{2,1,0:T(8,128)(2,1)S(1)}, bf16[8,16,1024]{2,1,0:T(8,128)(2,1)}, u32[]{:S(2)}, u32[]{:S(2)}) collective-permute-start(bf16[8,16,1024]{2,1,0:T(8,128)(2,1)S(1)} %convert_element_type.7), channel_id=1, source_target_pairs={{0,5},{1,6},{2,7},{3,4},{4,1},{5,2},{6,3},{7,0},{8,13},{9,14},{10,... | collective-permute-start | bytes 786440 | tf_op jit(solution)/shard_map/ppermute | solution.py:156
  129.9 2.4 %collective-permute-start.6 = (bf16[4,4,16,1024]{3,2,1,0:T(8,128)(2,1)S(1)}, bf16[4,4,16,1024]{3,2,1,0:T(8,128)(2,1)S(1)}, u32[]{:S(2)}, u32[]{:S(2)}) collective-permute-start(bf16[4,4,16,1024]{3,2,1,0:T(8,128)(2,1)S(1)} %get-tuple-element.17), channel_id=1, source_target_pairs={{0,24},{8,0},{16,8},{24,16},{1,25},{9,1},{17,9},{25,17},{2,26},{10... | collective-permute-start | bytes 1572872 | tf_op jit(solution)/shard_map/ppermute | solution.py:140
  132.4 16.9 %collective-permute-done.9 = bf16[8,16,1024]{2,1,0:T(8,128)(2,1)S(1)} collective-permute-done((bf16[8,16,1024]{2,1,0:T(8,128)(2,1)S(1)}, bf16[8,16,1024]{2,1,0:T(8,128)(2,1)S(1)}, u32[]{:S(2)}, u32[]{:S(2)}) %collective-permute-start.9) | collective-permute-done | bytes 262176 | tf_op jit(solution)/shard_map/ppermute | solution.py:156
  149.2 2.7 %collective-permute-start.7 = (bf16[4,4,16,1024]{3,2,1,0:T(8,128)(2,1)S(1)}, bf16[4,4,16,1024]{3,2,1,0:T(8,128)(2,1)S(1)}, u32[]{:S(2)}, u32[]{:S(2)}) collective-permute-start(bf16[4,4,16,1024]{3,2,1,0:T(8,128)(2,1)S(1)} %get-tuple-element.17), channel_id=1, source_target_pairs={{0,16},{8,24},{16,0},{24,8},{1,17},{9,25},{17,1},{25,9},{2,18},{10... | collective-permute-start | bytes 1572872 | tf_op jit(solution)/shard_map/ppermute | solution.py:140
  151.9 3.0 %collective-permute-done.10 = bf16[8,16,1024]{2,1,0:T(8,128)(2,1)S(1)} collective-permute-done((bf16[8,16,1024]{2,1,0:T(8,128)(2,1)S(1)}, bf16[8,16,1024]{2,1,0:T(8,128)(2,1)S(1)}, u32[]{:S(2)}, u32[]{:S(2)}) %collective-permute-start.10) | collective-permute-done | bytes 262176 | tf_op jit(solution)/shard_map/ppermute | solution.py:156
  154.9 1.2 collective-permute-start.8
  156.1 5.9 %collective-permute-done.11 = bf16[8,16,1024]{2,1,0:T(8,128)(2,1)} collective-permute-done((bf16[8,16,1024]{2,1,0:T(8,128)(2,1)S(1)}, bf16[8,16,1024]{2,1,0:T(8,128)(2,1)}, u32[]{:S(2)}, u32[]{:S(2)}) %collective-permute-start.11) | collective-permute-done | bytes 262176 | tf_op jit(solution)/shard_map/ppermute | solution.py:156
  162.0 6.2 %collective-permute-done.12 = bf16[8,16,1024]{2,1,0:T(8,128)(2,1)} collective-permute-done((bf16[8,16,1024]{2,1,0:T(8,128)(2,1)S(1)}, bf16[8,16,1024]{2,1,0:T(8,128)(2,1)}, u32[]{:S(2)}, u32[]{:S(2)}) %collective-permute-start.12) | collective-permute-done | bytes 262176 | tf_op jit(solution)/shard_map/ppermute | solution.py:156
  168.3 3.3 %fusion.3 = bf16[4,8,16,1024]{3,2,1,0:T(8,128)(2,1)} fusion(s32[]{:T(128)S(6)} %select_n.44, bf16[1,8,16,1024]{3,2,1,0:T(8,128)(2,1)S(1)} %bitcast.50, bf16[1,8,16,1024]{3,2,1,0:T(8,128)(2,1)S(1)} %bitcast.51, bf16[1,8,16,1024]{3,2,1,0:T(8,128)(2,1)} %bitcast.20, bf16[1,8,16,1024]{3,2,1,0:T(8,128)(2,1)} %bitcast.21), kind=kLoop, calls=%fused_computation.30 | loop fusion | flops 3670016 | bytes 2097156 | tf_op jit(solution)/shard_map/jit(_roll_dynamic)/concatenate | solution.py:157
  171.7 6.5 %collective-permute-done.8 = bf16[4,4,16,1024]{3,2,1,0:T(8,128)(2,1)S(1)} collective-permute-done((bf16[4,4,16,1024]{3,2,1,0:T(8,128)(2,1)S(1)}, bf16[4,4,16,1024]{3,2,1,0:T(8,128)(2,1)S(1)}, u32[]{:S(2)}, u32[]{:S(2)}) %collective-permute-start.8) | collective-permute-done | bytes 524320 | tf_op jit(solution)/shard_map/ppermute | solution.py:140
  178.6 3.9 %pad_maximum_fusion.mine_ref = bf16[4,4,8,16,1024]{4,3,2,1,0:T(8,128)(2,1)} fusion(bf16[4,4,4,16,1024]{4,3,2,1,0:T(8,128)(2,1)S(1)} %constant_dynamic-slice_fusion, bf16[4,4,4,16,1024]{4,3,2,1,0:T(8,128)(2,1)} %bitcast.43), kind=kLoop, calls=%fused_computation | loop fusion | flops 2097152 | bytes 8388608 | tf_op jit(solution)/shard_map/concatenate | solution.py:82
  183.2 1.9 maximum_select_fusion
  185.1 1.6 copy.7
  186.7 3.7 %collective-permute-done.13.theirs_ref = bf16[4,4,8,16,1024]{4,3,2,1,0:T(8,128)(2,1)} collective-permute-done((bf16[4,4,8,16,1024]{4,3,2,1,0:T(8,128)(2,1)}, bf16[4,4,8,16,1024]{4,3,2,1,0:T(8,128)(2,1)}, u32[]{:S(2)}, u32[]{:S(2)}) %collective-permute-start.13) | collective-permute-done | bytes 4194336 | tf_op jit(solution)/shard_map/ppermute | solution.py:91
  190.3 10.4 %shard_map.47 = f32[2,8,128,512]{3,2,1,0:T(8,128)} custom-call(s32[1]{0:T(128)} %bitcast.core_ref, bf16[8,128,1024]{2,1,0:T(8,128)(2,1)} %bitcast.40, bf16[4,4,8,16,1024]{4,3,2,1,0:T(8,128)(2,1)} %pad_maximum_fusion.mine_ref, bf16[4,4,8,16,1024]{4,3,2,1,0:T(8,128)(2,1)} %collective-permute-done.13.theirs_ref), custom_call_target="tpu_custom_call" | custom-call | tf_op jit(solution)/shard_map/pallas_call | solution.py:121
  (29 shorter events, 5.9 us)
Async XLA Ops:
  6.5 76.3 %reduce-scatter.2.cloned.1.call-start = ((), (), s32[]{:S(2)}) async-start(), calls=%async_computation.1 | async-start | bytes 4718592 | tf_op jit(solution)/shard_map/reduce_scatter | solution.py:175
  26.5 152.1 %all-gather.3.cloned.1.call-start = ((), (), s32[]{:S(2)}) async-start(), calls=%async_computation.2 | async-start | bytes 2621440 | tf_op jit(solution)/shard_map/all_gather | solution.py:84
  83.9 9.7 %collective-permute-start.4 = (bf16[8,16,1024]{2,1,0:T(8,128)(2,1)S(1)}, bf16[8,16,1024]{2,1,0:T(8,128)(2,1)S(1)}, u32[]{:S(2)}, u32[]{:S(2)}) collective-permute-start(bf16[8,16,1024]{2,1,0:T(8,128)(2,1)S(1)} %convert_element_type.7), channel_id=1, source_target_pairs={{0,2},{1,3},{2,0},{3,1},{4,6},{5,7},{6,4},{7,5},{8,10},{9,11},{10,... | collective-permute-start | bytes 786440 | tf_op jit(solution)/shard_map/ppermute | solution.py:140
  86.8 11.2 %collective-permute-start.5 = (bf16[8,16,1024]{2,1,0:T(8,128)(2,1)S(1)}, bf16[8,16,1024]{2,1,0:T(8,128)(2,1)S(1)}, u32[]{:S(2)}, u32[]{:S(2)}) collective-permute-start(bf16[8,16,1024]{2,1,0:T(8,128)(2,1)S(1)} %convert_element_type.7), channel_id=1, source_target_pairs={{0,1},{1,2},{2,3},{3,0},{4,5},{5,6},{6,7},{7,4},{8,9},{9,10},{10,1... | collective-permute-start | bytes 786440 | tf_op jit(solution)/shard_map/ppermute | solution.py:140
  87.1 10.9 %collective-permute-start = (bf16[8,16,1024]{2,1,0:T(8,128)(2,1)S(1)}, bf16[8,16,1024]{2,1,0:T(8,128)(2,1)S(1)}, u32[]{:S(2)}, u32[]{:S(2)}) collective-permute-start(bf16[8,16,1024]{2,1,0:T(8,128)(2,1)S(1)} %convert_element_type.7), channel_id=1, source_target_pairs={{0,192},{64,0},{128,64},{192,128},{1,193},{65,1},{129,65},{193,129... | collective-permute-start | bytes 786440 | tf_op jit(solution)/shard_map/ppermute | solution.py:140
  87.1 19.3 %collective-permute-start.1 = (bf16[8,16,1024]{2,1,0:T(8,128)(2,1)S(1)}, bf16[8,16,1024]{2,1,0:T(8,128)(2,1)S(1)}, u32[]{:S(2)}, u32[]{:S(2)}) collective-permute-start(bf16[8,16,1024]{2,1,0:T(8,128)(2,1)S(1)} %convert_element_type.7), channel_id=1, source_target_pairs={{0,128},{64,192},{128,0},{192,64},{1,129},{65,193},{129,1},{193,65... | collective-permute-start | bytes 786440 | tf_op jit(solution)/shard_map/ppermute | solution.py:140
  89.5 22.5 %collective-permute-start.2 = (bf16[8,16,1024]{2,1,0:T(8,128)(2,1)S(1)}, bf16[8,16,1024]{2,1,0:T(8,128)(2,1)S(1)}, u32[]{:S(2)}, u32[]{:S(2)}) collective-permute-start(bf16[8,16,1024]{2,1,0:T(8,128)(2,1)S(1)} %convert_element_type.7), channel_id=1, source_target_pairs={{0,64},{64,128},{128,192},{192,0},{1,65},{65,129},{129,193},{193,1... | collective-permute-start | bytes 786440 | tf_op jit(solution)/shard_map/ppermute | solution.py:140
  93.6 18.4 %collective-permute-start.3 = (bf16[8,16,1024]{2,1,0:T(8,128)(2,1)S(1)}, bf16[8,16,1024]{2,1,0:T(8,128)(2,1)S(1)}, u32[]{:S(2)}, u32[]{:S(2)}) collective-permute-start(bf16[8,16,1024]{2,1,0:T(8,128)(2,1)S(1)} %convert_element_type.7), channel_id=1, source_target_pairs={{0,3},{1,0},{2,1},{3,2},{4,7},{5,4},{6,5},{7,6},{8,11},{9,8},{10,9... | collective-permute-start | bytes 786440 | tf_op jit(solution)/shard_map/ppermute | solution.py:140
  112.0 0.7 copy-start
  112.0 0.8 copy-start.1
  117.3 31.9 %collective-permute-start.9 = (bf16[8,16,1024]{2,1,0:T(8,128)(2,1)S(1)}, bf16[8,16,1024]{2,1,0:T(8,128)(2,1)S(1)}, u32[]{:S(2)}, u32[]{:S(2)}) collective-permute-start(bf16[8,16,1024]{2,1,0:T(8,128)(2,1)S(1)} %convert_element_type.7), channel_id=1, source_target_pairs={{0,4},{1,5},{2,6},{3,7},{4,0},{5,1},{6,2},{7,3},{8,12},{9,13},{10,... | collective-permute-start | bytes 786440 | tf_op jit(solution)/shard_map/ppermute | solution.py:156
  121.5 33.4 %collective-permute-start.10 = (bf16[8,16,1024]{2,1,0:T(8,128)(2,1)S(1)}, bf16[8,16,1024]{2,1,0:T(8,128)(2,1)S(1)}, u32[]{:S(2)}, u32[]{:S(2)}) collective-permute-start(bf16[8,16,1024]{2,1,0:T(8,128)(2,1)S(1)} %convert_element_type.7), channel_id=1, source_target_pairs={{0,7},{1,4},{2,5},{3,6},{4,3},{5,0},{6,1},{7,2},{8,15},{9,12},{10,... | collective-permute-start | bytes 786440 | tf_op jit(solution)/shard_map/ppermute | solution.py:156
  124.9 37.2 %collective-permute-start.11 = (bf16[8,16,1024]{2,1,0:T(8,128)(2,1)S(1)}, bf16[8,16,1024]{2,1,0:T(8,128)(2,1)}, u32[]{:S(2)}, u32[]{:S(2)}) collective-permute-start(bf16[8,16,1024]{2,1,0:T(8,128)(2,1)S(1)} %convert_element_type.7), channel_id=1, source_target_pairs={{0,6},{1,7},{2,4},{3,5},{4,2},{5,3},{6,0},{7,1},{8,14},{9,15},{10,... | collective-permute-start | bytes 786440 | tf_op jit(solution)/shard_map/ppermute | solution.py:156
  127.8 40.4 %collective-permute-start.12 = (bf16[8,16,1024]{2,1,0:T(8,128)(2,1)S(1)}, bf16[8,16,1024]{2,1,0:T(8,128)(2,1)}, u32[]{:S(2)}, u32[]{:S(2)}) collective-permute-start(bf16[8,16,1024]{2,1,0:T(8,128)(2,1)S(1)} %convert_element_type.7), channel_id=1, source_target_pairs={{0,5},{1,6},{2,7},{3,4},{4,1},{5,2},{6,3},{7,0},{8,13},{9,14},{10,... | collective-permute-start | bytes 786440 | tf_op jit(solution)/shard_map/ppermute | solution.py:156
  129.9 41.6 %collective-permute-start.6 = (bf16[4,4,16,1024]{3,2,1,0:T(8,128)(2,1)S(1)}, bf16[4,4,16,1024]{3,2,1,0:T(8,128)(2,1)S(1)}, u32[]{:S(2)}, u32[]{:S(2)}) collective-permute-start(bf16[4,4,16,1024]{3,2,1,0:T(8,128)(2,1)S(1)} %get-tuple-element.17), channel_id=1, source_target_pairs={{0,24},{8,0},{16,8},{24,16},{1,25},{9,1},{17,9},{25,17},{2,26},{10... | collective-permute-start | bytes 1572872 | tf_op jit(solution)/shard_map/ppermute | solution.py:140
  149.2 22.4 %collective-permute-start.7 = (bf16[4,4,16,1024]{3,2,1,0:T(8,128)(2,1)S(1)}, bf16[4,4,16,1024]{3,2,1,0:T(8,128)(2,1)S(1)}, u32[]{:S(2)}, u32[]{:S(2)}) collective-permute-start(bf16[4,4,16,1024]{3,2,1,0:T(8,128)(2,1)S(1)} %get-tuple-element.17), channel_id=1, source_target_pairs={{0,16},{8,24},{16,0},{24,8},{1,17},{9,25},{17,1},{25,9},{2,18},{10... | collective-permute-start | bytes 1572872 | tf_op jit(solution)/shard_map/ppermute | solution.py:140
  154.9 23.2 %collective-permute-start.8 = (bf16[4,4,16,1024]{3,2,1,0:T(8,128)(2,1)S(1)}, bf16[4,4,16,1024]{3,2,1,0:T(8,128)(2,1)S(1)}, u32[]{:S(2)}, u32[]{:S(2)}) collective-permute-start(bf16[4,4,16,1024]{3,2,1,0:T(8,128)(2,1)S(1)} %get-tuple-element.17), channel_id=1, source_target_pairs={{0,8},{8,16},{16,24},{24,0},{1,9},{9,17},{17,25},{25,1},{2,10},{10... | collective-permute-start | bytes 1572872 | tf_op jit(solution)/shard_map/ppermute | solution.py:140
  182.5 7.8 %collective-permute-start.13 = (bf16[4,4,8,16,1024]{4,3,2,1,0:T(8,128)(2,1)}, bf16[4,4,8,16,1024]{4,3,2,1,0:T(8,128)(2,1)}, u32[]{:S(2)}, u32[]{:S(2)}) collective-permute-start(bf16[4,4,8,16,1024]{4,3,2,1,0:T(8,128)(2,1)} %pad_maximum_fusion.mine_ref), channel_id=1, source_target_pairs={{0,32},{32,0},{1,33},{33,1},{2,34},{34,2},{3,35},{35,3},{4,36},{36... | collective-permute-start | bytes 12582920 | tf_op jit(solution)/shard_map/ppermute | solution.py:91
Sparse Core Ops, SparseCore 0:
  26.6 56.1 reduce-scatter.1
  117.5 49.1 all-gather.2

commit v19 on v17

--- a/solution.py
+++ b/solution.py
@@ -10,7 +10,7 @@
 DIRS = 512
 FREQS = 8
 GRID = 1024
-NODE_TILE = 256
+NODE_TILE = 512
 
 
 def unit_phasor(turn):

time: 196 us -> 195 us (level)
  no operation moved by 1% of the time
where the time goes in v19:
time: 195 us; the launch traced here: 194 us
  waiting for transfers between devices  123 us (63%)
  Pallas kernels  24.9 us (13%)
  starting transfers between devices  20.4 us (10%)
  between operations  13.4 us (7%)
  other arithmetic  9.98 us (5%)
  local copies, waits for them, and re-layouts  3.11 us (2%)
    reduce_scatter x1, waiting for transfers between devices, local(): lax.psum_scatter(partial_amp, ('zlo', 'core'), scatter_dimension=1, tiled...  56.3 us
    ppermute x4, waiting for transfers between devices, from_other_half(): ahead.append(lax.ppermute(piece, ('zhi', 'y'), perm=perm))  38.4 us
    ppermute x6, waiting for transfers between devices, gather_by_permutes(): lax.ppermute(piece, axis_name, perm=[(i, (i - shift) % count) for i in ra...  22.6 us
    pallas_call x1, Pallas kernels, partial_amplitudes(): pl.pallas_call(amp_kernel, out_shape=jax.ShapeDtypeStruct((FREQS, rows, 2...  14.4 us
    ppermute x4, starting transfers between devices, from_other_half(): ahead.append(lax.ppermute(piece, ('zhi', 'y'), perm=perm))  12.5 us
    pallas_call x1, Pallas kernels, cross_spectra(): pl.pallas_call(spec_kernel, out_shape=jax.ShapeDtypeStruct((2, freqs, row...  10.4 us
    ppermute x6, starting transfers between devices, gather_by_permutes(): lax.ppermute(piece, axis_name, perm=[(i, (i - shift) % count) for i in ra...  6.46 us
    ppermute x1, waiting for transfers between devices, gather_cols(): theirs = lax.ppermute(mine, 'core', perm=[(0, 1), (1, 0)])  5.22 us
  transfers between devices with their start and end apart: 13, of which 10 were waited for; matrix products, arithmetic and copies ran while one was open for 2% of the time, Pallas kernels for 0%

profile of v19, /device:TPU:33, one launch (start us, length us, event | category | flops | bytes accessed | tf_op | source)
XLA Modules:
  0.0 194.4 jit_solution(16422487418582222415)
XLA Ops:
  6.5 0.8 fusion.22
  7.3 0.8 fusion.21
  8.1 1.3 multiply_sqrt_fusion.spread_ref
  9.4 1.7 multiply_add_fusion.proj_ref
  11.1 14.4 %shard_map.46 = f32[8,128,1024]{2,1,0:T(8,128)} custom-call(s32[1024,512]{1,0:T(8,128)} %multiply_add_fusion.proj_ref, f32[8,512]{1,0:T(8,128)} %multiply_sqrt_fusion.spread_ref, bf16[2,8,128,1024]{3,2,1,0:T(8,128)(2,1)} %resp_ref.1), custom_call_target="tpu_custom_call" | custom-call | tf_op jit(solution)/shard_map/pallas_call | solution.py:61
  25.6 56.3 %reduce-scatter.2.cloned.1.call-done = f32[8,16,1024]{2,1,0:T(8,128)} async-done(((f32[8,128,1024]{2,1,0:T(8,128)}), f32[8,16,1024]{2,1,0:T(8,128)}) %reduce-scatter.2.cloned.1.call-update) | async-done | bytes 524304 | tf_op jit(solution)/shard_map/reduce_scatter | solution.py:168
  81.9 1.1 convert_element_type.7
  83.0 1.3 collective-permute-start.5
  84.2 2.4 %collective-permute-start.4 = (bf16[8,16,1024]{2,1,0:T(8,128)(2,1)S(1)}, bf16[8,16,1024]{2,1,0:T(8,128)(2,1)S(1)}, u32[]{:S(2)}, u32[]{:S(2)}) collective-permute-start(bf16[8,16,1024]{2,1,0:T(8,128)(2,1)S(1)} %convert_element_type.7), channel_id=1, source_target_pairs={{0,2},{1,3},{2,0},{3,1},{4,6},{5,7},{6,4},{7,5},{8,10},{9,11},{10,... | collective-permute-start | bytes 786440 | tf_op jit(solution)/shard_map/ppermute | solution.py:133
  86.7 1.2 collective-permute-start.3
  87.8 1.2 collective-permute-start.2
  89.1 0.4 collective-permute-start.1
  89.4 1.4 collective-permute-done.5
  90.9 1.1 convert_bitcast_fusion
  91.9 6.0 %collective-permute-done.4 = bf16[8,16,1024]{2,1,0:T(8,128)(2,1)S(1)} collective-permute-done((bf16[8,16,1024]{2,1,0:T(8,128)(2,1)S(1)}, bf16[8,16,1024]{2,1,0:T(8,128)(2,1)S(1)}, u32[]{:S(2)}, u32[]{:S(2)}) %collective-permute-start.4) | collective-permute-done | bytes 262176 | tf_op jit(solution)/shard_map/ppermute | solution.py:133
  97.9 14.1 %collective-permute-done.1 = bf16[8,16,1024]{2,1,0:T(8,128)(2,1)S(1)} collective-permute-done((bf16[8,16,1024]{2,1,0:T(8,128)(2,1)S(1)}, bf16[8,16,1024]{2,1,0:T(8,128)(2,1)S(1)}, u32[]{:S(2)}, u32[]{:S(2)}) %collective-permute-start.1) | collective-permute-done | bytes 262176 | tf_op jit(solution)/shard_map/ppermute | solution.py:133
  112.1 1.0 collective-permute-done
  113.1 3.3 %fusion.10 = (bf16[4,8,16,1024]{3,2,1,0:T(8,128)(2,1)S(1)}, bf16[4,8,16,1024]{3,2,1,0:T(8,128)(2,1)}) fusion(s32[]{:T(128)S(6)} %select_n.32, bf16[1,8,16,1024]{3,2,1,0:T(8,128)(2,1)S(1)} %bitcast.35, bf16[1,8,16,1024]{3,2,1,0:T(8,128)(2,1)S(1)} %bitcast.34, bf16[1,8,16,1024]{3,2,1,0:T(8,128)(2,1)S(1)} %bitcast.33, ...), kind=kLoop, calls=%fused_computation.36 | loop fusion | flops 7340032 | bytes 3932168 | tf_op jit(solution)/shard_map/jit(_roll_dynamic)/concatenate | solution.py:135
  116.4 4.8 %collective-permute-start.9 = (bf16[8,16,1024]{2,1,0:T(8,128)(2,1)S(1)}, bf16[8,16,1024]{2,1,0:T(8,128)(2,1)S(1)}, u32[]{:S(2)}, u32[]{:S(2)}) collective-permute-start(bf16[8,16,1024]{2,1,0:T(8,128)(2,1)S(1)} %convert_element_type.7), channel_id=1, source_target_pairs={{0,5},{1,6},{2,7},{3,4},{4,1},{5,2},{6,3},{7,0},{8,13},{9,14},{10,... | collective-permute-start | bytes 786440 | tf_op jit(solution)/shard_map/ppermute | solution.py:149
  121.2 1.5 collective-permute-start.8
  122.7 5.3 %collective-permute-start.7 = (bf16[8,16,1024]{2,1,0:T(8,128)(2,1)S(1)}, bf16[8,16,1024]{2,1,0:T(8,128)(2,1)S(1)}, u32[]{:S(2)}, u32[]{:S(2)}) collective-permute-start(bf16[8,16,1024]{2,1,0:T(8,128)(2,1)S(1)} %convert_element_type.7), channel_id=1, source_target_pairs={{0,7},{1,4},{2,5},{3,6},{4,3},{5,0},{6,1},{7,2},{8,15},{9,12},{10,... | collective-permute-start | bytes 786440 | tf_op jit(solution)/shard_map/ppermute | solution.py:149
  128.0 0.9 collective-permute-start.6
  128.9 7.7 %collective-permute-done.9 = bf16[8,16,1024]{2,1,0:T(8,128)(2,1)S(1)} collective-permute-done((bf16[8,16,1024]{2,1,0:T(8,128)(2,1)S(1)}, bf16[8,16,1024]{2,1,0:T(8,128)(2,1)S(1)}, u32[]{:S(2)}, u32[]{:S(2)}) %collective-permute-start.9) | collective-permute-done | bytes 262176 | tf_op jit(solution)/shard_map/ppermute | solution.py:149
  136.6 20.4 %collective-permute-done.8 = bf16[8,16,1024]{2,1,0:T(8,128)(2,1)S(1)} collective-permute-done((bf16[8,16,1024]{2,1,0:T(8,128)(2,1)S(1)}, bf16[8,16,1024]{2,1,0:T(8,128)(2,1)S(1)}, u32[]{:S(2)}, u32[]{:S(2)}) %collective-permute-start.8) | collective-permute-done | bytes 262176 | tf_op jit(solution)/shard_map/ppermute | solution.py:149
  157.1 3.9 %collective-permute-done.7 = bf16[8,16,1024]{2,1,0:T(8,128)(2,1)S(1)} collective-permute-done((bf16[8,16,1024]{2,1,0:T(8,128)(2,1)S(1)}, bf16[8,16,1024]{2,1,0:T(8,128)(2,1)S(1)}, u32[]{:S(2)}, u32[]{:S(2)}) %collective-permute-start.7) | collective-permute-done | bytes 262176 | tf_op jit(solution)/shard_map/ppermute | solution.py:149
  160.9 6.4 %collective-permute-done.6 = bf16[8,16,1024]{2,1,0:T(8,128)(2,1)S(1)} collective-permute-done((bf16[8,16,1024]{2,1,0:T(8,128)(2,1)S(1)}, bf16[8,16,1024]{2,1,0:T(8,128)(2,1)S(1)}, u32[]{:S(2)}, u32[]{:S(2)}) %collective-permute-start.6) | collective-permute-done | bytes 262176 | tf_op jit(solution)/shard_map/ppermute | solution.py:149
  167.3 1.2 fusion.3
  168.6 1.4 collective-permute-start.10
  170.0 0.3 maximum_select_fusion
  170.3 1.6 copy.7
  171.9 5.2 %collective-permute-done.10.theirs_ref = bf16[4,4,8,16,1024]{4,3,2,1,0:T(8,128)(2,1)} collective-permute-done((bf16[4,4,8,16,1024]{4,3,2,1,0:T(8,128)(2,1)}, bf16[4,4,8,16,1024]{4,3,2,1,0:T(8,128)(2,1)}, u32[]{:S(2)}, u32[]{:S(2)}) %collective-permute-start.10) | collective-permute-done | bytes 4194336 | tf_op jit(solution)/shard_map/ppermute | solution.py:84
  177.1 10.4 %shard_map.47 = f32[2,8,128,512]{3,2,1,0:T(8,128)} custom-call(s32[1]{0:T(128)} %bitcast.core_ref, bf16[8,128,1024]{2,1,0:T(8,128)(2,1)} %bitcast.28, bf16[4,4,8,16,1024]{4,3,2,1,0:T(8,128)(2,1)} %bitcast.30, bf16[4,4,8,16,1024]{4,3,2,1,0:T(8,128)(2,1)} %collective-permute-done.10.theirs_ref), custom_call_target="tpu_custom_call" | custom-call | tf_op jit(solution)/shard_map/pallas_call | solution.py:114
  (8 shorter events, 0.1 us)
Async XLA Ops:
  6.5 75.4 %reduce-scatter.2.cloned.1.call-start = ((), (), s32[]{:S(2)}) async-start(), calls=%async_computation.1 | async-start | bytes 4718592 | tf_op jit(solution)/shard_map/reduce_scatter | solution.py:168
  25.5 143.0 %all-gather.3.cloned.1.call-start = ((), (), s32[]{:S(2)}) async-start(), calls=%async_computation.2 | async-start | bytes 5242880 | tf_op jit(solution)/shard_map/all_gather | solution.py:81
  83.0 7.9 %collective-permute-start.5 = (bf16[8,16,1024]{2,1,0:T(8,128)(2,1)S(1)}, bf16[8,16,1024]{2,1,0:T(8,128)(2,1)S(1)}, u32[]{:S(2)}, u32[]{:S(2)}) collective-permute-start(bf16[8,16,1024]{2,1,0:T(8,128)(2,1)S(1)} %convert_element_type.7), channel_id=1, source_target_pairs={{0,1},{1,2},{2,3},{3,0},{4,5},{5,6},{6,7},{7,4},{8,9},{9,10},{10,1... | collective-permute-start | bytes 786440 | tf_op jit(solution)/shard_map/ppermute | solution.py:133
  84.2 13.7 %collective-permute-start.4 = (bf16[8,16,1024]{2,1,0:T(8,128)(2,1)S(1)}, bf16[8,16,1024]{2,1,0:T(8,128)(2,1)S(1)}, u32[]{:S(2)}, u32[]{:S(2)}) collective-permute-start(bf16[8,16,1024]{2,1,0:T(8,128)(2,1)S(1)} %convert_element_type.7), channel_id=1, source_target_pairs={{0,2},{1,3},{2,0},{3,1},{4,6},{5,7},{6,4},{7,5},{8,10},{9,11},{10,... | collective-permute-start | bytes 786440 | tf_op jit(solution)/shard_map/ppermute | solution.py:133
  86.7 11.2 %collective-permute-start.3 = (bf16[8,16,1024]{2,1,0:T(8,128)(2,1)S(1)}, bf16[8,16,1024]{2,1,0:T(8,128)(2,1)S(1)}, u32[]{:S(2)}, u32[]{:S(2)}) collective-permute-start(bf16[8,16,1024]{2,1,0:T(8,128)(2,1)S(1)} %convert_element_type.7), channel_id=1, source_target_pairs={{0,3},{1,0},{2,1},{3,2},{4,7},{5,4},{6,5},{7,6},{8,11},{9,8},{10,9... | collective-permute-start | bytes 786440 | tf_op jit(solution)/shard_map/ppermute | solution.py:133
  87.8 10.1 %collective-permute-start.2 = (bf16[8,16,1024]{2,1,0:T(8,128)(2,1)S(1)}, bf16[8,16,1024]{2,1,0:T(8,128)(2,1)S(1)}, u32[]{:S(2)}, u32[]{:S(2)}) collective-permute-start(bf16[8,16,1024]{2,1,0:T(8,128)(2,1)S(1)} %convert_element_type.7), channel_id=1, source_target_pairs={{0,64},{64,128},{128,192},{192,0},{1,65},{65,129},{129,193},{193,1... | collective-permute-start | bytes 786440 | tf_op jit(solution)/shard_map/ppermute | solution.py:133
  89.1 23.0 %collective-permute-start.1 = (bf16[8,16,1024]{2,1,0:T(8,128)(2,1)S(1)}, bf16[8,16,1024]{2,1,0:T(8,128)(2,1)S(1)}, u32[]{:S(2)}, u32[]{:S(2)}) collective-permute-start(bf16[8,16,1024]{2,1,0:T(8,128)(2,1)S(1)} %convert_element_type.7), channel_id=1, source_target_pairs={{0,128},{64,192},{128,0},{192,64},{1,129},{65,193},{129,1},{193,65... | collective-permute-start | bytes 786440 | tf_op jit(solution)/shard_map/ppermute | solution.py:133
  90.9 22.2 %collective-permute-start = (bf16[8,16,1024]{2,1,0:T(8,128)(2,1)S(1)}, bf16[8,16,1024]{2,1,0:T(8,128)(2,1)S(1)}, u32[]{:S(2)}, u32[]{:S(2)}) collective-permute-start(bf16[8,16,1024]{2,1,0:T(8,128)(2,1)S(1)} %convert_element_type.7), channel_id=1, source_target_pairs={{0,192},{64,0},{128,64},{192,128},{1,193},{65,1},{129,65},{193,129... | collective-permute-start | bytes 786440 | tf_op jit(solution)/shard_map/ppermute | solution.py:133
  116.4 20.2 %collective-permute-start.9 = (bf16[8,16,1024]{2,1,0:T(8,128)(2,1)S(1)}, bf16[8,16,1024]{2,1,0:T(8,128)(2,1)S(1)}, u32[]{:S(2)}, u32[]{:S(2)}) collective-permute-start(bf16[8,16,1024]{2,1,0:T(8,128)(2,1)S(1)} %convert_element_type.7), channel_id=1, source_target_pairs={{0,5},{1,6},{2,7},{3,4},{4,1},{5,2},{6,3},{7,0},{8,13},{9,14},{10,... | collective-permute-start | bytes 786440 | tf_op jit(solution)/shard_map/ppermute | solution.py:149
  121.2 35.9 %collective-permute-start.8 = (bf16[8,16,1024]{2,1,0:T(8,128)(2,1)S(1)}, bf16[8,16,1024]{2,1,0:T(8,128)(2,1)S(1)}, u32[]{:S(2)}, u32[]{:S(2)}) collective-permute-start(bf16[8,16,1024]{2,1,0:T(8,128)(2,1)S(1)} %convert_element_type.7), channel_id=1, source_target_pairs={{0,6},{1,7},{2,4},{3,5},{4,2},{5,3},{6,0},{7,1},{8,14},{9,15},{10,... | collective-permute-start | bytes 786440 | tf_op jit(solution)/shard_map/ppermute | solution.py:149
  122.7 38.3 %collective-permute-start.7 = (bf16[8,16,1024]{2,1,0:T(8,128)(2,1)S(1)}, bf16[8,16,1024]{2,1,0:T(8,128)(2,1)S(1)}, u32[]{:S(2)}, u32[]{:S(2)}) collective-permute-start(bf16[8,16,1024]{2,1,0:T(8,128)(2,1)S(1)} %convert_element_type.7), channel_id=1, source_target_pairs={{0,7},{1,4},{2,5},{3,6},{4,3},{5,0},{6,1},{7,2},{8,15},{9,12},{10,... | collective-permute-start | bytes 786440 | tf_op jit(solution)/shard_map/ppermute | solution.py:149
  128.0 39.3 %collective-permute-start.6 = (bf16[8,16,1024]{2,1,0:T(8,128)(2,1)S(1)}, bf16[8,16,1024]{2,1,0:T(8,128)(2,1)S(1)}, u32[]{:S(2)}, u32[]{:S(2)}) collective-permute-start(bf16[8,16,1024]{2,1,0:T(8,128)(2,1)S(1)} %convert_element_type.7), channel_id=1, source_target_pairs={{0,4},{1,5},{2,6},{3,7},{4,0},{5,1},{6,2},{7,3},{8,12},{9,13},{10,... | collective-permute-start | bytes 786440 | tf_op jit(solution)/shard_map/ppermute | solution.py:149
  168.6 8.6 %collective-permute-start.10 = (bf16[4,4,8,16,1024]{4,3,2,1,0:T(8,128)(2,1)}, bf16[4,4,8,16,1024]{4,3,2,1,0:T(8,128)(2,1)}, u32[]{:S(2)}, u32[]{:S(2)}) collective-permute-start(bf16[4,4,8,16,1024]{4,3,2,1,0:T(8,128)(2,1)} %bitcast.29), channel_id=1, source_target_pairs={{0,32},{32,0},{1,33},{33,1},{2,34},{34,2},{3,35},{35,3},{4,36},{36... | collective-permute-start | bytes 12582920 | tf_op jit(solution)/shard_map/ppermute | solution.py:84
Sparse Core Ops, SparseCore 0:
  25.7 56.1 reduce-scatter.1
  116.5 49.2 all-gather.2

commit v20 on v19

--- a/solution.py
+++ b/solution.py
@@ -96,14 +96,26 @@
 
     zlo_count = mine_ref.shape[1]
     block = 2 * mine_ref.shape[0] * mine_ref.shape[3]
+    half = block // 2
     for z in range(zlo_count):
         own = mine_ref[:, z, 0].reshape(-1, mine_ref.shape[-1])
         other = theirs_ref[:, z, 0].reshape(-1, mine_ref.shape[-1])
-        cols = jnp.where(
-            first, jnp.concatenate([own, other], axis=0), jnp.concatenate([other, own], axis=0)
-        )
-        out_ref[0, 0, :, z * block : (z + 1) * block] = dot(rows, cols)
-        out_ref[1, 0, :, z * block : (z + 1) * block] = dot(rows_im, cols)
+        parts = (dot(rows, own), dot(rows_im, own), dot(rows, other), dot(rows_im, other))
+        start = z * block
+
+        @pl.when(first)
+        def _():
+            out_ref[0, 0, :, start : start + half] = parts[0]
+            out_ref[1, 0, :, start : start + half] = parts[1]
+            out_ref[0, 0, :, start + half : start + block] = parts[2]
+            out_ref[1, 0, :, start + half : start + block] = parts[3]
+
+        @pl.when(jnp.logical_not(first))
+        def _():
+            out_ref[0, 0, :, start : start + half] = parts[2]
+            out_ref[1, 0, :, start : start + half] = parts[3]
+            out_ref[0, 0, :, start + half : start + block] = parts[0]
+            out_ref[1, 0, :, start + half : start + block] = parts[1]
 
 
 def cross_spectra(rows, mine, theirs):

time: 195 us -> 203 us (1.041)
  Pallas kernels: 24.9 us -> 33.5 us
    pallas_call x1, Pallas kernels: 10.4 us -> 19.1 us  [cross_spectra(): pl.pallas_call(spec_kernel, out_shape=jax.ShapeDtypeStruct((2, freqs, row...]
where the time goes in v20:
time: 203 us
  waiting for transfers between devices  123 us (61%)
  Pallas kernels  33.5 us (17%)
  starting transfers between devices  20.4 us (10%)
  between operations  13.4 us (7%)
  other arithmetic  9.98 us (5%)
  local copies, waits for them, and re-layouts  3.11 us (2%)
    reduce_scatter x1, waiting for transfers between devices, local(): lax.psum_scatter(partial_amp, ('zlo', 'core'), scatter_dimension=1, tiled...  56.3 us
    ppermute x4, waiting for transfers between devices, from_other_half(): ahead.append(lax.ppermute(piece, ('zhi', 'y'), perm=perm))  38.4 us
    ppermute x6, waiting for transfers between devices, gather_by_permutes(): lax.ppermute(piece, axis_name, perm=[(i, (i - shift) % count) for i in ra...  22.6 us
    pallas_call x1, Pallas kernels, cross_spectra(): pl.pallas_call(spec_kernel, out_shape=jax.ShapeDtypeStruct((2, freqs, row...  19.1 us
    pallas_call x1, Pallas kernels, partial_amplitudes(): pl.pallas_call(amp_kernel, out_shape=jax.ShapeDtypeStruct((FREQS, rows, 2...  14.4 us
    ppermute x4, starting transfers between devices, from_other_half(): ahead.append(lax.ppermute(piece, ('zhi', 'y'), perm=perm))  12.5 us
    ppermute x6, starting transfers between devices, gather_by_permutes(): lax.ppermute(piece, axis_name, perm=[(i, (i - shift) % count) for i in ra...  6.46 us
    ppermute x1, waiting for transfers between devices, gather_cols(): theirs = lax.ppermute(mine, 'core', perm=[(0, 1), (1, 0)])  5.22 us
  transfers between devices with their start and end apart: 13, of which 10 were waited for; matrix products, arithmetic and copies ran while one was open for 2% of the time, Pallas kernels for 0%

profile of v20, /device:TPU:33, one launch (start us, length us, event | category | flops | bytes accessed | tf_op | source)
XLA Modules:
  0.0 203.0 jit_solution(1742623620365682015)
XLA Ops:
  6.5 0.8 fusion.22
  7.3 0.8 fusion.21
  8.1 1.3 multiply_sqrt_fusion.spread_ref
  9.4 1.7 multiply_add_fusion.proj_ref
  11.1 14.4 %shard_map.46 = f32[8,128,1024]{2,1,0:T(8,128)} custom-call(s32[1024,512]{1,0:T(8,128)} %multiply_add_fusion.proj_ref, f32[8,512]{1,0:T(8,128)} %multiply_sqrt_fusion.spread_ref, bf16[2,8,128,1024]{3,2,1,0:T(8,128)(2,1)} %resp_ref.1), custom_call_target="tpu_custom_call" | custom-call | tf_op jit(solution)/shard_map/pallas_call | solution.py:61
  25.6 56.3 %reduce-scatter.2.cloned.1.call-done = f32[8,16,1024]{2,1,0:T(8,128)} async-done(((f32[8,128,1024]{2,1,0:T(8,128)}), f32[8,16,1024]{2,1,0:T(8,128)}) %reduce-scatter.2.cloned.1.call-update) | async-done | bytes 524304 | tf_op jit(solution)/shard_map/reduce_scatter | solution.py:180
  81.9 1.1 convert_element_type.7
  83.0 1.3 collective-permute-start.5
  84.2 2.4 %collective-permute-start.4 = (bf16[8,16,1024]{2,1,0:T(8,128)(2,1)S(1)}, bf16[8,16,1024]{2,1,0:T(8,128)(2,1)S(1)}, u32[]{:S(2)}, u32[]{:S(2)}) collective-permute-start(bf16[8,16,1024]{2,1,0:T(8,128)(2,1)S(1)} %convert_element_type.7), channel_id=1, source_target_pairs={{0,2},{1,3},{2,0},{3,1},{4,6},{5,7},{6,4},{7,5},{8,10},{9,11},{10,... | collective-permute-start | bytes 786440 | tf_op jit(solution)/shard_map/ppermute | solution.py:145
  86.7 1.2 collective-permute-start.3
  87.8 1.2 collective-permute-start.2
  89.1 0.4 collective-permute-start.1
  89.4 1.4 collective-permute-done.5
  90.9 1.1 convert_bitcast_fusion
  91.9 6.0 %collective-permute-done.4 = bf16[8,16,1024]{2,1,0:T(8,128)(2,1)S(1)} collective-permute-done((bf16[8,16,1024]{2,1,0:T(8,128)(2,1)S(1)}, bf16[8,16,1024]{2,1,0:T(8,128)(2,1)S(1)}, u32[]{:S(2)}, u32[]{:S(2)}) %collective-permute-start.4) | collective-permute-done | bytes 262176 | tf_op jit(solution)/shard_map/ppermute | solution.py:145
  97.9 14.1 %collective-permute-done.1 = bf16[8,16,1024]{2,1,0:T(8,128)(2,1)S(1)} collective-permute-done((bf16[8,16,1024]{2,1,0:T(8,128)(2,1)S(1)}, bf16[8,16,1024]{2,1,0:T(8,128)(2,1)S(1)}, u32[]{:S(2)}, u32[]{:S(2)}) %collective-permute-start.1) | collective-permute-done | bytes 262176 | tf_op jit(solution)/shard_map/ppermute | solution.py:145
  112.1 1.0 collective-permute-done
  113.1 3.3 %fusion.10 = (bf16[4,8,16,1024]{3,2,1,0:T(8,128)(2,1)S(1)}, bf16[4,8,16,1024]{3,2,1,0:T(8,128)(2,1)}) fusion(s32[]{:T(128)S(6)} %select_n.32, bf16[1,8,16,1024]{3,2,1,0:T(8,128)(2,1)S(1)} %bitcast.35, bf16[1,8,16,1024]{3,2,1,0:T(8,128)(2,1)S(1)} %bitcast.34, bf16[1,8,16,1024]{3,2,1,0:T(8,128)(2,1)S(1)} %bitcast.33, ...), kind=kLoop, calls=%fused_computation.36 | loop fusion | flops 7340032 | bytes 3932168 | tf_op jit(solution)/shard_map/jit(_roll_dynamic)/concatenate | solution.py:147
  116.4 4.8 %collective-permute-start.9 = (bf16[8,16,1024]{2,1,0:T(8,128)(2,1)S(1)}, bf16[8,16,1024]{2,1,0:T(8,128)(2,1)S(1)}, u32[]{:S(2)}, u32[]{:S(2)}) collective-permute-start(bf16[8,16,1024]{2,1,0:T(8,128)(2,1)S(1)} %convert_element_type.7), channel_id=1, source_target_pairs={{0,5},{1,6},{2,7},{3,4},{4,1},{5,2},{6,3},{7,0},{8,13},{9,14},{10,... | collective-permute-start | bytes 786440 | tf_op jit(solution)/shard_map/ppermute | solution.py:161
  121.2 1.5 collective-permute-start.8
  122.7 5.3 %collective-permute-start.7 = (bf16[8,16,1024]{2,1,0:T(8,128)(2,1)S(1)}, bf16[8,16,1024]{2,1,0:T(8,128)(2,1)S(1)}, u32[]{:S(2)}, u32[]{:S(2)}) collective-permute-start(bf16[8,16,1024]{2,1,0:T(8,128)(2,1)S(1)} %convert_element_type.7), channel_id=1, source_target_pairs={{0,7},{1,4},{2,5},{3,6},{4,3},{5,0},{6,1},{7,2},{8,15},{9,12},{10,... | collective-permute-start | bytes 786440 | tf_op jit(solution)/shard_map/ppermute | solution.py:161
  128.0 0.9 collective-permute-start.6
  128.9 7.7 %collective-permute-done.9 = bf16[8,16,1024]{2,1,0:T(8,128)(2,1)S(1)} collective-permute-done((bf16[8,16,1024]{2,1,0:T(8,128)(2,1)S(1)}, bf16[8,16,1024]{2,1,0:T(8,128)(2,1)S(1)}, u32[]{:S(2)}, u32[]{:S(2)}) %collective-permute-start.9) | collective-permute-done | bytes 262176 | tf_op jit(solution)/shard_map/ppermute | solution.py:161
  136.6 20.4 %collective-permute-done.8 = bf16[8,16,1024]{2,1,0:T(8,128)(2,1)S(1)} collective-permute-done((bf16[8,16,1024]{2,1,0:T(8,128)(2,1)S(1)}, bf16[8,16,1024]{2,1,0:T(8,128)(2,1)S(1)}, u32[]{:S(2)}, u32[]{:S(2)}) %collective-permute-start.8) | collective-permute-done | bytes 262176 | tf_op jit(solution)/shard_map/ppermute | solution.py:161
  157.1 3.9 %collective-permute-done.7 = bf16[8,16,1024]{2,1,0:T(8,128)(2,1)S(1)} collective-permute-done((bf16[8,16,1024]{2,1,0:T(8,128)(2,1)S(1)}, bf16[8,16,1024]{2,1,0:T(8,128)(2,1)S(1)}, u32[]{:S(2)}, u32[]{:S(2)}) %collective-permute-start.7) | collective-permute-done | bytes 262176 | tf_op jit(solution)/shard_map/ppermute | solution.py:161
  160.9 6.4 %collective-permute-done.6 = bf16[8,16,1024]{2,1,0:T(8,128)(2,1)S(1)} collective-permute-done((bf16[8,16,1024]{2,1,0:T(8,128)(2,1)S(1)}, bf16[8,16,1024]{2,1,0:T(8,128)(2,1)S(1)}, u32[]{:S(2)}, u32[]{:S(2)}) %collective-permute-start.6) | collective-permute-done | bytes 262176 | tf_op jit(solution)/shard_map/ppermute | solution.py:161
  167.3 1.2 fusion.3
  168.6 1.4 collective-permute-start.10
  170.0 0.3 maximum_select_fusion
  170.3 1.6 copy.7
  171.9 5.2 %collective-permute-done.10.theirs_ref = bf16[4,4,8,16,1024]{4,3,2,1,0:T(8,128)(2,1)} collective-permute-done((bf16[4,4,8,16,1024]{4,3,2,1,0:T(8,128)(2,1)}, bf16[4,4,8,16,1024]{4,3,2,1,0:T(8,128)(2,1)}, u32[]{:S(2)}, u32[]{:S(2)}) %collective-permute-start.10) | collective-permute-done | bytes 4194336 | tf_op jit(solution)/shard_map/ppermute | solution.py:84
  177.1 19.1 %shard_map.47 = f32[2,8,128,512]{3,2,1,0:T(8,128)} custom-call(s32[1]{0:T(128)} %bitcast.core_ref, bf16[8,128,1024]{2,1,0:T(8,128)(2,1)} %bitcast.28, bf16[4,4,8,16,1024]{4,3,2,1,0:T(8,128)(2,1)} %bitcast.30, bf16[4,4,8,16,1024]{4,3,2,1,0:T(8,128)(2,1)} %collective-permute-done.10.theirs_ref), custom_call_target="tpu_custom_call" | custom-call | tf_op jit(solution)/shard_map/pallas_call | solution.py:126
  (8 shorter events, 0.1 us)
Async XLA Ops:
  6.5 75.4 %reduce-scatter.2.cloned.1.call-start = ((), (), s32[]{:S(2)}) async-start(), calls=%async_computation.1 | async-start | bytes 4718592 | tf_op jit(solution)/shard_map/reduce_scatter | solution.py:180
  25.5 143.0 %all-gather.3.cloned.1.call-start = ((), (), s32[]{:S(2)}) async-start(), calls=%async_computation.2 | async-start | bytes 5242880 | tf_op jit(solution)/shard_map/all_gather | solution.py:81
  83.0 7.9 %collective-permute-start.5 = (bf16[8,16,1024]{2,1,0:T(8,128)(2,1)S(1)}, bf16[8,16,1024]{2,1,0:T(8,128)(2,1)S(1)}, u32[]{:S(2)}, u32[]{:S(2)}) collective-permute-start(bf16[8,16,1024]{2,1,0:T(8,128)(2,1)S(1)} %convert_element_type.7), channel_id=1, source_target_pairs={{0,1},{1,2},{2,3},{3,0},{4,5},{5,6},{6,7},{7,4},{8,9},{9,10},{10,1... | collective-permute-start | bytes 786440 | tf_op jit(solution)/shard_map/ppermute | solution.py:145
  84.2 13.7 %collective-permute-start.4 = (bf16[8,16,1024]{2,1,0:T(8,128)(2,1)S(1)}, bf16[8,16,1024]{2,1,0:T(8,128)(2,1)S(1)}, u32[]{:S(2)}, u32[]{:S(2)}) collective-permute-start(bf16[8,16,1024]{2,1,0:T(8,128)(2,1)S(1)} %convert_element_type.7), channel_id=1, source_target_pairs={{0,2},{1,3},{2,0},{3,1},{4,6},{5,7},{6,4},{7,5},{8,10},{9,11},{10,... | collective-permute-start | bytes 786440 | tf_op jit(solution)/shard_map/ppermute | solution.py:145
  86.7 11.2 %collective-permute-start.3 = (bf16[8,16,1024]{2,1,0:T(8,128)(2,1)S(1)}, bf16[8,16,1024]{2,1,0:T(8,128)(2,1)S(1)}, u32[]{:S(2)}, u32[]{:S(2)}) collective-permute-start(bf16[8,16,1024]{2,1,0:T(8,128)(2,1)S(1)} %convert_element_type.7), channel_id=1, source_target_pairs={{0,3},{1,0},{2,1},{3,2},{4,7},{5,4},{6,5},{7,6},{8,11},{9,8},{10,9... | collective-permute-start | bytes 786440 | tf_op jit(solution)/shard_map/ppermute | solution.py:145
  87.8 10.1 %collective-permute-start.2 = (bf16[8,16,1024]{2,1,0:T(8,128)(2,1)S(1)}, bf16[8,16,1024]{2,1,0:T(8,128)(2,1)S(1)}, u32[]{:S(2)}, u32[]{:S(2)}) collective-permute-start(bf16[8,16,1024]{2,1,0:T(8,128)(2,1)S(1)} %convert_element_type.7), channel_id=1, source_target_pairs={{0,64},{64,128},{128,192},{192,0},{1,65},{65,129},{129,193},{193,1... | collective-permute-start | bytes 786440 | tf_op jit(solution)/shard_map/ppermute | solution.py:145
  89.1 23.0 %collective-permute-start.1 = (bf16[8,16,1024]{2,1,0:T(8,128)(2,1)S(1)}, bf16[8,16,1024]{2,1,0:T(8,128)(2,1)S(1)}, u32[]{:S(2)}, u32[]{:S(2)}) collective-permute-start(bf16[8,16,1024]{2,1,0:T(8,128)(2,1)S(1)} %convert_element_type.7), channel_id=1, source_target_pairs={{0,128},{64,192},{128,0},{192,64},{1,129},{65,193},{129,1},{193,65... | collective-permute-start | bytes 786440 | tf_op jit(solution)/shard_map/ppermute | solution.py:145
  90.9 22.2 %collective-permute-start = (bf16[8,16,1024]{2,1,0:T(8,128)(2,1)S(1)}, bf16[8,16,1024]{2,1,0:T(8,128)(2,1)S(1)}, u32[]{:S(2)}, u32[]{:S(2)}) collective-permute-start(bf16[8,16,1024]{2,1,0:T(8,128)(2,1)S(1)} %convert_element_type.7), channel_id=1, source_target_pairs={{0,192},{64,0},{128,64},{192,128},{1,193},{65,1},{129,65},{193,129... | collective-permute-start | bytes 786440 | tf_op jit(solution)/shard_map/ppermute | solution.py:145
  116.4 20.2 %collective-permute-start.9 = (bf16[8,16,1024]{2,1,0:T(8,128)(2,1)S(1)}, bf16[8,16,1024]{2,1,0:T(8,128)(2,1)S(1)}, u32[]{:S(2)}, u32[]{:S(2)}) collective-permute-start(bf16[8,16,1024]{2,1,0:T(8,128)(2,1)S(1)} %convert_element_type.7), channel_id=1, source_target_pairs={{0,5},{1,6},{2,7},{3,4},{4,1},{5,2},{6,3},{7,0},{8,13},{9,14},{10,... | collective-permute-start | bytes 786440 | tf_op jit(solution)/shard_map/ppermute | solution.py:161
  121.2 35.9 %collective-permute-start.8 = (bf16[8,16,1024]{2,1,0:T(8,128)(2,1)S(1)}, bf16[8,16,1024]{2,1,0:T(8,128)(2,1)S(1)}, u32[]{:S(2)}, u32[]{:S(2)}) collective-permute-start(bf16[8,16,1024]{2,1,0:T(8,128)(2,1)S(1)} %convert_element_type.7), channel_id=1, source_target_pairs={{0,6},{1,7},{2,4},{3,5},{4,2},{5,3},{6,0},{7,1},{8,14},{9,15},{10,... | collective-permute-start | bytes 786440 | tf_op jit(solution)/shard_map/ppermute | solution.py:161
  122.7 38.3 %collective-permute-start.7 = (bf16[8,16,1024]{2,1,0:T(8,128)(2,1)S(1)}, bf16[8,16,1024]{2,1,0:T(8,128)(2,1)S(1)}, u32[]{:S(2)}, u32[]{:S(2)}) collective-permute-start(bf16[8,16,1024]{2,1,0:T(8,128)(2,1)S(1)} %convert_element_type.7), channel_id=1, source_target_pairs={{0,7},{1,4},{2,5},{3,6},{4,3},{5,0},{6,1},{7,2},{8,15},{9,12},{10,... | collective-permute-start | bytes 786440 | tf_op jit(solution)/shard_map/ppermute | solution.py:161
  128.0 39.3 %collective-permute-start.6 = (bf16[8,16,1024]{2,1,0:T(8,128)(2,1)S(1)}, bf16[8,16,1024]{2,1,0:T(8,128)(2,1)S(1)}, u32[]{:S(2)}, u32[]{:S(2)}) collective-permute-start(bf16[8,16,1024]{2,1,0:T(8,128)(2,1)S(1)} %convert_element_type.7), channel_id=1, source_target_pairs={{0,4},{1,5},{2,6},{3,7},{4,0},{5,1},{6,2},{7,3},{8,12},{9,13},{10,... | collective-permute-start | bytes 786440 | tf_op jit(solution)/shard_map/ppermute | solution.py:161
  168.6 8.6 %collective-permute-start.10 = (bf16[4,4,8,16,1024]{4,3,2,1,0:T(8,128)(2,1)}, bf16[4,4,8,16,1024]{4,3,2,1,0:T(8,128)(2,1)}, u32[]{:S(2)}, u32[]{:S(2)}) collective-permute-start(bf16[4,4,8,16,1024]{4,3,2,1,0:T(8,128)(2,1)} %bitcast.29), channel_id=1, source_target_pairs={{0,32},{32,0},{1,33},{33,1},{2,34},{34,2},{3,35},{35,3},{4,36},{36... | collective-permute-start | bytes 12582920 | tf_op jit(solution)/shard_map/ppermute | solution.py:84
Sparse Core Ops, SparseCore 0:
  25.7 56.1 reduce-scatter.1
  116.5 49.2 all-gather.2

commit v21 on v19

--- a/solution.py
+++ b/solution.py
@@ -11,6 +11,7 @@
 FREQS = 8
 GRID = 1024
 NODE_TILE = 512
+FREQ_BLOCK = 2
 
 
 def unit_phasor(turn):
@@ -86,8 +87,6 @@
 
 
 def spec_kernel(core_ref, rows_ref, mine_ref, theirs_ref, out_ref):
-    rows = rows_ref[0]
-    rows_im = jnp.concatenate([rows[:, DIRS:], -rows[:, :DIRS]], axis=1)
     first = core_ref[0] == 0
     contract = (((1,), (1,)), ((), ()))
 
@@ -96,32 +95,37 @@
 
     zlo_count = mine_ref.shape[1]
     block = 2 * mine_ref.shape[0] * mine_ref.shape[3]
-    for z in range(zlo_count):
-        own = mine_ref[:, z, 0].reshape(-1, mine_ref.shape[-1])
-        other = theirs_ref[:, z, 0].reshape(-1, mine_ref.shape[-1])
-        cols = jnp.where(
-            first, jnp.concatenate([own, other], axis=0), jnp.concatenate([other, own], axis=0)
-        )
-        out_ref[0, 0, :, z * block : (z + 1) * block] = dot(rows, cols)
-        out_ref[1, 0, :, z * block : (z + 1) * block] = dot(rows_im, cols)
+    for g in range(rows_ref.shape[0]):
+        rows = rows_ref[g]
+        rows_im = jnp.concatenate([rows[:, DIRS:], -rows[:, :DIRS]], axis=1)
+        for z in range(zlo_count):
+            own = mine_ref[:, z, g].reshape(-1, mine_ref.shape[-1])
+            other = theirs_ref[:, z, g].reshape(-1, mine_ref.shape[-1])
+            cols = jnp.where(
+                first,
+                jnp.concatenate([own, other], axis=0),
+                jnp.concatenate([other, own], axis=0),
+            )
+            out_ref[0, g, :, z * block : (z + 1) * block] = dot(rows, cols)
+            out_ref[1, g, :, z * block : (z + 1) * block] = dot(rows_im, cols)
 
 
 def cross_spectra(rows, mine, theirs):
     freqs, row_count, width = rows.shape
     col_count = 2 * mine.shape[0] * mine.shape[1] * mine.shape[3]
     core = lax.axis_index("core").astype(jnp.int32).reshape(1)
-    col_spec = pl.BlockSpec(mine.shape[:2] + (1,) + mine.shape[3:], lambda f: (0, 0, f, 0, 0))
+    col_spec = pl.BlockSpec(mine.shape[:2] + (FREQ_BLOCK,) + mine.shape[3:], lambda f: (0, 0, f, 0, 0))
     return pl.pallas_call(
         spec_kernel,
         out_shape=jax.ShapeDtypeStruct((2, freqs, row_count, col_count), jnp.float32),
-        grid=(freqs,),
+        grid=(freqs // FREQ_BLOCK,),
         in_specs=[
             pl.BlockSpec(memory_space=pltpu.SMEM),
-            pl.BlockSpec((1, row_count, width), lambda f: (f, 0, 0)),
+            pl.BlockSpec((FREQ_BLOCK, row_count, width), lambda f: (f, 0, 0)),
             col_spec,
             col_spec,
         ],
-        out_specs=pl.BlockSpec((2, 1, row_count, col_count), lambda f: (0, f, 0, 0)),
+        out_specs=pl.BlockSpec((2, FREQ_BLOCK, row_count, col_count), lambda f: (0, f, 0, 0)),
         compiler_params=pltpu.CompilerParams(dimension_semantics=("arbitrary",)),
     )(core, rows, mine, theirs)
 

time: 195 us -> 193 us (0.990)
  no operation moved by 1% of the time
where the time goes in v21:
time: 193 us
  waiting for transfers between devices  123 us (64%)
  Pallas kernels  23.2 us (12%)
  starting transfers between devices  20.4 us (11%)
  between operations  13.4 us (7%)
  other arithmetic  9.98 us (5%)
  local copies, waits for them, and re-layouts  3.11 us (2%)
    reduce_scatter x1, waiting for transfers between devices, local(): lax.psum_scatter(partial_amp, ('zlo', 'core'), scatter_dimension=1, tiled...  56.3 us
    ppermute x4, waiting for transfers between devices, from_other_half(): ahead.append(lax.ppermute(piece, ('zhi', 'y'), perm=perm))  38.4 us
    ppermute x6, waiting for transfers between devices, gather_by_permutes(): lax.ppermute(piece, axis_name, perm=[(i, (i - shift) % count) for i in ra...  22.6 us
    pallas_call x1, Pallas kernels, partial_amplitudes(): pl.pallas_call(amp_kernel, out_shape=jax.ShapeDtypeStruct((FREQS, rows, 2...  14.4 us
    ppermute x4, starting transfers between devices, from_other_half(): ahead.append(lax.ppermute(piece, ('zhi', 'y'), perm=perm))  12.5 us
    pallas_call x1, Pallas kernels, cross_spectra(): pl.pallas_call(spec_kernel, out_shape=jax.ShapeDtypeStruct((2, freqs, row...  8.76 us
    ppermute x6, starting transfers between devices, gather_by_permutes(): lax.ppermute(piece, axis_name, perm=[(i, (i - shift) % count) for i in ra...  6.46 us
    ppermute x1, waiting for transfers between devices, gather_cols(): theirs = lax.ppermute(mine, 'core', perm=[(0, 1), (1, 0)])  5.22 us
  transfers between devices with their start and end apart: 13, of which 10 were waited for; matrix products, arithmetic and copies ran while one was open for 2% of the time, Pallas kernels for 0%

profile of v21, /device:TPU:33, one launch (start us, length us, event | category | flops | bytes accessed | tf_op | source)
XLA Modules:
  0.0 192.7 jit_solution(10848301038531160571)
XLA Ops:
  6.5 0.8 fusion.22
  7.3 0.8 fusion.21
  8.1 1.3 multiply_sqrt_fusion.spread_ref
  9.4 1.7 multiply_add_fusion.proj_ref
  11.1 14.4 %shard_map.46 = f32[8,128,1024]{2,1,0:T(8,128)} custom-call(s32[1024,512]{1,0:T(8,128)} %multiply_add_fusion.proj_ref, f32[8,512]{1,0:T(8,128)} %multiply_sqrt_fusion.spread_ref, bf16[2,8,128,1024]{3,2,1,0:T(8,128)(2,1)} %resp_ref.1), custom_call_target="tpu_custom_call" | custom-call | tf_op jit(solution)/shard_map/pallas_call | solution.py:62
  25.6 56.3 %reduce-scatter.2.cloned.1.call-done = f32[8,16,1024]{2,1,0:T(8,128)} async-done(((f32[8,128,1024]{2,1,0:T(8,128)}), f32[8,16,1024]{2,1,0:T(8,128)}) %reduce-scatter.2.cloned.1.call-update) | async-done | bytes 524304 | tf_op jit(solution)/shard_map/reduce_scatter | solution.py:172
  81.9 1.1 convert_element_type.7
  83.0 1.3 collective-permute-start.5
  84.2 2.4 %collective-permute-start.4 = (bf16[8,16,1024]{2,1,0:T(8,128)(2,1)S(1)}, bf16[8,16,1024]{2,1,0:T(8,128)(2,1)S(1)}, u32[]{:S(2)}, u32[]{:S(2)}) collective-permute-start(bf16[8,16,1024]{2,1,0:T(8,128)(2,1)S(1)} %convert_element_type.7), channel_id=1, source_target_pairs={{0,2},{1,3},{2,0},{3,1},{4,6},{5,7},{6,4},{7,5},{8,10},{9,11},{10,... | collective-permute-start | bytes 786440 | tf_op jit(solution)/shard_map/ppermute | solution.py:137
  86.7 1.2 collective-permute-start.3
  87.8 1.2 collective-permute-start.2
  89.1 0.4 collective-permute-start.1
  89.4 1.4 collective-permute-done.5
  90.9 1.1 convert_bitcast_fusion
  91.9 6.0 %collective-permute-done.4 = bf16[8,16,1024]{2,1,0:T(8,128)(2,1)S(1)} collective-permute-done((bf16[8,16,1024]{2,1,0:T(8,128)(2,1)S(1)}, bf16[8,16,1024]{2,1,0:T(8,128)(2,1)S(1)}, u32[]{:S(2)}, u32[]{:S(2)}) %collective-permute-start.4) | collective-permute-done | bytes 262176 | tf_op jit(solution)/shard_map/ppermute | solution.py:137
  97.9 14.1 %collective-permute-done.1 = bf16[8,16,1024]{2,1,0:T(8,128)(2,1)S(1)} collective-permute-done((bf16[8,16,1024]{2,1,0:T(8,128)(2,1)S(1)}, bf16[8,16,1024]{2,1,0:T(8,128)(2,1)S(1)}, u32[]{:S(2)}, u32[]{:S(2)}) %collective-permute-start.1) | collective-permute-done | bytes 262176 | tf_op jit(solution)/shard_map/ppermute | solution.py:137
  112.1 1.0 collective-permute-done
  113.1 3.3 %fusion.10 = (bf16[4,8,16,1024]{3,2,1,0:T(8,128)(2,1)S(1)}, bf16[4,8,16,1024]{3,2,1,0:T(8,128)(2,1)}) fusion(s32[]{:T(128)S(6)} %select_n.32, bf16[1,8,16,1024]{3,2,1,0:T(8,128)(2,1)S(1)} %bitcast.35, bf16[1,8,16,1024]{3,2,1,0:T(8,128)(2,1)S(1)} %bitcast.34, bf16[1,8,16,1024]{3,2,1,0:T(8,128)(2,1)S(1)} %bitcast.33, ...), kind=kLoop, calls=%fused_computation.36 | loop fusion | flops 7340032 | bytes 3932168 | tf_op jit(solution)/shard_map/jit(_roll_dynamic)/concatenate | solution.py:139
  116.4 4.8 %collective-permute-start.9 = (bf16[8,16,1024]{2,1,0:T(8,128)(2,1)S(1)}, bf16[8,16,1024]{2,1,0:T(8,128)(2,1)S(1)}, u32[]{:S(2)}, u32[]{:S(2)}) collective-permute-start(bf16[8,16,1024]{2,1,0:T(8,128)(2,1)S(1)} %convert_element_type.7), channel_id=1, source_target_pairs={{0,5},{1,6},{2,7},{3,4},{4,1},{5,2},{6,3},{7,0},{8,13},{9,14},{10,... | collective-permute-start | bytes 786440 | tf_op jit(solution)/shard_map/ppermute | solution.py:153
  121.2 1.5 collective-permute-start.8
  122.7 5.3 %collective-permute-start.7 = (bf16[8,16,1024]{2,1,0:T(8,128)(2,1)S(1)}, bf16[8,16,1024]{2,1,0:T(8,128)(2,1)S(1)}, u32[]{:S(2)}, u32[]{:S(2)}) collective-permute-start(bf16[8,16,1024]{2,1,0:T(8,128)(2,1)S(1)} %convert_element_type.7), channel_id=1, source_target_pairs={{0,7},{1,4},{2,5},{3,6},{4,3},{5,0},{6,1},{7,2},{8,15},{9,12},{10,... | collective-permute-start | bytes 786440 | tf_op jit(solution)/shard_map/ppermute | solution.py:153
  128.0 0.9 collective-permute-start.6
  128.9 7.7 %collective-permute-done.9 = bf16[8,16,1024]{2,1,0:T(8,128)(2,1)S(1)} collective-permute-done((bf16[8,16,1024]{2,1,0:T(8,128)(2,1)S(1)}, bf16[8,16,1024]{2,1,0:T(8,128)(2,1)S(1)}, u32[]{:S(2)}, u32[]{:S(2)}) %collective-permute-start.9) | collective-permute-done | bytes 262176 | tf_op jit(solution)/shard_map/ppermute | solution.py:153
  136.6 20.4 %collective-permute-done.8 = bf16[8,16,1024]{2,1,0:T(8,128)(2,1)S(1)} collective-permute-done((bf16[8,16,1024]{2,1,0:T(8,128)(2,1)S(1)}, bf16[8,16,1024]{2,1,0:T(8,128)(2,1)S(1)}, u32[]{:S(2)}, u32[]{:S(2)}) %collective-permute-start.8) | collective-permute-done | bytes 262176 | tf_op jit(solution)/shard_map/ppermute | solution.py:153
  157.1 3.9 %collective-permute-done.7 = bf16[8,16,1024]{2,1,0:T(8,128)(2,1)S(1)} collective-permute-done((bf16[8,16,1024]{2,1,0:T(8,128)(2,1)S(1)}, bf16[8,16,1024]{2,1,0:T(8,128)(2,1)S(1)}, u32[]{:S(2)}, u32[]{:S(2)}) %collective-permute-start.7) | collective-permute-done | bytes 262176 | tf_op jit(solution)/shard_map/ppermute | solution.py:153
  160.9 6.4 %collective-permute-done.6 = bf16[8,16,1024]{2,1,0:T(8,128)(2,1)S(1)} collective-permute-done((bf16[8,16,1024]{2,1,0:T(8,128)(2,1)S(1)}, bf16[8,16,1024]{2,1,0:T(8,128)(2,1)S(1)}, u32[]{:S(2)}, u32[]{:S(2)}) %collective-permute-start.6) | collective-permute-done | bytes 262176 | tf_op jit(solution)/shard_map/ppermute | solution.py:153
  167.3 1.2 fusion.3
  168.6 1.4 collective-permute-start.10
  170.0 0.3 maximum_select_fusion
  170.3 1.6 copy.7
  171.9 5.2 %collective-permute-done.10.theirs_ref = bf16[4,4,8,16,1024]{4,3,2,1,0:T(8,128)(2,1)} collective-permute-done((bf16[4,4,8,16,1024]{4,3,2,1,0:T(8,128)(2,1)}, bf16[4,4,8,16,1024]{4,3,2,1,0:T(8,128)(2,1)}, u32[]{:S(2)}, u32[]{:S(2)}) %collective-permute-start.10) | collective-permute-done | bytes 4194336 | tf_op jit(solution)/shard_map/ppermute | solution.py:85
  177.1 8.8 %shard_map.47 = f32[2,8,128,512]{3,2,1,0:T(8,128)} custom-call(s32[1]{0:T(128)} %bitcast.core_ref, bf16[8,128,1024]{2,1,0:T(8,128)(2,1)} %bitcast.28, bf16[4,4,8,16,1024]{4,3,2,1,0:T(8,128)(2,1)} %bitcast.30, bf16[4,4,8,16,1024]{4,3,2,1,0:T(8,128)(2,1)} %collective-permute-done.10.theirs_ref), custom_call_target="tpu_custom_call" | custom-call | tf_op jit(solution)/shard_map/pallas_call | solution.py:118
  (8 shorter events, 0.1 us)
Async XLA Ops:
  6.5 75.4 %reduce-scatter.2.cloned.1.call-start = ((), (), s32[]{:S(2)}) async-start(), calls=%async_computation.1 | async-start | bytes 4718592 | tf_op jit(solution)/shard_map/reduce_scatter | solution.py:172
  25.5 143.0 %all-gather.3.cloned.1.call-start = ((), (), s32[]{:S(2)}) async-start(), calls=%async_computation.2 | async-start | bytes 5242880 | tf_op jit(solution)/shard_map/all_gather | solution.py:82
  83.0 7.9 %collective-permute-start.5 = (bf16[8,16,1024]{2,1,0:T(8,128)(2,1)S(1)}, bf16[8,16,1024]{2,1,0:T(8,128)(2,1)S(1)}, u32[]{:S(2)}, u32[]{:S(2)}) collective-permute-start(bf16[8,16,1024]{2,1,0:T(8,128)(2,1)S(1)} %convert_element_type.7), channel_id=1, source_target_pairs={{0,1},{1,2},{2,3},{3,0},{4,5},{5,6},{6,7},{7,4},{8,9},{9,10},{10,1... | collective-permute-start | bytes 786440 | tf_op jit(solution)/shard_map/ppermute | solution.py:137
  84.2 13.7 %collective-permute-start.4 = (bf16[8,16,1024]{2,1,0:T(8,128)(2,1)S(1)}, bf16[8,16,1024]{2,1,0:T(8,128)(2,1)S(1)}, u32[]{:S(2)}, u32[]{:S(2)}) collective-permute-start(bf16[8,16,1024]{2,1,0:T(8,128)(2,1)S(1)} %convert_element_type.7), channel_id=1, source_target_pairs={{0,2},{1,3},{2,0},{3,1},{4,6},{5,7},{6,4},{7,5},{8,10},{9,11},{10,... | collective-permute-start | bytes 786440 | tf_op jit(solution)/shard_map/ppermute | solution.py:137
  86.7 11.2 %collective-permute-start.3 = (bf16[8,16,1024]{2,1,0:T(8,128)(2,1)S(1)}, bf16[8,16,1024]{2,1,0:T(8,128)(2,1)S(1)}, u32[]{:S(2)}, u32[]{:S(2)}) collective-permute-start(bf16[8,16,1024]{2,1,0:T(8,128)(2,1)S(1)} %convert_element_type.7), channel_id=1, source_target_pairs={{0,3},{1,0},{2,1},{3,2},{4,7},{5,4},{6,5},{7,6},{8,11},{9,8},{10,9... | collective-permute-start | bytes 786440 | tf_op jit(solution)/shard_map/ppermute | solution.py:137
  87.8 10.1 %collective-permute-start.2 = (bf16[8,16,1024]{2,1,0:T(8,128)(2,1)S(1)}, bf16[8,16,1024]{2,1,0:T(8,128)(2,1)S(1)}, u32[]{:S(2)}, u32[]{:S(2)}) collective-permute-start(bf16[8,16,1024]{2,1,0:T(8,128)(2,1)S(1)} %convert_element_type.7), channel_id=1, source_target_pairs={{0,64},{64,128},{128,192},{192,0},{1,65},{65,129},{129,193},{193,1... | collective-permute-start | bytes 786440 | tf_op jit(solution)/shard_map/ppermute | solution.py:137
  89.1 23.0 %collective-permute-start.1 = (bf16[8,16,1024]{2,1,0:T(8,128)(2,1)S(1)}, bf16[8,16,1024]{2,1,0:T(8,128)(2,1)S(1)}, u32[]{:S(2)}, u32[]{:S(2)}) collective-permute-start(bf16[8,16,1024]{2,1,0:T(8,128)(2,1)S(1)} %convert_element_type.7), channel_id=1, source_target_pairs={{0,128},{64,192},{128,0},{192,64},{1,129},{65,193},{129,1},{193,65... | collective-permute-start | bytes 786440 | tf_op jit(solution)/shard_map/ppermute | solution.py:137
  90.9 22.2 %collective-permute-start = (bf16[8,16,1024]{2,1,0:T(8,128)(2,1)S(1)}, bf16[8,16,1024]{2,1,0:T(8,128)(2,1)S(1)}, u32[]{:S(2)}, u32[]{:S(2)}) collective-permute-start(bf16[8,16,1024]{2,1,0:T(8,128)(2,1)S(1)} %convert_element_type.7), channel_id=1, source_target_pairs={{0,192},{64,0},{128,64},{192,128},{1,193},{65,1},{129,65},{193,129... | collective-permute-start | bytes 786440 | tf_op jit(solution)/shard_map/ppermute | solution.py:137
  116.4 20.2 %collective-permute-start.9 = (bf16[8,16,1024]{2,1,0:T(8,128)(2,1)S(1)}, bf16[8,16,1024]{2,1,0:T(8,128)(2,1)S(1)}, u32[]{:S(2)}, u32[]{:S(2)}) collective-permute-start(bf16[8,16,1024]{2,1,0:T(8,128)(2,1)S(1)} %convert_element_type.7), channel_id=1, source_target_pairs={{0,5},{1,6},{2,7},{3,4},{4,1},{5,2},{6,3},{7,0},{8,13},{9,14},{10,... | collective-permute-start | bytes 786440 | tf_op jit(solution)/shard_map/ppermute | solution.py:153
  121.2 35.9 %collective-permute-start.8 = (bf16[8,16,1024]{2,1,0:T(8,128)(2,1)S(1)}, bf16[8,16,1024]{2,1,0:T(8,128)(2,1)S(1)}, u32[]{:S(2)}, u32[]{:S(2)}) collective-permute-start(bf16[8,16,1024]{2,1,0:T(8,128)(2,1)S(1)} %convert_element_type.7), channel_id=1, source_target_pairs={{0,6},{1,7},{2,4},{3,5},{4,2},{5,3},{6,0},{7,1},{8,14},{9,15},{10,... | collective-permute-start | bytes 786440 | tf_op jit(solution)/shard_map/ppermute | solution.py:153
  122.7 38.3 %collective-permute-start.7 = (bf16[8,16,1024]{2,1,0:T(8,128)(2,1)S(1)}, bf16[8,16,1024]{2,1,0:T(8,128)(2,1)S(1)}, u32[]{:S(2)}, u32[]{:S(2)}) collective-permute-start(bf16[8,16,1024]{2,1,0:T(8,128)(2,1)S(1)} %convert_element_type.7), channel_id=1, source_target_pairs={{0,7},{1,4},{2,5},{3,6},{4,3},{5,0},{6,1},{7,2},{8,15},{9,12},{10,... | collective-permute-start | bytes 786440 | tf_op jit(solution)/shard_map/ppermute | solution.py:153
  128.0 39.3 %collective-permute-start.6 = (bf16[8,16,1024]{2,1,0:T(8,128)(2,1)S(1)}, bf16[8,16,1024]{2,1,0:T(8,128)(2,1)S(1)}, u32[]{:S(2)}, u32[]{:S(2)}) collective-permute-start(bf16[8,16,1024]{2,1,0:T(8,128)(2,1)S(1)} %convert_element_type.7), channel_id=1, source_target_pairs={{0,4},{1,5},{2,6},{3,7},{4,0},{5,1},{6,2},{7,3},{8,12},{9,13},{10,... | collective-permute-start | bytes 786440 | tf_op jit(solution)/shard_map/ppermute | solution.py:153
  168.6 8.6 %collective-permute-start.10 = (bf16[4,4,8,16,1024]{4,3,2,1,0:T(8,128)(2,1)}, bf16[4,4,8,16,1024]{4,3,2,1,0:T(8,128)(2,1)}, u32[]{:S(2)}, u32[]{:S(2)}) collective-permute-start(bf16[4,4,8,16,1024]{4,3,2,1,0:T(8,128)(2,1)} %bitcast.29), channel_id=1, source_target_pairs={{0,32},{32,0},{1,33},{33,1},{2,34},{34,2},{3,35},{35,3},{4,36},{36... | collective-permute-start | bytes 12582920 | tf_op jit(solution)/shard_map/ppermute | solution.py:85
Sparse Core Ops, SparseCore 0:
  25.7 56.1 reduce-scatter.1
  116.5 49.2 all-gather.2

commit v22 on v21

--- a/solution.py
+++ b/solution.py
@@ -11,7 +11,7 @@
 FREQS = 8
 GRID = 1024
 NODE_TILE = 512
-FREQ_BLOCK = 2
+FREQ_BLOCK = 4
 
 
 def unit_phasor(turn):

time: 193 us -> 193 us (level)
  no operation moved by 1% of the time
where the time goes in v22:
time: 193 us
  waiting for transfers between devices  123 us (64%)
  Pallas kernels  23 us (12%)
  starting transfers between devices  20.4 us (11%)
  between operations  13.4 us (7%)
  other arithmetic  9.98 us (5%)
  local copies, waits for them, and re-layouts  3.11 us (2%)
    reduce_scatter x1, waiting for transfers between devices, local(): lax.psum_scatter(partial_amp, ('zlo', 'core'), scatter_dimension=1, tiled...  56.3 us
    ppermute x4, waiting for transfers between devices, from_other_half(): ahead.append(lax.ppermute(piece, ('zhi', 'y'), perm=perm))  38.4 us
    ppermute x6, waiting for transfers between devices, gather_by_permutes(): lax.ppermute(piece, axis_name, perm=[(i, (i - shift) % count) for i in ra...  22.6 us
    pallas_call x1, Pallas kernels, partial_amplitudes(): pl.pallas_call(amp_kernel, out_shape=jax.ShapeDtypeStruct((FREQS, rows, 2...  14.4 us
    ppermute x4, starting transfers between devices, from_other_half(): ahead.append(lax.ppermute(piece, ('zhi', 'y'), perm=perm))  12.5 us
    pallas_call x1, Pallas kernels, cross_spectra(): pl.pallas_call(spec_kernel, out_shape=jax.ShapeDtypeStruct((2, freqs, row...  8.6 us
    ppermute x6, starting transfers between devices, gather_by_permutes(): lax.ppermute(piece, axis_name, perm=[(i, (i - shift) % count) for i in ra...  6.46 us
    ppermute x1, waiting for transfers between devices, gather_cols(): theirs = lax.ppermute(mine, 'core', perm=[(0, 1), (1, 0)])  5.22 us
  transfers between devices with their start and end apart: 13, of which 10 were waited for; matrix products, arithmetic and copies ran while one was open for 2% of the time, Pallas kernels for 0%

profile of v22, /device:TPU:33, one launch (start us, length us, event | category | flops | bytes accessed | tf_op | source)
XLA Modules:
  0.0 192.6 jit_solution(10811725349207522024)
XLA Ops:
  6.5 0.8 fusion.22
  7.3 0.8 fusion.21
  8.1 1.3 multiply_sqrt_fusion.spread_ref
  9.4 1.7 multiply_add_fusion.proj_ref
  11.1 14.4 %shard_map.46 = f32[8,128,1024]{2,1,0:T(8,128)} custom-call(s32[1024,512]{1,0:T(8,128)} %multiply_add_fusion.proj_ref, f32[8,512]{1,0:T(8,128)} %multiply_sqrt_fusion.spread_ref, bf16[2,8,128,1024]{3,2,1,0:T(8,128)(2,1)} %resp_ref.1), custom_call_target="tpu_custom_call" | custom-call | tf_op jit(solution)/shard_map/pallas_call | solution.py:62
  25.6 56.3 %reduce-scatter.2.cloned.1.call-done = f32[8,16,1024]{2,1,0:T(8,128)} async-done(((f32[8,128,1024]{2,1,0:T(8,128)}), f32[8,16,1024]{2,1,0:T(8,128)}) %reduce-scatter.2.cloned.1.call-update) | async-done | bytes 524304 | tf_op jit(solution)/shard_map/reduce_scatter | solution.py:172
  81.9 1.1 convert_element_type.7
  83.0 1.3 collective-permute-start.5
  84.2 2.4 %collective-permute-start.4 = (bf16[8,16,1024]{2,1,0:T(8,128)(2,1)S(1)}, bf16[8,16,1024]{2,1,0:T(8,128)(2,1)S(1)}, u32[]{:S(2)}, u32[]{:S(2)}) collective-permute-start(bf16[8,16,1024]{2,1,0:T(8,128)(2,1)S(1)} %convert_element_type.7), channel_id=1, source_target_pairs={{0,2},{1,3},{2,0},{3,1},{4,6},{5,7},{6,4},{7,5},{8,10},{9,11},{10,... | collective-permute-start | bytes 786440 | tf_op jit(solution)/shard_map/ppermute | solution.py:137
  86.7 1.2 collective-permute-start.3
  87.8 1.2 collective-permute-start.2
  89.1 0.4 collective-permute-start.1
  89.4 1.4 collective-permute-done.5
  90.9 1.1 convert_bitcast_fusion
  91.9 6.0 %collective-permute-done.4 = bf16[8,16,1024]{2,1,0:T(8,128)(2,1)S(1)} collective-permute-done((bf16[8,16,1024]{2,1,0:T(8,128)(2,1)S(1)}, bf16[8,16,1024]{2,1,0:T(8,128)(2,1)S(1)}, u32[]{:S(2)}, u32[]{:S(2)}) %collective-permute-start.4) | collective-permute-done | bytes 262176 | tf_op jit(solution)/shard_map/ppermute | solution.py:137
  97.9 14.1 %collective-permute-done.1 = bf16[8,16,1024]{2,1,0:T(8,128)(2,1)S(1)} collective-permute-done((bf16[8,16,1024]{2,1,0:T(8,128)(2,1)S(1)}, bf16[8,16,1024]{2,1,0:T(8,128)(2,1)S(1)}, u32[]{:S(2)}, u32[]{:S(2)}) %collective-permute-start.1) | collective-permute-done | bytes 262176 | tf_op jit(solution)/shard_map/ppermute | solution.py:137
  112.1 1.0 collective-permute-done
  113.1 3.3 %fusion.10 = (bf16[4,8,16,1024]{3,2,1,0:T(8,128)(2,1)S(1)}, bf16[4,8,16,1024]{3,2,1,0:T(8,128)(2,1)}) fusion(s32[]{:T(128)S(6)} %select_n.32, bf16[1,8,16,1024]{3,2,1,0:T(8,128)(2,1)S(1)} %bitcast.35, bf16[1,8,16,1024]{3,2,1,0:T(8,128)(2,1)S(1)} %bitcast.34, bf16[1,8,16,1024]{3,2,1,0:T(8,128)(2,1)S(1)} %bitcast.33, ...), kind=kLoop, calls=%fused_computation.36 | loop fusion | flops 7340032 | bytes 3932168 | tf_op jit(solution)/shard_map/jit(_roll_dynamic)/concatenate | solution.py:139
  116.4 4.8 %collective-permute-start.9 = (bf16[8,16,1024]{2,1,0:T(8,128)(2,1)S(1)}, bf16[8,16,1024]{2,1,0:T(8,128)(2,1)S(1)}, u32[]{:S(2)}, u32[]{:S(2)}) collective-permute-start(bf16[8,16,1024]{2,1,0:T(8,128)(2,1)S(1)} %convert_element_type.7), channel_id=1, source_target_pairs={{0,5},{1,6},{2,7},{3,4},{4,1},{5,2},{6,3},{7,0},{8,13},{9,14},{10,... | collective-permute-start | bytes 786440 | tf_op jit(solution)/shard_map/ppermute | solution.py:153
  121.2 1.5 collective-permute-start.8
  122.7 5.3 %collective-permute-start.7 = (bf16[8,16,1024]{2,1,0:T(8,128)(2,1)S(1)}, bf16[8,16,1024]{2,1,0:T(8,128)(2,1)S(1)}, u32[]{:S(2)}, u32[]{:S(2)}) collective-permute-start(bf16[8,16,1024]{2,1,0:T(8,128)(2,1)S(1)} %convert_element_type.7), channel_id=1, source_target_pairs={{0,7},{1,4},{2,5},{3,6},{4,3},{5,0},{6,1},{7,2},{8,15},{9,12},{10,... | collective-permute-start | bytes 786440 | tf_op jit(solution)/shard_map/ppermute | solution.py:153
  128.0 0.9 collective-permute-start.6
  128.9 7.7 %collective-permute-done.9 = bf16[8,16,1024]{2,1,0:T(8,128)(2,1)S(1)} collective-permute-done((bf16[8,16,1024]{2,1,0:T(8,128)(2,1)S(1)}, bf16[8,16,1024]{2,1,0:T(8,128)(2,1)S(1)}, u32[]{:S(2)}, u32[]{:S(2)}) %collective-permute-start.9) | collective-permute-done | bytes 262176 | tf_op jit(solution)/shard_map/ppermute | solution.py:153
  136.6 20.4 %collective-permute-done.8 = bf16[8,16,1024]{2,1,0:T(8,128)(2,1)S(1)} collective-permute-done((bf16[8,16,1024]{2,1,0:T(8,128)(2,1)S(1)}, bf16[8,16,1024]{2,1,0:T(8,128)(2,1)S(1)}, u32[]{:S(2)}, u32[]{:S(2)}) %collective-permute-start.8) | collective-permute-done | bytes 262176 | tf_op jit(solution)/shard_map/ppermute | solution.py:153
  157.1 3.9 %collective-permute-done.7 = bf16[8,16,1024]{2,1,0:T(8,128)(2,1)S(1)} collective-permute-done((bf16[8,16,1024]{2,1,0:T(8,128)(2,1)S(1)}, bf16[8,16,1024]{2,1,0:T(8,128)(2,1)S(1)}, u32[]{:S(2)}, u32[]{:S(2)}) %collective-permute-start.7) | collective-permute-done | bytes 262176 | tf_op jit(solution)/shard_map/ppermute | solution.py:153
  160.9 6.4 %collective-permute-done.6 = bf16[8,16,1024]{2,1,0:T(8,128)(2,1)S(1)} collective-permute-done((bf16[8,16,1024]{2,1,0:T(8,128)(2,1)S(1)}, bf16[8,16,1024]{2,1,0:T(8,128)(2,1)S(1)}, u32[]{:S(2)}, u32[]{:S(2)}) %collective-permute-start.6) | collective-permute-done | bytes 262176 | tf_op jit(solution)/shard_map/ppermute | solution.py:153
  167.3 1.2 fusion.3
  168.6 1.4 collective-permute-start.10
  170.0 0.3 maximum_select_fusion
  170.3 1.6 copy.7
  171.9 5.2 %collective-permute-done.10.theirs_ref = bf16[4,4,8,16,1024]{4,3,2,1,0:T(8,128)(2,1)} collective-permute-done((bf16[4,4,8,16,1024]{4,3,2,1,0:T(8,128)(2,1)}, bf16[4,4,8,16,1024]{4,3,2,1,0:T(8,128)(2,1)}, u32[]{:S(2)}, u32[]{:S(2)}) %collective-permute-start.10) | collective-permute-done | bytes 4194336 | tf_op jit(solution)/shard_map/ppermute | solution.py:85
  177.1 8.6 %shard_map.47 = f32[2,8,128,512]{3,2,1,0:T(8,128)} custom-call(s32[1]{0:T(128)} %bitcast.core_ref, bf16[8,128,1024]{2,1,0:T(8,128)(2,1)} %bitcast.28, bf16[4,4,8,16,1024]{4,3,2,1,0:T(8,128)(2,1)} %bitcast.30, bf16[4,4,8,16,1024]{4,3,2,1,0:T(8,128)(2,1)} %collective-permute-done.10.theirs_ref), custom_call_target="tpu_custom_call" | custom-call | tf_op jit(solution)/shard_map/pallas_call | solution.py:118
  (8 shorter events, 0.1 us)
Async XLA Ops:
  6.5 75.4 %reduce-scatter.2.cloned.1.call-start = ((), (), s32[]{:S(2)}) async-start(), calls=%async_computation.1 | async-start | bytes 4718592 | tf_op jit(solution)/shard_map/reduce_scatter | solution.py:172
  25.5 143.0 %all-gather.3.cloned.1.call-start = ((), (), s32[]{:S(2)}) async-start(), calls=%async_computation.2 | async-start | bytes 5242880 | tf_op jit(solution)/shard_map/all_gather | solution.py:82
  83.0 7.9 %collective-permute-start.5 = (bf16[8,16,1024]{2,1,0:T(8,128)(2,1)S(1)}, bf16[8,16,1024]{2,1,0:T(8,128)(2,1)S(1)}, u32[]{:S(2)}, u32[]{:S(2)}) collective-permute-start(bf16[8,16,1024]{2,1,0:T(8,128)(2,1)S(1)} %convert_element_type.7), channel_id=1, source_target_pairs={{0,1},{1,2},{2,3},{3,0},{4,5},{5,6},{6,7},{7,4},{8,9},{9,10},{10,1... | collective-permute-start | bytes 786440 | tf_op jit(solution)/shard_map/ppermute | solution.py:137
  84.2 13.7 %collective-permute-start.4 = (bf16[8,16,1024]{2,1,0:T(8,128)(2,1)S(1)}, bf16[8,16,1024]{2,1,0:T(8,128)(2,1)S(1)}, u32[]{:S(2)}, u32[]{:S(2)}) collective-permute-start(bf16[8,16,1024]{2,1,0:T(8,128)(2,1)S(1)} %convert_element_type.7), channel_id=1, source_target_pairs={{0,2},{1,3},{2,0},{3,1},{4,6},{5,7},{6,4},{7,5},{8,10},{9,11},{10,... | collective-permute-start | bytes 786440 | tf_op jit(solution)/shard_map/ppermute | solution.py:137
  86.7 11.2 %collective-permute-start.3 = (bf16[8,16,1024]{2,1,0:T(8,128)(2,1)S(1)}, bf16[8,16,1024]{2,1,0:T(8,128)(2,1)S(1)}, u32[]{:S(2)}, u32[]{:S(2)}) collective-permute-start(bf16[8,16,1024]{2,1,0:T(8,128)(2,1)S(1)} %convert_element_type.7), channel_id=1, source_target_pairs={{0,3},{1,0},{2,1},{3,2},{4,7},{5,4},{6,5},{7,6},{8,11},{9,8},{10,9... | collective-permute-start | bytes 786440 | tf_op jit(solution)/shard_map/ppermute | solution.py:137
  87.8 10.1 %collective-permute-start.2 = (bf16[8,16,1024]{2,1,0:T(8,128)(2,1)S(1)}, bf16[8,16,1024]{2,1,0:T(8,128)(2,1)S(1)}, u32[]{:S(2)}, u32[]{:S(2)}) collective-permute-start(bf16[8,16,1024]{2,1,0:T(8,128)(2,1)S(1)} %convert_element_type.7), channel_id=1, source_target_pairs={{0,64},{64,128},{128,192},{192,0},{1,65},{65,129},{129,193},{193,1... | collective-permute-start | bytes 786440 | tf_op jit(solution)/shard_map/ppermute | solution.py:137
  89.1 23.0 %collective-permute-start.1 = (bf16[8,16,1024]{2,1,0:T(8,128)(2,1)S(1)}, bf16[8,16,1024]{2,1,0:T(8,128)(2,1)S(1)}, u32[]{:S(2)}, u32[]{:S(2)}) collective-permute-start(bf16[8,16,1024]{2,1,0:T(8,128)(2,1)S(1)} %convert_element_type.7), channel_id=1, source_target_pairs={{0,128},{64,192},{128,0},{192,64},{1,129},{65,193},{129,1},{193,65... | collective-permute-start | bytes 786440 | tf_op jit(solution)/shard_map/ppermute | solution.py:137
  90.9 22.2 %collective-permute-start = (bf16[8,16,1024]{2,1,0:T(8,128)(2,1)S(1)}, bf16[8,16,1024]{2,1,0:T(8,128)(2,1)S(1)}, u32[]{:S(2)}, u32[]{:S(2)}) collective-permute-start(bf16[8,16,1024]{2,1,0:T(8,128)(2,1)S(1)} %convert_element_type.7), channel_id=1, source_target_pairs={{0,192},{64,0},{128,64},{192,128},{1,193},{65,1},{129,65},{193,129... | collective-permute-start | bytes 786440 | tf_op jit(solution)/shard_map/ppermute | solution.py:137
  116.4 20.2 %collective-permute-start.9 = (bf16[8,16,1024]{2,1,0:T(8,128)(2,1)S(1)}, bf16[8,16,1024]{2,1,0:T(8,128)(2,1)S(1)}, u32[]{:S(2)}, u32[]{:S(2)}) collective-permute-start(bf16[8,16,1024]{2,1,0:T(8,128)(2,1)S(1)} %convert_element_type.7), channel_id=1, source_target_pairs={{0,5},{1,6},{2,7},{3,4},{4,1},{5,2},{6,3},{7,0},{8,13},{9,14},{10,... | collective-permute-start | bytes 786440 | tf_op jit(solution)/shard_map/ppermute | solution.py:153
  121.2 35.9 %collective-permute-start.8 = (bf16[8,16,1024]{2,1,0:T(8,128)(2,1)S(1)}, bf16[8,16,1024]{2,1,0:T(8,128)(2,1)S(1)}, u32[]{:S(2)}, u32[]{:S(2)}) collective-permute-start(bf16[8,16,1024]{2,1,0:T(8,128)(2,1)S(1)} %convert_element_type.7), channel_id=1, source_target_pairs={{0,6},{1,7},{2,4},{3,5},{4,2},{5,3},{6,0},{7,1},{8,14},{9,15},{10,... | collective-permute-start | bytes 786440 | tf_op jit(solution)/shard_map/ppermute | solution.py:153
  122.7 38.3 %collective-permute-start.7 = (bf16[8,16,1024]{2,1,0:T(8,128)(2,1)S(1)}, bf16[8,16,1024]{2,1,0:T(8,128)(2,1)S(1)}, u32[]{:S(2)}, u32[]{:S(2)}) collective-permute-start(bf16[8,16,1024]{2,1,0:T(8,128)(2,1)S(1)} %convert_element_type.7), channel_id=1, source_target_pairs={{0,7},{1,4},{2,5},{3,6},{4,3},{5,0},{6,1},{7,2},{8,15},{9,12},{10,... | collective-permute-start | bytes 786440 | tf_op jit(solution)/shard_map/ppermute | solution.py:153
  128.0 39.3 %collective-permute-start.6 = (bf16[8,16,1024]{2,1,0:T(8,128)(2,1)S(1)}, bf16[8,16,1024]{2,1,0:T(8,128)(2,1)S(1)}, u32[]{:S(2)}, u32[]{:S(2)}) collective-permute-start(bf16[8,16,1024]{2,1,0:T(8,128)(2,1)S(1)} %convert_element_type.7), channel_id=1, source_target_pairs={{0,4},{1,5},{2,6},{3,7},{4,0},{5,1},{6,2},{7,3},{8,12},{9,13},{10,... | collective-permute-start | bytes 786440 | tf_op jit(solution)/shard_map/ppermute | solution.py:153
  168.6 8.6 %collective-permute-start.10 = (bf16[4,4,8,16,1024]{4,3,2,1,0:T(8,128)(2,1)}, bf16[4,4,8,16,1024]{4,3,2,1,0:T(8,128)(2,1)}, u32[]{:S(2)}, u32[]{:S(2)}) collective-permute-start(bf16[4,4,8,16,1024]{4,3,2,1,0:T(8,128)(2,1)} %bitcast.29), channel_id=1, source_target_pairs={{0,32},{32,0},{1,33},{33,1},{2,34},{34,2},{3,35},{35,3},{4,36},{36... | collective-permute-start | bytes 12582920 | tf_op jit(solution)/shard_map/ppermute | solution.py:85
Sparse Core Ops, SparseCore 0:
  25.7 56.1 reduce-scatter.1
  116.5 49.2 all-gather.2
